TPU v7x, 128 devices: a whole 4x4x4 slice. The times are simulated.
128 devices in a mesh: tm: 16 (over y, z), rows: 8 (over x, core).
Axes of the slice: x: 4, y: 4, z: 4, core: 2. Of those that a mesh axis runs over, the one named last changes fastest.
Arguments:
- generator_latent_rows: bfloat16 [16, 64, 2560], P('tm', 'rows'), may hold values from -6 to 6
- slot_group_row: int32 [16, 64], P('tm', 'rows'), may hold values from 0 to 63, each once within a row
- frame_clip_number: int32 [64], replicated, may hold values from 0 to 4, never falling along the last dimension, each value on 1 to 21 neighbouring positions
- input_convolution_weight: bfloat16 [3, 3, 3, 16, 384], replicated, may hold values from -0.3125 to 0.3125
- first_norm_gain: float32 [384], replicated, may hold values from 0.5 to 1.5
- first_convolution_weight: bfloat16 [3, 3, 3, 384, 384], replicated, may hold values from -0.0625 to 0.0625
- second_norm_gain: float32 [384], replicated, may hold values from 0.5 to 1.5
- second_convolution_weight: bfloat16 [3, 3, 3, 384, 384], replicated, may hold values from -0.0625 to 0.0625
Outputs:
- decoded: bfloat16 [64, 16, 160, 384], P('tm', 'rows')
Inputs may be any that keep to these rules, and one draw needn't show every extreme that they name: For each frame group, slot_group_row lists every row index of the group's 4 frames once: slot j holds the group's row (f % 4) * 16 + h.
All inputs are finite; a program needn't handle non-finite values.
Results may differ from a plain program's by a relative error of at most 0.0058.
Values may be sent and summed in bfloat16 or wider, within the bound.
No kernel may reach another device: no remote copies, remote signals or barrier semaphores. Data moves between devices by JAX's collectives and lax.ppermute only.
A program may use at most 128 MiB of HBM per device.

v0:
```python
import functools

import jax
import jax.numpy as jnp
from jax import lax
from jax.experimental import pallas as pl
from jax.experimental.pallas import tpu as pltpu
from jax.sharding import PartitionSpec as P

LATENT_CHANNELS = 16
F_DEV = 4
ID_LANES = 128

EPSILON = 1e-06


def shifted(x, axis, by):
    devices = lax.axis_size(axis)
    pairs = [(i, i + by) for i in range(devices) if 0 <= i + by < devices]
    return lax.ppermute(x, axis, pairs)


def diagonal(x, by_tm, by_rows):
    groups, parts = lax.axis_size("tm"), lax.axis_size("rows")
    pairs = []
    for g in range(groups):
        for r in range(parts):
            dg, dr = g + by_tm, r + by_rows
            if 0 <= dg < groups and 0 <= dr < parts:
                pairs.append((g * parts + r, dg * parts + dr))
    return lax.ppermute(x, ("tm", "rows"), pairs)


def norm_act(field, gain_vec):
    values_f = field.astype(jnp.float32)
    inverse = lax.rsqrt(jnp.mean(values_f * values_f, axis=-1, keepdims=True) + EPSILON)
    return jax.nn.silu(values_f * inverse * gain_vec).astype(jnp.bfloat16)


def local_conv(extended, weight, keep_masks):
    frame_count = extended.shape[0] - 2
    height = extended.shape[1] - 2
    columns = extended.shape[2]
    channels = extended.shape[3]
    outputs = weight.shape[-1]
    padded = jnp.pad(extended, ((0, 0), (0, 0), (1, 1), (0, 0)))
    running = jnp.zeros((frame_count, height, columns, outputs), jnp.float32)
    for tap_time in range(3):
        pieces = []
        for tap_row in range(3):
            for tap_col in range(3):
                pieces.append(
                    padded[
                        tap_time : tap_time + frame_count,
                        tap_row : tap_row + height,
                        tap_col : tap_col + columns,
                    ]
                )
        stacked = jnp.concatenate(pieces, axis=-1).reshape(-1, 9 * channels)
        partial_value = jnp.dot(
            stacked,
            weight[tap_time].reshape(9 * channels, outputs),
            preferred_element_type=jnp.float32,
        )
        partial_value = partial_value.reshape(frame_count, height, columns, outputs)
        running = running + jnp.where(
            keep_masks[tap_time][:, None, None, None], partial_value, jnp.float32(0.0)
        )
    return running


def conv_kernel(keep_ref, *refs, layout, mode, per_step):
    sources = refs[: len(layout)]
    w_hbm, side_ref, o_ref, col_ref, w_ref, w_sem = refs[len(layout) :]
    step = pl.program_id(0)
    steps = pl.num_programs(0)
    columns, channels = sources[0].shape[-2:]
    frame_count = keep_ref.shape[0] // 3
    cells = col_ref.shape[0]
    band = cells // per_step
    height = band // columns
    taps = 9 * channels

    def weight_copy(j, b):
        return pltpu.make_async_copy(
            w_hbm.at[pl.ds((j * 3 + b) * channels, channels)],
            w_ref.at[b, pl.ds(j * channels, channels)],
            w_sem.at[b],
        )

    def weight_wait(b):
        pltpu.make_async_copy(w_hbm.at[pl.ds(0, taps)], w_ref.at[b], w_sem.at[b]).wait()

    @pl.when(step == 0)
    def _():
        for b in (1, 0, 2):
            for j in range(9):
                weight_copy(j, b).start()

    def row_of(ext_frame, ext_row):
        for name, (frame_lo, frame_hi, row_lo, row_hi) in layout.items():
            if frame_lo <= ext_frame < frame_hi and row_lo <= ext_row < row_hi:
                return sources[list(layout).index(name)][ext_frame - frame_lo, ext_row - row_lo]
        raise ValueError("no source")

    for first in range(0, frame_count, per_step):

        @pl.when(step == first // per_step)
        def _():
            for fl in range(per_step):
                f = first + fl
                for k in range(3):
                    kept = keep_ref[k * frame_count + f] != 0
                    for a in range(3):
                        j = k * 3 + a
                        for i in range(height):
                            piece = row_of(f + k, a + i)
                            col_ref[
                                pl.ds(fl * band + i * columns, columns), pl.ds(j * channels, channels)
                            ] = jnp.where(kept, piece, jnp.zeros_like(piece))

    outputs = w_ref.shape[-1]
    position = lax.broadcasted_iota(jnp.int32, (cells, outputs), 0) % columns
    running = None
    for b in (1, 0, 2):

        @pl.when(step == 0)
        def _():
            weight_wait(b)

        part = jnp.dot(col_ref[...], w_ref[b], preferred_element_type=jnp.float32)
        if b == 0:
            part = jnp.where(position == 0, 0.0, pltpu.roll(part, 1, 0))
        elif b == 2:
            part = jnp.where(position == columns - 1, 0.0, pltpu.roll(part, cells - 1, 0))
        running = part if running is None else running + part
    if mode == "act":
        values_f = running.astype(jnp.bfloat16).astype(jnp.float32)
        inverse = lax.rsqrt(jnp.mean(values_f * values_f, axis=-1, keepdims=True) + EPSILON)
        scaled = values_f * inverse * side_ref[...]
        o_ref[...] = (scaled / (1.0 + jnp.exp(-scaled))).astype(o_ref.dtype)
    else:
        residual = side_ref[pl.ds(2 + step * per_step, per_step), 1 : 1 + height]
        o_ref[...] = (residual.reshape(cells, outputs).astype(jnp.float32) + running).astype(
            o_ref.dtype
        )


def whole(x):
    return pl.BlockSpec(x.shape, lambda step: (0,) * x.ndim)


def conv_call(layout, sources, weight, keep, side, mode, per_step=2):
    columns, channels = sources[0].shape[-2:]
    frame_count = keep.shape[0] // 3
    rows_in = max(hi for (_, _, _, hi) in layout.values())
    band = (rows_in - 2) * columns
    cells = frame_count * band
    outputs = weight.shape[-1]
    weight_rows = weight.reshape(27 * channels, outputs)
    out = pl.pallas_call(
        functools.partial(conv_kernel, layout=layout, mode=mode, per_step=per_step),
        out_shape=jax.ShapeDtypeStruct((cells, outputs), jnp.bfloat16),
        in_specs=[pl.BlockSpec(memory_space=pltpu.SMEM)]
        + [whole(x) for x in sources]
        + [pl.BlockSpec(memory_space=pl.ANY), whole(side)],
        out_specs=pl.BlockSpec((per_step * band, outputs), lambda step: (step, 0)),
        grid=(frame_count // per_step,),
        scratch_shapes=[
            pltpu.VMEM((per_step * band, 9 * channels), jnp.bfloat16),
            pltpu.VMEM((3, 9 * channels, outputs), jnp.bfloat16),
            pltpu.SemaphoreType.DMA((3,)),
        ],
        cost_estimate=pl.CostEstimate(
            flops=2 * cells * 27 * channels * outputs,
            transcendentals=cells * outputs,
            bytes_accessed=2 * (27 * channels * outputs + 3 * cells * outputs),
        ),
        compiler_params=pltpu.CompilerParams(vmem_limit_bytes=60 * 1024 * 1024),
    )(keep, *sources, weight_rows, side)
    return out.reshape(frame_count, rows_in - 2, columns, outputs)


def on_device(
    generator_latent_rows,
    slot_group_row,
    frame_clip_number,
    input_convolution_weight,
    first_norm_gain,
    first_convolution_weight,
    second_norm_gain,
    second_convolution_weight,
):
    frame_count = F_DEV
    slots_here = generator_latent_rows.shape[1]
    packed_rows = generator_latent_rows.shape[2]
    parts_count = lax.axis_size("rows")
    rows_here = slots_here // frame_count
    height = rows_here * parts_count
    columns = packed_rows // LATENT_CHANNELS
    band_index = lax.axis_index("rows")
    frame_group_index = lax.axis_index("tm")

    ids = jnp.broadcast_to(
        slot_group_row.astype(jnp.bfloat16)[:, :, None], (1, slots_here, ID_LANES)
    )
    packed = jnp.concatenate([generator_latent_rows, ids], axis=-1)
    earlier = shifted(packed, "tm", 1)
    both = jnp.concatenate([earlier, packed], axis=0)
    parts_total = lax.axis_size("rows")
    pieces = [both]
    for by in range(1, parts_total):
        ring = [(i, (i + by) % parts_total) for i in range(parts_total)]
        pieces.append(lax.ppermute(both, "rows", ring))
    gathered = jnp.concatenate(pieces, axis=1)
    values = gathered[:, :, :packed_rows]
    slot_ids = gathered[:, :, packed_rows].astype(jnp.int32)

    window_rows = rows_here + 4
    frame_of = jnp.arange(frame_count, dtype=jnp.int32)[:, None]
    row_of = band_index * rows_here - 2 + jnp.arange(window_rows, dtype=jnp.int32)[None, :]
    wanted = (frame_of * height + row_of).reshape(-1)
    valid = jnp.broadcast_to((row_of >= 0) & (row_of < height), (frame_count, window_rows)).reshape(-1)
    selector = ((wanted[None, :, None] == slot_ids[:, None, :]) & valid[None, :, None]).astype(
        jnp.bfloat16
    )
    latent = jnp.einsum("qij,qjc->qic", selector, values, preferred_element_type=jnp.float32)
    latent = latent.astype(jnp.bfloat16).reshape(
        2 * frame_count, window_rows, columns, LATENT_CHANNELS
    )

    padded_clips = jnp.concatenate([jnp.full((4,), -1, jnp.int32), frame_clip_number])
    window = lax.dynamic_slice_in_dim(padded_clips, frame_group_index * frame_count, frame_count + 4)
    current_ext = window[2:]
    keep_ext = [window[k : k + frame_count + 2] == current_ext for k in range(3)]
    current = window[4:]
    keep_own = jnp.stack(
        [(window[k + 2 : k + 2 + frame_count] == current) for k in range(3)]
    ).astype(jnp.int32).reshape(-1)

    base_ext = local_conv(latent, input_convolution_weight, keep_ext).astype(jnp.bfloat16)
    first_act = norm_act(base_ext, first_norm_gain)
    ext_rows = band_index * rows_here - 1 + jnp.arange(rows_here + 2, dtype=jnp.int32)
    row_ok = (ext_rows >= 0) & (ext_rows < height)
    first_act = jnp.where(row_ok[None, :, None, None], first_act, jnp.zeros((), jnp.bfloat16))

    gain = second_norm_gain.reshape(1, -1)
    ext_frames, ext_rows_n = first_act.shape[:2]
    second_act = conv_call(
        {"x": (0, ext_frames, 0, ext_rows_n)},
        [first_act],
        first_convolution_weight,
        keep_own,
        gain,
        "act",
    )

    last = second_act[frame_count - 2 :]
    from_above = shifted(second_act[:, rows_here - 1 :], "rows", 1)
    from_below = shifted(second_act[:, :1], "rows", -1)
    prev_mid = shifted(last, "tm", 1)
    prev_above = diagonal(last[:, rows_here - 1 :], 1, 1)
    prev_below = diagonal(last[:, :1], 1, -1)
    layout = {
        "own": (2, 2 + frame_count, 1, 1 + rows_here),
        "above": (2, 2 + frame_count, 0, 1),
        "below": (2, 2 + frame_count, 1 + rows_here, 2 + rows_here),
        "mid": (0, 2, 1, 1 + rows_here),
        "corner_above": (0, 2, 0, 1),
        "corner_below": (0, 2, 1 + rows_here, 2 + rows_here),
    }
    return conv_call(
        layout,
        [second_act, from_above, from_below, prev_mid, prev_above, prev_below],
        second_convolution_weight,
        keep_own,
        base_ext,
        "res",
    )


def solution(mesh):
    in_specs = (P("tm", "rows", None), P("tm", "rows"), P(), P(), P(), P(), P(), P())
    out_specs = P("tm", "rows", None, None)
    return jax.shard_map(
        on_device, mesh=mesh, in_specs=in_specs, out_specs=out_specs, check_vma=False
    )
```

profile of v0, /device:TPU:21, one launch (start us, length us, event | category | flops | bytes accessed | tf_op | source)
XLA Modules:
  0.0 117.7 jit_solution(1955900204027751744)
XLA Ops:
  0.0 0.7 convert_bitcast_fusion
  0.7 0.8 pad_maximum_fusion.2
  1.5 3.5 %collective-permute-start = (bf16[1,8,2688]{2,1,0:T(8,128)(2,1)S(1)}, bf16[1,8,2688]{2,1,0:T(8,128)(2,1)S(1)}, u32[]{:S(2)}, u32[]{:S(2)}) collective-permute-start(bf16[1,8,2688]{2,1,0:T(8,128)(2,1)S(1)} %pad_maximum_fusion.2), channel_id=1, source_target_pairs={{0,8},{8,16},{16,24},{24,32},{32,40},{40,48},{48,56},{56,64},{64,7... | collective-permute-start | bytes 129032 | tf_op jit(solution)/shard_map/ppermute | solution.py:20
  5.1 0.7 pad_dynamic-slice_fusion
  6.0 1.0 fusion.18
  7.4 0.6 reshape.101.keep_ref
  8.0 1.2 %reshape.97.refs_2_ = f32[1,384]{1,0:T(1,128)} reshape(f32[384]{0:T(512)} %param.14) | data formatting | bytes 3072 | tf_op jit(solution)/shard_map/reshape | solution.py:247
  9.2 0.8 pad_maximum_fusion
  10.0 1.8 %collective-permute-start.1 = (bf16[2,8,2688]{2,1,0:T(8,128)(2,1)S(1)}, bf16[2,8,2688]{2,1,0:T(8,128)(2,1)S(1)}, u32[]{:S(2)}, u32[]{:S(2)}) collective-permute-start(bf16[2,8,2688]{2,1,0:T(8,128)(2,1)S(1)} %get-tuple-element.23), channel_id=1, source_target_pairs={{0,1},{1,2},{2,3},{3,4},{4,5},{5,6},{6,7},{7,0},{8,9},{9,10},{10,1... | collective-permute-start | bytes 258056 | tf_op jit(solution)/shard_map/ppermute | solution.py:214
  11.8 0.2 collective-permute-start.2
  12.0 0.7 collective-permute-start.3
  12.7 2.5 %collective-permute-start.4 = (bf16[2,8,2688]{2,1,0:T(8,128)(2,1)S(1)}, bf16[2,8,2688]{2,1,0:T(8,128)(2,1)S(1)}, u32[]{:S(2)}, u32[]{:S(2)}) collective-permute-start(bf16[2,8,2688]{2,1,0:T(8,128)(2,1)S(1)} %get-tuple-element.23), channel_id=1, source_target_pairs={{0,4},{1,5},{2,6},{3,7},{4,0},{5,1},{6,2},{7,3},{8,12},{9,13},{10,... | collective-permute-start | bytes 258056 | tf_op jit(solution)/shard_map/ppermute | solution.py:214
  15.2 1.0 collective-permute-start.5
  16.2 0.9 collective-permute-start.6
  17.1 0.2 collective-permute-start.7
  17.3 0.9 collective-permute-done.3
  18.2 1.7 %collective-permute-done.4 = bf16[2,8,2688]{2,1,0:T(8,128)(2,1)S(1)} collective-permute-done((bf16[2,8,2688]{2,1,0:T(8,128)(2,1)S(1)}, bf16[2,8,2688]{2,1,0:T(8,128)(2,1)S(1)}, u32[]{:S(2)}, u32[]{:S(2)}) %collective-permute-start.4) | collective-permute-done | bytes 86048 | tf_op jit(solution)/shard_map/ppermute | solution.py:214
  19.9 0.8 collective-permute-done.5
  20.7 0.8 collective-permute-done.6
  21.5 1.3 %collective-permute-done.7 = bf16[2,8,2688]{2,1,0:T(8,128)(2,1)S(1)} collective-permute-done((bf16[2,8,2688]{2,1,0:T(8,128)(2,1)S(1)}, bf16[2,8,2688]{2,1,0:T(8,128)(2,1)S(1)}, u32[]{:S(2)}, u32[]{:S(2)}) %collective-permute-start.7) | collective-permute-done | bytes 86048 | tf_op jit(solution)/shard_map/ppermute | solution.py:214
  23.0 0.3 convolution_convert_fusion
  23.3 1.6 %reshape.95 = bf16[8,6,160,16]{3,2,1,0:T(8,128)(2,1)S(1)} reshape(bf16[2,24,2560]{2,1,0:T(8,128)(2,1)S(1)} %convolution_convert_fusion) | data formatting | bytes 491520 | tf_op jit(solution)/shard_map/reshape | solution.py:228
  24.8 1.0 copy.19
  25.9 0.1 slice_dynamic-update-slice_fusion.14
  26.0 0.1 slice_dynamic-update-slice_fusion.13
  26.3 0.1 slice_dynamic-update-slice_fusion.11
  26.5 0.2 slice_dynamic-update-slice_fusion.10
  26.7 0.2 slice_dynamic-update-slice_fusion.9
  27.1 0.1 slice_dynamic-update-slice_fusion.23
  27.4 0.2 slice_dynamic-update-slice_fusion.21
  28.1 1.3 %fusion.20 = f32[6,4,160,384]{3,2,1,0:T(8,128)S(1)} fusion(bf16[6,4,160,144]{2,3,1,0:T(8,128)(2,1)S(1)} %slice_dynamic-update-slice_fusion.15, bf16[144,384,1,1]{1,0,3,2:T(8,128)(2,1)S(1)} %bitcast.39), kind=kOutput, calls=%fused_computation.75 | convolution fusion | flops 424673280 | bytes 7114752 | tf_op jit(solution)/shard_map/dot_general | solution.py:60
  29.4 1.3 %fusion.19 = f32[6,4,160,384]{3,2,1,0:T(8,128)S(1)} fusion(bf16[6,4,160,144]{2,3,1,0:T(8,128)(2,1)S(1)} %get-tuple-element.16, bf16[144,384,1,1]{1,0,3,2:T(8,128)(2,1)S(1)} %bitcast.38), kind=kOutput, calls=%fused_computation.74 | convolution fusion | flops 424673280 | bytes 7114752 | tf_op jit(solution)/shard_map/dot_general | solution.py:60
  30.7 3.1 %fusion = (f32[6,4,160]{2,1,0:T(4,128)S(1)}, bf16[6,4,160,384]{3,2,1,0:T(8,128)(2,1)S(1)}) fusion(bf16[6,4,160,144]{2,3,1,0:T(8,128)(2,1)S(1)} %get-tuple-element.9, bf16[144,384,1,1]{1,0,3,2:T(8,128)(2,1)S(1)} %bitcast.37, f32[6,4,160,384]{3,2,1,0:T(8,128)S(1)} %fusion.20, pred[6]{0:T(512)(128)(4,1)S(1)} %get-tuple-element.26, ...), kind=kOutput, calls=%fused_computation.2 | convolution fusion | flops 436465920 | bytes 15977484 | tf_op jit(solution)/shard_map/dot_general | solution.py:60
  33.8 3.1 %fusion.8.refs_0_ = bf16[6,4,160,384]{3,2,1,0:T(8,128)(2,1)} fusion(bf16[6,4,160,384]{3,2,1,0:T(8,128)(2,1)S(1)} %get-tuple-element.30.refs_7_, f32[384]{0:T(512)S(1)} %copy-done.1, f32[6,4,160]{2,1,0:T(4,128)S(1)} %add_rsqrt_fusion, pred[4]{0:T(512)(128)(4,1)S(1)} %compare_and_fusion.1), kind=kLoop, calls=%fused_computation.12 | loop fusion | flops 13271040 | bytes 5915140 | tf_op jit(solution)/shard_map/jit(_where)/select_n | solution.py:245
  37.0 21.8 %shard_map.82 = bf16[1280,384]{1,0:T(8,128)(2,1)} custom-call(s32[12]{0:T(128)} %reshape.101.keep_ref, bf16[6,4,160,384]{3,2,1,0:T(8,128)(2,1)} %fusion.8.refs_0_, bf16[10368,384]{1,0:T(8,128)(2,1)} %bitcast.40, f32[1,384]{1,0:T(1,128)} %reshape.97.refs_2_), custom_call_target="tpu_custom_call" | custom-call | flops 10192158720 | bytes 10911744 | tf_op jit(solution)/shard_map/pallas_call | solution.py:161
  58.8 1.1 slice.200
  59.9 1.3 %fusion.16 = (bf16[4,1,160,384]{3,2,1,0:T(8,128)(2,1)S(1)}, bf16[4,1,160,384]{3,2,1,0:T(8,128)(2,1)S(1)}) fusion(bf16[4,2,160,384]{3,2,1,0:T(8,128)(2,1)} %bitcast.33), kind=kLoop, calls=%fused_computation.71 | loop fusion | bytes 1966080 | tf_op jit(solution)/shard_map/slice | solution.py:260
  61.1 3.6 %collective-permute-start.8 = (bf16[4,1,160,384]{3,2,1,0:T(8,128)(2,1)S(1)}, bf16[4,1,160,384]{3,2,1,0:T(8,128)(2,1)S(1)}, u32[]{:S(2)}, u32[]{:S(2)}) collective-permute-start(bf16[4,1,160,384]{3,2,1,0:T(8,128)(2,1)S(1)} %get-tuple-element.6), channel_id=1, source_target_pairs={{0,1},{1,2},{2,3},{3,4},{4,5},{5,6},{6,7},{8,9},{9,10},{10,11},{11... | collective-permute-start | bytes 1474568 | tf_op jit(solution)/shard_map/ppermute | solution.py:20
  64.8 1.9 %collective-permute-start.9 = (bf16[4,1,160,384]{3,2,1,0:T(8,128)(2,1)S(1)}, bf16[4,1,160,384]{3,2,1,0:T(8,128)(2,1)S(1)}, u32[]{:S(2)}, u32[]{:S(2)}) collective-permute-start(bf16[4,1,160,384]{3,2,1,0:T(8,128)(2,1)S(1)} %get-tuple-element.5), channel_id=1, source_target_pairs={{1,0},{2,1},{3,2},{4,3},{5,4},{6,5},{7,6},{9,8},{10,9},{11,10},{12... | collective-permute-start | bytes 1474568 | tf_op jit(solution)/shard_map/ppermute | solution.py:20
  66.7 3.5 %collective-permute-start.10 = (bf16[2,2,160,384]{3,2,1,0:T(8,128)(2,1)S(1)}, bf16[2,2,160,384]{3,2,1,0:T(8,128)(2,1)S(1)}, u32[]{:S(2)}, u32[]{:S(2)}) collective-permute-start(bf16[2,2,160,384]{3,2,1,0:T(8,128)(2,1)S(1)} %bitcast.35), channel_id=1, source_target_pairs={{0,8},{8,16},{16,24},{24,32},{32,40},{40,48},{48,56},{56,64},{64,7... | collective-permute-start | bytes 1474568 | tf_op jit(solution)/shard_map/ppermute | solution.py:20
  70.3 5.0 %collective-permute-start.11 = (bf16[2,1,160,384]{3,2,1,0:T(8,128)(2,1)S(1)}, bf16[2,1,160,384]{3,2,1,0:T(8,128)(2,1)S(1)}, u32[]{:S(2)}, u32[]{:S(2)}) collective-permute-start(bf16[2,1,160,384]{3,2,1,0:T(8,128)(2,1)S(1)} %get-tuple-element.8), channel_id=1, source_target_pairs={{0,9},{1,10},{2,11},{3,12},{4,13},{5,14},{6,15},{8,17},{9,18},{10,... | collective-permute-start | bytes 737288 | tf_op jit(solution)/shard_map/ppermute | solution.py:31
  75.3 1.9 %collective-permute-start.12 = (bf16[2,1,160,384]{3,2,1,0:T(8,128)(2,1)S(1)}, bf16[2,1,160,384]{3,2,1,0:T(8,128)(2,1)S(1)}, u32[]{:S(2)}, u32[]{:S(2)}) collective-permute-start(bf16[2,1,160,384]{3,2,1,0:T(8,128)(2,1)S(1)} %get-tuple-element.7), channel_id=1, source_target_pairs={{1,8},{2,9},{3,10},{4,11},{5,12},{6,13},{7,14},{9,16},{10,17},{11,... | collective-permute-start | bytes 737288 | tf_op jit(solution)/shard_map/ppermute | solution.py:31
  77.2 17.0 %collective-permute-done.11.refs_4_ = bf16[2,1,160,384]{3,2,1,0:T(8,128)(2,1)S(1)} collective-permute-done((bf16[2,1,160,384]{3,2,1,0:T(8,128)(2,1)S(1)}, bf16[2,1,160,384]{3,2,1,0:T(8,128)(2,1)S(1)}, u32[]{:S(2)}, u32[]{:S(2)}) %collective-permute-start.11) | collective-permute-done | bytes 245792 | tf_op jit(solution)/shard_map/ppermute | solution.py:31
  94.3 0.7 copy-done.5
  95.0 0.2 copy-done.2
  95.2 0.2 copy-done.3
  95.3 0.1 copy-done.4
  95.5 22.0 %shard_map.83 = bf16[1280,384]{1,0:T(8,128)(2,1)} custom-call(s32[12]{0:T(128)} %reshape.101.keep_ref, bf16[4,2,160,384]{3,2,1,0:T(8,128)(2,1)} %bitcast.34, bf16[4,1,160,384]{3,2,1,0:T(8,128)(2,1)} %copy-done.2, bf16[4,1,160,384]{3,2,1,0:T(8,128)(2,1)} %copy-done.3, bf16[2,2,160,384]{3,2,1,0:T(8,128)(2,1)} %copy-done.4, bf16[2,1,160,384]{3,2,1,0:T(8,128)(2,1)} %copy-done.5, ...), custom_call_target="tpu_custom_call" | custom-call | flops 10192158720 | bytes 10911744 | tf_op jit(solution)/shard_map/pallas_call | solution.py:161
  (54 shorter events, 2.0 us)
Async XLA Ops:
  1.5 7.7 %collective-permute-start = (bf16[1,8,2688]{2,1,0:T(8,128)(2,1)S(1)}, bf16[1,8,2688]{2,1,0:T(8,128)(2,1)S(1)}, u32[]{:S(2)}, u32[]{:S(2)}) collective-permute-start(bf16[1,8,2688]{2,1,0:T(8,128)(2,1)S(1)} %pad_maximum_fusion.2), channel_id=1, source_target_pairs={{0,8},{8,16},{16,24},{24,32},{32,40},{40,48},{48,56},{56,64},{64,7... | collective-permute-start | bytes 129032 | tf_op jit(solution)/shard_map/ppermute | solution.py:20
  10.0 6.2 %collective-permute-start.1 = (bf16[2,8,2688]{2,1,0:T(8,128)(2,1)S(1)}, bf16[2,8,2688]{2,1,0:T(8,128)(2,1)S(1)}, u32[]{:S(2)}, u32[]{:S(2)}) collective-permute-start(bf16[2,8,2688]{2,1,0:T(8,128)(2,1)S(1)} %get-tuple-element.23), channel_id=1, source_target_pairs={{0,1},{1,2},{2,3},{3,4},{4,5},{5,6},{6,7},{7,0},{8,9},{9,10},{10,1... | collective-permute-start | bytes 258056 | tf_op jit(solution)/shard_map/ppermute | solution.py:214
  11.8 5.2 %collective-permute-start.2 = (bf16[2,8,2688]{2,1,0:T(8,128)(2,1)S(1)}, bf16[2,8,2688]{2,1,0:T(8,128)(2,1)S(1)}, u32[]{:S(2)}, u32[]{:S(2)}) collective-permute-start(bf16[2,8,2688]{2,1,0:T(8,128)(2,1)S(1)} %get-tuple-element.23), channel_id=1, source_target_pairs={{0,2},{1,3},{2,4},{3,5},{4,6},{5,7},{6,0},{7,1},{8,10},{9,11},{10,... | collective-permute-start | bytes 258056 | tf_op jit(solution)/shard_map/ppermute | solution.py:214
  12.0 6.1 %collective-permute-start.3 = (bf16[2,8,2688]{2,1,0:T(8,128)(2,1)S(1)}, bf16[2,8,2688]{2,1,0:T(8,128)(2,1)S(1)}, u32[]{:S(2)}, u32[]{:S(2)}) collective-permute-start(bf16[2,8,2688]{2,1,0:T(8,128)(2,1)S(1)} %get-tuple-element.23), channel_id=1, source_target_pairs={{0,3},{1,4},{2,5},{3,6},{4,7},{5,0},{6,1},{7,2},{8,11},{9,12},{10,... | collective-permute-start | bytes 258056 | tf_op jit(solution)/shard_map/ppermute | solution.py:214
  12.7 7.1 %collective-permute-start.4 = (bf16[2,8,2688]{2,1,0:T(8,128)(2,1)S(1)}, bf16[2,8,2688]{2,1,0:T(8,128)(2,1)S(1)}, u32[]{:S(2)}, u32[]{:S(2)}) collective-permute-start(bf16[2,8,2688]{2,1,0:T(8,128)(2,1)S(1)} %get-tuple-element.23), channel_id=1, source_target_pairs={{0,4},{1,5},{2,6},{3,7},{4,0},{5,1},{6,2},{7,3},{8,12},{9,13},{10,... | collective-permute-start | bytes 258056 | tf_op jit(solution)/shard_map/ppermute | solution.py:214
  15.2 5.5 %collective-permute-start.5 = (bf16[2,8,2688]{2,1,0:T(8,128)(2,1)S(1)}, bf16[2,8,2688]{2,1,0:T(8,128)(2,1)S(1)}, u32[]{:S(2)}, u32[]{:S(2)}) collective-permute-start(bf16[2,8,2688]{2,1,0:T(8,128)(2,1)S(1)} %get-tuple-element.23), channel_id=1, source_target_pairs={{0,5},{1,6},{2,7},{3,0},{4,1},{5,2},{6,3},{7,4},{8,13},{9,14},{10,... | collective-permute-start | bytes 258056 | tf_op jit(solution)/shard_map/ppermute | solution.py:214
  16.2 5.3 %collective-permute-start.6 = (bf16[2,8,2688]{2,1,0:T(8,128)(2,1)S(1)}, bf16[2,8,2688]{2,1,0:T(8,128)(2,1)S(1)}, u32[]{:S(2)}, u32[]{:S(2)}) collective-permute-start(bf16[2,8,2688]{2,1,0:T(8,128)(2,1)S(1)} %get-tuple-element.23), channel_id=1, source_target_pairs={{0,6},{1,7},{2,0},{3,1},{4,2},{5,3},{6,4},{7,5},{8,14},{9,15},{10,... | collective-permute-start | bytes 258056 | tf_op jit(solution)/shard_map/ppermute | solution.py:214
  17.1 5.8 %collective-permute-start.7 = (bf16[2,8,2688]{2,1,0:T(8,128)(2,1)S(1)}, bf16[2,8,2688]{2,1,0:T(8,128)(2,1)S(1)}, u32[]{:S(2)}, u32[]{:S(2)}) collective-permute-start(bf16[2,8,2688]{2,1,0:T(8,128)(2,1)S(1)} %get-tuple-element.23), channel_id=1, source_target_pairs={{0,7},{1,0},{2,1},{3,2},{4,3},{5,4},{6,5},{7,6},{8,15},{9,8},{10,9... | collective-permute-start | bytes 258056 | tf_op jit(solution)/shard_map/ppermute | solution.py:214
  30.6 3.2 %copy-start.1 = (f32[384]{0:T(512)S(1)}, f32[384]{0:T(512)}, u32[]{:S(2)}) copy-start(f32[384]{0:T(512)} %param.12) | copy-start | bytes 4612
  33.8 3.2 %copy-start = (bf16[6,4,160,384]{3,2,1,0:T(8,128)(2,1)}, bf16[6,4,160,384]{3,2,1,0:T(8,128)(2,1)S(1)}, u32[]{:S(2)}) copy-start(bf16[6,4,160,384]{3,2,1,0:T(8,128)(2,1)S(1)} %get-tuple-element.30.refs_7_) | copy-start | bytes 8847364
  61.1 33.1 %collective-permute-start.8 = (bf16[4,1,160,384]{3,2,1,0:T(8,128)(2,1)S(1)}, bf16[4,1,160,384]{3,2,1,0:T(8,128)(2,1)S(1)}, u32[]{:S(2)}, u32[]{:S(2)}) collective-permute-start(bf16[4,1,160,384]{3,2,1,0:T(8,128)(2,1)S(1)} %get-tuple-element.6), channel_id=1, source_target_pairs={{0,1},{1,2},{2,3},{3,4},{4,5},{5,6},{6,7},{8,9},{9,10},{10,11},{11... | collective-permute-start | bytes 1474568 | tf_op jit(solution)/shard_map/ppermute | solution.py:20
  64.8 29.4 %collective-permute-start.9 = (bf16[4,1,160,384]{3,2,1,0:T(8,128)(2,1)S(1)}, bf16[4,1,160,384]{3,2,1,0:T(8,128)(2,1)S(1)}, u32[]{:S(2)}, u32[]{:S(2)}) collective-permute-start(bf16[4,1,160,384]{3,2,1,0:T(8,128)(2,1)S(1)} %get-tuple-element.5), channel_id=1, source_target_pairs={{1,0},{2,1},{3,2},{4,3},{5,4},{6,5},{7,6},{9,8},{10,9},{11,10},{12... | collective-permute-start | bytes 1474568 | tf_op jit(solution)/shard_map/ppermute | solution.py:20
  66.7 27.5 %collective-permute-start.10 = (bf16[2,2,160,384]{3,2,1,0:T(8,128)(2,1)S(1)}, bf16[2,2,160,384]{3,2,1,0:T(8,128)(2,1)S(1)}, u32[]{:S(2)}, u32[]{:S(2)}) collective-permute-start(bf16[2,2,160,384]{3,2,1,0:T(8,128)(2,1)S(1)} %bitcast.35), channel_id=1, source_target_pairs={{0,8},{8,16},{16,24},{24,32},{32,40},{40,48},{48,56},{56,64},{64,7... | collective-permute-start | bytes 1474568 | tf_op jit(solution)/shard_map/ppermute | solution.py:20
  70.3 23.9 %collective-permute-start.11 = (bf16[2,1,160,384]{3,2,1,0:T(8,128)(2,1)S(1)}, bf16[2,1,160,384]{3,2,1,0:T(8,128)(2,1)S(1)}, u32[]{:S(2)}, u32[]{:S(2)}) collective-permute-start(bf16[2,1,160,384]{3,2,1,0:T(8,128)(2,1)S(1)} %get-tuple-element.8), channel_id=1, source_target_pairs={{0,9},{1,10},{2,11},{3,12},{4,13},{5,14},{6,15},{8,17},{9,18},{10,... | collective-permute-start | bytes 737288 | tf_op jit(solution)/shard_map/ppermute | solution.py:31
  75.3 18.9 %collective-permute-start.12 = (bf16[2,1,160,384]{3,2,1,0:T(8,128)(2,1)S(1)}, bf16[2,1,160,384]{3,2,1,0:T(8,128)(2,1)S(1)}, u32[]{:S(2)}, u32[]{:S(2)}) collective-permute-start(bf16[2,1,160,384]{3,2,1,0:T(8,128)(2,1)S(1)} %get-tuple-element.7), channel_id=1, source_target_pairs={{1,8},{2,9},{3,10},{4,11},{5,12},{6,13},{7,14},{9,16},{10,17},{11,... | collective-permute-start | bytes 737288 | tf_op jit(solution)/shard_map/ppermute | solution.py:31
  94.2 0.7 copy-start.5
  94.2 0.8 copy-start.6
  94.2 1.0 copy-start.2
  94.2 1.1 copy-start.3
  94.3 1.2 %copy-start.4 = (bf16[2,2,160,384]{3,2,1,0:T(8,128)(2,1)}, bf16[2,2,160,384]{3,2,1,0:T(8,128)(2,1)S(1)}, u32[]{:S(2)}) copy-start(bf16[2,2,160,384]{3,2,1,0:T(8,128)(2,1)S(1)} %collective-permute-done.10.refs_3_) | copy-start | bytes 1474564
where the time goes:
time: 118 us
  Pallas kernels  43.8 us (37%)
  starting transfers between devices  26.7 us (23%)
  waiting for transfers between devices  22.5 us (19%)
  local copies, waits for them, and re-layouts  12.3 us (10%)
  matrix products  5.93 us (5%)
  other arithmetic  5.83 us (5%)
    pallas_call x2, Pallas kernels, conv_call(): pl.pallas_call(functools.partial(conv_kernel, layout=layout, mode=mode, p...  43.8 us
    ppermute x2, waiting for transfers between devices, diagonal(): return lax.ppermute(x, ('tm', 'rows'), pairs)  17 us
    ppermute x4, starting transfers between devices, shifted(): return lax.ppermute(x, axis, pairs)  12.6 us
    ppermute x7, starting transfers between devices, on_device(): pieces.append(lax.ppermute(both, 'rows', ring))  7.19 us
    ppermute x2, starting transfers between devices, diagonal(): return lax.ppermute(x, ('tm', 'rows'), pairs)  6.91 us
    dot_general x3, matrix products, local_conv(): jnp.dot(stacked, weight[tap_time].reshape(9 * channels, outputs), preferr...  5.65 us
    ppermute x7, waiting for transfers between devices, on_device(): pieces.append(lax.ppermute(both, 'rows', ring))  5.53 us
    select_n x1, other arithmetic, on_device(): jnp.where(row_ok[None, :, None, None], first_act, jnp.zeros((), jnp.bfloa...  3.14 us
  transfers between devices with their start and end apart: 13, of which 6 were waited for; matrix products, arithmetic and copies ran while one was open for 4% of the time, Pallas kernels for 0%

commit v1 on v0

--- a/solution.py
+++ b/solution.py
@@ -69,9 +69,10 @@
     return running
 
 
-def conv_kernel(keep_ref, *refs, layout, mode, per_step):
+def conv_kernel(keep_ref, *refs, layout, mode, per_step, firsts):
     sources = refs[: len(layout)]
-    w_hbm, side_ref, o_ref, col_ref, w_ref, w_sem = refs[len(layout) :]
+    w_hbm, side_ref = refs[len(layout) : len(layout) + 2]
+    o_ref, col_ref, w_ref, w_sem = refs[-4:]
     step = pl.program_id(0)
     steps = pl.num_programs(0)
     columns, channels = sources[0].shape[-2:]
@@ -103,9 +104,9 @@
                 return sources[list(layout).index(name)][ext_frame - frame_lo, ext_row - row_lo]
         raise ValueError("no source")
 
-    for first in range(0, frame_count, per_step):
-
-        @pl.when(step == first // per_step)
+    for index, first in enumerate(firsts):
+
+        @pl.when(step == index)
         def _():
             for fl in range(per_step):
                 f = first + fl
@@ -140,7 +141,7 @@
         scaled = values_f * inverse * side_ref[...]
         o_ref[...] = (scaled / (1.0 + jnp.exp(-scaled))).astype(o_ref.dtype)
     else:
-        residual = side_ref[pl.ds(2 + step * per_step, per_step), 1 : 1 + height]
+        residual = side_ref[pl.ds(2 + firsts[0] + step * per_step, per_step), 1 : 1 + height]
         o_ref[...] = (residual.reshape(cells, outputs).astype(jnp.float32) + running).astype(
             o_ref.dtype
         )
@@ -150,7 +151,7 @@
     return pl.BlockSpec(x.shape, lambda step: (0,) * x.ndim)
 
 
-def conv_call(layout, sources, weight, keep, side, mode, per_step=2):
+def conv_call(layout, sources, weight, keep, side, mode, per_step=2, firsts=None, into=None):
     columns, channels = sources[0].shape[-2:]
     frame_count = keep.shape[0] // 3
     rows_in = max(hi for (_, _, _, hi) in layout.values())
@@ -158,26 +159,37 @@
     cells = frame_count * band
     outputs = weight.shape[-1]
     weight_rows = weight.reshape(27 * channels, outputs)
+    if firsts is None:
+        firsts = tuple(range(0, frame_count, per_step))
+    block_at = firsts[0] // per_step
+    operands = [keep, *sources, weight_rows, side]
+    extra_specs, aliases = [], {}
+    if into is not None:
+        extra_specs = [pl.BlockSpec(memory_space=pl.ANY)]
+        aliases = {len(operands): 0}
+        operands.append(into.reshape(cells, outputs))
     out = pl.pallas_call(
-        functools.partial(conv_kernel, layout=layout, mode=mode, per_step=per_step),
+        functools.partial(conv_kernel, layout=layout, mode=mode, per_step=per_step, firsts=firsts),
         out_shape=jax.ShapeDtypeStruct((cells, outputs), jnp.bfloat16),
         in_specs=[pl.BlockSpec(memory_space=pltpu.SMEM)]
         + [whole(x) for x in sources]
-        + [pl.BlockSpec(memory_space=pl.ANY), whole(side)],
-        out_specs=pl.BlockSpec((per_step * band, outputs), lambda step: (step, 0)),
-        grid=(frame_count // per_step,),
+        + [pl.BlockSpec(memory_space=pl.ANY), whole(side)]
+        + extra_specs,
+        out_specs=pl.BlockSpec((per_step * band, outputs), lambda step: (step + block_at, 0)),
+        grid=(len(firsts),),
+        input_output_aliases=aliases,
         scratch_shapes=[
             pltpu.VMEM((per_step * band, 9 * channels), jnp.bfloat16),
             pltpu.VMEM((3, 9 * channels, outputs), jnp.bfloat16),
             pltpu.SemaphoreType.DMA((3,)),
         ],
         cost_estimate=pl.CostEstimate(
-            flops=2 * cells * 27 * channels * outputs,
-            transcendentals=cells * outputs,
-            bytes_accessed=2 * (27 * channels * outputs + 3 * cells * outputs),
+            flops=2 * len(firsts) * per_step * band * 27 * channels * outputs,
+            transcendentals=len(firsts) * per_step * band * outputs,
+            bytes_accessed=2 * (27 * channels * outputs + 3 * len(firsts) * per_step * band * outputs),
         ),
         compiler_params=pltpu.CompilerParams(vmem_limit_bytes=60 * 1024 * 1024),
-    )(keep, *sources, weight_rows, side)
+    )(*operands)
     return out.reshape(frame_count, rows_in - 2, columns, outputs)
 
 
@@ -269,6 +281,12 @@
         "corner_above": (0, 2, 0, 1),
         "corner_below": (0, 2, 1 + rows_here, 2 + rows_here),
     }
+    late_layout = {name: layout[name] for name in ("own", "above", "below")}
+    late_sources = [second_act, from_above, from_below]
+    decoded = conv_call(
+        late_layout, late_sources, second_convolution_weight, keep_own, base_ext, "res",
+        firsts=(frame_count - 2,),
+    )
     return conv_call(
         layout,
         [second_act, from_above, from_below, prev_mid, prev_above, prev_below],
@@ -276,6 +294,8 @@
         keep_own,
         base_ext,
         "res",
+        firsts=(0,),
+        into=decoded,
     )
 
 

time: 118 us -> 109 us (0.924)
  waiting for transfers between devices: 22.5 us -> 8.12 us
  Pallas kernels: 43.8 us -> 48.4 us
    ppermute x2, waiting for transfers between devices: 17 us -> 2.57 us  [diagonal(): return lax.ppermute(x, ('tm', 'rows'), pairs)]
    pallas_call x2 -> x3, Pallas kernels: 43.8 us -> 48.4 us  [conv_call(): pl.pallas_call(functools.partial(conv_kernel, layout=layout, mode=mode, p...]
    unnamed x38 -> x40, local copies, waits for them, and re-layouts: 2.87 us -> 4.16 us
  transfers between devices with their start and end apart: 13 -> 13, of which waited for: 6 -> 6; matrix products, arithmetic and copies ran while one was open for 4% -> 4% of each run, Pallas kernels for 0% -> 12%
where the time goes in v1:
time: 109 us
  Pallas kernels  48.4 us (44%)
  starting transfers between devices  26.9 us (25%)
  local copies, waits for them, and re-layouts  12.8 us (12%)
  waiting for transfers between devices  8.12 us (7%)
  matrix products  5.93 us (5%)
  other arithmetic  5.84 us (5%)
    pallas_call x3, Pallas kernels, conv_call(): pl.pallas_call(functools.partial(conv_kernel, layout=layout, mode=mode, p...  48.4 us
    ppermute x4, starting transfers between devices, shifted(): return lax.ppermute(x, axis, pairs)  12.6 us
    ppermute x7, starting transfers between devices, on_device(): pieces.append(lax.ppermute(both, 'rows', ring))  7.17 us
    ppermute x2, starting transfers between devices, diagonal(): return lax.ppermute(x, ('tm', 'rows'), pairs)  7.13 us
    dot_general x3, matrix products, local_conv(): jnp.dot(stacked, weight[tap_time].reshape(9 * channels, outputs), preferr...  5.65 us
    ppermute x7, waiting for transfers between devices, on_device(): pieces.append(lax.ppermute(both, 'rows', ring))  5.53 us
    unnamed x40, local copies, waits for them, and re-layouts  4.16 us
    select_n x1, other arithmetic, on_device(): jnp.where(row_ok[None, :, None, None], first_act, jnp.zeros((), jnp.bfloa...  3.15 us
  transfers between devices with their start and end apart: 13, of which 6 were waited for; matrix products, arithmetic and copies ran while one was open for 4% of the time, Pallas kernels for 12%

profile of v1, /device:TPU:21, one launch (start us, length us, event | category | flops | bytes accessed | tf_op | source)
XLA Modules:
  0.0 108.6 jit_solution(6674903746988459948)
XLA Ops:
  0.0 0.7 convert_bitcast_fusion
  0.7 0.8 pad_maximum_fusion.2
  1.5 3.5 %collective-permute-start = (bf16[1,8,2688]{2,1,0:T(8,128)(2,1)S(1)}, bf16[1,8,2688]{2,1,0:T(8,128)(2,1)S(1)}, u32[]{:S(2)}, u32[]{:S(2)}) collective-permute-start(bf16[1,8,2688]{2,1,0:T(8,128)(2,1)S(1)} %pad_maximum_fusion.2), channel_id=1, source_target_pairs={{0,8},{8,16},{16,24},{24,32},{32,40},{40,48},{48,56},{56,64},{64,7... | collective-permute-start | bytes 129032 | tf_op jit(solution)/shard_map/ppermute | solution.py:20
  5.1 0.7 pad_dynamic-slice_fusion
  6.0 1.0 fusion.18
  7.4 0.7 reshape.102.keep_ref
  8.1 1.2 %reshape.98.refs_2_ = f32[1,384]{1,0:T(1,128)} reshape(f32[384]{0:T(512)} %param.14) | data formatting | bytes 3072 | tf_op jit(solution)/shard_map/reshape | solution.py:259
  9.3 0.8 pad_maximum_fusion
  10.1 1.8 %collective-permute-start.1 = (bf16[2,8,2688]{2,1,0:T(8,128)(2,1)S(1)}, bf16[2,8,2688]{2,1,0:T(8,128)(2,1)S(1)}, u32[]{:S(2)}, u32[]{:S(2)}) collective-permute-start(bf16[2,8,2688]{2,1,0:T(8,128)(2,1)S(1)} %get-tuple-element.23), channel_id=1, source_target_pairs={{0,1},{1,2},{2,3},{3,4},{4,5},{5,6},{6,7},{7,0},{8,9},{9,10},{10,1... | collective-permute-start | bytes 258056 | tf_op jit(solution)/shard_map/ppermute | solution.py:226
  11.9 0.2 collective-permute-start.2
  12.1 0.7 collective-permute-start.3
  12.8 2.5 %collective-permute-start.4 = (bf16[2,8,2688]{2,1,0:T(8,128)(2,1)S(1)}, bf16[2,8,2688]{2,1,0:T(8,128)(2,1)S(1)}, u32[]{:S(2)}, u32[]{:S(2)}) collective-permute-start(bf16[2,8,2688]{2,1,0:T(8,128)(2,1)S(1)} %get-tuple-element.23), channel_id=1, source_target_pairs={{0,4},{1,5},{2,6},{3,7},{4,0},{5,1},{6,2},{7,3},{8,12},{9,13},{10,... | collective-permute-start | bytes 258056 | tf_op jit(solution)/shard_map/ppermute | solution.py:226
  15.3 1.0 collective-permute-start.5
  16.3 0.9 collective-permute-start.6
  17.2 0.2 collective-permute-start.7
  17.4 0.9 collective-permute-done.3
  18.3 1.7 %collective-permute-done.4 = bf16[2,8,2688]{2,1,0:T(8,128)(2,1)S(1)} collective-permute-done((bf16[2,8,2688]{2,1,0:T(8,128)(2,1)S(1)}, bf16[2,8,2688]{2,1,0:T(8,128)(2,1)S(1)}, u32[]{:S(2)}, u32[]{:S(2)}) %collective-permute-start.4) | collective-permute-done | bytes 86048 | tf_op jit(solution)/shard_map/ppermute | solution.py:226
  20.0 0.8 collective-permute-done.5
  20.8 0.8 collective-permute-done.6
  21.6 1.3 %collective-permute-done.7 = bf16[2,8,2688]{2,1,0:T(8,128)(2,1)S(1)} collective-permute-done((bf16[2,8,2688]{2,1,0:T(8,128)(2,1)S(1)}, bf16[2,8,2688]{2,1,0:T(8,128)(2,1)S(1)}, u32[]{:S(2)}, u32[]{:S(2)}) %collective-permute-start.7) | collective-permute-done | bytes 86048 | tf_op jit(solution)/shard_map/ppermute | solution.py:226
  23.1 0.3 convolution_convert_fusion
  23.4 1.6 %reshape.96 = bf16[8,6,160,16]{3,2,1,0:T(8,128)(2,1)S(1)} reshape(bf16[2,24,2560]{2,1,0:T(8,128)(2,1)S(1)} %convolution_convert_fusion) | data formatting | bytes 491520 | tf_op jit(solution)/shard_map/reshape | solution.py:240
  24.9 1.0 copy.20
  26.0 0.1 slice_dynamic-update-slice_fusion.14
  26.1 0.1 slice_dynamic-update-slice_fusion.13
  26.4 0.1 slice_dynamic-update-slice_fusion.11
  26.5 0.2 slice_dynamic-update-slice_fusion.10
  26.8 0.2 slice_dynamic-update-slice_fusion.9
  27.5 0.2 slice_dynamic-update-slice_fusion.21
  27.8 0.1 slice_dynamic-update-slice_fusion.17
  28.2 1.3 %fusion.20 = f32[6,4,160,384]{3,2,1,0:T(8,128)S(1)} fusion(bf16[6,4,160,144]{2,3,1,0:T(8,128)(2,1)S(1)} %slice_dynamic-update-slice_fusion.15, bf16[144,384,1,1]{1,0,3,2:T(8,128)(2,1)S(1)} %bitcast.40), kind=kOutput, calls=%fused_computation.75 | convolution fusion | flops 424673280 | bytes 7114752 | tf_op jit(solution)/shard_map/dot_general | solution.py:60
  29.5 1.3 %fusion.19 = f32[6,4,160,384]{3,2,1,0:T(8,128)S(1)} fusion(bf16[6,4,160,144]{2,3,1,0:T(8,128)(2,1)S(1)} %get-tuple-element.16, bf16[144,384,1,1]{1,0,3,2:T(8,128)(2,1)S(1)} %bitcast.39), kind=kOutput, calls=%fused_computation.74 | convolution fusion | flops 424673280 | bytes 7114752 | tf_op jit(solution)/shard_map/dot_general | solution.py:60
  30.7 3.1 %fusion = (f32[6,4,160]{2,1,0:T(4,128)S(1)}, bf16[6,4,160,384]{3,2,1,0:T(8,128)(2,1)S(1)}) fusion(bf16[6,4,160,144]{2,3,1,0:T(8,128)(2,1)S(1)} %get-tuple-element.9, bf16[144,384,1,1]{1,0,3,2:T(8,128)(2,1)S(1)} %bitcast.38, f32[6,4,160,384]{3,2,1,0:T(8,128)S(1)} %fusion.20, pred[6]{0:T(512)(128)(4,1)S(1)} %get-tuple-element.26, ...), kind=kOutput, calls=%fused_computation.2 | convolution fusion | flops 436465920 | bytes 15977484 | tf_op jit(solution)/shard_map/dot_general | solution.py:60
  33.9 3.2 %fusion.8.refs_0_ = bf16[6,4,160,384]{3,2,1,0:T(8,128)(2,1)} fusion(bf16[6,4,160,384]{3,2,1,0:T(8,128)(2,1)S(1)} %get-tuple-element.30.refs_4_.refs_7_, f32[384]{0:T(512)S(1)} %copy-done.2, f32[6,4,160]{2,1,0:T(4,128)S(1)} %add_rsqrt_fusion, pred[4]{0:T(512)(128)(4,1)S(1)} %compare_and_fusion.1), kind=kLoop, calls=%fused_computation.12 | loop fusion | flops 13271040 | bytes 5915140 | tf_op jit(solution)/shard_map/jit(_where)/select_n | solution.py:257
  37.1 21.8 %shard_map.82 = bf16[1280,384]{1,0:T(8,128)(2,1)} custom-call(s32[12]{0:T(128)} %reshape.102.keep_ref, bf16[6,4,160,384]{3,2,1,0:T(8,128)(2,1)} %fusion.8.refs_0_, bf16[10368,384]{1,0:T(8,128)(2,1)} %bitcast.41, f32[1,384]{1,0:T(1,128)} %reshape.98.refs_2_), custom_call_target="tpu_custom_call" | custom-call | flops 10192158720 | bytes 10911744 | tf_op jit(solution)/shard_map/pallas_call | solution.py:171
  58.9 1.4 %fusion.16 = (bf16[4,1,160,384]{3,2,1,0:T(8,128)(2,1)S(1)}, bf16[4,1,160,384]{3,2,1,0:T(8,128)(2,1)S(1)}) fusion(bf16[4,2,160,384]{3,2,1,0:T(8,128)(2,1)} %bitcast.33), kind=kLoop, calls=%fused_computation.71 | loop fusion | bytes 1966080 | tf_op jit(solution)/shard_map/slice | solution.py:272
  60.3 3.6 %collective-permute-start.8 = (bf16[4,1,160,384]{3,2,1,0:T(8,128)(2,1)S(1)}, bf16[4,1,160,384]{3,2,1,0:T(8,128)(2,1)S(1)}, u32[]{:S(2)}, u32[]{:S(2)}) collective-permute-start(bf16[4,1,160,384]{3,2,1,0:T(8,128)(2,1)S(1)} %get-tuple-element.6), channel_id=1, source_target_pairs={{0,1},{1,2},{2,3},{3,4},{4,5},{5,6},{6,7},{8,9},{9,10},{10,11},{11... | collective-permute-start | bytes 1474568 | tf_op jit(solution)/shard_map/ppermute | solution.py:20
  63.9 1.9 %collective-permute-start.9 = (bf16[4,1,160,384]{3,2,1,0:T(8,128)(2,1)S(1)}, bf16[4,1,160,384]{3,2,1,0:T(8,128)(2,1)S(1)}, u32[]{:S(2)}, u32[]{:S(2)}) collective-permute-start(bf16[4,1,160,384]{3,2,1,0:T(8,128)(2,1)S(1)} %get-tuple-element.5), channel_id=1, source_target_pairs={{1,0},{2,1},{3,2},{4,3},{5,4},{6,5},{7,6},{9,8},{10,9},{11,10},{12... | collective-permute-start | bytes 1474568 | tf_op jit(solution)/shard_map/ppermute | solution.py:20
  65.9 3.5 %collective-permute-start.10 = (bf16[2,2,160,384]{3,2,1,0:T(8,128)(2,1)S(1)}, bf16[2,2,160,384]{3,2,1,0:T(8,128)(2,1)S(1)}, u32[]{:S(2)}, u32[]{:S(2)}) collective-permute-start(bf16[2,2,160,384]{3,2,1,0:T(8,128)(2,1)S(1)} %bitcast.36), channel_id=1, source_target_pairs={{0,8},{8,16},{16,24},{24,32},{32,40},{40,48},{48,56},{56,64},{64,7... | collective-permute-start | bytes 1474568 | tf_op jit(solution)/shard_map/ppermute | solution.py:20
  69.5 5.0 %collective-permute-start.11 = (bf16[2,1,160,384]{3,2,1,0:T(8,128)(2,1)S(1)}, bf16[2,1,160,384]{3,2,1,0:T(8,128)(2,1)S(1)}, u32[]{:S(2)}, u32[]{:S(2)}) collective-permute-start(bf16[2,1,160,384]{3,2,1,0:T(8,128)(2,1)S(1)} %get-tuple-element.8), channel_id=1, source_target_pairs={{0,9},{1,10},{2,11},{3,12},{4,13},{5,14},{6,15},{8,17},{9,18},{10,... | collective-permute-start | bytes 737288 | tf_op jit(solution)/shard_map/ppermute | solution.py:31
  74.5 2.1 %collective-permute-start.12 = (bf16[2,1,160,384]{3,2,1,0:T(8,128)(2,1)S(1)}, bf16[2,1,160,384]{3,2,1,0:T(8,128)(2,1)S(1)}, u32[]{:S(2)}, u32[]{:S(2)}) collective-permute-start(bf16[2,1,160,384]{3,2,1,0:T(8,128)(2,1)S(1)} %get-tuple-element.7), channel_id=1, source_target_pairs={{1,8},{2,9},{3,10},{4,11},{5,12},{6,13},{7,14},{9,16},{10,17},{11,... | collective-permute-start | bytes 737288 | tf_op jit(solution)/shard_map/ppermute | solution.py:31
  76.7 0.8 copy-done.3
  77.5 0.2 copy-done.4
  77.6 13.2 %shard_map.83.refs_8_ = bf16[1280,384]{1,0:T(8,128)(2,1)} custom-call(s32[12]{0:T(128)} %reshape.102.keep_ref, bf16[4,2,160,384]{3,2,1,0:T(8,128)(2,1)} %bitcast.34, bf16[4,1,160,384]{3,2,1,0:T(8,128)(2,1)} %copy-done.3, bf16[4,1,160,384]{3,2,1,0:T(8,128)(2,1)} %copy-done.4, bf16[10368,384]{1,0:T(8,128)(2,1)} %bitcast.42, bf16[6,4,160,384]{3,2,1,0:T(8,128)(2,1)} %copy-done), custom_call_target="tpu_custom_call" | custom-call | flops 5096079360 | bytes 9437184 | tf_op jit(solution)/shard_map/pallas_call | solution.py:171
  90.8 2.6 %collective-permute-done.11.refs_4_ = bf16[2,1,160,384]{3,2,1,0:T(8,128)(2,1)S(1)} collective-permute-done((bf16[2,1,160,384]{3,2,1,0:T(8,128)(2,1)S(1)}, bf16[2,1,160,384]{3,2,1,0:T(8,128)(2,1)S(1)}, u32[]{:S(2)}, u32[]{:S(2)}) %collective-permute-start.11) | collective-permute-done | bytes 245792 | tf_op jit(solution)/shard_map/ppermute | solution.py:31
  93.4 0.7 copy-done.6
  94.2 0.8 copy-done.5
  95.0 13.5 %shard_map.84 = bf16[1280,384]{1,0:T(8,128)(2,1)} custom-call(s32[12]{0:T(128)} %reshape.102.keep_ref, bf16[4,2,160,384]{3,2,1,0:T(8,128)(2,1)} %bitcast.35, bf16[4,1,160,384]{3,2,1,0:T(8,128)(2,1)} %copy-done.3, bf16[4,1,160,384]{3,2,1,0:T(8,128)(2,1)} %copy-done.4, bf16[2,2,160,384]{3,2,1,0:T(8,128)(2,1)} %copy-done.5, ...), custom_call_target="tpu_custom_call", output_to_operand_aliasing={{}: (9, {})} | custom-call | flops 5096079360 | bytes 9437184 | tf_op jit(solution)/shard_map/pallas_call | solution.py:171
  (57 shorter events, 2.1 us)
Async XLA Ops:
  1.5 7.8 %collective-permute-start = (bf16[1,8,2688]{2,1,0:T(8,128)(2,1)S(1)}, bf16[1,8,2688]{2,1,0:T(8,128)(2,1)S(1)}, u32[]{:S(2)}, u32[]{:S(2)}) collective-permute-start(bf16[1,8,2688]{2,1,0:T(8,128)(2,1)S(1)} %pad_maximum_fusion.2), channel_id=1, source_target_pairs={{0,8},{8,16},{16,24},{24,32},{32,40},{40,48},{48,56},{56,64},{64,7... | collective-permute-start | bytes 129032 | tf_op jit(solution)/shard_map/ppermute | solution.py:20
  10.1 6.1 %collective-permute-start.1 = (bf16[2,8,2688]{2,1,0:T(8,128)(2,1)S(1)}, bf16[2,8,2688]{2,1,0:T(8,128)(2,1)S(1)}, u32[]{:S(2)}, u32[]{:S(2)}) collective-permute-start(bf16[2,8,2688]{2,1,0:T(8,128)(2,1)S(1)} %get-tuple-element.23), channel_id=1, source_target_pairs={{0,1},{1,2},{2,3},{3,4},{4,5},{5,6},{6,7},{7,0},{8,9},{9,10},{10,1... | collective-permute-start | bytes 258056 | tf_op jit(solution)/shard_map/ppermute | solution.py:226
  11.9 5.2 %collective-permute-start.2 = (bf16[2,8,2688]{2,1,0:T(8,128)(2,1)S(1)}, bf16[2,8,2688]{2,1,0:T(8,128)(2,1)S(1)}, u32[]{:S(2)}, u32[]{:S(2)}) collective-permute-start(bf16[2,8,2688]{2,1,0:T(8,128)(2,1)S(1)} %get-tuple-element.23), channel_id=1, source_target_pairs={{0,2},{1,3},{2,4},{3,5},{4,6},{5,7},{6,0},{7,1},{8,10},{9,11},{10,... | collective-permute-start | bytes 258056 | tf_op jit(solution)/shard_map/ppermute | solution.py:226
  12.1 6.1 %collective-permute-start.3 = (bf16[2,8,2688]{2,1,0:T(8,128)(2,1)S(1)}, bf16[2,8,2688]{2,1,0:T(8,128)(2,1)S(1)}, u32[]{:S(2)}, u32[]{:S(2)}) collective-permute-start(bf16[2,8,2688]{2,1,0:T(8,128)(2,1)S(1)} %get-tuple-element.23), channel_id=1, source_target_pairs={{0,3},{1,4},{2,5},{3,6},{4,7},{5,0},{6,1},{7,2},{8,11},{9,12},{10,... | collective-permute-start | bytes 258056 | tf_op jit(solution)/shard_map/ppermute | solution.py:226
  12.8 7.1 %collective-permute-start.4 = (bf16[2,8,2688]{2,1,0:T(8,128)(2,1)S(1)}, bf16[2,8,2688]{2,1,0:T(8,128)(2,1)S(1)}, u32[]{:S(2)}, u32[]{:S(2)}) collective-permute-start(bf16[2,8,2688]{2,1,0:T(8,128)(2,1)S(1)} %get-tuple-element.23), channel_id=1, source_target_pairs={{0,4},{1,5},{2,6},{3,7},{4,0},{5,1},{6,2},{7,3},{8,12},{9,13},{10,... | collective-permute-start | bytes 258056 | tf_op jit(solution)/shard_map/ppermute | solution.py:226
  15.3 5.5 %collective-permute-start.5 = (bf16[2,8,2688]{2,1,0:T(8,128)(2,1)S(1)}, bf16[2,8,2688]{2,1,0:T(8,128)(2,1)S(1)}, u32[]{:S(2)}, u32[]{:S(2)}) collective-permute-start(bf16[2,8,2688]{2,1,0:T(8,128)(2,1)S(1)} %get-tuple-element.23), channel_id=1, source_target_pairs={{0,5},{1,6},{2,7},{3,0},{4,1},{5,2},{6,3},{7,4},{8,13},{9,14},{10,... | collective-permute-start | bytes 258056 | tf_op jit(solution)/shard_map/ppermute | solution.py:226
  16.3 5.3 %collective-permute-start.6 = (bf16[2,8,2688]{2,1,0:T(8,128)(2,1)S(1)}, bf16[2,8,2688]{2,1,0:T(8,128)(2,1)S(1)}, u32[]{:S(2)}, u32[]{:S(2)}) collective-permute-start(bf16[2,8,2688]{2,1,0:T(8,128)(2,1)S(1)} %get-tuple-element.23), channel_id=1, source_target_pairs={{0,6},{1,7},{2,0},{3,1},{4,2},{5,3},{6,4},{7,5},{8,14},{9,15},{10,... | collective-permute-start | bytes 258056 | tf_op jit(solution)/shard_map/ppermute | solution.py:226
  17.2 5.8 %collective-permute-start.7 = (bf16[2,8,2688]{2,1,0:T(8,128)(2,1)S(1)}, bf16[2,8,2688]{2,1,0:T(8,128)(2,1)S(1)}, u32[]{:S(2)}, u32[]{:S(2)}) collective-permute-start(bf16[2,8,2688]{2,1,0:T(8,128)(2,1)S(1)} %get-tuple-element.23), channel_id=1, source_target_pairs={{0,7},{1,0},{2,1},{3,2},{4,3},{5,4},{6,5},{7,6},{8,15},{9,8},{10,9... | collective-permute-start | bytes 258056 | tf_op jit(solution)/shard_map/ppermute | solution.py:226
  30.7 3.2 %copy-start.2 = (f32[384]{0:T(512)S(1)}, f32[384]{0:T(512)}, u32[]{:S(2)}) copy-start(f32[384]{0:T(512)} %param.12) | copy-start | bytes 4612
  33.9 3.2 %copy-start = (bf16[6,4,160,384]{3,2,1,0:T(8,128)(2,1)}, bf16[6,4,160,384]{3,2,1,0:T(8,128)(2,1)S(1)}, u32[]{:S(2)}) copy-start(bf16[6,4,160,384]{3,2,1,0:T(8,128)(2,1)S(1)} %get-tuple-element.30.refs_4_.refs_7_) | copy-start | bytes 8847364
  58.9 7.0 %copy-start.1 = (bf16[1280,384]{1,0:T(8,128)(2,1)S(1)}, bf16[1280,384]{1,0:T(8,128)(2,1)}, u32[]{:S(2)}) copy-start(bf16[1280,384]{1,0:T(8,128)(2,1)} %shard_map.82) | copy-start | bytes 2949124
  60.3 16.4 %collective-permute-start.8 = (bf16[4,1,160,384]{3,2,1,0:T(8,128)(2,1)S(1)}, bf16[4,1,160,384]{3,2,1,0:T(8,128)(2,1)S(1)}, u32[]{:S(2)}, u32[]{:S(2)}) collective-permute-start(bf16[4,1,160,384]{3,2,1,0:T(8,128)(2,1)S(1)} %get-tuple-element.6), channel_id=1, source_target_pairs={{0,1},{1,2},{2,3},{3,4},{4,5},{5,6},{6,7},{8,9},{9,10},{10,11},{11... | collective-permute-start | bytes 1474568 | tf_op jit(solution)/shard_map/ppermute | solution.py:20
  63.9 12.8 %collective-permute-start.9 = (bf16[4,1,160,384]{3,2,1,0:T(8,128)(2,1)S(1)}, bf16[4,1,160,384]{3,2,1,0:T(8,128)(2,1)S(1)}, u32[]{:S(2)}, u32[]{:S(2)}) collective-permute-start(bf16[4,1,160,384]{3,2,1,0:T(8,128)(2,1)S(1)} %get-tuple-element.5), channel_id=1, source_target_pairs={{1,0},{2,1},{3,2},{4,3},{5,4},{6,5},{7,6},{9,8},{10,9},{11,10},{12... | collective-permute-start | bytes 1474568 | tf_op jit(solution)/shard_map/ppermute | solution.py:20
  65.9 27.5 %collective-permute-start.10 = (bf16[2,2,160,384]{3,2,1,0:T(8,128)(2,1)S(1)}, bf16[2,2,160,384]{3,2,1,0:T(8,128)(2,1)S(1)}, u32[]{:S(2)}, u32[]{:S(2)}) collective-permute-start(bf16[2,2,160,384]{3,2,1,0:T(8,128)(2,1)S(1)} %bitcast.36), channel_id=1, source_target_pairs={{0,8},{8,16},{16,24},{24,32},{32,40},{40,48},{48,56},{56,64},{64,7... | collective-permute-start | bytes 1474568 | tf_op jit(solution)/shard_map/ppermute | solution.py:20
  69.5 23.9 %collective-permute-start.11 = (bf16[2,1,160,384]{3,2,1,0:T(8,128)(2,1)S(1)}, bf16[2,1,160,384]{3,2,1,0:T(8,128)(2,1)S(1)}, u32[]{:S(2)}, u32[]{:S(2)}) collective-permute-start(bf16[2,1,160,384]{3,2,1,0:T(8,128)(2,1)S(1)} %get-tuple-element.8), channel_id=1, source_target_pairs={{0,9},{1,10},{2,11},{3,12},{4,13},{5,14},{6,15},{8,17},{9,18},{10,... | collective-permute-start | bytes 737288 | tf_op jit(solution)/shard_map/ppermute | solution.py:31
  74.5 18.9 %collective-permute-start.12 = (bf16[2,1,160,384]{3,2,1,0:T(8,128)(2,1)S(1)}, bf16[2,1,160,384]{3,2,1,0:T(8,128)(2,1)S(1)}, u32[]{:S(2)}, u32[]{:S(2)}) collective-permute-start(bf16[2,1,160,384]{3,2,1,0:T(8,128)(2,1)S(1)} %get-tuple-element.7), channel_id=1, source_target_pairs={{1,8},{2,9},{3,10},{4,11},{5,12},{6,13},{7,14},{9,16},{10,17},{11,... | collective-permute-start | bytes 737288 | tf_op jit(solution)/shard_map/ppermute | solution.py:31
  76.7 0.8 copy-start.3
  76.7 1.0 copy-start.4
  93.4 0.7 copy-start.6
  93.4 0.8 copy-start.7
  94.2 0.8 copy-start.5

commit v2 on v1

--- a/solution.py
+++ b/solution.py
@@ -220,11 +220,12 @@
     earlier = shifted(packed, "tm", 1)
     both = jnp.concatenate([earlier, packed], axis=0)
     parts_total = lax.axis_size("rows")
-    pieces = [both]
-    for by in range(1, parts_total):
-        ring = [(i, (i + by) % parts_total) for i in range(parts_total)]
-        pieces.append(lax.ppermute(both, "rows", ring))
-    gathered = jnp.concatenate(pieces, axis=1)
+    gathered = both
+    span = 1
+    while span < parts_total:
+        swap = [(i, i ^ span) for i in range(parts_total)]
+        gathered = jnp.concatenate([gathered, lax.ppermute(gathered, "rows", swap)], axis=1)
+        span *= 2
     values = gathered[:, :, :packed_rows]
     slot_ids = gathered[:, :, packed_rows].astype(jnp.int32)
 

time: 109 us -> 119 us (1.092)
  waiting for transfers between devices: 8.12 us -> 20.7 us
  starting transfers between devices: 26.9 us -> 21.7 us
  other arithmetic: 5.84 us -> 7.48 us
    ppermute x7 -> x3, waiting for transfers between devices: 5.53 us -> 14 us  [on_device(): lax.ppermute(gathered, 'rows', swap)]
    ppermute x7 -> x3, starting transfers between devices: 7.17 us -> 3.04 us  [on_device(): lax.ppermute(gathered, 'rows', swap)]
    ppermute x4, waiting for transfers between devices: 0.01 us -> 2.26 us  [shifted(): return lax.ppermute(x, axis, pairs)]
    ppermute x2, waiting for transfers between devices: 2.57 us -> 4.4 us  [diagonal(): return lax.ppermute(x, ('tm', 'rows'), pairs)]
    concatenate x0 -> x2, other arithmetic: none -> 1.61 us  [on_device(): jnp.concatenate([gathered, lax.ppermute(gathered, 'rows', swap)], axis=1)]
    unnamed x40 -> x36, local copies, waits for them, and re-layouts: 4.16 us -> 4.1 us
  transfers between devices with their start and end apart: 13 -> 9, of which waited for: 6 -> 4; matrix products, arithmetic and copies ran while one was open for 4% -> 4% of each run, Pallas kernels for 12% -> 11%
where the time goes in v2:
time: 119 us; the launch traced here: 118 us
  Pallas kernels  48.4 us (41%)
  starting transfers between devices  21.7 us (18%)
  waiting for transfers between devices  20.7 us (17%)
  local copies, waits for them, and re-layouts  12.7 us (11%)
  other arithmetic  7.48 us (6%)
  matrix products  5.94 us (5%)
    pallas_call x3, Pallas kernels, conv_call(): pl.pallas_call(functools.partial(conv_kernel, layout=layout, mode=mode, p...  48.4 us
    ppermute x3, waiting for transfers between devices, on_device(): lax.ppermute(gathered, 'rows', swap)  14 us
    ppermute x4, starting transfers between devices, shifted(): return lax.ppermute(x, axis, pairs)  11.8 us
    ppermute x2, starting transfers between devices, diagonal(): return lax.ppermute(x, ('tm', 'rows'), pairs)  6.94 us
    dot_general x3, matrix products, local_conv(): jnp.dot(stacked, weight[tap_time].reshape(9 * channels, outputs), preferr...  5.65 us
    ppermute x2, waiting for transfers between devices, diagonal(): return lax.ppermute(x, ('tm', 'rows'), pairs)  4.4 us
    unnamed x36, local copies, waits for them, and re-layouts  4.1 us
    select_n x1, other arithmetic, on_device(): jnp.where(row_ok[None, :, None, None], first_act, jnp.zeros((), jnp.bfloa...  3.19 us
  transfers between devices with their start and end apart: 9, of which 4 were waited for; matrix products, arithmetic and copies ran while one was open for 4% of the time, Pallas kernels for 11%

profile of v2, /device:TPU:21, one launch (start us, length us, event | category | flops | bytes accessed | tf_op | source)
XLA Modules:
  0.0 117.5 jit_solution(5761676078156255270)
XLA Ops:
  0.0 0.7 convert_bitcast_fusion
  0.7 0.8 pad_maximum_fusion.12
  1.5 3.5 %collective-permute-start = (bf16[1,8,2688]{2,1,0:T(8,128)(2,1)S(1)}, bf16[1,8,2688]{2,1,0:T(8,128)(2,1)S(1)}, u32[]{:S(2)}, u32[]{:S(2)}) collective-permute-start(bf16[1,8,2688]{2,1,0:T(8,128)(2,1)S(1)} %pad_maximum_fusion.12), channel_id=1, source_target_pairs={{0,8},{8,16},{16,24},{24,32},{32,40},{40,48},{48,56},{56,64},{64,7... | collective-permute-start | bytes 129032 | tf_op jit(solution)/shard_map/ppermute | solution.py:20
  5.1 0.7 pad_dynamic-slice_fusion
  6.2 2.2 %collective-permute-done = bf16[1,8,2688]{2,1,0:T(8,128)(2,1)S(1)} collective-permute-done((bf16[1,8,2688]{2,1,0:T(8,128)(2,1)S(1)}, bf16[1,8,2688]{2,1,0:T(8,128)(2,1)S(1)}, u32[]{:S(2)}, u32[]{:S(2)}) %collective-permute-start) | collective-permute-done | bytes 43040 | tf_op jit(solution)/shard_map/ppermute | solution.py:20
  8.5 0.8 maximum_maximum_fusion
  9.3 1.7 %collective-permute-start.1 = (bf16[2,8,2688]{2,1,0:T(8,128)(2,1)S(1)}, bf16[2,8,2688]{2,1,0:T(8,128)(2,1)S(1)}, u32[]{:S(2)}, u32[]{:S(2)}) collective-permute-start(bf16[2,8,2688]{2,1,0:T(8,128)(2,1)S(1)} %maximum_maximum_fusion), channel_id=1, source_target_pairs={{0,1},{1,0},{2,3},{3,2},{4,5},{5,4},{6,7},{7,6},{8,9},{9,8},{10,11... | collective-permute-start | bytes 258056 | tf_op jit(solution)/shard_map/ppermute | solution.py:227
  11.1 0.7 reshape.102.keep_ref
  11.8 1.2 %reshape.98.refs_2_ = f32[1,384]{1,0:T(1,128)} reshape(f32[384]{0:T(512)} %param.14) | data formatting | bytes 3072 | tf_op jit(solution)/shard_map/reshape | solution.py:260
  13.0 0.8 pad_maximum_fusion.11
  13.8 1.0 collective-permute-start.2
  14.9 5.0 %collective-permute-done.2 = bf16[2,16,2688]{2,1,0:T(8,128)(2,1)S(1)} collective-permute-done((bf16[2,16,2688]{2,1,0:T(8,128)(2,1)S(1)}, bf16[2,16,2688]{2,1,0:T(8,128)(2,1)S(1)}, u32[]{:S(2)}, u32[]{:S(2)}) %collective-permute-start.2) | collective-permute-done | bytes 172064 | tf_op jit(solution)/shard_map/ppermute | solution.py:227
  19.9 0.8 pad_maximum_fusion.10
  20.7 0.3 collective-permute-start.3
  21.0 1.0 fusion.18
  22.1 9.0 %collective-permute-done.3 = bf16[2,32,2688]{2,1,0:T(8,128)(2,1)S(1)} collective-permute-done((bf16[2,32,2688]{2,1,0:T(8,128)(2,1)S(1)}, bf16[2,32,2688]{2,1,0:T(8,128)(2,1)S(1)}, u32[]{:S(2)}, u32[]{:S(2)}) %collective-permute-start.3) | collective-permute-done | bytes 344096 | tf_op jit(solution)/shard_map/ppermute | solution.py:227
  31.2 0.3 convolution_convert_fusion
  31.5 1.6 %reshape.96 = bf16[8,6,160,16]{3,2,1,0:T(8,128)(2,1)S(1)} reshape(bf16[2,24,2560]{2,1,0:T(8,128)(2,1)S(1)} %convolution_convert_fusion) | data formatting | bytes 491520 | tf_op jit(solution)/shard_map/reshape | solution.py:241
  33.1 1.0 copy.20
  34.1 0.1 slice_dynamic-update-slice_fusion.14
  34.3 0.1 slice_dynamic-update-slice_fusion.13
  34.4 0.1 slice_dynamic-update-slice_fusion.12
  34.5 0.1 slice_dynamic-update-slice_fusion.11
  34.7 0.2 slice_dynamic-update-slice_fusion.10
  34.9 0.2 slice_dynamic-update-slice_fusion.9
  35.1 0.1 slice_dynamic-update-slice_fusion.24
  35.3 0.1 slice_dynamic-update-slice_fusion.23
  35.6 0.2 slice_dynamic-update-slice_fusion.21
  35.9 0.1 slice_dynamic-update-slice_fusion.17
  36.2 0.1 slice_dynamic-update-slice_fusion.15
  36.3 1.3 %fusion.20 = f32[6,4,160,384]{3,2,1,0:T(8,128)S(1)} fusion(bf16[6,4,160,144]{2,3,1,0:T(8,128)(2,1)S(1)} %slice_dynamic-update-slice_fusion.15, bf16[144,384,1,1]{1,0,3,2:T(8,128)(2,1)S(1)} %bitcast.40), kind=kOutput, calls=%fused_computation.74 | convolution fusion | flops 424673280 | bytes 7114752 | tf_op jit(solution)/shard_map/dot_general | solution.py:60
  37.6 1.3 %fusion.19 = f32[6,4,160,384]{3,2,1,0:T(8,128)S(1)} fusion(bf16[6,4,160,144]{2,3,1,0:T(8,128)(2,1)S(1)} %get-tuple-element.16, bf16[144,384,1,1]{1,0,3,2:T(8,128)(2,1)S(1)} %bitcast.39), kind=kOutput, calls=%fused_computation.73 | convolution fusion | flops 424673280 | bytes 7114752 | tf_op jit(solution)/shard_map/dot_general | solution.py:60
  38.9 3.1 %fusion = (f32[6,4,160]{2,1,0:T(4,128)S(1)}, bf16[6,4,160,384]{3,2,1,0:T(8,128)(2,1)S(1)}) fusion(bf16[6,4,160,144]{2,3,1,0:T(8,128)(2,1)S(1)} %get-tuple-element.9, bf16[144,384,1,1]{1,0,3,2:T(8,128)(2,1)S(1)} %bitcast.38, f32[6,4,160,384]{3,2,1,0:T(8,128)S(1)} %fusion.20, pred[6]{0:T(512)(128)(4,1)S(1)} %get-tuple-element.24, ...), kind=kOutput, calls=%fused_computation.2 | convolution fusion | flops 436465920 | bytes 15977484 | tf_op jit(solution)/shard_map/dot_general | solution.py:60
  42.0 3.2 %fusion.8.refs_0_ = bf16[6,4,160,384]{3,2,1,0:T(8,128)(2,1)} fusion(bf16[6,4,160,384]{3,2,1,0:T(8,128)(2,1)S(1)} %get-tuple-element.28.refs_4_.refs_7_, f32[384]{0:T(512)S(1)} %copy-done.3, f32[6,4,160]{2,1,0:T(4,128)S(1)} %add_rsqrt_fusion, pred[4]{0:T(512)(128)(4,1)S(1)} %compare_and_fusion.1), kind=kLoop, calls=%fused_computation.12 | loop fusion | flops 13271040 | bytes 5915140 | tf_op jit(solution)/shard_map/jit(_where)/select_n | solution.py:258
  45.2 21.8 %shard_map.82 = bf16[1280,384]{1,0:T(8,128)(2,1)} custom-call(s32[12]{0:T(128)} %reshape.102.keep_ref, bf16[6,4,160,384]{3,2,1,0:T(8,128)(2,1)} %fusion.8.refs_0_, bf16[10368,384]{1,0:T(8,128)(2,1)} %bitcast.41, f32[1,384]{1,0:T(1,128)} %reshape.98.refs_2_), custom_call_target="tpu_custom_call" | custom-call | flops 10192158720 | bytes 10911744 | tf_op jit(solution)/shard_map/pallas_call | solution.py:171
  67.1 1.4 %fusion.16 = (bf16[4,1,160,384]{3,2,1,0:T(8,128)(2,1)S(1)}, bf16[4,1,160,384]{3,2,1,0:T(8,128)(2,1)S(1)}) fusion(bf16[4,2,160,384]{3,2,1,0:T(8,128)(2,1)} %bitcast.33), kind=kLoop, calls=%fused_computation.70 | loop fusion | bytes 1966080 | tf_op jit(solution)/shard_map/slice | solution.py:273
  68.4 4.4 %collective-permute-start.4 = (bf16[4,1,160,384]{3,2,1,0:T(8,128)(2,1)S(1)}, bf16[4,1,160,384]{3,2,1,0:T(8,128)(2,1)S(1)}, u32[]{:S(2)}, u32[]{:S(2)}) collective-permute-start(bf16[4,1,160,384]{3,2,1,0:T(8,128)(2,1)S(1)} %get-tuple-element.6), channel_id=1, source_target_pairs={{0,1},{1,2},{2,3},{3,4},{4,5},{5,6},{6,7},{8,9},{9,10},{10,11},{11... | collective-permute-start | bytes 1474568 | tf_op jit(solution)/shard_map/ppermute | solution.py:20
  72.8 1.9 %collective-permute-start.5 = (bf16[4,1,160,384]{3,2,1,0:T(8,128)(2,1)S(1)}, bf16[4,1,160,384]{3,2,1,0:T(8,128)(2,1)S(1)}, u32[]{:S(2)}, u32[]{:S(2)}) collective-permute-start(bf16[4,1,160,384]{3,2,1,0:T(8,128)(2,1)S(1)} %get-tuple-element.5), channel_id=1, source_target_pairs={{1,0},{2,1},{3,2},{4,3},{5,4},{6,5},{7,6},{9,8},{10,9},{11,10},{12... | collective-permute-start | bytes 1474568 | tf_op jit(solution)/shard_map/ppermute | solution.py:20
  74.8 1.9 %collective-permute-start.6 = (bf16[2,2,160,384]{3,2,1,0:T(8,128)(2,1)S(1)}, bf16[2,2,160,384]{3,2,1,0:T(8,128)(2,1)S(1)}, u32[]{:S(2)}, u32[]{:S(2)}) collective-permute-start(bf16[2,2,160,384]{3,2,1,0:T(8,128)(2,1)S(1)} %bitcast.36), channel_id=1, source_target_pairs={{0,8},{8,16},{16,24},{24,32},{32,40},{40,48},{48,56},{56,64},{64,7... | collective-permute-start | bytes 1474568 | tf_op jit(solution)/shard_map/ppermute | solution.py:20
  76.8 4.8 %collective-permute-start.7 = (bf16[2,1,160,384]{3,2,1,0:T(8,128)(2,1)S(1)}, bf16[2,1,160,384]{3,2,1,0:T(8,128)(2,1)S(1)}, u32[]{:S(2)}, u32[]{:S(2)}) collective-permute-start(bf16[2,1,160,384]{3,2,1,0:T(8,128)(2,1)S(1)} %get-tuple-element.8), channel_id=1, source_target_pairs={{0,9},{1,10},{2,11},{3,12},{4,13},{5,14},{6,15},{8,17},{9,18},{10,... | collective-permute-start | bytes 737288 | tf_op jit(solution)/shard_map/ppermute | solution.py:31
  81.6 2.1 %collective-permute-start.8 = (bf16[2,1,160,384]{3,2,1,0:T(8,128)(2,1)S(1)}, bf16[2,1,160,384]{3,2,1,0:T(8,128)(2,1)S(1)}, u32[]{:S(2)}, u32[]{:S(2)}) collective-permute-start(bf16[2,1,160,384]{3,2,1,0:T(8,128)(2,1)S(1)} %get-tuple-element.7), channel_id=1, source_target_pairs={{1,8},{2,9},{3,10},{4,11},{5,12},{6,13},{7,14},{9,16},{10,17},{11,... | collective-permute-start | bytes 737288 | tf_op jit(solution)/shard_map/ppermute | solution.py:31
  83.8 0.8 copy-done.4
  84.6 0.2 copy-done.5
  84.7 13.2 %shard_map.83.refs_8_ = bf16[1280,384]{1,0:T(8,128)(2,1)} custom-call(s32[12]{0:T(128)} %reshape.102.keep_ref, bf16[4,2,160,384]{3,2,1,0:T(8,128)(2,1)} %bitcast.34, bf16[4,1,160,384]{3,2,1,0:T(8,128)(2,1)} %copy-done.4, bf16[4,1,160,384]{3,2,1,0:T(8,128)(2,1)} %copy-done.5, bf16[10368,384]{1,0:T(8,128)(2,1)} %bitcast.42, bf16[6,4,160,384]{3,2,1,0:T(8,128)(2,1)} %copy-done), custom_call_target="tpu_custom_call" | custom-call | flops 5096079360 | bytes 9437184 | tf_op jit(solution)/shard_map/pallas_call | solution.py:171
  97.9 4.4 %collective-permute-done.7.refs_4_ = bf16[2,1,160,384]{3,2,1,0:T(8,128)(2,1)S(1)} collective-permute-done((bf16[2,1,160,384]{3,2,1,0:T(8,128)(2,1)S(1)}, bf16[2,1,160,384]{3,2,1,0:T(8,128)(2,1)S(1)}, u32[]{:S(2)}, u32[]{:S(2)}) %collective-permute-start.7) | collective-permute-done | bytes 245792 | tf_op jit(solution)/shard_map/ppermute | solution.py:31
  102.3 0.7 copy-done.7
  103.1 0.8 copy-done.6
  103.9 13.5 %shard_map.84 = bf16[1280,384]{1,0:T(8,128)(2,1)} custom-call(s32[12]{0:T(128)} %reshape.102.keep_ref, bf16[4,2,160,384]{3,2,1,0:T(8,128)(2,1)} %bitcast.35, bf16[4,1,160,384]{3,2,1,0:T(8,128)(2,1)} %copy-done.4, bf16[4,1,160,384]{3,2,1,0:T(8,128)(2,1)} %copy-done.5, bf16[2,2,160,384]{3,2,1,0:T(8,128)(2,1)} %copy-done.6, ...), custom_call_target="tpu_custom_call", output_to_operand_aliasing={{}: (9, {})} | custom-call | flops 5096079360 | bytes 9437184 | tf_op jit(solution)/shard_map/pallas_call | solution.py:171
  (46 shorter events, 1.5 us)
Async XLA Ops:
  0.0 31.1 %copy-start.2 = (bf16[1,8,2560]{2,1,0:T(8,128)(2,1)S(1)}, bf16[1,8,2560]{2,1,0:T(8,128)(2,1)}, u32[]{:S(2)}) copy-start(bf16[1,8,2560]{2,1,0:T(8,128)(2,1)} %param.8) | copy-start | bytes 122884
  1.5 6.9 %collective-permute-start = (bf16[1,8,2688]{2,1,0:T(8,128)(2,1)S(1)}, bf16[1,8,2688]{2,1,0:T(8,128)(2,1)S(1)}, u32[]{:S(2)}, u32[]{:S(2)}) collective-permute-start(bf16[1,8,2688]{2,1,0:T(8,128)(2,1)S(1)} %pad_maximum_fusion.12), channel_id=1, source_target_pairs={{0,8},{8,16},{16,24},{24,32},{32,40},{40,48},{48,56},{56,64},{64,7... | collective-permute-start | bytes 129032 | tf_op jit(solution)/shard_map/ppermute | solution.py:20
  9.3 3.8 %collective-permute-start.1 = (bf16[2,8,2688]{2,1,0:T(8,128)(2,1)S(1)}, bf16[2,8,2688]{2,1,0:T(8,128)(2,1)S(1)}, u32[]{:S(2)}, u32[]{:S(2)}) collective-permute-start(bf16[2,8,2688]{2,1,0:T(8,128)(2,1)S(1)} %maximum_maximum_fusion), channel_id=1, source_target_pairs={{0,1},{1,0},{2,3},{3,2},{4,5},{5,4},{6,7},{7,6},{8,9},{9,8},{10,11... | collective-permute-start | bytes 258056 | tf_op jit(solution)/shard_map/ppermute | solution.py:227
  13.8 6.1 %collective-permute-start.2 = (bf16[2,16,2688]{2,1,0:T(8,128)(2,1)S(1)}, bf16[2,16,2688]{2,1,0:T(8,128)(2,1)S(1)}, u32[]{:S(2)}, u32[]{:S(2)}) collective-permute-start(bf16[2,16,2688]{2,1,0:T(8,128)(2,1)S(1)} %pad_maximum_fusion.11), channel_id=1, source_target_pairs={{0,2},{1,3},{2,0},{3,1},{4,6},{5,7},{6,4},{7,5},{8,10},{9,11},{10,... | collective-permute-start | bytes 516104 | tf_op jit(solution)/shard_map/ppermute | solution.py:227
  20.7 10.4 %collective-permute-start.3 = (bf16[2,32,2688]{2,1,0:T(8,128)(2,1)S(1)}, bf16[2,32,2688]{2,1,0:T(8,128)(2,1)S(1)}, u32[]{:S(2)}, u32[]{:S(2)}) collective-permute-start(bf16[2,32,2688]{2,1,0:T(8,128)(2,1)S(1)} %pad_maximum_fusion.10), channel_id=1, source_target_pairs={{0,4},{1,5},{2,6},{3,7},{4,0},{5,1},{6,2},{7,3},{8,12},{9,13},{10,... | collective-permute-start | bytes 1032200 | tf_op jit(solution)/shard_map/ppermute | solution.py:227
  38.9 3.2 %copy-start.3 = (f32[384]{0:T(512)S(1)}, f32[384]{0:T(512)}, u32[]{:S(2)}) copy-start(f32[384]{0:T(512)} %param.12) | copy-start | bytes 4612
  42.0 3.2 %copy-start = (bf16[6,4,160,384]{3,2,1,0:T(8,128)(2,1)}, bf16[6,4,160,384]{3,2,1,0:T(8,128)(2,1)S(1)}, u32[]{:S(2)}) copy-start(bf16[6,4,160,384]{3,2,1,0:T(8,128)(2,1)S(1)} %get-tuple-element.28.refs_4_.refs_7_) | copy-start | bytes 8847364
  67.1 7.7 %copy-start.1 = (bf16[1280,384]{1,0:T(8,128)(2,1)S(1)}, bf16[1280,384]{1,0:T(8,128)(2,1)}, u32[]{:S(2)}) copy-start(bf16[1280,384]{1,0:T(8,128)(2,1)} %shard_map.82) | copy-start | bytes 2949124
  68.4 15.3 %collective-permute-start.4 = (bf16[4,1,160,384]{3,2,1,0:T(8,128)(2,1)S(1)}, bf16[4,1,160,384]{3,2,1,0:T(8,128)(2,1)S(1)}, u32[]{:S(2)}, u32[]{:S(2)}) collective-permute-start(bf16[4,1,160,384]{3,2,1,0:T(8,128)(2,1)S(1)} %get-tuple-element.6), channel_id=1, source_target_pairs={{0,1},{1,2},{2,3},{3,4},{4,5},{5,6},{6,7},{8,9},{9,10},{10,11},{11... | collective-permute-start | bytes 1474568 | tf_op jit(solution)/shard_map/ppermute | solution.py:20
  72.8 11.0 %collective-permute-start.5 = (bf16[4,1,160,384]{3,2,1,0:T(8,128)(2,1)S(1)}, bf16[4,1,160,384]{3,2,1,0:T(8,128)(2,1)S(1)}, u32[]{:S(2)}, u32[]{:S(2)}) collective-permute-start(bf16[4,1,160,384]{3,2,1,0:T(8,128)(2,1)S(1)} %get-tuple-element.5), channel_id=1, source_target_pairs={{1,0},{2,1},{3,2},{4,3},{5,4},{6,5},{7,6},{9,8},{10,9},{11,10},{12... | collective-permute-start | bytes 1474568 | tf_op jit(solution)/shard_map/ppermute | solution.py:20
  74.8 27.5 %collective-permute-start.6 = (bf16[2,2,160,384]{3,2,1,0:T(8,128)(2,1)S(1)}, bf16[2,2,160,384]{3,2,1,0:T(8,128)(2,1)S(1)}, u32[]{:S(2)}, u32[]{:S(2)}) collective-permute-start(bf16[2,2,160,384]{3,2,1,0:T(8,128)(2,1)S(1)} %bitcast.36), channel_id=1, source_target_pairs={{0,8},{8,16},{16,24},{24,32},{32,40},{40,48},{48,56},{56,64},{64,7... | collective-permute-start | bytes 1474568 | tf_op jit(solution)/shard_map/ppermute | solution.py:20
  76.8 25.5 %collective-permute-start.7 = (bf16[2,1,160,384]{3,2,1,0:T(8,128)(2,1)S(1)}, bf16[2,1,160,384]{3,2,1,0:T(8,128)(2,1)S(1)}, u32[]{:S(2)}, u32[]{:S(2)}) collective-permute-start(bf16[2,1,160,384]{3,2,1,0:T(8,128)(2,1)S(1)} %get-tuple-element.8), channel_id=1, source_target_pairs={{0,9},{1,10},{2,11},{3,12},{4,13},{5,14},{6,15},{8,17},{9,18},{10,... | collective-permute-start | bytes 737288 | tf_op jit(solution)/shard_map/ppermute | solution.py:31
  81.6 20.7 %collective-permute-start.8 = (bf16[2,1,160,384]{3,2,1,0:T(8,128)(2,1)S(1)}, bf16[2,1,160,384]{3,2,1,0:T(8,128)(2,1)S(1)}, u32[]{:S(2)}, u32[]{:S(2)}) collective-permute-start(bf16[2,1,160,384]{3,2,1,0:T(8,128)(2,1)S(1)} %get-tuple-element.7), channel_id=1, source_target_pairs={{1,8},{2,9},{3,10},{4,11},{5,12},{6,13},{7,14},{9,16},{10,17},{11,... | collective-permute-start | bytes 737288 | tf_op jit(solution)/shard_map/ppermute | solution.py:31
  83.8 0.8 copy-start.4
  83.8 0.9 copy-start.5
  102.3 0.7 copy-start.7
  102.3 0.8 copy-start.8
  103.1 0.8 copy-start.6

commit v3 on v1

--- a/solution.py
+++ b/solution.py
@@ -217,27 +217,24 @@
         slot_group_row.astype(jnp.bfloat16)[:, :, None], (1, slots_here, ID_LANES)
     )
     packed = jnp.concatenate([generator_latent_rows, ids], axis=-1)
-    earlier = shifted(packed, "tm", 1)
-    both = jnp.concatenate([earlier, packed], axis=0)
     parts_total = lax.axis_size("rows")
-    pieces = [both]
+    pieces = [packed]
     for by in range(1, parts_total):
         ring = [(i, (i + by) % parts_total) for i in range(parts_total)]
-        pieces.append(lax.ppermute(both, "rows", ring))
-    gathered = jnp.concatenate(pieces, axis=1)
-    values = gathered[:, :, :packed_rows]
-    slot_ids = gathered[:, :, packed_rows].astype(jnp.int32)
+        pieces.append(lax.ppermute(packed, "rows", ring))
+    gathered = jnp.concatenate(pieces, axis=1)[0]
+    values = gathered[:, :packed_rows]
+    slot_ids = gathered[:, packed_rows].astype(jnp.int32)
 
     window_rows = rows_here + 4
     frame_of = jnp.arange(frame_count, dtype=jnp.int32)[:, None]
     row_of = band_index * rows_here - 2 + jnp.arange(window_rows, dtype=jnp.int32)[None, :]
     wanted = (frame_of * height + row_of).reshape(-1)
     valid = jnp.broadcast_to((row_of >= 0) & (row_of < height), (frame_count, window_rows)).reshape(-1)
-    selector = ((wanted[None, :, None] == slot_ids[:, None, :]) & valid[None, :, None]).astype(
-        jnp.bfloat16
-    )
-    latent = jnp.einsum("qij,qjc->qic", selector, values, preferred_element_type=jnp.float32)
-    latent = latent.astype(jnp.bfloat16).reshape(
+    selector = ((wanted[:, None] == slot_ids[None, :]) & valid[:, None]).astype(jnp.bfloat16)
+    own_window = jnp.dot(selector, values, preferred_element_type=jnp.float32).astype(jnp.bfloat16)
+    prev_window = shifted(own_window, "tm", 1)
+    latent = jnp.concatenate([prev_window, own_window], axis=0).reshape(
         2 * frame_count, window_rows, columns, LATENT_CHANNELS
     )
 

time: 109 us -> 111 us (1.018)
  waiting for transfers between devices: 8.12 us -> 12.4 us
    ppermute x4, waiting for transfers between devices: 0.01 us -> 4.53 us  [shifted(): return lax.ppermute(x, axis, pairs)]
    ppermute x7, waiting for transfers between devices: 5.53 us -> 3.23 us  [on_device(): pieces.append(lax.ppermute(packed, 'rows', ring))]
    ppermute x2, waiting for transfers between devices: 2.57 us -> 4.66 us  [diagonal(): return lax.ppermute(x, ('tm', 'rows'), pairs)]
    unnamed x40 -> x42, local copies, waits for them, and re-layouts: 4.16 us -> 4.14 us
  transfers between devices with their start and end apart: 13 -> 13, of which waited for: 6 -> 5; matrix products, arithmetic and copies ran while one was open for 4% -> 3% of each run, Pallas kernels for 12% -> 12%
where the time goes in v3:
time: 111 us; the launch traced here: 110 us
  Pallas kernels  48.4 us (44%)
  starting transfers between devices  25.8 us (23%)
  waiting for transfers between devices  12.4 us (11%)
  local copies, waits for them, and re-layouts  12 us (11%)
  matrix products  5.89 us (5%)
  other arithmetic  5.05 us (5%)
    pallas_call x3, Pallas kernels, conv_call(): pl.pallas_call(functools.partial(conv_kernel, layout=layout, mode=mode, p...  48.4 us
    ppermute x4, starting transfers between devices, shifted(): return lax.ppermute(x, axis, pairs)  12 us
    ppermute x7, starting transfers between devices, on_device(): pieces.append(lax.ppermute(packed, 'rows', ring))  6.88 us
    ppermute x2, starting transfers between devices, diagonal(): return lax.ppermute(x, ('tm', 'rows'), pairs)  6.86 us
    dot_general x3, matrix products, local_conv(): jnp.dot(stacked, weight[tap_time].reshape(9 * channels, outputs), preferr...  5.65 us
    ppermute x2, waiting for transfers between devices, diagonal(): return lax.ppermute(x, ('tm', 'rows'), pairs)  4.66 us
    ppermute x4, waiting for transfers between devices, shifted(): return lax.ppermute(x, axis, pairs)  4.53 us
    unnamed x42, local copies, waits for them, and re-layouts  4.14 us
  transfers between devices with their start and end apart: 13, of which 5 were waited for; matrix products, arithmetic and copies ran while one was open for 3% of the time, Pallas kernels for 12%

profile of v3, /device:TPU:21, one launch (start us, length us, event | category | flops | bytes accessed | tf_op | source)
XLA Modules:
  0.0 110.1 jit_solution(9453949126978236357)
XLA Ops:
  0.0 0.7 convert_bitcast_fusion
  0.7 0.8 pad_maximum_fusion.1
  1.5 1.5 %collective-permute-start = (bf16[1,8,2688]{2,1,0:T(8,128)(2,1)S(1)}, bf16[1,8,2688]{2,1,0:T(8,128)(2,1)S(1)}, u32[]{:S(2)}, u32[]{:S(2)}) collective-permute-start(bf16[1,8,2688]{2,1,0:T(8,128)(2,1)S(1)} %get-tuple-element.23), channel_id=1, source_target_pairs={{0,1},{1,2},{2,3},{3,4},{4,5},{5,6},{6,7},{7,0},{8,9},{9,10},{10,1... | collective-permute-start | bytes 129032 | tf_op jit(solution)/shard_map/ppermute | solution.py:224
  3.0 0.2 collective-permute-start.1
  3.2 0.7 collective-permute-start.2
  3.9 2.5 %collective-permute-start.3 = (bf16[1,8,2688]{2,1,0:T(8,128)(2,1)S(1)}, bf16[1,8,2688]{2,1,0:T(8,128)(2,1)S(1)}, u32[]{:S(2)}, u32[]{:S(2)}) collective-permute-start(bf16[1,8,2688]{2,1,0:T(8,128)(2,1)S(1)} %get-tuple-element.23), channel_id=1, source_target_pairs={{0,4},{1,5},{2,6},{3,7},{4,0},{5,1},{6,2},{7,3},{8,12},{9,13},{10,... | collective-permute-start | bytes 129032 | tf_op jit(solution)/shard_map/ppermute | solution.py:224
  6.3 1.0 collective-permute-start.4
  7.4 1.0 fusion.17
  8.4 0.7 pad_dynamic-slice_fusion
  9.7 0.9 collective-permute-start.5
  10.5 0.2 collective-permute-start.6
  10.8 0.5 collective-permute-done.4
  11.3 1.7 %collective-permute-done.5 = bf16[1,8,2688]{2,1,0:T(8,128)(2,1)S(1)} collective-permute-done((bf16[1,8,2688]{2,1,0:T(8,128)(2,1)S(1)}, bf16[1,8,2688]{2,1,0:T(8,128)(2,1)S(1)}, u32[]{:S(2)}, u32[]{:S(2)}) %collective-permute-start.5) | collective-permute-done | bytes 43040 | tf_op jit(solution)/shard_map/ppermute | solution.py:224
  13.0 1.0 collective-permute-done.6
  14.1 0.2 convolution_convert_fusion
  14.4 3.5 %collective-permute-start.7 = (bf16[24,2560]{1,0:T(8,128)(2,1)S(1)}, bf16[24,2560]{1,0:T(8,128)(2,1)S(1)}, u32[]{:S(2)}, u32[]{:S(2)}) collective-permute-start(bf16[24,2560]{1,0:T(8,128)(2,1)S(1)} %convolution_convert_fusion), channel_id=1, source_target_pairs={{0,8},{8,16},{16,24},{24,32},{32,40},{40,48},{48,56},{56,64},{64,7... | collective-permute-start | bytes 368648 | tf_op jit(solution)/shard_map/ppermute | solution.py:20
  18.0 0.6 reshape.102.keep_ref
  18.6 0.6 reshape.98.refs_2_
  19.2 4.5 %collective-permute-done.7 = bf16[24,2560]{1,0:T(8,128)(2,1)S(1)} collective-permute-done((bf16[24,2560]{1,0:T(8,128)(2,1)S(1)}, bf16[24,2560]{1,0:T(8,128)(2,1)S(1)}, u32[]{:S(2)}, u32[]{:S(2)}) %collective-permute-start.7) | collective-permute-done | bytes 122912 | tf_op jit(solution)/shard_map/ppermute | solution.py:20
  23.7 1.6 %reshape.96 = bf16[8,6,160,16]{3,2,1,0:T(8,128)(2,1)S(1)} reshape(bf16[48,2560]{1,0:T(8,128)(2,1)S(1)} %pad_maximum_fusion) | data formatting | bytes 491520 | tf_op jit(solution)/shard_map/reshape | solution.py:237
  25.3 1.0 copy.20
  26.3 0.1 slice_dynamic-update-slice_fusion.14
  26.5 0.1 slice_dynamic-update-slice_fusion.13
  26.8 0.1 slice_dynamic-update-slice_fusion.11
  26.9 0.2 slice_dynamic-update-slice_fusion.10
  27.1 0.2 slice_dynamic-update-slice_fusion.9
  27.5 0.1 slice_dynamic-update-slice_fusion.23
  27.8 0.2 slice_dynamic-update-slice_fusion.21
  28.1 0.1 slice_dynamic-update-slice_fusion.17
  28.4 0.1 slice_dynamic-update-slice_fusion.15
  28.6 1.3 %fusion.19 = f32[6,4,160,384]{3,2,1,0:T(8,128)S(1)} fusion(bf16[6,4,160,144]{2,3,1,0:T(8,128)(2,1)S(1)} %slice_dynamic-update-slice_fusion.15, bf16[144,384,1,1]{1,0,3,2:T(8,128)(2,1)S(1)} %bitcast.41), kind=kOutput, calls=%fused_computation.74 | convolution fusion | flops 424673280 | bytes 7114752 | tf_op jit(solution)/shard_map/dot_general | solution.py:60
  29.8 1.3 %fusion.18 = f32[6,4,160,384]{3,2,1,0:T(8,128)S(1)} fusion(bf16[6,4,160,144]{2,3,1,0:T(8,128)(2,1)S(1)} %get-tuple-element.16, bf16[144,384,1,1]{1,0,3,2:T(8,128)(2,1)S(1)} %bitcast.40), kind=kOutput, calls=%fused_computation.73 | convolution fusion | flops 424673280 | bytes 7114752 | tf_op jit(solution)/shard_map/dot_general | solution.py:60
  31.1 3.1 %fusion = (f32[6,4,160]{2,1,0:T(4,128)S(1)}, bf16[6,4,160,384]{3,2,1,0:T(8,128)(2,1)S(1)}) fusion(bf16[6,4,160,144]{2,3,1,0:T(8,128)(2,1)S(1)} %get-tuple-element.9, bf16[144,384,1,1]{1,0,3,2:T(8,128)(2,1)S(1)} %bitcast.39, f32[6,4,160,384]{3,2,1,0:T(8,128)S(1)} %fusion.19, pred[6]{0:T(512)(128)(4,1)S(1)} %get-tuple-element.26, ...), kind=kOutput, calls=%fused_computation.2 | convolution fusion | flops 436465920 | bytes 15977484 | tf_op jit(solution)/shard_map/dot_general | solution.py:60
  34.3 3.1 %fusion.8.refs_0_ = bf16[6,4,160,384]{3,2,1,0:T(8,128)(2,1)} fusion(bf16[6,4,160,384]{3,2,1,0:T(8,128)(2,1)S(1)} %get-tuple-element.30.refs_4_.refs_7_, f32[384]{0:T(512)S(1)} %copy-done.2, f32[6,4,160]{2,1,0:T(4,128)S(1)} %add_rsqrt_fusion, pred[4]{0:T(512)(128)(4,1)S(1)} %compare_and_fusion.1), kind=kLoop, calls=%fused_computation.12 | loop fusion | flops 13271040 | bytes 5915140 | tf_op jit(solution)/shard_map/jit(_where)/select_n | solution.py:254
  37.4 21.8 %shard_map.82 = bf16[1280,384]{1,0:T(8,128)(2,1)} custom-call(s32[12]{0:T(128)} %reshape.102.keep_ref, bf16[6,4,160,384]{3,2,1,0:T(8,128)(2,1)} %fusion.8.refs_0_, bf16[10368,384]{1,0:T(8,128)(2,1)} %bitcast.44, f32[1,384]{1,0:T(1,128)} %reshape.98.refs_2_), custom_call_target="tpu_custom_call" | custom-call | flops 10192158720 | bytes 10911744 | tf_op jit(solution)/shard_map/pallas_call | solution.py:171
  59.2 1.4 %fusion.15 = (bf16[4,1,160,384]{3,2,1,0:T(8,128)(2,1)S(1)}, bf16[4,1,160,384]{3,2,1,0:T(8,128)(2,1)S(1)}) fusion(bf16[4,2,160,384]{3,2,1,0:T(8,128)(2,1)} %bitcast.34), kind=kLoop, calls=%fused_computation.70 | loop fusion | bytes 1966080 | tf_op jit(solution)/shard_map/slice | solution.py:269
  60.6 4.6 %collective-permute-start.8 = (bf16[4,1,160,384]{3,2,1,0:T(8,128)(2,1)S(1)}, bf16[4,1,160,384]{3,2,1,0:T(8,128)(2,1)S(1)}, u32[]{:S(2)}, u32[]{:S(2)}) collective-permute-start(bf16[4,1,160,384]{3,2,1,0:T(8,128)(2,1)S(1)} %get-tuple-element.6), channel_id=1, source_target_pairs={{0,1},{1,2},{2,3},{3,4},{4,5},{5,6},{6,7},{8,9},{9,10},{10,11},{11... | collective-permute-start | bytes 1474568 | tf_op jit(solution)/shard_map/ppermute | solution.py:20
  65.3 1.9 %collective-permute-start.9 = (bf16[4,1,160,384]{3,2,1,0:T(8,128)(2,1)S(1)}, bf16[4,1,160,384]{3,2,1,0:T(8,128)(2,1)S(1)}, u32[]{:S(2)}, u32[]{:S(2)}) collective-permute-start(bf16[4,1,160,384]{3,2,1,0:T(8,128)(2,1)S(1)} %get-tuple-element.5), channel_id=1, source_target_pairs={{1,0},{2,1},{3,2},{4,3},{5,4},{6,5},{7,6},{9,8},{10,9},{11,10},{12... | collective-permute-start | bytes 1474568 | tf_op jit(solution)/shard_map/ppermute | solution.py:20
  67.3 1.9 %collective-permute-start.10 = (bf16[2,2,160,384]{3,2,1,0:T(8,128)(2,1)S(1)}, bf16[2,2,160,384]{3,2,1,0:T(8,128)(2,1)S(1)}, u32[]{:S(2)}, u32[]{:S(2)}) collective-permute-start(bf16[2,2,160,384]{3,2,1,0:T(8,128)(2,1)S(1)} %bitcast.37), channel_id=1, source_target_pairs={{0,8},{8,16},{16,24},{24,32},{32,40},{40,48},{48,56},{56,64},{64,7... | collective-permute-start | bytes 1474568 | tf_op jit(solution)/shard_map/ppermute | solution.py:20
  69.2 4.7 %collective-permute-start.11 = (bf16[2,1,160,384]{3,2,1,0:T(8,128)(2,1)S(1)}, bf16[2,1,160,384]{3,2,1,0:T(8,128)(2,1)S(1)}, u32[]{:S(2)}, u32[]{:S(2)}) collective-permute-start(bf16[2,1,160,384]{3,2,1,0:T(8,128)(2,1)S(1)} %get-tuple-element.8), channel_id=1, source_target_pairs={{0,9},{1,10},{2,11},{3,12},{4,13},{5,14},{6,15},{8,17},{9,18},{10,... | collective-permute-start | bytes 737288 | tf_op jit(solution)/shard_map/ppermute | solution.py:31
  74.0 2.1 %collective-permute-start.12 = (bf16[2,1,160,384]{3,2,1,0:T(8,128)(2,1)S(1)}, bf16[2,1,160,384]{3,2,1,0:T(8,128)(2,1)S(1)}, u32[]{:S(2)}, u32[]{:S(2)}) collective-permute-start(bf16[2,1,160,384]{3,2,1,0:T(8,128)(2,1)S(1)} %get-tuple-element.7), channel_id=1, source_target_pairs={{1,8},{2,9},{3,10},{4,11},{5,12},{6,13},{7,14},{9,16},{10,17},{11,... | collective-permute-start | bytes 737288 | tf_op jit(solution)/shard_map/ppermute | solution.py:31
  76.2 0.8 copy-done.4
  76.9 0.2 copy-done.5
  77.1 13.2 %shard_map.83.refs_8_ = bf16[1280,384]{1,0:T(8,128)(2,1)} custom-call(s32[12]{0:T(128)} %reshape.102.keep_ref, bf16[4,2,160,384]{3,2,1,0:T(8,128)(2,1)} %bitcast.35, bf16[4,1,160,384]{3,2,1,0:T(8,128)(2,1)} %copy-done.4, bf16[4,1,160,384]{3,2,1,0:T(8,128)(2,1)} %copy-done.5, bf16[10368,384]{1,0:T(8,128)(2,1)} %bitcast.45, bf16[6,4,160,384]{3,2,1,0:T(8,128)(2,1)} %copy-done), custom_call_target="tpu_custom_call" | custom-call | flops 5096079360 | bytes 9437184 | tf_op jit(solution)/shard_map/pallas_call | solution.py:171
  90.3 4.7 %collective-permute-done.11.refs_4_ = bf16[2,1,160,384]{3,2,1,0:T(8,128)(2,1)S(1)} collective-permute-done((bf16[2,1,160,384]{3,2,1,0:T(8,128)(2,1)S(1)}, bf16[2,1,160,384]{3,2,1,0:T(8,128)(2,1)S(1)}, u32[]{:S(2)}, u32[]{:S(2)}) %collective-permute-start.11) | collective-permute-done | bytes 245792 | tf_op jit(solution)/shard_map/ppermute | solution.py:31
  94.9 0.7 copy-done.7
  95.7 0.8 copy-done.6
  96.5 13.5 %shard_map.84 = bf16[1280,384]{1,0:T(8,128)(2,1)} custom-call(s32[12]{0:T(128)} %reshape.102.keep_ref, bf16[4,2,160,384]{3,2,1,0:T(8,128)(2,1)} %bitcast.36, bf16[4,1,160,384]{3,2,1,0:T(8,128)(2,1)} %copy-done.4, bf16[4,1,160,384]{3,2,1,0:T(8,128)(2,1)} %copy-done.5, bf16[2,2,160,384]{3,2,1,0:T(8,128)(2,1)} %copy-done.6, ...), custom_call_target="tpu_custom_call", output_to_operand_aliasing={{}: (9, {})} | custom-call | flops 5096079360 | bytes 9437184 | tf_op jit(solution)/shard_map/pallas_call | solution.py:171
  (59 shorter events, 1.8 us)
Async XLA Ops:
  0.0 18.6 %copy-start.3 = (f32[384]{0:T(512)S(1)}, f32[384]{0:T(512)}, u32[]{:S(2)}) copy-start(f32[384]{0:T(512)} %param.14) | copy-start | bytes 4612
  1.5 8.1 %collective-permute-start = (bf16[1,8,2688]{2,1,0:T(8,128)(2,1)S(1)}, bf16[1,8,2688]{2,1,0:T(8,128)(2,1)S(1)}, u32[]{:S(2)}, u32[]{:S(2)}) collective-permute-start(bf16[1,8,2688]{2,1,0:T(8,128)(2,1)S(1)} %get-tuple-element.23), channel_id=1, source_target_pairs={{0,1},{1,2},{2,3},{3,4},{4,5},{5,6},{6,7},{7,0},{8,9},{9,10},{10,1... | collective-permute-start | bytes 129032 | tf_op jit(solution)/shard_map/ppermute | solution.py:224
  3.0 7.5 %collective-permute-start.1 = (bf16[1,8,2688]{2,1,0:T(8,128)(2,1)S(1)}, bf16[1,8,2688]{2,1,0:T(8,128)(2,1)S(1)}, u32[]{:S(2)}, u32[]{:S(2)}) collective-permute-start(bf16[1,8,2688]{2,1,0:T(8,128)(2,1)S(1)} %get-tuple-element.23), channel_id=1, source_target_pairs={{0,2},{1,3},{2,4},{3,5},{4,6},{5,7},{6,0},{7,1},{8,10},{9,11},{10,... | collective-permute-start | bytes 129032 | tf_op jit(solution)/shard_map/ppermute | solution.py:224
  3.2 7.5 %collective-permute-start.2 = (bf16[1,8,2688]{2,1,0:T(8,128)(2,1)S(1)}, bf16[1,8,2688]{2,1,0:T(8,128)(2,1)S(1)}, u32[]{:S(2)}, u32[]{:S(2)}) collective-permute-start(bf16[1,8,2688]{2,1,0:T(8,128)(2,1)S(1)} %get-tuple-element.23), channel_id=1, source_target_pairs={{0,3},{1,4},{2,5},{3,6},{4,7},{5,0},{6,1},{7,2},{8,11},{9,12},{10,... | collective-permute-start | bytes 129032 | tf_op jit(solution)/shard_map/ppermute | solution.py:224
  3.9 6.9 %collective-permute-start.3 = (bf16[1,8,2688]{2,1,0:T(8,128)(2,1)S(1)}, bf16[1,8,2688]{2,1,0:T(8,128)(2,1)S(1)}, u32[]{:S(2)}, u32[]{:S(2)}) collective-permute-start(bf16[1,8,2688]{2,1,0:T(8,128)(2,1)S(1)} %get-tuple-element.23), channel_id=1, source_target_pairs={{0,4},{1,5},{2,6},{3,7},{4,0},{5,1},{6,2},{7,3},{8,12},{9,13},{10,... | collective-permute-start | bytes 129032 | tf_op jit(solution)/shard_map/ppermute | solution.py:224
  6.3 5.0 %collective-permute-start.4 = (bf16[1,8,2688]{2,1,0:T(8,128)(2,1)S(1)}, bf16[1,8,2688]{2,1,0:T(8,128)(2,1)S(1)}, u32[]{:S(2)}, u32[]{:S(2)}) collective-permute-start(bf16[1,8,2688]{2,1,0:T(8,128)(2,1)S(1)} %get-tuple-element.23), channel_id=1, source_target_pairs={{0,5},{1,6},{2,7},{3,0},{4,1},{5,2},{6,3},{7,4},{8,13},{9,14},{10,... | collective-permute-start | bytes 129032 | tf_op jit(solution)/shard_map/ppermute | solution.py:224
  9.7 3.3 %collective-permute-start.5 = (bf16[1,8,2688]{2,1,0:T(8,128)(2,1)S(1)}, bf16[1,8,2688]{2,1,0:T(8,128)(2,1)S(1)}, u32[]{:S(2)}, u32[]{:S(2)}) collective-permute-start(bf16[1,8,2688]{2,1,0:T(8,128)(2,1)S(1)} %get-tuple-element.23), channel_id=1, source_target_pairs={{0,6},{1,7},{2,0},{3,1},{4,2},{5,3},{6,4},{7,5},{8,14},{9,15},{10,... | collective-permute-start | bytes 129032 | tf_op jit(solution)/shard_map/ppermute | solution.py:224
  10.5 3.5 %collective-permute-start.6 = (bf16[1,8,2688]{2,1,0:T(8,128)(2,1)S(1)}, bf16[1,8,2688]{2,1,0:T(8,128)(2,1)S(1)}, u32[]{:S(2)}, u32[]{:S(2)}) collective-permute-start(bf16[1,8,2688]{2,1,0:T(8,128)(2,1)S(1)} %get-tuple-element.23), channel_id=1, source_target_pairs={{0,7},{1,0},{2,1},{3,2},{4,3},{5,4},{6,5},{7,6},{8,15},{9,8},{10,9... | collective-permute-start | bytes 129032 | tf_op jit(solution)/shard_map/ppermute | solution.py:224
  14.4 9.3 %collective-permute-start.7 = (bf16[24,2560]{1,0:T(8,128)(2,1)S(1)}, bf16[24,2560]{1,0:T(8,128)(2,1)S(1)}, u32[]{:S(2)}, u32[]{:S(2)}) collective-permute-start(bf16[24,2560]{1,0:T(8,128)(2,1)S(1)} %convolution_convert_fusion), channel_id=1, source_target_pairs={{0,8},{8,16},{16,24},{24,32},{32,40},{40,48},{48,56},{56,64},{64,7... | collective-permute-start | bytes 368648 | tf_op jit(solution)/shard_map/ppermute | solution.py:20
  31.1 3.2 %copy-start.2 = (f32[384]{0:T(512)S(1)}, f32[384]{0:T(512)}, u32[]{:S(2)}) copy-start(f32[384]{0:T(512)} %param.12) | copy-start | bytes 4612
  34.2 3.2 %copy-start = (bf16[6,4,160,384]{3,2,1,0:T(8,128)(2,1)}, bf16[6,4,160,384]{3,2,1,0:T(8,128)(2,1)S(1)}, u32[]{:S(2)}) copy-start(bf16[6,4,160,384]{3,2,1,0:T(8,128)(2,1)S(1)} %get-tuple-element.30.refs_4_.refs_7_) | copy-start | bytes 8847364
  59.2 8.0 %copy-start.1 = (bf16[1280,384]{1,0:T(8,128)(2,1)S(1)}, bf16[1280,384]{1,0:T(8,128)(2,1)}, u32[]{:S(2)}) copy-start(bf16[1280,384]{1,0:T(8,128)(2,1)} %shard_map.82) | copy-start | bytes 2949124
  60.6 15.5 %collective-permute-start.8 = (bf16[4,1,160,384]{3,2,1,0:T(8,128)(2,1)S(1)}, bf16[4,1,160,384]{3,2,1,0:T(8,128)(2,1)S(1)}, u32[]{:S(2)}, u32[]{:S(2)}) collective-permute-start(bf16[4,1,160,384]{3,2,1,0:T(8,128)(2,1)S(1)} %get-tuple-element.6), channel_id=1, source_target_pairs={{0,1},{1,2},{2,3},{3,4},{4,5},{5,6},{6,7},{8,9},{9,10},{10,11},{11... | collective-permute-start | bytes 1474568 | tf_op jit(solution)/shard_map/ppermute | solution.py:20
  65.3 10.9 %collective-permute-start.9 = (bf16[4,1,160,384]{3,2,1,0:T(8,128)(2,1)S(1)}, bf16[4,1,160,384]{3,2,1,0:T(8,128)(2,1)S(1)}, u32[]{:S(2)}, u32[]{:S(2)}) collective-permute-start(bf16[4,1,160,384]{3,2,1,0:T(8,128)(2,1)S(1)} %get-tuple-element.5), channel_id=1, source_target_pairs={{1,0},{2,1},{3,2},{4,3},{5,4},{6,5},{7,6},{9,8},{10,9},{11,10},{12... | collective-permute-start | bytes 1474568 | tf_op jit(solution)/shard_map/ppermute | solution.py:20
  67.3 27.7 %collective-permute-start.10 = (bf16[2,2,160,384]{3,2,1,0:T(8,128)(2,1)S(1)}, bf16[2,2,160,384]{3,2,1,0:T(8,128)(2,1)S(1)}, u32[]{:S(2)}, u32[]{:S(2)}) collective-permute-start(bf16[2,2,160,384]{3,2,1,0:T(8,128)(2,1)S(1)} %bitcast.37), channel_id=1, source_target_pairs={{0,8},{8,16},{16,24},{24,32},{32,40},{40,48},{48,56},{56,64},{64,7... | collective-permute-start | bytes 1474568 | tf_op jit(solution)/shard_map/ppermute | solution.py:20
  69.2 25.7 %collective-permute-start.11 = (bf16[2,1,160,384]{3,2,1,0:T(8,128)(2,1)S(1)}, bf16[2,1,160,384]{3,2,1,0:T(8,128)(2,1)S(1)}, u32[]{:S(2)}, u32[]{:S(2)}) collective-permute-start(bf16[2,1,160,384]{3,2,1,0:T(8,128)(2,1)S(1)} %get-tuple-element.8), channel_id=1, source_target_pairs={{0,9},{1,10},{2,11},{3,12},{4,13},{5,14},{6,15},{8,17},{9,18},{10,... | collective-permute-start | bytes 737288 | tf_op jit(solution)/shard_map/ppermute | solution.py:31
  74.0 21.0 %collective-permute-start.12 = (bf16[2,1,160,384]{3,2,1,0:T(8,128)(2,1)S(1)}, bf16[2,1,160,384]{3,2,1,0:T(8,128)(2,1)S(1)}, u32[]{:S(2)}, u32[]{:S(2)}) collective-permute-start(bf16[2,1,160,384]{3,2,1,0:T(8,128)(2,1)S(1)} %get-tuple-element.7), channel_id=1, source_target_pairs={{1,8},{2,9},{3,10},{4,11},{5,12},{6,13},{7,14},{9,16},{10,17},{11,... | collective-permute-start | bytes 737288 | tf_op jit(solution)/shard_map/ppermute | solution.py:31
  76.1 0.8 copy-start.4
  76.1 1.0 copy-start.5
  94.9 0.7 copy-start.7
  94.9 0.8 copy-start.8
  95.7 0.8 copy-start.6

commit v4 on v3

--- a/solution.py
+++ b/solution.py
@@ -268,8 +268,6 @@
     from_above = shifted(second_act[:, rows_here - 1 :], "rows", 1)
     from_below = shifted(second_act[:, :1], "rows", -1)
     prev_mid = shifted(last, "tm", 1)
-    prev_above = diagonal(last[:, rows_here - 1 :], 1, 1)
-    prev_below = diagonal(last[:, :1], 1, -1)
     layout = {
         "own": (2, 2 + frame_count, 1, 1 + rows_here),
         "above": (2, 2 + frame_count, 0, 1),
@@ -284,6 +282,9 @@
         late_layout, late_sources, second_convolution_weight, keep_own, base_ext, "res",
         firsts=(frame_count - 2,),
     )
+    decoded, prev_mid = lax.optimization_barrier((decoded, prev_mid))
+    prev_above = shifted(prev_mid[:, rows_here - 1 :], "rows", 1)
+    prev_below = shifted(prev_mid[:, :1], "rows", -1)
     return conv_call(
         layout,
         [second_act, from_above, from_below, prev_mid, prev_above, prev_below],

time: 111 us -> 114 us (1.027)
  waiting for transfers between devices: 12.4 us -> 19.2 us
  starting transfers between devices: 25.8 us -> 23.5 us
    ppermute x4 -> x6, waiting for transfers between devices: 4.53 us -> 15.9 us  [shifted(): return lax.ppermute(x, axis, pairs)]
    ppermute x2 -> x0, starting transfers between devices: 6.86 us -> none  [diagonal(): return lax.ppermute(x, ('tm', 'rows'), pairs)]
    ppermute x2 -> x0, waiting for transfers between devices: 4.66 us -> none  [diagonal(): return lax.ppermute(x, ('tm', 'rows'), pairs)]
    ppermute x4 -> x6, starting transfers between devices: 12 us -> 16.6 us  [shifted(): return lax.ppermute(x, axis, pairs)]
  transfers between devices with their start and end apart: 13 -> 13, of which waited for: 5 -> 8; matrix products, arithmetic and copies ran while one was open for 3% -> 3% of each run, Pallas kernels for 12% -> 12%
where the time goes in v4:
time: 114 us
  Pallas kernels  48.4 us (42%)
  starting transfers between devices  23.5 us (21%)
  waiting for transfers between devices  19.2 us (17%)
  local copies, waits for them, and re-layouts  11 us (10%)
  matrix products  5.89 us (5%)
  other arithmetic  5.05 us (4%)
    pallas_call x3, Pallas kernels, conv_call(): pl.pallas_call(functools.partial(conv_kernel, layout=layout, mode=mode, p...  48.4 us
    ppermute x6, starting transfers between devices, shifted(): return lax.ppermute(x, axis, pairs)  16.6 us
    ppermute x6, waiting for transfers between devices, shifted(): return lax.ppermute(x, axis, pairs)  15.9 us
    ppermute x7, starting transfers between devices, on_device(): pieces.append(lax.ppermute(packed, 'rows', ring))  6.88 us
    dot_general x3, matrix products, local_conv(): jnp.dot(stacked, weight[tap_time].reshape(9 * channels, outputs), preferr...  5.65 us
    ppermute x7, waiting for transfers between devices, on_device(): pieces.append(lax.ppermute(packed, 'rows', ring))  3.23 us
    select_n x1, other arithmetic, on_device(): jnp.where(row_ok[None, :, None, None], first_act, jnp.zeros((), jnp.bfloa...  3.14 us
    unnamed x42, local copies, waits for them, and re-layouts  3.11 us
  transfers between devices with their start and end apart: 13, of which 8 were waited for; matrix products, arithmetic and copies ran while one was open for 3% of the time, Pallas kernels for 12%

profile of v4, /device:TPU:21, one launch (start us, length us, event | category | flops | bytes accessed | tf_op | source)
XLA Modules:
  0.0 113.5 jit_solution(10109344570165531078)
XLA Ops:
  0.0 0.7 convert_bitcast_fusion
  0.7 0.8 pad_maximum_fusion.1
  1.5 1.5 %collective-permute-start = (bf16[1,8,2688]{2,1,0:T(8,128)(2,1)S(1)}, bf16[1,8,2688]{2,1,0:T(8,128)(2,1)S(1)}, u32[]{:S(2)}, u32[]{:S(2)}) collective-permute-start(bf16[1,8,2688]{2,1,0:T(8,128)(2,1)S(1)} %get-tuple-element.27), channel_id=1, source_target_pairs={{0,1},{1,2},{2,3},{3,4},{4,5},{5,6},{6,7},{7,0},{8,9},{9,10},{10,1... | collective-permute-start | bytes 129032 | tf_op jit(solution)/shard_map/ppermute | solution.py:224
  3.0 0.2 collective-permute-start.1
  3.2 0.7 collective-permute-start.2
  3.9 2.5 %collective-permute-start.3 = (bf16[1,8,2688]{2,1,0:T(8,128)(2,1)S(1)}, bf16[1,8,2688]{2,1,0:T(8,128)(2,1)S(1)}, u32[]{:S(2)}, u32[]{:S(2)}) collective-permute-start(bf16[1,8,2688]{2,1,0:T(8,128)(2,1)S(1)} %get-tuple-element.27), channel_id=1, source_target_pairs={{0,4},{1,5},{2,6},{3,7},{4,0},{5,1},{6,2},{7,3},{8,12},{9,13},{10,... | collective-permute-start | bytes 129032 | tf_op jit(solution)/shard_map/ppermute | solution.py:224
  6.3 1.0 collective-permute-start.4
  7.4 1.0 fusion.17
  8.4 0.7 pad_dynamic-slice_fusion
  9.7 0.9 collective-permute-start.5
  10.5 0.2 collective-permute-start.6
  10.8 0.5 collective-permute-done.4
  11.3 1.7 %collective-permute-done.5 = bf16[1,8,2688]{2,1,0:T(8,128)(2,1)S(1)} collective-permute-done((bf16[1,8,2688]{2,1,0:T(8,128)(2,1)S(1)}, bf16[1,8,2688]{2,1,0:T(8,128)(2,1)S(1)}, u32[]{:S(2)}, u32[]{:S(2)}) %collective-permute-start.5) | collective-permute-done | bytes 43040 | tf_op jit(solution)/shard_map/ppermute | solution.py:224
  13.0 1.0 collective-permute-done.6
  14.1 0.2 convolution_convert_fusion
  14.4 3.5 %collective-permute-start.7 = (bf16[24,2560]{1,0:T(8,128)(2,1)S(1)}, bf16[24,2560]{1,0:T(8,128)(2,1)S(1)}, u32[]{:S(2)}, u32[]{:S(2)}) collective-permute-start(bf16[24,2560]{1,0:T(8,128)(2,1)S(1)} %convolution_convert_fusion), channel_id=1, source_target_pairs={{0,8},{8,16},{16,24},{24,32},{32,40},{40,48},{48,56},{56,64},{64,7... | collective-permute-start | bytes 368648 | tf_op jit(solution)/shard_map/ppermute | solution.py:20
  18.0 0.6 reshape.110.keep_ref
  18.6 0.6 reshape.104.refs_2_
  19.2 4.5 %collective-permute-done.7 = bf16[24,2560]{1,0:T(8,128)(2,1)S(1)} collective-permute-done((bf16[24,2560]{1,0:T(8,128)(2,1)S(1)}, bf16[24,2560]{1,0:T(8,128)(2,1)S(1)}, u32[]{:S(2)}, u32[]{:S(2)}) %collective-permute-start.7) | collective-permute-done | bytes 122912 | tf_op jit(solution)/shard_map/ppermute | solution.py:20
  23.7 1.6 %reshape.102 = bf16[8,6,160,16]{3,2,1,0:T(8,128)(2,1)S(1)} reshape(bf16[48,2560]{1,0:T(8,128)(2,1)S(1)} %pad_maximum_fusion) | data formatting | bytes 491520 | tf_op jit(solution)/shard_map/reshape | solution.py:237
  25.3 1.0 copy.20
  26.3 0.1 slice_dynamic-update-slice_fusion.14
  26.5 0.1 slice_dynamic-update-slice_fusion.13
  26.9 0.2 slice_dynamic-update-slice_fusion.10
  27.1 0.2 slice_dynamic-update-slice_fusion.9
  27.5 0.1 slice_dynamic-update-slice_fusion.23
  27.8 0.2 slice_dynamic-update-slice_fusion.21
  28.1 0.1 slice_dynamic-update-slice_fusion.17
  28.4 0.1 slice_dynamic-update-slice_fusion.15
  28.6 1.3 %fusion.19 = f32[6,4,160,384]{3,2,1,0:T(8,128)S(1)} fusion(bf16[6,4,160,144]{2,3,1,0:T(8,128)(2,1)S(1)} %slice_dynamic-update-slice_fusion.15, bf16[144,384,1,1]{1,0,3,2:T(8,128)(2,1)S(1)} %bitcast.42), kind=kOutput, calls=%fused_computation.74 | convolution fusion | flops 424673280 | bytes 7114752 | tf_op jit(solution)/shard_map/dot_general | solution.py:60
  29.8 1.3 %fusion.18 = f32[6,4,160,384]{3,2,1,0:T(8,128)S(1)} fusion(bf16[6,4,160,144]{2,3,1,0:T(8,128)(2,1)S(1)} %get-tuple-element.20, bf16[144,384,1,1]{1,0,3,2:T(8,128)(2,1)S(1)} %bitcast.41), kind=kOutput, calls=%fused_computation.73 | convolution fusion | flops 424673280 | bytes 7114752 | tf_op jit(solution)/shard_map/dot_general | solution.py:60
  31.1 3.1 %fusion = (f32[6,4,160]{2,1,0:T(4,128)S(1)}, bf16[6,4,160,384]{3,2,1,0:T(8,128)(2,1)S(1)}) fusion(bf16[6,4,160,144]{2,3,1,0:T(8,128)(2,1)S(1)} %get-tuple-element.13, bf16[144,384,1,1]{1,0,3,2:T(8,128)(2,1)S(1)} %bitcast.40, f32[6,4,160,384]{3,2,1,0:T(8,128)S(1)} %fusion.19, pred[6]{0:T(512)(128)(4,1)S(1)} %get-tuple-element.30, ...), kind=kOutput, calls=%fused_computation.2 | convolution fusion | flops 436465920 | bytes 15977484 | tf_op jit(solution)/shard_map/dot_general | solution.py:60
  34.3 3.1 %fusion.8.refs_0_ = bf16[6,4,160,384]{3,2,1,0:T(8,128)(2,1)} fusion(bf16[6,4,160,384]{3,2,1,0:T(8,128)(2,1)S(1)} %get-tuple-element.34.refs_4_.refs_7_, f32[384]{0:T(512)S(1)} %copy-done.3, f32[6,4,160]{2,1,0:T(4,128)S(1)} %add_rsqrt_fusion, pred[4]{0:T(512)(128)(4,1)S(1)} %compare_and_fusion.1), kind=kLoop, calls=%fused_computation.12 | loop fusion | flops 13271040 | bytes 5915140 | tf_op jit(solution)/shard_map/jit(_where)/select_n | solution.py:254
  37.4 21.8 %shard_map.82 = bf16[1280,384]{1,0:T(8,128)(2,1)} custom-call(s32[12]{0:T(128)} %reshape.110.keep_ref, bf16[6,4,160,384]{3,2,1,0:T(8,128)(2,1)} %fusion.8.refs_0_, bf16[10368,384]{1,0:T(8,128)(2,1)} %bitcast.45, f32[1,384]{1,0:T(1,128)} %reshape.104.refs_2_), custom_call_target="tpu_custom_call" | custom-call | flops 10192158720 | bytes 10911744 | tf_op jit(solution)/shard_map/pallas_call | solution.py:171
  59.2 1.4 %fusion.15 = (bf16[4,1,160,384]{3,2,1,0:T(8,128)(2,1)S(1)}, bf16[4,1,160,384]{3,2,1,0:T(8,128)(2,1)S(1)}) fusion(bf16[4,2,160,384]{3,2,1,0:T(8,128)(2,1)} %bitcast.36), kind=kLoop, calls=%fused_computation.70 | loop fusion | bytes 1966080 | tf_op jit(solution)/shard_map/slice | solution.py:269
  60.6 4.6 %collective-permute-start.8 = (bf16[4,1,160,384]{3,2,1,0:T(8,128)(2,1)S(1)}, bf16[4,1,160,384]{3,2,1,0:T(8,128)(2,1)S(1)}, u32[]{:S(2)}, u32[]{:S(2)}) collective-permute-start(bf16[4,1,160,384]{3,2,1,0:T(8,128)(2,1)S(1)} %get-tuple-element.10), channel_id=1, source_target_pairs={{0,1},{1,2},{2,3},{3,4},{4,5},{5,6},{6,7},{8,9},{9,10},{10,11},{11... | collective-permute-start | bytes 1474568 | tf_op jit(solution)/shard_map/ppermute | solution.py:20
  65.3 1.9 %collective-permute-start.9 = (bf16[4,1,160,384]{3,2,1,0:T(8,128)(2,1)S(1)}, bf16[4,1,160,384]{3,2,1,0:T(8,128)(2,1)S(1)}, u32[]{:S(2)}, u32[]{:S(2)}) collective-permute-start(bf16[4,1,160,384]{3,2,1,0:T(8,128)(2,1)S(1)} %get-tuple-element.9), channel_id=1, source_target_pairs={{1,0},{2,1},{3,2},{4,3},{5,4},{6,5},{7,6},{9,8},{10,9},{11,10},{12... | collective-permute-start | bytes 1474568 | tf_op jit(solution)/shard_map/ppermute | solution.py:20
  67.3 2.1 %collective-permute-start.10 = (bf16[2,2,160,384]{3,2,1,0:T(8,128)(2,1)S(1)}, bf16[2,2,160,384]{3,2,1,0:T(8,128)(2,1)S(1)}, u32[]{:S(2)}, u32[]{:S(2)}) collective-permute-start(bf16[2,2,160,384]{3,2,1,0:T(8,128)(2,1)S(1)} %bitcast.39), channel_id=1, source_target_pairs={{0,8},{8,16},{16,24},{24,32},{32,40},{40,48},{48,56},{56,64},{64,7... | collective-permute-start | bytes 1474568 | tf_op jit(solution)/shard_map/ppermute | solution.py:20
  69.4 1.6 %collective-permute-done.8.refs_1_ = bf16[4,1,160,384]{3,2,1,0:T(8,128)(2,1)S(1)} collective-permute-done((bf16[4,1,160,384]{3,2,1,0:T(8,128)(2,1)S(1)}, bf16[4,1,160,384]{3,2,1,0:T(8,128)(2,1)S(1)}, u32[]{:S(2)}, u32[]{:S(2)}) %collective-permute-start.8) | collective-permute-done | bytes 491552 | tf_op jit(solution)/shard_map/ppermute | solution.py:20
  71.0 4.7 %collective-permute-done.9.refs_2_ = bf16[4,1,160,384]{3,2,1,0:T(8,128)(2,1)S(1)} collective-permute-done((bf16[4,1,160,384]{3,2,1,0:T(8,128)(2,1)S(1)}, bf16[4,1,160,384]{3,2,1,0:T(8,128)(2,1)S(1)}, u32[]{:S(2)}, u32[]{:S(2)}) %collective-permute-start.9) | collective-permute-done | bytes 491552 | tf_op jit(solution)/shard_map/ppermute | solution.py:20
  75.7 0.8 copy-done.6
  76.5 13.2 %shard_map.83 = bf16[1280,384]{1,0:T(8,128)(2,1)} custom-call(s32[12]{0:T(128)} %reshape.110.keep_ref, bf16[4,2,160,384]{3,2,1,0:T(8,128)(2,1)} %bitcast.37, bf16[4,1,160,384]{3,2,1,0:T(8,128)(2,1)} %copy-done.5, bf16[4,1,160,384]{3,2,1,0:T(8,128)(2,1)} %copy-done.6, bf16[10368,384]{1,0:T(8,128)(2,1)} %bitcast.46, bf16[6,4,160,384]{3,2,1,0:T(8,128)(2,1)} %copy-done), custom_call_target="tpu_custom_call" | custom-call | flops 5096079360 | bytes 9437184 | tf_op jit(solution)/shard_map/pallas_call | solution.py:171
  89.7 1.9 %collective-permute-start.11 = (bf16[2,1,160,384]{3,2,1,0:T(8,128)(2,1)S(1)}, bf16[2,1,160,384]{3,2,1,0:T(8,128)(2,1)S(1)}, u32[]{:S(2)}, u32[]{:S(2)}) collective-permute-start(bf16[2,1,160,384]{3,2,1,0:T(8,128)(2,1)S(1)} %get-tuple-element.12), channel_id=1, source_target_pairs={{0,1},{1,2},{2,3},{3,4},{4,5},{5,6},{6,7},{8,9},{9,10},{10,11},{11... | collective-permute-start | bytes 737288 | tf_op jit(solution)/shard_map/ppermute | solution.py:20
  91.7 2.4 %collective-permute-start.12 = (bf16[2,1,160,384]{3,2,1,0:T(8,128)(2,1)S(1)}, bf16[2,1,160,384]{3,2,1,0:T(8,128)(2,1)S(1)}, u32[]{:S(2)}, u32[]{:S(2)}) collective-permute-start(bf16[2,1,160,384]{3,2,1,0:T(8,128)(2,1)S(1)} %get-tuple-element.11), channel_id=1, source_target_pairs={{1,0},{2,1},{3,2},{4,3},{5,4},{6,5},{7,6},{9,8},{10,9},{11,10},{12... | collective-permute-start | bytes 737288 | tf_op jit(solution)/shard_map/ppermute | solution.py:20
  94.1 0.7 collective-permute-done.11.refs_4_
  94.8 4.4 %collective-permute-done.12.refs_5_ = bf16[2,1,160,384]{3,2,1,0:T(8,128)(2,1)S(1)} collective-permute-done((bf16[2,1,160,384]{3,2,1,0:T(8,128)(2,1)S(1)}, bf16[2,1,160,384]{3,2,1,0:T(8,128)(2,1)S(1)}, u32[]{:S(2)}, u32[]{:S(2)}) %collective-permute-start.12) | collective-permute-done | bytes 245792 | tf_op jit(solution)/shard_map/ppermute | solution.py:20
  99.2 0.7 copy-done.8
  99.9 13.5 %shard_map.84 = bf16[1280,384]{1,0:T(8,128)(2,1)} custom-call(s32[12]{0:T(128)} %reshape.110.keep_ref, bf16[4,2,160,384]{3,2,1,0:T(8,128)(2,1)} %bitcast.38, bf16[4,1,160,384]{3,2,1,0:T(8,128)(2,1)} %copy-done.5, bf16[4,1,160,384]{3,2,1,0:T(8,128)(2,1)} %copy-done.6, bf16[2,2,160,384]{3,2,1,0:T(8,128)(2,1)} %copy-done.2, ...), custom_call_target="tpu_custom_call", output_to_operand_aliasing={{}: (9, {})} | custom-call | flops 5096079360 | bytes 9437184 | tf_op jit(solution)/shard_map/pallas_call | solution.py:171
  (59 shorter events, 1.9 us)
Async XLA Ops:
  0.0 18.6 %copy-start.4 = (f32[384]{0:T(512)S(1)}, f32[384]{0:T(512)}, u32[]{:S(2)}) copy-start(f32[384]{0:T(512)} %param.14) | copy-start | bytes 4612
  1.5 8.1 %collective-permute-start = (bf16[1,8,2688]{2,1,0:T(8,128)(2,1)S(1)}, bf16[1,8,2688]{2,1,0:T(8,128)(2,1)S(1)}, u32[]{:S(2)}, u32[]{:S(2)}) collective-permute-start(bf16[1,8,2688]{2,1,0:T(8,128)(2,1)S(1)} %get-tuple-element.27), channel_id=1, source_target_pairs={{0,1},{1,2},{2,3},{3,4},{4,5},{5,6},{6,7},{7,0},{8,9},{9,10},{10,1... | collective-permute-start | bytes 129032 | tf_op jit(solution)/shard_map/ppermute | solution.py:224
  3.0 7.5 %collective-permute-start.1 = (bf16[1,8,2688]{2,1,0:T(8,128)(2,1)S(1)}, bf16[1,8,2688]{2,1,0:T(8,128)(2,1)S(1)}, u32[]{:S(2)}, u32[]{:S(2)}) collective-permute-start(bf16[1,8,2688]{2,1,0:T(8,128)(2,1)S(1)} %get-tuple-element.27), channel_id=1, source_target_pairs={{0,2},{1,3},{2,4},{3,5},{4,6},{5,7},{6,0},{7,1},{8,10},{9,11},{10,... | collective-permute-start | bytes 129032 | tf_op jit(solution)/shard_map/ppermute | solution.py:224
  3.2 7.5 %collective-permute-start.2 = (bf16[1,8,2688]{2,1,0:T(8,128)(2,1)S(1)}, bf16[1,8,2688]{2,1,0:T(8,128)(2,1)S(1)}, u32[]{:S(2)}, u32[]{:S(2)}) collective-permute-start(bf16[1,8,2688]{2,1,0:T(8,128)(2,1)S(1)} %get-tuple-element.27), channel_id=1, source_target_pairs={{0,3},{1,4},{2,5},{3,6},{4,7},{5,0},{6,1},{7,2},{8,11},{9,12},{10,... | collective-permute-start | bytes 129032 | tf_op jit(solution)/shard_map/ppermute | solution.py:224
  3.9 6.9 %collective-permute-start.3 = (bf16[1,8,2688]{2,1,0:T(8,128)(2,1)S(1)}, bf16[1,8,2688]{2,1,0:T(8,128)(2,1)S(1)}, u32[]{:S(2)}, u32[]{:S(2)}) collective-permute-start(bf16[1,8,2688]{2,1,0:T(8,128)(2,1)S(1)} %get-tuple-element.27), channel_id=1, source_target_pairs={{0,4},{1,5},{2,6},{3,7},{4,0},{5,1},{6,2},{7,3},{8,12},{9,13},{10,... | collective-permute-start | bytes 129032 | tf_op jit(solution)/shard_map/ppermute | solution.py:224
  6.3 5.0 %collective-permute-start.4 = (bf16[1,8,2688]{2,1,0:T(8,128)(2,1)S(1)}, bf16[1,8,2688]{2,1,0:T(8,128)(2,1)S(1)}, u32[]{:S(2)}, u32[]{:S(2)}) collective-permute-start(bf16[1,8,2688]{2,1,0:T(8,128)(2,1)S(1)} %get-tuple-element.27), channel_id=1, source_target_pairs={{0,5},{1,6},{2,7},{3,0},{4,1},{5,2},{6,3},{7,4},{8,13},{9,14},{10,... | collective-permute-start | bytes 129032 | tf_op jit(solution)/shard_map/ppermute | solution.py:224
  9.7 3.3 %collective-permute-start.5 = (bf16[1,8,2688]{2,1,0:T(8,128)(2,1)S(1)}, bf16[1,8,2688]{2,1,0:T(8,128)(2,1)S(1)}, u32[]{:S(2)}, u32[]{:S(2)}) collective-permute-start(bf16[1,8,2688]{2,1,0:T(8,128)(2,1)S(1)} %get-tuple-element.27), channel_id=1, source_target_pairs={{0,6},{1,7},{2,0},{3,1},{4,2},{5,3},{6,4},{7,5},{8,14},{9,15},{10,... | collective-permute-start | bytes 129032 | tf_op jit(solution)/shard_map/ppermute | solution.py:224
  10.5 3.5 %collective-permute-start.6 = (bf16[1,8,2688]{2,1,0:T(8,128)(2,1)S(1)}, bf16[1,8,2688]{2,1,0:T(8,128)(2,1)S(1)}, u32[]{:S(2)}, u32[]{:S(2)}) collective-permute-start(bf16[1,8,2688]{2,1,0:T(8,128)(2,1)S(1)} %get-tuple-element.27), channel_id=1, source_target_pairs={{0,7},{1,0},{2,1},{3,2},{4,3},{5,4},{6,5},{7,6},{8,15},{9,8},{10,9... | collective-permute-start | bytes 129032 | tf_op jit(solution)/shard_map/ppermute | solution.py:224
  14.4 9.3 %collective-permute-start.7 = (bf16[24,2560]{1,0:T(8,128)(2,1)S(1)}, bf16[24,2560]{1,0:T(8,128)(2,1)S(1)}, u32[]{:S(2)}, u32[]{:S(2)}) collective-permute-start(bf16[24,2560]{1,0:T(8,128)(2,1)S(1)} %convolution_convert_fusion), channel_id=1, source_target_pairs={{0,8},{8,16},{16,24},{24,32},{32,40},{40,48},{48,56},{56,64},{64,7... | collective-permute-start | bytes 368648 | tf_op jit(solution)/shard_map/ppermute | solution.py:20
  31.1 3.2 %copy-start.3 = (f32[384]{0:T(512)S(1)}, f32[384]{0:T(512)}, u32[]{:S(2)}) copy-start(f32[384]{0:T(512)} %param.12) | copy-start | bytes 4612
  34.2 3.2 %copy-start = (bf16[6,4,160,384]{3,2,1,0:T(8,128)(2,1)}, bf16[6,4,160,384]{3,2,1,0:T(8,128)(2,1)S(1)}, u32[]{:S(2)}) copy-start(bf16[6,4,160,384]{3,2,1,0:T(8,128)(2,1)S(1)} %get-tuple-element.34.refs_4_.refs_7_) | copy-start | bytes 8847364
  59.2 8.0 %copy-start.1 = (bf16[1280,384]{1,0:T(8,128)(2,1)S(1)}, bf16[1280,384]{1,0:T(8,128)(2,1)}, u32[]{:S(2)}) copy-start(bf16[1280,384]{1,0:T(8,128)(2,1)} %shard_map.82) | copy-start | bytes 2949124
  60.6 10.4 %collective-permute-start.8 = (bf16[4,1,160,384]{3,2,1,0:T(8,128)(2,1)S(1)}, bf16[4,1,160,384]{3,2,1,0:T(8,128)(2,1)S(1)}, u32[]{:S(2)}, u32[]{:S(2)}) collective-permute-start(bf16[4,1,160,384]{3,2,1,0:T(8,128)(2,1)S(1)} %get-tuple-element.10), channel_id=1, source_target_pairs={{0,1},{1,2},{2,3},{3,4},{4,5},{5,6},{6,7},{8,9},{9,10},{10,11},{11... | collective-permute-start | bytes 1474568 | tf_op jit(solution)/shard_map/ppermute | solution.py:20
  65.3 10.4 %collective-permute-start.9 = (bf16[4,1,160,384]{3,2,1,0:T(8,128)(2,1)S(1)}, bf16[4,1,160,384]{3,2,1,0:T(8,128)(2,1)S(1)}, u32[]{:S(2)}, u32[]{:S(2)}) collective-permute-start(bf16[4,1,160,384]{3,2,1,0:T(8,128)(2,1)S(1)} %get-tuple-element.9), channel_id=1, source_target_pairs={{1,0},{2,1},{3,2},{4,3},{5,4},{6,5},{7,6},{9,8},{10,9},{11,10},{12... | collective-permute-start | bytes 1474568 | tf_op jit(solution)/shard_map/ppermute | solution.py:20
  67.3 22.4 %collective-permute-start.10 = (bf16[2,2,160,384]{3,2,1,0:T(8,128)(2,1)S(1)}, bf16[2,2,160,384]{3,2,1,0:T(8,128)(2,1)S(1)}, u32[]{:S(2)}, u32[]{:S(2)}) collective-permute-start(bf16[2,2,160,384]{3,2,1,0:T(8,128)(2,1)S(1)} %bitcast.39), channel_id=1, source_target_pairs={{0,8},{8,16},{16,24},{24,32},{32,40},{40,48},{48,56},{56,64},{64,7... | collective-permute-start | bytes 1474568 | tf_op jit(solution)/shard_map/ppermute | solution.py:20
  71.0 4.7 %copy-start.5 = (bf16[4,1,160,384]{3,2,1,0:T(8,128)(2,1)}, bf16[4,1,160,384]{3,2,1,0:T(8,128)(2,1)S(1)}, u32[]{:S(2)}) copy-start(bf16[4,1,160,384]{3,2,1,0:T(8,128)(2,1)S(1)} %collective-permute-done.8.refs_1_) | copy-start | bytes 1474564
  75.7 0.8 copy-start.6
  89.7 9.5 %copy-start.2 = (bf16[2,2,160,384]{3,2,1,0:T(8,128)(2,1)}, bf16[2,2,160,384]{3,2,1,0:T(8,128)(2,1)S(1)}, u32[]{:S(2)}) copy-start(bf16[2,2,160,384]{3,2,1,0:T(8,128)(2,1)S(1)} %collective-permute-done.10.refs_3_) | copy-start | bytes 1474564
  89.7 5.0 %collective-permute-start.11 = (bf16[2,1,160,384]{3,2,1,0:T(8,128)(2,1)S(1)}, bf16[2,1,160,384]{3,2,1,0:T(8,128)(2,1)S(1)}, u32[]{:S(2)}, u32[]{:S(2)}) collective-permute-start(bf16[2,1,160,384]{3,2,1,0:T(8,128)(2,1)S(1)} %get-tuple-element.12), channel_id=1, source_target_pairs={{0,1},{1,2},{2,3},{3,4},{4,5},{5,6},{6,7},{8,9},{9,10},{10,11},{11... | collective-permute-start | bytes 737288 | tf_op jit(solution)/shard_map/ppermute | solution.py:20
  91.7 7.5 %collective-permute-start.12 = (bf16[2,1,160,384]{3,2,1,0:T(8,128)(2,1)S(1)}, bf16[2,1,160,384]{3,2,1,0:T(8,128)(2,1)S(1)}, u32[]{:S(2)}, u32[]{:S(2)}) collective-permute-start(bf16[2,1,160,384]{3,2,1,0:T(8,128)(2,1)S(1)} %get-tuple-element.11), channel_id=1, source_target_pairs={{1,0},{2,1},{3,2},{4,3},{5,4},{6,5},{7,6},{9,8},{10,9},{11,10},{12... | collective-permute-start | bytes 737288 | tf_op jit(solution)/shard_map/ppermute | solution.py:20
  94.8 4.4 %copy-start.7 = (bf16[2,1,160,384]{3,2,1,0:T(8,128)(2,1)}, bf16[2,1,160,384]{3,2,1,0:T(8,128)(2,1)S(1)}, u32[]{:S(2)}) copy-start(bf16[2,1,160,384]{3,2,1,0:T(8,128)(2,1)S(1)} %collective-permute-done.11.refs_4_) | copy-start | bytes 737284
  99.2 0.7 copy-start.8

commit v5 on v3

--- a/solution.py
+++ b/solution.py
@@ -82,15 +82,19 @@
     height = band // columns
     taps = 9 * channels
 
+    outputs = w_ref.shape[-1] // 3
+
     def weight_copy(j, b):
         return pltpu.make_async_copy(
             w_hbm.at[pl.ds((j * 3 + b) * channels, channels)],
-            w_ref.at[b, pl.ds(j * channels, channels)],
+            w_ref.at[pl.ds(j * channels, channels), pl.ds(b * outputs, outputs)],
             w_sem.at[b],
         )
 
     def weight_wait(b):
-        pltpu.make_async_copy(w_hbm.at[pl.ds(0, taps)], w_ref.at[b], w_sem.at[b]).wait()
+        pltpu.make_async_copy(
+            w_hbm.at[pl.ds(0, taps)], w_ref.at[:, pl.ds(b * outputs, outputs)], w_sem.at[b]
+        ).wait()
 
     @pl.when(step == 0)
     def _():
@@ -120,16 +124,17 @@
                                 pl.ds(fl * band + i * columns, columns), pl.ds(j * channels, channels)
                             ] = jnp.where(kept, piece, jnp.zeros_like(piece))
 
-    outputs = w_ref.shape[-1]
     position = lax.broadcasted_iota(jnp.int32, (cells, outputs), 0) % columns
+
+    @pl.when(step == 0)
+    def _():
+        for b in (1, 0, 2):
+            weight_wait(b)
+
+    product = jnp.dot(col_ref[...], w_ref[...], preferred_element_type=jnp.float32)
     running = None
     for b in (1, 0, 2):
-
-        @pl.when(step == 0)
-        def _():
-            weight_wait(b)
-
-        part = jnp.dot(col_ref[...], w_ref[b], preferred_element_type=jnp.float32)
+        part = product[:, b * outputs : (b + 1) * outputs]
         if b == 0:
             part = jnp.where(position == 0, 0.0, pltpu.roll(part, 1, 0))
         elif b == 2:
@@ -180,7 +185,7 @@
         input_output_aliases=aliases,
         scratch_shapes=[
             pltpu.VMEM((per_step * band, 9 * channels), jnp.bfloat16),
-            pltpu.VMEM((3, 9 * channels, outputs), jnp.bfloat16),
+            pltpu.VMEM((9 * channels, 3 * outputs), jnp.bfloat16),
             pltpu.SemaphoreType.DMA((3,)),
         ],
         cost_estimate=pl.CostEstimate(

time: 111 us -> 107 us (0.964)
  Pallas kernels: 48.4 us -> 44.7 us
    pallas_call x3, Pallas kernels: 48.4 us -> 44.7 us  [conv_call(): pl.pallas_call(functools.partial(conv_kernel, layout=layout, mode=mode, p...]
where the time goes in v5:
time: 107 us
  Pallas kernels  44.7 us (42%)
  starting transfers between devices  25.5 us (24%)
  waiting for transfers between devices  13.3 us (12%)
  local copies, waits for them, and re-layouts  12 us (11%)
  matrix products  5.89 us (6%)
  other arithmetic  5.05 us (5%)
    pallas_call x3, Pallas kernels, conv_call(): pl.pallas_call(functools.partial(conv_kernel, layout=layout, mode=mode, p...  44.7 us
    ppermute x4, starting transfers between devices, shifted(): return lax.ppermute(x, axis, pairs)  12 us
    ppermute x7, starting transfers between devices, on_device(): pieces.append(lax.ppermute(packed, 'rows', ring))  6.88 us
    ppermute x2, starting transfers between devices, diagonal(): return lax.ppermute(x, ('tm', 'rows'), pairs)  6.63 us
    dot_general x3, matrix products, local_conv(): jnp.dot(stacked, weight[tap_time].reshape(9 * channels, outputs), preferr...  5.65 us
    ppermute x2, waiting for transfers between devices, diagonal(): return lax.ppermute(x, ('tm', 'rows'), pairs)  5.49 us
    ppermute x4, waiting for transfers between devices, shifted(): return lax.ppermute(x, axis, pairs)  4.53 us
    unnamed x42, local copies, waits for them, and re-layouts  4.14 us
  transfers between devices with their start and end apart: 13, of which 5 were waited for; matrix products, arithmetic and copies ran while one was open for 3% of the time, Pallas kernels for 12%

profile of v5, /device:TPU:21, one launch (start us, length us, event | category | flops | bytes accessed | tf_op | source)
XLA Modules:
  0.0 107.0 jit_solution(11191257076724534586)
XLA Ops:
  0.0 0.7 convert_bitcast_fusion
  0.7 0.8 pad_maximum_fusion.1
  1.5 1.5 %collective-permute-start = (bf16[1,8,2688]{2,1,0:T(8,128)(2,1)S(1)}, bf16[1,8,2688]{2,1,0:T(8,128)(2,1)S(1)}, u32[]{:S(2)}, u32[]{:S(2)}) collective-permute-start(bf16[1,8,2688]{2,1,0:T(8,128)(2,1)S(1)} %get-tuple-element.23), channel_id=1, source_target_pairs={{0,1},{1,2},{2,3},{3,4},{4,5},{5,6},{6,7},{7,0},{8,9},{9,10},{10,1... | collective-permute-start | bytes 129032 | tf_op jit(solution)/shard_map/ppermute | solution.py:229
  3.0 0.2 collective-permute-start.1
  3.2 0.7 collective-permute-start.2
  3.9 2.5 %collective-permute-start.3 = (bf16[1,8,2688]{2,1,0:T(8,128)(2,1)S(1)}, bf16[1,8,2688]{2,1,0:T(8,128)(2,1)S(1)}, u32[]{:S(2)}, u32[]{:S(2)}) collective-permute-start(bf16[1,8,2688]{2,1,0:T(8,128)(2,1)S(1)} %get-tuple-element.23), channel_id=1, source_target_pairs={{0,4},{1,5},{2,6},{3,7},{4,0},{5,1},{6,2},{7,3},{8,12},{9,13},{10,... | collective-permute-start | bytes 129032 | tf_op jit(solution)/shard_map/ppermute | solution.py:229
  6.3 1.0 collective-permute-start.4
  7.4 1.0 fusion.17
  8.4 0.7 pad_dynamic-slice_fusion
  9.7 0.9 collective-permute-start.5
  10.5 0.2 collective-permute-start.6
  10.8 0.5 collective-permute-done.4
  11.3 1.7 %collective-permute-done.5 = bf16[1,8,2688]{2,1,0:T(8,128)(2,1)S(1)} collective-permute-done((bf16[1,8,2688]{2,1,0:T(8,128)(2,1)S(1)}, bf16[1,8,2688]{2,1,0:T(8,128)(2,1)S(1)}, u32[]{:S(2)}, u32[]{:S(2)}) %collective-permute-start.5) | collective-permute-done | bytes 43040 | tf_op jit(solution)/shard_map/ppermute | solution.py:229
  13.0 1.0 collective-permute-done.6
  14.1 0.2 convolution_convert_fusion
  14.4 3.5 %collective-permute-start.7 = (bf16[24,2560]{1,0:T(8,128)(2,1)S(1)}, bf16[24,2560]{1,0:T(8,128)(2,1)S(1)}, u32[]{:S(2)}, u32[]{:S(2)}) collective-permute-start(bf16[24,2560]{1,0:T(8,128)(2,1)S(1)} %convolution_convert_fusion), channel_id=1, source_target_pairs={{0,8},{8,16},{16,24},{24,32},{32,40},{40,48},{48,56},{56,64},{64,7... | collective-permute-start | bytes 368648 | tf_op jit(solution)/shard_map/ppermute | solution.py:20
  18.0 0.6 reshape.102.keep_ref
  18.6 0.6 reshape.98.refs_2_
  19.2 4.5 %collective-permute-done.7 = bf16[24,2560]{1,0:T(8,128)(2,1)S(1)} collective-permute-done((bf16[24,2560]{1,0:T(8,128)(2,1)S(1)}, bf16[24,2560]{1,0:T(8,128)(2,1)S(1)}, u32[]{:S(2)}, u32[]{:S(2)}) %collective-permute-start.7) | collective-permute-done | bytes 122912 | tf_op jit(solution)/shard_map/ppermute | solution.py:20
  23.7 1.6 %reshape.96 = bf16[8,6,160,16]{3,2,1,0:T(8,128)(2,1)S(1)} reshape(bf16[48,2560]{1,0:T(8,128)(2,1)S(1)} %pad_maximum_fusion) | data formatting | bytes 491520 | tf_op jit(solution)/shard_map/reshape | solution.py:242
  25.3 1.0 copy.20
  26.3 0.1 slice_dynamic-update-slice_fusion.14
  26.5 0.1 slice_dynamic-update-slice_fusion.13
  26.8 0.1 slice_dynamic-update-slice_fusion.11
  26.9 0.2 slice_dynamic-update-slice_fusion.10
  27.1 0.2 slice_dynamic-update-slice_fusion.9
  27.5 0.1 slice_dynamic-update-slice_fusion.23
  27.8 0.2 slice_dynamic-update-slice_fusion.21
  28.1 0.1 slice_dynamic-update-slice_fusion.17
  28.4 0.1 slice_dynamic-update-slice_fusion.15
  28.6 1.3 %fusion.19 = f32[6,4,160,384]{3,2,1,0:T(8,128)S(1)} fusion(bf16[6,4,160,144]{2,3,1,0:T(8,128)(2,1)S(1)} %slice_dynamic-update-slice_fusion.15, bf16[144,384,1,1]{1,0,3,2:T(8,128)(2,1)S(1)} %bitcast.41), kind=kOutput, calls=%fused_computation.74 | convolution fusion | flops 424673280 | bytes 7114752 | tf_op jit(solution)/shard_map/dot_general | solution.py:60
  29.8 1.3 %fusion.18 = f32[6,4,160,384]{3,2,1,0:T(8,128)S(1)} fusion(bf16[6,4,160,144]{2,3,1,0:T(8,128)(2,1)S(1)} %get-tuple-element.16, bf16[144,384,1,1]{1,0,3,2:T(8,128)(2,1)S(1)} %bitcast.40), kind=kOutput, calls=%fused_computation.73 | convolution fusion | flops 424673280 | bytes 7114752 | tf_op jit(solution)/shard_map/dot_general | solution.py:60
  31.1 3.1 %fusion = (f32[6,4,160]{2,1,0:T(4,128)S(1)}, bf16[6,4,160,384]{3,2,1,0:T(8,128)(2,1)S(1)}) fusion(bf16[6,4,160,144]{2,3,1,0:T(8,128)(2,1)S(1)} %get-tuple-element.9, bf16[144,384,1,1]{1,0,3,2:T(8,128)(2,1)S(1)} %bitcast.39, f32[6,4,160,384]{3,2,1,0:T(8,128)S(1)} %fusion.19, pred[6]{0:T(512)(128)(4,1)S(1)} %get-tuple-element.26, ...), kind=kOutput, calls=%fused_computation.2 | convolution fusion | flops 436465920 | bytes 15977484 | tf_op jit(solution)/shard_map/dot_general | solution.py:60
  34.3 3.1 %fusion.8.refs_0_ = bf16[6,4,160,384]{3,2,1,0:T(8,128)(2,1)} fusion(bf16[6,4,160,384]{3,2,1,0:T(8,128)(2,1)S(1)} %get-tuple-element.30.refs_4_.refs_7_, f32[384]{0:T(512)S(1)} %copy-done.2, f32[6,4,160]{2,1,0:T(4,128)S(1)} %add_rsqrt_fusion, pred[4]{0:T(512)(128)(4,1)S(1)} %compare_and_fusion.1), kind=kLoop, calls=%fused_computation.12 | loop fusion | flops 13271040 | bytes 5915140 | tf_op jit(solution)/shard_map/jit(_where)/select_n | solution.py:259
  37.4 19.3 %shard_map.82 = bf16[1280,384]{1,0:T(8,128)(2,1)} custom-call(s32[12]{0:T(128)} %reshape.102.keep_ref, bf16[6,4,160,384]{3,2,1,0:T(8,128)(2,1)} %fusion.8.refs_0_, bf16[10368,384]{1,0:T(8,128)(2,1)} %bitcast.44, f32[1,384]{1,0:T(1,128)} %reshape.98.refs_2_), custom_call_target="tpu_custom_call" | custom-call | flops 10192158720 | bytes 10911744 | tf_op jit(solution)/shard_map/pallas_call | solution.py:176
  56.7 1.4 %fusion.15 = (bf16[4,1,160,384]{3,2,1,0:T(8,128)(2,1)S(1)}, bf16[4,1,160,384]{3,2,1,0:T(8,128)(2,1)S(1)}) fusion(bf16[4,2,160,384]{3,2,1,0:T(8,128)(2,1)} %bitcast.34), kind=kLoop, calls=%fused_computation.70 | loop fusion | bytes 1966080 | tf_op jit(solution)/shard_map/slice | solution.py:274
  58.1 4.6 %collective-permute-start.8 = (bf16[4,1,160,384]{3,2,1,0:T(8,128)(2,1)S(1)}, bf16[4,1,160,384]{3,2,1,0:T(8,128)(2,1)S(1)}, u32[]{:S(2)}, u32[]{:S(2)}) collective-permute-start(bf16[4,1,160,384]{3,2,1,0:T(8,128)(2,1)S(1)} %get-tuple-element.6), channel_id=1, source_target_pairs={{0,1},{1,2},{2,3},{3,4},{4,5},{5,6},{6,7},{8,9},{9,10},{10,11},{11... | collective-permute-start | bytes 1474568 | tf_op jit(solution)/shard_map/ppermute | solution.py:20
  62.7 1.9 %collective-permute-start.9 = (bf16[4,1,160,384]{3,2,1,0:T(8,128)(2,1)S(1)}, bf16[4,1,160,384]{3,2,1,0:T(8,128)(2,1)S(1)}, u32[]{:S(2)}, u32[]{:S(2)}) collective-permute-start(bf16[4,1,160,384]{3,2,1,0:T(8,128)(2,1)S(1)} %get-tuple-element.5), channel_id=1, source_target_pairs={{1,0},{2,1},{3,2},{4,3},{5,4},{6,5},{7,6},{9,8},{10,9},{11,10},{12... | collective-permute-start | bytes 1474568 | tf_op jit(solution)/shard_map/ppermute | solution.py:20
  64.7 1.9 %collective-permute-start.10 = (bf16[2,2,160,384]{3,2,1,0:T(8,128)(2,1)S(1)}, bf16[2,2,160,384]{3,2,1,0:T(8,128)(2,1)S(1)}, u32[]{:S(2)}, u32[]{:S(2)}) collective-permute-start(bf16[2,2,160,384]{3,2,1,0:T(8,128)(2,1)S(1)} %bitcast.37), channel_id=1, source_target_pairs={{0,8},{8,16},{16,24},{24,32},{32,40},{40,48},{48,56},{56,64},{64,7... | collective-permute-start | bytes 1474568 | tf_op jit(solution)/shard_map/ppermute | solution.py:20
  66.7 4.7 %collective-permute-start.11 = (bf16[2,1,160,384]{3,2,1,0:T(8,128)(2,1)S(1)}, bf16[2,1,160,384]{3,2,1,0:T(8,128)(2,1)S(1)}, u32[]{:S(2)}, u32[]{:S(2)}) collective-permute-start(bf16[2,1,160,384]{3,2,1,0:T(8,128)(2,1)S(1)} %get-tuple-element.8), channel_id=1, source_target_pairs={{0,9},{1,10},{2,11},{3,12},{4,13},{5,14},{6,15},{8,17},{9,18},{10,... | collective-permute-start | bytes 737288 | tf_op jit(solution)/shard_map/ppermute | solution.py:31
  71.4 1.9 %collective-permute-start.12 = (bf16[2,1,160,384]{3,2,1,0:T(8,128)(2,1)S(1)}, bf16[2,1,160,384]{3,2,1,0:T(8,128)(2,1)S(1)}, u32[]{:S(2)}, u32[]{:S(2)}) collective-permute-start(bf16[2,1,160,384]{3,2,1,0:T(8,128)(2,1)S(1)} %get-tuple-element.7), channel_id=1, source_target_pairs={{1,8},{2,9},{3,10},{4,11},{5,12},{6,13},{7,14},{9,16},{10,17},{11,... | collective-permute-start | bytes 737288 | tf_op jit(solution)/shard_map/ppermute | solution.py:31
  73.4 0.8 copy-done.4
  74.2 0.2 copy-done.5
  74.4 12.5 %shard_map.83.refs_8_ = bf16[1280,384]{1,0:T(8,128)(2,1)} custom-call(s32[12]{0:T(128)} %reshape.102.keep_ref, bf16[4,2,160,384]{3,2,1,0:T(8,128)(2,1)} %bitcast.35, bf16[4,1,160,384]{3,2,1,0:T(8,128)(2,1)} %copy-done.4, bf16[4,1,160,384]{3,2,1,0:T(8,128)(2,1)} %copy-done.5, bf16[10368,384]{1,0:T(8,128)(2,1)} %bitcast.45, bf16[6,4,160,384]{3,2,1,0:T(8,128)(2,1)} %copy-done), custom_call_target="tpu_custom_call" | custom-call | flops 5096079360 | bytes 9437184 | tf_op jit(solution)/shard_map/pallas_call | solution.py:176
  86.9 5.5 %collective-permute-done.11.refs_4_ = bf16[2,1,160,384]{3,2,1,0:T(8,128)(2,1)S(1)} collective-permute-done((bf16[2,1,160,384]{3,2,1,0:T(8,128)(2,1)S(1)}, bf16[2,1,160,384]{3,2,1,0:T(8,128)(2,1)S(1)}, u32[]{:S(2)}, u32[]{:S(2)}) %collective-permute-start.11) | collective-permute-done | bytes 245792 | tf_op jit(solution)/shard_map/ppermute | solution.py:31
  92.4 0.7 copy-done.7
  93.2 0.8 copy-done.6
  94.0 12.8 %shard_map.84 = bf16[1280,384]{1,0:T(8,128)(2,1)} custom-call(s32[12]{0:T(128)} %reshape.102.keep_ref, bf16[4,2,160,384]{3,2,1,0:T(8,128)(2,1)} %bitcast.36, bf16[4,1,160,384]{3,2,1,0:T(8,128)(2,1)} %copy-done.4, bf16[4,1,160,384]{3,2,1,0:T(8,128)(2,1)} %copy-done.5, bf16[2,2,160,384]{3,2,1,0:T(8,128)(2,1)} %copy-done.6, ...), custom_call_target="tpu_custom_call", output_to_operand_aliasing={{}: (9, {})} | custom-call | flops 5096079360 | bytes 9437184 | tf_op jit(solution)/shard_map/pallas_call | solution.py:176
  (59 shorter events, 1.8 us)
Async XLA Ops:
  0.0 18.6 %copy-start.3 = (f32[384]{0:T(512)S(1)}, f32[384]{0:T(512)}, u32[]{:S(2)}) copy-start(f32[384]{0:T(512)} %param.14) | copy-start | bytes 4612
  1.5 8.1 %collective-permute-start = (bf16[1,8,2688]{2,1,0:T(8,128)(2,1)S(1)}, bf16[1,8,2688]{2,1,0:T(8,128)(2,1)S(1)}, u32[]{:S(2)}, u32[]{:S(2)}) collective-permute-start(bf16[1,8,2688]{2,1,0:T(8,128)(2,1)S(1)} %get-tuple-element.23), channel_id=1, source_target_pairs={{0,1},{1,2},{2,3},{3,4},{4,5},{5,6},{6,7},{7,0},{8,9},{9,10},{10,1... | collective-permute-start | bytes 129032 | tf_op jit(solution)/shard_map/ppermute | solution.py:229
  3.0 7.5 %collective-permute-start.1 = (bf16[1,8,2688]{2,1,0:T(8,128)(2,1)S(1)}, bf16[1,8,2688]{2,1,0:T(8,128)(2,1)S(1)}, u32[]{:S(2)}, u32[]{:S(2)}) collective-permute-start(bf16[1,8,2688]{2,1,0:T(8,128)(2,1)S(1)} %get-tuple-element.23), channel_id=1, source_target_pairs={{0,2},{1,3},{2,4},{3,5},{4,6},{5,7},{6,0},{7,1},{8,10},{9,11},{10,... | collective-permute-start | bytes 129032 | tf_op jit(solution)/shard_map/ppermute | solution.py:229
  3.2 7.5 %collective-permute-start.2 = (bf16[1,8,2688]{2,1,0:T(8,128)(2,1)S(1)}, bf16[1,8,2688]{2,1,0:T(8,128)(2,1)S(1)}, u32[]{:S(2)}, u32[]{:S(2)}) collective-permute-start(bf16[1,8,2688]{2,1,0:T(8,128)(2,1)S(1)} %get-tuple-element.23), channel_id=1, source_target_pairs={{0,3},{1,4},{2,5},{3,6},{4,7},{5,0},{6,1},{7,2},{8,11},{9,12},{10,... | collective-permute-start | bytes 129032 | tf_op jit(solution)/shard_map/ppermute | solution.py:229
  3.9 6.9 %collective-permute-start.3 = (bf16[1,8,2688]{2,1,0:T(8,128)(2,1)S(1)}, bf16[1,8,2688]{2,1,0:T(8,128)(2,1)S(1)}, u32[]{:S(2)}, u32[]{:S(2)}) collective-permute-start(bf16[1,8,2688]{2,1,0:T(8,128)(2,1)S(1)} %get-tuple-element.23), channel_id=1, source_target_pairs={{0,4},{1,5},{2,6},{3,7},{4,0},{5,1},{6,2},{7,3},{8,12},{9,13},{10,... | collective-permute-start | bytes 129032 | tf_op jit(solution)/shard_map/ppermute | solution.py:229
  6.3 5.0 %collective-permute-start.4 = (bf16[1,8,2688]{2,1,0:T(8,128)(2,1)S(1)}, bf16[1,8,2688]{2,1,0:T(8,128)(2,1)S(1)}, u32[]{:S(2)}, u32[]{:S(2)}) collective-permute-start(bf16[1,8,2688]{2,1,0:T(8,128)(2,1)S(1)} %get-tuple-element.23), channel_id=1, source_target_pairs={{0,5},{1,6},{2,7},{3,0},{4,1},{5,2},{6,3},{7,4},{8,13},{9,14},{10,... | collective-permute-start | bytes 129032 | tf_op jit(solution)/shard_map/ppermute | solution.py:229
  9.7 3.3 %collective-permute-start.5 = (bf16[1,8,2688]{2,1,0:T(8,128)(2,1)S(1)}, bf16[1,8,2688]{2,1,0:T(8,128)(2,1)S(1)}, u32[]{:S(2)}, u32[]{:S(2)}) collective-permute-start(bf16[1,8,2688]{2,1,0:T(8,128)(2,1)S(1)} %get-tuple-element.23), channel_id=1, source_target_pairs={{0,6},{1,7},{2,0},{3,1},{4,2},{5,3},{6,4},{7,5},{8,14},{9,15},{10,... | collective-permute-start | bytes 129032 | tf_op jit(solution)/shard_map/ppermute | solution.py:229
  10.5 3.5 %collective-permute-start.6 = (bf16[1,8,2688]{2,1,0:T(8,128)(2,1)S(1)}, bf16[1,8,2688]{2,1,0:T(8,128)(2,1)S(1)}, u32[]{:S(2)}, u32[]{:S(2)}) collective-permute-start(bf16[1,8,2688]{2,1,0:T(8,128)(2,1)S(1)} %get-tuple-element.23), channel_id=1, source_target_pairs={{0,7},{1,0},{2,1},{3,2},{4,3},{5,4},{6,5},{7,6},{8,15},{9,8},{10,9... | collective-permute-start | bytes 129032 | tf_op jit(solution)/shard_map/ppermute | solution.py:229
  14.4 9.3 %collective-permute-start.7 = (bf16[24,2560]{1,0:T(8,128)(2,1)S(1)}, bf16[24,2560]{1,0:T(8,128)(2,1)S(1)}, u32[]{:S(2)}, u32[]{:S(2)}) collective-permute-start(bf16[24,2560]{1,0:T(8,128)(2,1)S(1)} %convolution_convert_fusion), channel_id=1, source_target_pairs={{0,8},{8,16},{16,24},{24,32},{32,40},{40,48},{48,56},{56,64},{64,7... | collective-permute-start | bytes 368648 | tf_op jit(solution)/shard_map/ppermute | solution.py:20
  31.1 3.2 %copy-start.2 = (f32[384]{0:T(512)S(1)}, f32[384]{0:T(512)}, u32[]{:S(2)}) copy-start(f32[384]{0:T(512)} %param.12) | copy-start | bytes 4612
  34.2 3.2 %copy-start = (bf16[6,4,160,384]{3,2,1,0:T(8,128)(2,1)}, bf16[6,4,160,384]{3,2,1,0:T(8,128)(2,1)S(1)}, u32[]{:S(2)}) copy-start(bf16[6,4,160,384]{3,2,1,0:T(8,128)(2,1)S(1)} %get-tuple-element.30.refs_4_.refs_7_) | copy-start | bytes 8847364
  56.7 8.0 %copy-start.1 = (bf16[1280,384]{1,0:T(8,128)(2,1)S(1)}, bf16[1280,384]{1,0:T(8,128)(2,1)}, u32[]{:S(2)}) copy-start(bf16[1280,384]{1,0:T(8,128)(2,1)} %shard_map.82) | copy-start | bytes 2949124
  58.1 15.3 %collective-permute-start.8 = (bf16[4,1,160,384]{3,2,1,0:T(8,128)(2,1)S(1)}, bf16[4,1,160,384]{3,2,1,0:T(8,128)(2,1)S(1)}, u32[]{:S(2)}, u32[]{:S(2)}) collective-permute-start(bf16[4,1,160,384]{3,2,1,0:T(8,128)(2,1)S(1)} %get-tuple-element.6), channel_id=1, source_target_pairs={{0,1},{1,2},{2,3},{3,4},{4,5},{5,6},{6,7},{8,9},{9,10},{10,11},{11... | collective-permute-start | bytes 1474568 | tf_op jit(solution)/shard_map/ppermute | solution.py:20
  62.7 10.7 %collective-permute-start.9 = (bf16[4,1,160,384]{3,2,1,0:T(8,128)(2,1)S(1)}, bf16[4,1,160,384]{3,2,1,0:T(8,128)(2,1)S(1)}, u32[]{:S(2)}, u32[]{:S(2)}) collective-permute-start(bf16[4,1,160,384]{3,2,1,0:T(8,128)(2,1)S(1)} %get-tuple-element.5), channel_id=1, source_target_pairs={{1,0},{2,1},{3,2},{4,3},{5,4},{6,5},{7,6},{9,8},{10,9},{11,10},{12... | collective-permute-start | bytes 1474568 | tf_op jit(solution)/shard_map/ppermute | solution.py:20
  64.7 27.7 %collective-permute-start.10 = (bf16[2,2,160,384]{3,2,1,0:T(8,128)(2,1)S(1)}, bf16[2,2,160,384]{3,2,1,0:T(8,128)(2,1)S(1)}, u32[]{:S(2)}, u32[]{:S(2)}) collective-permute-start(bf16[2,2,160,384]{3,2,1,0:T(8,128)(2,1)S(1)} %bitcast.37), channel_id=1, source_target_pairs={{0,8},{8,16},{16,24},{24,32},{32,40},{40,48},{48,56},{56,64},{64,7... | collective-permute-start | bytes 1474568 | tf_op jit(solution)/shard_map/ppermute | solution.py:20
  66.7 25.7 %collective-permute-start.11 = (bf16[2,1,160,384]{3,2,1,0:T(8,128)(2,1)S(1)}, bf16[2,1,160,384]{3,2,1,0:T(8,128)(2,1)S(1)}, u32[]{:S(2)}, u32[]{:S(2)}) collective-permute-start(bf16[2,1,160,384]{3,2,1,0:T(8,128)(2,1)S(1)} %get-tuple-element.8), channel_id=1, source_target_pairs={{0,9},{1,10},{2,11},{3,12},{4,13},{5,14},{6,15},{8,17},{9,18},{10,... | collective-permute-start | bytes 737288 | tf_op jit(solution)/shard_map/ppermute | solution.py:31
  71.4 21.0 %collective-permute-start.12 = (bf16[2,1,160,384]{3,2,1,0:T(8,128)(2,1)S(1)}, bf16[2,1,160,384]{3,2,1,0:T(8,128)(2,1)S(1)}, u32[]{:S(2)}, u32[]{:S(2)}) collective-permute-start(bf16[2,1,160,384]{3,2,1,0:T(8,128)(2,1)S(1)} %get-tuple-element.7), channel_id=1, source_target_pairs={{1,8},{2,9},{3,10},{4,11},{5,12},{6,13},{7,14},{9,16},{10,17},{11,... | collective-permute-start | bytes 737288 | tf_op jit(solution)/shard_map/ppermute | solution.py:31
  73.4 0.8 copy-start.4
  73.4 1.0 copy-start.5
  92.4 0.7 copy-start.7
  92.4 0.8 copy-start.8
  93.2 0.8 copy-start.6

commit v6 on v5

--- a/solution.py
+++ b/solution.py
@@ -88,18 +88,20 @@
         return pltpu.make_async_copy(
             w_hbm.at[pl.ds((j * 3 + b) * channels, channels)],
             w_ref.at[pl.ds(j * channels, channels), pl.ds(b * outputs, outputs)],
-            w_sem.at[b],
-        )
-
-    def weight_wait(b):
+            w_sem.at[(j // 3) * 3 + b],
+        )
+
+    def weight_wait(k, b):
         pltpu.make_async_copy(
-            w_hbm.at[pl.ds(0, taps)], w_ref.at[:, pl.ds(b * outputs, outputs)], w_sem.at[b]
+            w_hbm.at[pl.ds(0, 3 * channels)],
+            w_ref.at[pl.ds(k * 3 * channels, 3 * channels), pl.ds(b * outputs, outputs)],
+            w_sem.at[k * 3 + b],
         ).wait()
 
     @pl.when(step == 0)
     def _():
-        for b in (1, 0, 2):
-            for j in range(9):
+        for j in range(9):
+            for b in range(3):
                 weight_copy(j, b).start()
 
     def row_of(ext_frame, ext_row):
@@ -126,12 +128,17 @@
 
     position = lax.broadcasted_iota(jnp.int32, (cells, outputs), 0) % columns
 
-    @pl.when(step == 0)
-    def _():
-        for b in (1, 0, 2):
-            weight_wait(b)
-
-    product = jnp.dot(col_ref[...], w_ref[...], preferred_element_type=jnp.float32)
+    product = None
+    for k in range(3):
+
+        @pl.when(step == 0)
+        def _():
+            for b in range(3):
+                weight_wait(k, b)
+
+        lanes = pl.ds(k * 3 * channels, 3 * channels)
+        term = jnp.dot(col_ref[:, lanes], w_ref[lanes, :], preferred_element_type=jnp.float32)
+        product = term if product is None else product + term
     running = None
     for b in (1, 0, 2):
         part = product[:, b * outputs : (b + 1) * outputs]
@@ -146,7 +153,7 @@
         scaled = values_f * inverse * side_ref[...]
         o_ref[...] = (scaled / (1.0 + jnp.exp(-scaled))).astype(o_ref.dtype)
     else:
-        residual = side_ref[pl.ds(2 + firsts[0] + step * per_step, per_step), 1 : 1 + height]
+        residual = side_ref[:, 1 : 1 + height]
         o_ref[...] = (residual.reshape(cells, outputs).astype(jnp.float32) + running).astype(
             o_ref.dtype
         )
@@ -167,6 +174,12 @@
     if firsts is None:
         firsts = tuple(range(0, frame_count, per_step))
     block_at = firsts[0] // per_step
+    if mode == "act":
+        side_spec = whole(side)
+    else:
+        side_spec = pl.BlockSpec(
+            (per_step,) + side.shape[1:], lambda step: (1 + block_at + step, 0, 0, 0)
+        )
     operands = [keep, *sources, weight_rows, side]
     extra_specs, aliases = [], {}
     if into is not None:
@@ -178,7 +191,7 @@
         out_shape=jax.ShapeDtypeStruct((cells, outputs), jnp.bfloat16),
         in_specs=[pl.BlockSpec(memory_space=pltpu.SMEM)]
         + [whole(x) for x in sources]
-        + [pl.BlockSpec(memory_space=pl.ANY), whole(side)]
+        + [pl.BlockSpec(memory_space=pl.ANY), side_spec]
         + extra_specs,
         out_specs=pl.BlockSpec((per_step * band, outputs), lambda step: (step + block_at, 0)),
         grid=(len(firsts),),
@@ -186,7 +199,7 @@
         scratch_shapes=[
             pltpu.VMEM((per_step * band, 9 * channels), jnp.bfloat16),
             pltpu.VMEM((9 * channels, 3 * outputs), jnp.bfloat16),
-            pltpu.SemaphoreType.DMA((3,)),
+            pltpu.SemaphoreType.DMA((9,)),
         ],
         cost_estimate=pl.CostEstimate(
             flops=2 * len(firsts) * per_step * band * 27 * channels * outputs,

time: 107 us -> 109 us (1.019)
  Pallas kernels: 44.7 us -> 46.2 us
    pallas_call x3, Pallas kernels: 44.7 us -> 46.2 us  [conv_call(): pl.pallas_call(functools.partial(conv_kernel, layout=layout, mode=mode, p...]
  transfers between devices with their start and end apart: 13 -> 13, of which waited for: 5 -> 5; matrix products, arithmetic and copies ran while one was open for 3% -> 3% of each run, Pallas kernels for 12% -> 11%
where the time goes in v6:
time: 109 us
  Pallas kernels  46.2 us (42%)
  starting transfers between devices  25.8 us (24%)
  waiting for transfers between devices  13.2 us (12%)
  local copies, waits for them, and re-layouts  12 us (11%)
  matrix products  5.89 us (5%)
  other arithmetic  5.05 us (5%)
    pallas_call x3, Pallas kernels, conv_call(): pl.pallas_call(functools.partial(conv_kernel, layout=layout, mode=mode, p...  46.2 us
    ppermute x4, starting transfers between devices, shifted(): return lax.ppermute(x, axis, pairs)  12 us
    ppermute x7, starting transfers between devices, on_device(): pieces.append(lax.ppermute(packed, 'rows', ring))  6.88 us
    ppermute x2, starting transfers between devices, diagonal(): return lax.ppermute(x, ('tm', 'rows'), pairs)  6.85 us
    dot_general x3, matrix products, local_conv(): jnp.dot(stacked, weight[tap_time].reshape(9 * channels, outputs), preferr...  5.65 us
    ppermute x2, waiting for transfers between devices, diagonal(): return lax.ppermute(x, ('tm', 'rows'), pairs)  5.43 us
    ppermute x4, waiting for transfers between devices, shifted(): return lax.ppermute(x, axis, pairs)  4.53 us
    unnamed x42, local copies, waits for them, and re-layouts  4.14 us
  transfers between devices with their start and end apart: 13, of which 5 were waited for; matrix products, arithmetic and copies ran while one was open for 3% of the time, Pallas kernels for 11%

profile of v6, /device:TPU:21, one launch (start us, length us, event | category | flops | bytes accessed | tf_op | source)
XLA Modules:
  0.0 108.7 jit_solution(1475277802910938251)
XLA Ops:
  0.0 0.7 convert_bitcast_fusion
  0.7 0.8 pad_maximum_fusion.1
  1.5 1.5 %collective-permute-start = (bf16[1,8,2688]{2,1,0:T(8,128)(2,1)S(1)}, bf16[1,8,2688]{2,1,0:T(8,128)(2,1)S(1)}, u32[]{:S(2)}, u32[]{:S(2)}) collective-permute-start(bf16[1,8,2688]{2,1,0:T(8,128)(2,1)S(1)} %get-tuple-element.23), channel_id=1, source_target_pairs={{0,1},{1,2},{2,3},{3,4},{4,5},{5,6},{6,7},{7,0},{8,9},{9,10},{10,1... | collective-permute-start | bytes 129032 | tf_op jit(solution)/shard_map/ppermute | solution.py:242
  3.0 0.2 collective-permute-start.1
  3.2 0.7 collective-permute-start.2
  3.9 2.5 %collective-permute-start.3 = (bf16[1,8,2688]{2,1,0:T(8,128)(2,1)S(1)}, bf16[1,8,2688]{2,1,0:T(8,128)(2,1)S(1)}, u32[]{:S(2)}, u32[]{:S(2)}) collective-permute-start(bf16[1,8,2688]{2,1,0:T(8,128)(2,1)S(1)} %get-tuple-element.23), channel_id=1, source_target_pairs={{0,4},{1,5},{2,6},{3,7},{4,0},{5,1},{6,2},{7,3},{8,12},{9,13},{10,... | collective-permute-start | bytes 129032 | tf_op jit(solution)/shard_map/ppermute | solution.py:242
  6.3 1.0 collective-permute-start.4
  7.4 1.0 fusion.17
  8.4 0.7 pad_dynamic-slice_fusion
  9.7 0.9 collective-permute-start.5
  10.5 0.2 collective-permute-start.6
  10.8 0.5 collective-permute-done.4
  11.3 1.7 %collective-permute-done.5 = bf16[1,8,2688]{2,1,0:T(8,128)(2,1)S(1)} collective-permute-done((bf16[1,8,2688]{2,1,0:T(8,128)(2,1)S(1)}, bf16[1,8,2688]{2,1,0:T(8,128)(2,1)S(1)}, u32[]{:S(2)}, u32[]{:S(2)}) %collective-permute-start.5) | collective-permute-done | bytes 43040 | tf_op jit(solution)/shard_map/ppermute | solution.py:242
  13.0 1.0 collective-permute-done.6
  14.1 0.2 convolution_convert_fusion
  14.4 3.5 %collective-permute-start.7 = (bf16[24,2560]{1,0:T(8,128)(2,1)S(1)}, bf16[24,2560]{1,0:T(8,128)(2,1)S(1)}, u32[]{:S(2)}, u32[]{:S(2)}) collective-permute-start(bf16[24,2560]{1,0:T(8,128)(2,1)S(1)} %convolution_convert_fusion), channel_id=1, source_target_pairs={{0,8},{8,16},{16,24},{24,32},{32,40},{40,48},{48,56},{56,64},{64,7... | collective-permute-start | bytes 368648 | tf_op jit(solution)/shard_map/ppermute | solution.py:20
  18.0 0.6 reshape.102.keep_ref
  18.6 0.6 reshape.98.refs_2_
  19.2 4.5 %collective-permute-done.7 = bf16[24,2560]{1,0:T(8,128)(2,1)S(1)} collective-permute-done((bf16[24,2560]{1,0:T(8,128)(2,1)S(1)}, bf16[24,2560]{1,0:T(8,128)(2,1)S(1)}, u32[]{:S(2)}, u32[]{:S(2)}) %collective-permute-start.7) | collective-permute-done | bytes 122912 | tf_op jit(solution)/shard_map/ppermute | solution.py:20
  23.7 1.6 %reshape.96 = bf16[8,6,160,16]{3,2,1,0:T(8,128)(2,1)S(1)} reshape(bf16[48,2560]{1,0:T(8,128)(2,1)S(1)} %pad_maximum_fusion) | data formatting | bytes 491520 | tf_op jit(solution)/shard_map/reshape | solution.py:255
  25.3 1.0 copy.20
  26.3 0.1 slice_dynamic-update-slice_fusion.14
  26.5 0.1 slice_dynamic-update-slice_fusion.13
  26.8 0.1 slice_dynamic-update-slice_fusion.11
  26.9 0.2 slice_dynamic-update-slice_fusion.10
  27.1 0.2 slice_dynamic-update-slice_fusion.9
  27.5 0.1 slice_dynamic-update-slice_fusion.23
  27.8 0.2 slice_dynamic-update-slice_fusion.21
  28.1 0.1 slice_dynamic-update-slice_fusion.17
  28.4 0.1 slice_dynamic-update-slice_fusion.15
  28.6 1.3 %fusion.19 = f32[6,4,160,384]{3,2,1,0:T(8,128)S(1)} fusion(bf16[6,4,160,144]{2,3,1,0:T(8,128)(2,1)S(1)} %slice_dynamic-update-slice_fusion.15, bf16[144,384,1,1]{1,0,3,2:T(8,128)(2,1)S(1)} %bitcast.41), kind=kOutput, calls=%fused_computation.74 | convolution fusion | flops 424673280 | bytes 7114752 | tf_op jit(solution)/shard_map/dot_general | solution.py:60
  29.8 1.3 %fusion.18 = f32[6,4,160,384]{3,2,1,0:T(8,128)S(1)} fusion(bf16[6,4,160,144]{2,3,1,0:T(8,128)(2,1)S(1)} %get-tuple-element.16, bf16[144,384,1,1]{1,0,3,2:T(8,128)(2,1)S(1)} %bitcast.40), kind=kOutput, calls=%fused_computation.73 | convolution fusion | flops 424673280 | bytes 7114752 | tf_op jit(solution)/shard_map/dot_general | solution.py:60
  31.1 3.1 %fusion = (f32[6,4,160]{2,1,0:T(4,128)S(1)}, bf16[6,4,160,384]{3,2,1,0:T(8,128)(2,1)S(1)}) fusion(bf16[6,4,160,144]{2,3,1,0:T(8,128)(2,1)S(1)} %get-tuple-element.9, bf16[144,384,1,1]{1,0,3,2:T(8,128)(2,1)S(1)} %bitcast.39, f32[6,4,160,384]{3,2,1,0:T(8,128)S(1)} %fusion.19, pred[6]{0:T(512)(128)(4,1)S(1)} %get-tuple-element.26, ...), kind=kOutput, calls=%fused_computation.2 | convolution fusion | flops 436465920 | bytes 15977484 | tf_op jit(solution)/shard_map/dot_general | solution.py:60
  34.3 3.1 %fusion.8.refs_0_ = bf16[6,4,160,384]{3,2,1,0:T(8,128)(2,1)} fusion(bf16[6,4,160,384]{3,2,1,0:T(8,128)(2,1)S(1)} %get-tuple-element.30.refs_4_.refs_7_, f32[384]{0:T(512)S(1)} %copy-done.2, f32[6,4,160]{2,1,0:T(4,128)S(1)} %add_rsqrt_fusion, pred[4]{0:T(512)(128)(4,1)S(1)} %compare_and_fusion.1), kind=kLoop, calls=%fused_computation.12 | loop fusion | flops 13271040 | bytes 5915140 | tf_op jit(solution)/shard_map/jit(_where)/select_n | solution.py:272
  37.4 21.2 %shard_map.82 = bf16[1280,384]{1,0:T(8,128)(2,1)} custom-call(s32[12]{0:T(128)} %reshape.102.keep_ref, bf16[6,4,160,384]{3,2,1,0:T(8,128)(2,1)} %fusion.8.refs_0_, bf16[10368,384]{1,0:T(8,128)(2,1)} %bitcast.44, f32[1,384]{1,0:T(1,128)} %reshape.98.refs_2_), custom_call_target="tpu_custom_call" | custom-call | flops 10192158720 | bytes 10911744 | tf_op jit(solution)/shard_map/pallas_call | solution.py:189
  58.6 1.4 %fusion.15 = (bf16[4,1,160,384]{3,2,1,0:T(8,128)(2,1)S(1)}, bf16[4,1,160,384]{3,2,1,0:T(8,128)(2,1)S(1)}) fusion(bf16[4,2,160,384]{3,2,1,0:T(8,128)(2,1)} %bitcast.34), kind=kLoop, calls=%fused_computation.70 | loop fusion | bytes 1966080 | tf_op jit(solution)/shard_map/slice | solution.py:287
  60.0 4.6 %collective-permute-start.8 = (bf16[4,1,160,384]{3,2,1,0:T(8,128)(2,1)S(1)}, bf16[4,1,160,384]{3,2,1,0:T(8,128)(2,1)S(1)}, u32[]{:S(2)}, u32[]{:S(2)}) collective-permute-start(bf16[4,1,160,384]{3,2,1,0:T(8,128)(2,1)S(1)} %get-tuple-element.6), channel_id=1, source_target_pairs={{0,1},{1,2},{2,3},{3,4},{4,5},{5,6},{6,7},{8,9},{9,10},{10,11},{11... | collective-permute-start | bytes 1474568 | tf_op jit(solution)/shard_map/ppermute | solution.py:20
  64.6 1.9 %collective-permute-start.9 = (bf16[4,1,160,384]{3,2,1,0:T(8,128)(2,1)S(1)}, bf16[4,1,160,384]{3,2,1,0:T(8,128)(2,1)S(1)}, u32[]{:S(2)}, u32[]{:S(2)}) collective-permute-start(bf16[4,1,160,384]{3,2,1,0:T(8,128)(2,1)S(1)} %get-tuple-element.5), channel_id=1, source_target_pairs={{1,0},{2,1},{3,2},{4,3},{5,4},{6,5},{7,6},{9,8},{10,9},{11,10},{12... | collective-permute-start | bytes 1474568 | tf_op jit(solution)/shard_map/ppermute | solution.py:20
  66.6 1.9 %collective-permute-start.10 = (bf16[2,2,160,384]{3,2,1,0:T(8,128)(2,1)S(1)}, bf16[2,2,160,384]{3,2,1,0:T(8,128)(2,1)S(1)}, u32[]{:S(2)}, u32[]{:S(2)}) collective-permute-start(bf16[2,2,160,384]{3,2,1,0:T(8,128)(2,1)S(1)} %bitcast.37), channel_id=1, source_target_pairs={{0,8},{8,16},{16,24},{24,32},{32,40},{40,48},{48,56},{56,64},{64,7... | collective-permute-start | bytes 1474568 | tf_op jit(solution)/shard_map/ppermute | solution.py:20
  68.6 4.7 %collective-permute-start.11 = (bf16[2,1,160,384]{3,2,1,0:T(8,128)(2,1)S(1)}, bf16[2,1,160,384]{3,2,1,0:T(8,128)(2,1)S(1)}, u32[]{:S(2)}, u32[]{:S(2)}) collective-permute-start(bf16[2,1,160,384]{3,2,1,0:T(8,128)(2,1)S(1)} %get-tuple-element.8), channel_id=1, source_target_pairs={{0,9},{1,10},{2,11},{3,12},{4,13},{5,14},{6,15},{8,17},{9,18},{10,... | collective-permute-start | bytes 737288 | tf_op jit(solution)/shard_map/ppermute | solution.py:31
  73.3 2.1 %collective-permute-start.12 = (bf16[2,1,160,384]{3,2,1,0:T(8,128)(2,1)S(1)}, bf16[2,1,160,384]{3,2,1,0:T(8,128)(2,1)S(1)}, u32[]{:S(2)}, u32[]{:S(2)}) collective-permute-start(bf16[2,1,160,384]{3,2,1,0:T(8,128)(2,1)S(1)} %get-tuple-element.7), channel_id=1, source_target_pairs={{1,8},{2,9},{3,10},{4,11},{5,12},{6,13},{7,14},{9,16},{10,17},{11,... | collective-permute-start | bytes 737288 | tf_op jit(solution)/shard_map/ppermute | solution.py:31
  75.5 0.8 copy-done.4
  76.3 0.2 copy-done.5
  76.4 12.4 %shard_map.83.refs_8_ = bf16[1280,384]{1,0:T(8,128)(2,1)} custom-call(s32[12]{0:T(128)} %reshape.102.keep_ref, bf16[4,2,160,384]{3,2,1,0:T(8,128)(2,1)} %bitcast.35, bf16[4,1,160,384]{3,2,1,0:T(8,128)(2,1)} %copy-done.4, bf16[4,1,160,384]{3,2,1,0:T(8,128)(2,1)} %copy-done.5, bf16[10368,384]{1,0:T(8,128)(2,1)} %bitcast.45, bf16[6,4,160,384]{3,2,1,0:T(8,128)(2,1)} %copy-done), custom_call_target="tpu_custom_call" | custom-call | flops 5096079360 | bytes 9437184 | tf_op jit(solution)/shard_map/pallas_call | solution.py:189
  88.8 5.4 %collective-permute-done.11.refs_4_ = bf16[2,1,160,384]{3,2,1,0:T(8,128)(2,1)S(1)} collective-permute-done((bf16[2,1,160,384]{3,2,1,0:T(8,128)(2,1)S(1)}, bf16[2,1,160,384]{3,2,1,0:T(8,128)(2,1)S(1)}, u32[]{:S(2)}, u32[]{:S(2)}) %collective-permute-start.11) | collective-permute-done | bytes 245792 | tf_op jit(solution)/shard_map/ppermute | solution.py:31
  94.3 0.7 copy-done.7
  95.0 0.8 copy-done.6
  95.8 12.7 %shard_map.84 = bf16[1280,384]{1,0:T(8,128)(2,1)} custom-call(s32[12]{0:T(128)} %reshape.102.keep_ref, bf16[4,2,160,384]{3,2,1,0:T(8,128)(2,1)} %bitcast.36, bf16[4,1,160,384]{3,2,1,0:T(8,128)(2,1)} %copy-done.4, bf16[4,1,160,384]{3,2,1,0:T(8,128)(2,1)} %copy-done.5, bf16[2,2,160,384]{3,2,1,0:T(8,128)(2,1)} %copy-done.6, ...), custom_call_target="tpu_custom_call", output_to_operand_aliasing={{}: (9, {})} | custom-call | flops 5096079360 | bytes 9437184 | tf_op jit(solution)/shard_map/pallas_call | solution.py:189
  (59 shorter events, 1.8 us)
Async XLA Ops:
  0.0 18.6 %copy-start.3 = (f32[384]{0:T(512)S(1)}, f32[384]{0:T(512)}, u32[]{:S(2)}) copy-start(f32[384]{0:T(512)} %param.14) | copy-start | bytes 4612
  1.5 8.1 %collective-permute-start = (bf16[1,8,2688]{2,1,0:T(8,128)(2,1)S(1)}, bf16[1,8,2688]{2,1,0:T(8,128)(2,1)S(1)}, u32[]{:S(2)}, u32[]{:S(2)}) collective-permute-start(bf16[1,8,2688]{2,1,0:T(8,128)(2,1)S(1)} %get-tuple-element.23), channel_id=1, source_target_pairs={{0,1},{1,2},{2,3},{3,4},{4,5},{5,6},{6,7},{7,0},{8,9},{9,10},{10,1... | collective-permute-start | bytes 129032 | tf_op jit(solution)/shard_map/ppermute | solution.py:242
  3.0 7.5 %collective-permute-start.1 = (bf16[1,8,2688]{2,1,0:T(8,128)(2,1)S(1)}, bf16[1,8,2688]{2,1,0:T(8,128)(2,1)S(1)}, u32[]{:S(2)}, u32[]{:S(2)}) collective-permute-start(bf16[1,8,2688]{2,1,0:T(8,128)(2,1)S(1)} %get-tuple-element.23), channel_id=1, source_target_pairs={{0,2},{1,3},{2,4},{3,5},{4,6},{5,7},{6,0},{7,1},{8,10},{9,11},{10,... | collective-permute-start | bytes 129032 | tf_op jit(solution)/shard_map/ppermute | solution.py:242
  3.2 7.5 %collective-permute-start.2 = (bf16[1,8,2688]{2,1,0:T(8,128)(2,1)S(1)}, bf16[1,8,2688]{2,1,0:T(8,128)(2,1)S(1)}, u32[]{:S(2)}, u32[]{:S(2)}) collective-permute-start(bf16[1,8,2688]{2,1,0:T(8,128)(2,1)S(1)} %get-tuple-element.23), channel_id=1, source_target_pairs={{0,3},{1,4},{2,5},{3,6},{4,7},{5,0},{6,1},{7,2},{8,11},{9,12},{10,... | collective-permute-start | bytes 129032 | tf_op jit(solution)/shard_map/ppermute | solution.py:242
  3.9 6.9 %collective-permute-start.3 = (bf16[1,8,2688]{2,1,0:T(8,128)(2,1)S(1)}, bf16[1,8,2688]{2,1,0:T(8,128)(2,1)S(1)}, u32[]{:S(2)}, u32[]{:S(2)}) collective-permute-start(bf16[1,8,2688]{2,1,0:T(8,128)(2,1)S(1)} %get-tuple-element.23), channel_id=1, source_target_pairs={{0,4},{1,5},{2,6},{3,7},{4,0},{5,1},{6,2},{7,3},{8,12},{9,13},{10,... | collective-permute-start | bytes 129032 | tf_op jit(solution)/shard_map/ppermute | solution.py:242
  6.3 5.0 %collective-permute-start.4 = (bf16[1,8,2688]{2,1,0:T(8,128)(2,1)S(1)}, bf16[1,8,2688]{2,1,0:T(8,128)(2,1)S(1)}, u32[]{:S(2)}, u32[]{:S(2)}) collective-permute-start(bf16[1,8,2688]{2,1,0:T(8,128)(2,1)S(1)} %get-tuple-element.23), channel_id=1, source_target_pairs={{0,5},{1,6},{2,7},{3,0},{4,1},{5,2},{6,3},{7,4},{8,13},{9,14},{10,... | collective-permute-start | bytes 129032 | tf_op jit(solution)/shard_map/ppermute | solution.py:242
  9.7 3.3 %collective-permute-start.5 = (bf16[1,8,2688]{2,1,0:T(8,128)(2,1)S(1)}, bf16[1,8,2688]{2,1,0:T(8,128)(2,1)S(1)}, u32[]{:S(2)}, u32[]{:S(2)}) collective-permute-start(bf16[1,8,2688]{2,1,0:T(8,128)(2,1)S(1)} %get-tuple-element.23), channel_id=1, source_target_pairs={{0,6},{1,7},{2,0},{3,1},{4,2},{5,3},{6,4},{7,5},{8,14},{9,15},{10,... | collective-permute-start | bytes 129032 | tf_op jit(solution)/shard_map/ppermute | solution.py:242
  10.5 3.5 %collective-permute-start.6 = (bf16[1,8,2688]{2,1,0:T(8,128)(2,1)S(1)}, bf16[1,8,2688]{2,1,0:T(8,128)(2,1)S(1)}, u32[]{:S(2)}, u32[]{:S(2)}) collective-permute-start(bf16[1,8,2688]{2,1,0:T(8,128)(2,1)S(1)} %get-tuple-element.23), channel_id=1, source_target_pairs={{0,7},{1,0},{2,1},{3,2},{4,3},{5,4},{6,5},{7,6},{8,15},{9,8},{10,9... | collective-permute-start | bytes 129032 | tf_op jit(solution)/shard_map/ppermute | solution.py:242
  14.4 9.3 %collective-permute-start.7 = (bf16[24,2560]{1,0:T(8,128)(2,1)S(1)}, bf16[24,2560]{1,0:T(8,128)(2,1)S(1)}, u32[]{:S(2)}, u32[]{:S(2)}) collective-permute-start(bf16[24,2560]{1,0:T(8,128)(2,1)S(1)} %convolution_convert_fusion), channel_id=1, source_target_pairs={{0,8},{8,16},{16,24},{24,32},{32,40},{40,48},{48,56},{56,64},{64,7... | collective-permute-start | bytes 368648 | tf_op jit(solution)/shard_map/ppermute | solution.py:20
  31.1 3.2 %copy-start.2 = (f32[384]{0:T(512)S(1)}, f32[384]{0:T(512)}, u32[]{:S(2)}) copy-start(f32[384]{0:T(512)} %param.12) | copy-start | bytes 4612
  34.2 3.2 %copy-start = (bf16[6,4,160,384]{3,2,1,0:T(8,128)(2,1)}, bf16[6,4,160,384]{3,2,1,0:T(8,128)(2,1)S(1)}, u32[]{:S(2)}) copy-start(bf16[6,4,160,384]{3,2,1,0:T(8,128)(2,1)S(1)} %get-tuple-element.30.refs_4_.refs_7_) | copy-start | bytes 8847364
  58.6 8.0 %copy-start.1 = (bf16[1280,384]{1,0:T(8,128)(2,1)S(1)}, bf16[1280,384]{1,0:T(8,128)(2,1)}, u32[]{:S(2)}) copy-start(bf16[1280,384]{1,0:T(8,128)(2,1)} %shard_map.82) | copy-start | bytes 2949124
  60.0 15.5 %collective-permute-start.8 = (bf16[4,1,160,384]{3,2,1,0:T(8,128)(2,1)S(1)}, bf16[4,1,160,384]{3,2,1,0:T(8,128)(2,1)S(1)}, u32[]{:S(2)}, u32[]{:S(2)}) collective-permute-start(bf16[4,1,160,384]{3,2,1,0:T(8,128)(2,1)S(1)} %get-tuple-element.6), channel_id=1, source_target_pairs={{0,1},{1,2},{2,3},{3,4},{4,5},{5,6},{6,7},{8,9},{9,10},{10,11},{11... | collective-permute-start | bytes 1474568 | tf_op jit(solution)/shard_map/ppermute | solution.py:20
  64.6 10.9 %collective-permute-start.9 = (bf16[4,1,160,384]{3,2,1,0:T(8,128)(2,1)S(1)}, bf16[4,1,160,384]{3,2,1,0:T(8,128)(2,1)S(1)}, u32[]{:S(2)}, u32[]{:S(2)}) collective-permute-start(bf16[4,1,160,384]{3,2,1,0:T(8,128)(2,1)S(1)} %get-tuple-element.5), channel_id=1, source_target_pairs={{1,0},{2,1},{3,2},{4,3},{5,4},{6,5},{7,6},{9,8},{10,9},{11,10},{12... | collective-permute-start | bytes 1474568 | tf_op jit(solution)/shard_map/ppermute | solution.py:20
  66.6 27.7 %collective-permute-start.10 = (bf16[2,2,160,384]{3,2,1,0:T(8,128)(2,1)S(1)}, bf16[2,2,160,384]{3,2,1,0:T(8,128)(2,1)S(1)}, u32[]{:S(2)}, u32[]{:S(2)}) collective-permute-start(bf16[2,2,160,384]{3,2,1,0:T(8,128)(2,1)S(1)} %bitcast.37), channel_id=1, source_target_pairs={{0,8},{8,16},{16,24},{24,32},{32,40},{40,48},{48,56},{56,64},{64,7... | collective-permute-start | bytes 1474568 | tf_op jit(solution)/shard_map/ppermute | solution.py:20
  68.6 25.7 %collective-permute-start.11 = (bf16[2,1,160,384]{3,2,1,0:T(8,128)(2,1)S(1)}, bf16[2,1,160,384]{3,2,1,0:T(8,128)(2,1)S(1)}, u32[]{:S(2)}, u32[]{:S(2)}) collective-permute-start(bf16[2,1,160,384]{3,2,1,0:T(8,128)(2,1)S(1)} %get-tuple-element.8), channel_id=1, source_target_pairs={{0,9},{1,10},{2,11},{3,12},{4,13},{5,14},{6,15},{8,17},{9,18},{10,... | collective-permute-start | bytes 737288 | tf_op jit(solution)/shard_map/ppermute | solution.py:31
  73.3 21.0 %collective-permute-start.12 = (bf16[2,1,160,384]{3,2,1,0:T(8,128)(2,1)S(1)}, bf16[2,1,160,384]{3,2,1,0:T(8,128)(2,1)S(1)}, u32[]{:S(2)}, u32[]{:S(2)}) collective-permute-start(bf16[2,1,160,384]{3,2,1,0:T(8,128)(2,1)S(1)} %get-tuple-element.7), channel_id=1, source_target_pairs={{1,8},{2,9},{3,10},{4,11},{5,12},{6,13},{7,14},{9,16},{10,17},{11,... | collective-permute-start | bytes 737288 | tf_op jit(solution)/shard_map/ppermute | solution.py:31
  75.5 0.8 copy-start.4
  75.5 1.0 copy-start.5
  94.3 0.7 copy-start.7
  94.3 0.8 copy-start.8
  95.0 0.8 copy-start.6

commit v7 on v5

--- a/solution.py
+++ b/solution.py
@@ -69,10 +69,14 @@
     return running
 
 
-def conv_kernel(keep_ref, *refs, layout, mode, per_step, firsts):
+def conv_kernel(keep_ref, *refs, layout, mode, per_step, firsts, pre_act):
     sources = refs[: len(layout)]
     w_hbm, side_ref = refs[len(layout) : len(layout) + 2]
-    o_ref, col_ref, w_ref, w_sem = refs[-4:]
+    if pre_act:
+        gain_ref, row_keep_ref = refs[len(layout) + 2 : len(layout) + 4]
+        o_ref, col_ref, w_ref, w_sem, act_ref = refs[-5:]
+    else:
+        o_ref, col_ref, w_ref, w_sem = refs[-4:]
     step = pl.program_id(0)
     steps = pl.num_programs(0)
     columns, channels = sources[0].shape[-2:]
@@ -101,6 +105,25 @@
         for b in (1, 0, 2):
             for j in range(9):
                 weight_copy(j, b).start()
+
+    if pre_act:
+        source = sources[0]
+
+        @pl.when(step == 0)
+        def _():
+            for e in range(source.shape[0]):
+                for i in range(source.shape[1]):
+                    values_f = source[e, i].astype(jnp.float32)
+                    inverse = lax.rsqrt(
+                        jnp.mean(values_f * values_f, axis=-1, keepdims=True) + EPSILON
+                    )
+                    scaled = values_f * inverse * gain_ref[...]
+                    active = scaled / (1.0 + jnp.exp(-scaled))
+                    act_ref[e, i] = jnp.where(
+                        row_keep_ref[i] != 0, active, jnp.zeros_like(active)
+                    ).astype(act_ref.dtype)
+
+        sources = (act_ref,)
 
     def row_of(ext_frame, ext_row):
         for name, (frame_lo, frame_hi, row_lo, row_hi) in layout.items():
@@ -156,7 +179,8 @@
     return pl.BlockSpec(x.shape, lambda step: (0,) * x.ndim)
 
 
-def conv_call(layout, sources, weight, keep, side, mode, per_step=2, firsts=None, into=None):
+def conv_call(layout, sources, weight, keep, side, mode, per_step=2, firsts=None, into=None,
+              pre_gain=None, row_keep=None):
     columns, channels = sources[0].shape[-2:]
     frame_count = keep.shape[0] // 3
     rows_in = max(hi for (_, _, _, hi) in layout.values())
@@ -169,12 +193,21 @@
     block_at = firsts[0] // per_step
     operands = [keep, *sources, weight_rows, side]
     extra_specs, aliases = [], {}
+    pre_act = pre_gain is not None
+    scratch = []
+    if pre_act:
+        extra_specs = [whole(pre_gain), pl.BlockSpec(memory_space=pltpu.SMEM)]
+        operands += [pre_gain, row_keep]
+        scratch = [pltpu.VMEM(sources[0].shape, jnp.bfloat16)]
     if into is not None:
-        extra_specs = [pl.BlockSpec(memory_space=pl.ANY)]
+        extra_specs = extra_specs + [pl.BlockSpec(memory_space=pl.ANY)]
         aliases = {len(operands): 0}
         operands.append(into.reshape(cells, outputs))
     out = pl.pallas_call(
-        functools.partial(conv_kernel, layout=layout, mode=mode, per_step=per_step, firsts=firsts),
+        functools.partial(
+            conv_kernel, layout=layout, mode=mode, per_step=per_step, firsts=firsts,
+            pre_act=pre_act,
+        ),
         out_shape=jax.ShapeDtypeStruct((cells, outputs), jnp.bfloat16),
         in_specs=[pl.BlockSpec(memory_space=pltpu.SMEM)]
         + [whole(x) for x in sources]
@@ -187,7 +220,7 @@
             pltpu.VMEM((per_step * band, 9 * channels), jnp.bfloat16),
             pltpu.VMEM((9 * channels, 3 * outputs), jnp.bfloat16),
             pltpu.SemaphoreType.DMA((3,)),
-        ],
+        ] + scratch,
         cost_estimate=pl.CostEstimate(
             flops=2 * len(firsts) * per_step * band * 27 * channels * outputs,
             transcendentals=len(firsts) * per_step * band * outputs,
@@ -253,20 +286,20 @@
     ).astype(jnp.int32).reshape(-1)
 
     base_ext = local_conv(latent, input_convolution_weight, keep_ext).astype(jnp.bfloat16)
-    first_act = norm_act(base_ext, first_norm_gain)
     ext_rows = band_index * rows_here - 1 + jnp.arange(rows_here + 2, dtype=jnp.int32)
-    row_ok = (ext_rows >= 0) & (ext_rows < height)
-    first_act = jnp.where(row_ok[None, :, None, None], first_act, jnp.zeros((), jnp.bfloat16))
+    row_ok = ((ext_rows >= 0) & (ext_rows < height)).astype(jnp.int32)
 
     gain = second_norm_gain.reshape(1, -1)
-    ext_frames, ext_rows_n = first_act.shape[:2]
+    ext_frames, ext_rows_n = base_ext.shape[:2]
     second_act = conv_call(
         {"x": (0, ext_frames, 0, ext_rows_n)},
-        [first_act],
+        [base_ext],
         first_convolution_weight,
         keep_own,
         gain,
         "act",
+        pre_gain=first_norm_gain.reshape(1, -1),
+        row_keep=row_ok,
     )
 
     last = second_act[frame_count - 2 :]

time: 107 us -> 108 us (level)
  Pallas kernels: 44.7 us -> 47.5 us
  other arithmetic: 5.05 us -> 2.39 us
  waiting for transfers between devices: 13.3 us -> 12 us
    select_n x1 -> x0, other arithmetic: 3.14 us -> none  [on_device(): jnp.where(row_ok[None, :, None, None], first_act, jnp.zeros((), jnp.bfloa...]
    pallas_call x3, Pallas kernels: 44.7 us -> 47.5 us  [conv_call(): pl.pallas_call(functools.partial(conv_kernel, layout=layout, mode=mode, p...]
    ppermute x4, waiting for transfers between devices: 4.53 us -> 3.42 us  [shifted(): return lax.ppermute(x, axis, pairs)]
    unnamed x42 -> x40, local copies, waits for them, and re-layouts: 4.14 us -> 4.1 us
  transfers between devices with their start and end apart: 13 -> 13, of which waited for: 5 -> 5; matrix products, arithmetic and copies ran while one was open for 3% -> 4% of each run, Pallas kernels for 12% -> 12%
where the time goes in v7:
time: 108 us; the launch traced here: 107 us
  Pallas kernels  47.5 us (44%)
  starting transfers between devices  25.8 us (24%)
  local copies, waits for them, and re-layouts  12.6 us (12%)
  waiting for transfers between devices  12 us (11%)
  matrix products  6.66 us (6%)
  other arithmetic  2.39 us (2%)
    pallas_call x3, Pallas kernels, conv_call(): pl.pallas_call(functools.partial(conv_kernel, layout=layout, mode=mode, p...  47.5 us
    ppermute x4, starting transfers between devices, shifted(): return lax.ppermute(x, axis, pairs)  12 us
    ppermute x7, starting transfers between devices, on_device(): pieces.append(lax.ppermute(packed, 'rows', ring))  6.88 us
    ppermute x2, starting transfers between devices, diagonal(): return lax.ppermute(x, ('tm', 'rows'), pairs)  6.85 us
    dot_general x3, matrix products, local_conv(): jnp.dot(stacked, weight[tap_time].reshape(9 * channels, outputs), preferr...  6.42 us
    ppermute x2, waiting for transfers between devices, diagonal(): return lax.ppermute(x, ('tm', 'rows'), pairs)  5.32 us
    unnamed x40, local copies, waits for them, and re-layouts  4.1 us
    ppermute x4, waiting for transfers between devices, shifted(): return lax.ppermute(x, axis, pairs)  3.42 us
  transfers between devices with their start and end apart: 13, of which 5 were waited for; matrix products, arithmetic and copies ran while one was open for 4% of the time, Pallas kernels for 12%

profile of v7, /device:TPU:21, one launch (start us, length us, event | category | flops | bytes accessed | tf_op | source)
XLA Modules:
  0.0 107.4 jit_solution(15093133518616704575)
XLA Ops:
  0.0 0.7 convert_bitcast_fusion
  0.8 0.8 pad_maximum_fusion.1
  1.6 1.5 %collective-permute-start = (bf16[1,8,2688]{2,1,0:T(8,128)(2,1)S(1)}, bf16[1,8,2688]{2,1,0:T(8,128)(2,1)S(1)}, u32[]{:S(2)}, u32[]{:S(2)}) collective-permute-start(bf16[1,8,2688]{2,1,0:T(8,128)(2,1)S(1)} %get-tuple-element.23), channel_id=1, source_target_pairs={{0,1},{1,2},{2,3},{3,4},{4,5},{5,6},{6,7},{7,0},{8,9},{9,10},{10,1... | collective-permute-start | bytes 129032 | tf_op jit(solution)/shard_map/ppermute | solution.py:262
  3.0 0.2 collective-permute-start.1
  3.2 0.7 collective-permute-start.2
  3.9 2.5 %collective-permute-start.3 = (bf16[1,8,2688]{2,1,0:T(8,128)(2,1)S(1)}, bf16[1,8,2688]{2,1,0:T(8,128)(2,1)S(1)}, u32[]{:S(2)}, u32[]{:S(2)}) collective-permute-start(bf16[1,8,2688]{2,1,0:T(8,128)(2,1)S(1)} %get-tuple-element.23), channel_id=1, source_target_pairs={{0,4},{1,5},{2,6},{3,7},{4,0},{5,1},{6,2},{7,3},{8,12},{9,13},{10,... | collective-permute-start | bytes 129032 | tf_op jit(solution)/shard_map/ppermute | solution.py:262
  6.4 1.0 collective-permute-start.4
  7.4 1.0 fusion.8
  8.4 0.7 pad_dynamic-slice_fusion
  9.7 0.9 collective-permute-start.5
  10.6 0.2 collective-permute-start.6
  10.8 0.5 collective-permute-done.4
  11.3 1.7 %collective-permute-done.5 = bf16[1,8,2688]{2,1,0:T(8,128)(2,1)S(1)} collective-permute-done((bf16[1,8,2688]{2,1,0:T(8,128)(2,1)S(1)}, bf16[1,8,2688]{2,1,0:T(8,128)(2,1)S(1)}, u32[]{:S(2)}, u32[]{:S(2)}) %collective-permute-start.5) | collective-permute-done | bytes 43040 | tf_op jit(solution)/shard_map/ppermute | solution.py:262
  13.0 1.0 collective-permute-done.6
  14.1 0.2 convolution_convert_fusion
  14.4 3.5 %collective-permute-start.7 = (bf16[24,2560]{1,0:T(8,128)(2,1)S(1)}, bf16[24,2560]{1,0:T(8,128)(2,1)S(1)}, u32[]{:S(2)}, u32[]{:S(2)}) collective-permute-start(bf16[24,2560]{1,0:T(8,128)(2,1)S(1)} %convolution_convert_fusion), channel_id=1, source_target_pairs={{0,8},{8,16},{16,24},{24,32},{32,40},{40,48},{48,56},{56,64},{64,7... | collective-permute-start | bytes 368648 | tf_op jit(solution)/shard_map/ppermute | solution.py:20
  18.0 0.7 reshape.90.keep_ref
  18.7 0.6 reshape.85.refs_2_
  19.2 0.6 reshape.86.refs_3_
  19.8 0.5 and_convert_fusion.refs_4_
  20.3 3.4 %collective-permute-done.7 = bf16[24,2560]{1,0:T(8,128)(2,1)S(1)} collective-permute-done((bf16[24,2560]{1,0:T(8,128)(2,1)S(1)}, bf16[24,2560]{1,0:T(8,128)(2,1)S(1)}, u32[]{:S(2)}, u32[]{:S(2)}) %collective-permute-start.7) | collective-permute-done | bytes 122912 | tf_op jit(solution)/shard_map/ppermute | solution.py:20
  23.7 1.6 %reshape.83 = bf16[8,6,160,16]{3,2,1,0:T(8,128)(2,1)S(1)} reshape(bf16[48,2560]{1,0:T(8,128)(2,1)S(1)} %pad_maximum_fusion) | data formatting | bytes 491520 | tf_op jit(solution)/shard_map/reshape | solution.py:275
  25.3 1.0 copy.20
  26.3 0.1 slice_dynamic-update-slice_fusion.14
  26.5 0.1 slice_dynamic-update-slice_fusion.13
  26.8 0.1 slice_dynamic-update-slice_fusion.11
  26.9 0.2 slice_dynamic-update-slice_fusion.10
  27.1 0.2 slice_dynamic-update-slice_fusion.9
  27.5 0.1 slice_dynamic-update-slice_fusion.23
  27.8 0.2 slice_dynamic-update-slice_fusion.21
  28.2 0.1 slice_dynamic-update-slice_fusion.17
  28.6 1.3 %fusion.10 = f32[6,4,160,384]{3,2,1,0:T(8,128)S(1)} fusion(bf16[6,4,160,144]{2,3,1,0:T(8,128)(2,1)S(1)} %slice_dynamic-update-slice_fusion.15, bf16[144,384,1,1]{1,0,3,2:T(8,128)(2,1)S(1)} %bitcast.41), kind=kOutput, calls=%fused_computation.62 | convolution fusion | flops 424673280 | bytes 7114752 | tf_op jit(solution)/shard_map/dot_general | solution.py:60
  29.8 1.3 %fusion.9 = f32[6,4,160,384]{3,2,1,0:T(8,128)S(1)} fusion(bf16[6,4,160,144]{2,3,1,0:T(8,128)(2,1)S(1)} %get-tuple-element.16, bf16[144,384,1,1]{1,0,3,2:T(8,128)(2,1)S(1)} %bitcast.40), kind=kOutput, calls=%fused_computation.61 | convolution fusion | flops 424673280 | bytes 7114752 | tf_op jit(solution)/shard_map/dot_general | solution.py:60
  31.1 3.9 %add_convert_fusion.refs_0_.refs_4_.refs_7_ = bf16[6,4,160,384]{3,2,1,0:T(8,128)(2,1)} fusion(f32[6,4,160,384]{3,2,1,0:T(8,128)S(1)} %fusion.10, f32[6,4,160,384]{3,2,1,0:T(8,128)S(1)} %fusion.9, pred[6]{0:T(512)(128)(4,1)S(1)} %get-tuple-element.26, pred[6]{0:T(512)(128)(4,1)S(1)} %get-tuple-element.25, bf16[6,4,160,144]{2,3,1,0:T(8,128)(2,1)S(1)} %get-tuple-element.9, ...), kind=kOutput, calls=%fused_computation | convolution fusion | flops 432046080 | bytes 15962124 | tf_op jit(solution)/shard_map/dot_general | solution.py:60
  35.0 22.1 %shard_map.82 = bf16[1280,384]{1,0:T(8,128)(2,1)} custom-call(s32[12]{0:T(128)} %reshape.90.keep_ref, bf16[6,4,160,384]{3,2,1,0:T(8,128)(2,1)} %add_convert_fusion.refs_0_.refs_4_.refs_7_, bf16[10368,384]{1,0:T(8,128)(2,1)} %bitcast.44, f32[1,384]{1,0:T(1,128)} %reshape.85.refs_2_, f32[1,384]{1,0:T(1,128)} %reshape.86.refs_3_, s32[4]{0:T(128)} %and_convert_fusion.refs_4_), custom_call_target="tpu_custom_call" | custom-call | flops 10192158720 | bytes 10911744 | tf_op jit(solution)/shard_map/pallas_call | solution.py:206
  57.2 1.4 %fusion.6 = (bf16[4,1,160,384]{3,2,1,0:T(8,128)(2,1)S(1)}, bf16[4,1,160,384]{3,2,1,0:T(8,128)(2,1)S(1)}) fusion(bf16[4,2,160,384]{3,2,1,0:T(8,128)(2,1)} %bitcast.34), kind=kLoop, calls=%fused_computation.58 | loop fusion | bytes 1966080 | tf_op jit(solution)/shard_map/slice | solution.py:307
  58.5 4.6 %collective-permute-start.8 = (bf16[4,1,160,384]{3,2,1,0:T(8,128)(2,1)S(1)}, bf16[4,1,160,384]{3,2,1,0:T(8,128)(2,1)S(1)}, u32[]{:S(2)}, u32[]{:S(2)}) collective-permute-start(bf16[4,1,160,384]{3,2,1,0:T(8,128)(2,1)S(1)} %get-tuple-element.6), channel_id=1, source_target_pairs={{0,1},{1,2},{2,3},{3,4},{4,5},{5,6},{6,7},{8,9},{9,10},{10,11},{11... | collective-permute-start | bytes 1474568 | tf_op jit(solution)/shard_map/ppermute | solution.py:20
  63.2 1.9 %collective-permute-start.9 = (bf16[4,1,160,384]{3,2,1,0:T(8,128)(2,1)S(1)}, bf16[4,1,160,384]{3,2,1,0:T(8,128)(2,1)S(1)}, u32[]{:S(2)}, u32[]{:S(2)}) collective-permute-start(bf16[4,1,160,384]{3,2,1,0:T(8,128)(2,1)S(1)} %get-tuple-element.5), channel_id=1, source_target_pairs={{1,0},{2,1},{3,2},{4,3},{5,4},{6,5},{7,6},{9,8},{10,9},{11,10},{12... | collective-permute-start | bytes 1474568 | tf_op jit(solution)/shard_map/ppermute | solution.py:20
  65.2 1.9 %collective-permute-start.10 = (bf16[2,2,160,384]{3,2,1,0:T(8,128)(2,1)S(1)}, bf16[2,2,160,384]{3,2,1,0:T(8,128)(2,1)S(1)}, u32[]{:S(2)}, u32[]{:S(2)}) collective-permute-start(bf16[2,2,160,384]{3,2,1,0:T(8,128)(2,1)S(1)} %bitcast.37), channel_id=1, source_target_pairs={{0,8},{8,16},{16,24},{24,32},{32,40},{40,48},{48,56},{56,64},{64,7... | collective-permute-start | bytes 1474568 | tf_op jit(solution)/shard_map/ppermute | solution.py:20
  67.2 4.7 %collective-permute-start.11 = (bf16[2,1,160,384]{3,2,1,0:T(8,128)(2,1)S(1)}, bf16[2,1,160,384]{3,2,1,0:T(8,128)(2,1)S(1)}, u32[]{:S(2)}, u32[]{:S(2)}) collective-permute-start(bf16[2,1,160,384]{3,2,1,0:T(8,128)(2,1)S(1)} %get-tuple-element.8), channel_id=1, source_target_pairs={{0,9},{1,10},{2,11},{3,12},{4,13},{5,14},{6,15},{8,17},{9,18},{10,... | collective-permute-start | bytes 737288 | tf_op jit(solution)/shard_map/ppermute | solution.py:31
  71.9 2.1 %collective-permute-start.12 = (bf16[2,1,160,384]{3,2,1,0:T(8,128)(2,1)S(1)}, bf16[2,1,160,384]{3,2,1,0:T(8,128)(2,1)S(1)}, u32[]{:S(2)}, u32[]{:S(2)}) collective-permute-start(bf16[2,1,160,384]{3,2,1,0:T(8,128)(2,1)S(1)} %get-tuple-element.7), channel_id=1, source_target_pairs={{1,8},{2,9},{3,10},{4,11},{5,12},{6,13},{7,14},{9,16},{10,17},{11,... | collective-permute-start | bytes 737288 | tf_op jit(solution)/shard_map/ppermute | solution.py:31
  74.1 0.8 copy-done.3
  74.8 0.2 copy-done.4
  75.0 12.5 %shard_map.83.refs_8_ = bf16[1280,384]{1,0:T(8,128)(2,1)} custom-call(s32[12]{0:T(128)} %reshape.90.keep_ref, bf16[4,2,160,384]{3,2,1,0:T(8,128)(2,1)} %bitcast.35, bf16[4,1,160,384]{3,2,1,0:T(8,128)(2,1)} %copy-done.3, bf16[4,1,160,384]{3,2,1,0:T(8,128)(2,1)} %copy-done.4, bf16[10368,384]{1,0:T(8,128)(2,1)} %bitcast.45, ...), custom_call_target="tpu_custom_call" | custom-call | flops 5096079360 | bytes 9437184 | tf_op jit(solution)/shard_map/pallas_call | solution.py:206
  87.5 5.3 %collective-permute-done.11.refs_4_ = bf16[2,1,160,384]{3,2,1,0:T(8,128)(2,1)S(1)} collective-permute-done((bf16[2,1,160,384]{3,2,1,0:T(8,128)(2,1)S(1)}, bf16[2,1,160,384]{3,2,1,0:T(8,128)(2,1)S(1)}, u32[]{:S(2)}, u32[]{:S(2)}) %collective-permute-start.11) | collective-permute-done | bytes 245792 | tf_op jit(solution)/shard_map/ppermute | solution.py:31
  92.9 0.7 copy-done.6
  93.6 0.8 copy-done.5
  94.4 12.8 %shard_map.84 = bf16[1280,384]{1,0:T(8,128)(2,1)} custom-call(s32[12]{0:T(128)} %reshape.90.keep_ref, bf16[4,2,160,384]{3,2,1,0:T(8,128)(2,1)} %bitcast.36, bf16[4,1,160,384]{3,2,1,0:T(8,128)(2,1)} %copy-done.3, bf16[4,1,160,384]{3,2,1,0:T(8,128)(2,1)} %copy-done.4, bf16[2,2,160,384]{3,2,1,0:T(8,128)(2,1)} %copy-done.5, ...), custom_call_target="tpu_custom_call", output_to_operand_aliasing={{}: (9, {})} | custom-call | flops 5096079360 | bytes 9437184 | tf_op jit(solution)/shard_map/pallas_call | solution.py:206
  (56 shorter events, 1.9 us)
Async XLA Ops:
  0.0 18.7 %copy-start.1 = (f32[384]{0:T(512)S(1)}, f32[384]{0:T(512)}, u32[]{:S(2)}) copy-start(f32[384]{0:T(512)} %param.14) | copy-start | bytes 4612
  0.0 19.2 %copy-start.2 = (f32[384]{0:T(512)S(1)}, f32[384]{0:T(512)}, u32[]{:S(2)}) copy-start(f32[384]{0:T(512)} %param.12) | copy-start | bytes 4612
  1.6 8.1 %collective-permute-start = (bf16[1,8,2688]{2,1,0:T(8,128)(2,1)S(1)}, bf16[1,8,2688]{2,1,0:T(8,128)(2,1)S(1)}, u32[]{:S(2)}, u32[]{:S(2)}) collective-permute-start(bf16[1,8,2688]{2,1,0:T(8,128)(2,1)S(1)} %get-tuple-element.23), channel_id=1, source_target_pairs={{0,1},{1,2},{2,3},{3,4},{4,5},{5,6},{6,7},{7,0},{8,9},{9,10},{10,1... | collective-permute-start | bytes 129032 | tf_op jit(solution)/shard_map/ppermute | solution.py:262
  3.0 7.5 %collective-permute-start.1 = (bf16[1,8,2688]{2,1,0:T(8,128)(2,1)S(1)}, bf16[1,8,2688]{2,1,0:T(8,128)(2,1)S(1)}, u32[]{:S(2)}, u32[]{:S(2)}) collective-permute-start(bf16[1,8,2688]{2,1,0:T(8,128)(2,1)S(1)} %get-tuple-element.23), channel_id=1, source_target_pairs={{0,2},{1,3},{2,4},{3,5},{4,6},{5,7},{6,0},{7,1},{8,10},{9,11},{10,... | collective-permute-start | bytes 129032 | tf_op jit(solution)/shard_map/ppermute | solution.py:262
  3.2 7.5 %collective-permute-start.2 = (bf16[1,8,2688]{2,1,0:T(8,128)(2,1)S(1)}, bf16[1,8,2688]{2,1,0:T(8,128)(2,1)S(1)}, u32[]{:S(2)}, u32[]{:S(2)}) collective-permute-start(bf16[1,8,2688]{2,1,0:T(8,128)(2,1)S(1)} %get-tuple-element.23), channel_id=1, source_target_pairs={{0,3},{1,4},{2,5},{3,6},{4,7},{5,0},{6,1},{7,2},{8,11},{9,12},{10,... | collective-permute-start | bytes 129032 | tf_op jit(solution)/shard_map/ppermute | solution.py:262
  3.9 6.9 %collective-permute-start.3 = (bf16[1,8,2688]{2,1,0:T(8,128)(2,1)S(1)}, bf16[1,8,2688]{2,1,0:T(8,128)(2,1)S(1)}, u32[]{:S(2)}, u32[]{:S(2)}) collective-permute-start(bf16[1,8,2688]{2,1,0:T(8,128)(2,1)S(1)} %get-tuple-element.23), channel_id=1, source_target_pairs={{0,4},{1,5},{2,6},{3,7},{4,0},{5,1},{6,2},{7,3},{8,12},{9,13},{10,... | collective-permute-start | bytes 129032 | tf_op jit(solution)/shard_map/ppermute | solution.py:262
  6.4 5.0 %collective-permute-start.4 = (bf16[1,8,2688]{2,1,0:T(8,128)(2,1)S(1)}, bf16[1,8,2688]{2,1,0:T(8,128)(2,1)S(1)}, u32[]{:S(2)}, u32[]{:S(2)}) collective-permute-start(bf16[1,8,2688]{2,1,0:T(8,128)(2,1)S(1)} %get-tuple-element.23), channel_id=1, source_target_pairs={{0,5},{1,6},{2,7},{3,0},{4,1},{5,2},{6,3},{7,4},{8,13},{9,14},{10,... | collective-permute-start | bytes 129032 | tf_op jit(solution)/shard_map/ppermute | solution.py:262
  9.7 3.3 %collective-permute-start.5 = (bf16[1,8,2688]{2,1,0:T(8,128)(2,1)S(1)}, bf16[1,8,2688]{2,1,0:T(8,128)(2,1)S(1)}, u32[]{:S(2)}, u32[]{:S(2)}) collective-permute-start(bf16[1,8,2688]{2,1,0:T(8,128)(2,1)S(1)} %get-tuple-element.23), channel_id=1, source_target_pairs={{0,6},{1,7},{2,0},{3,1},{4,2},{5,3},{6,4},{7,5},{8,14},{9,15},{10,... | collective-permute-start | bytes 129032 | tf_op jit(solution)/shard_map/ppermute | solution.py:262
  10.6 3.5 %collective-permute-start.6 = (bf16[1,8,2688]{2,1,0:T(8,128)(2,1)S(1)}, bf16[1,8,2688]{2,1,0:T(8,128)(2,1)S(1)}, u32[]{:S(2)}, u32[]{:S(2)}) collective-permute-start(bf16[1,8,2688]{2,1,0:T(8,128)(2,1)S(1)} %get-tuple-element.23), channel_id=1, source_target_pairs={{0,7},{1,0},{2,1},{3,2},{4,3},{5,4},{6,5},{7,6},{8,15},{9,8},{10,9... | collective-permute-start | bytes 129032 | tf_op jit(solution)/shard_map/ppermute | solution.py:262
  14.4 9.3 %collective-permute-start.7 = (bf16[24,2560]{1,0:T(8,128)(2,1)S(1)}, bf16[24,2560]{1,0:T(8,128)(2,1)S(1)}, u32[]{:S(2)}, u32[]{:S(2)}) collective-permute-start(bf16[24,2560]{1,0:T(8,128)(2,1)S(1)} %convolution_convert_fusion), channel_id=1, source_target_pairs={{0,8},{8,16},{16,24},{24,32},{32,40},{40,48},{48,56},{56,64},{64,7... | collective-permute-start | bytes 368648 | tf_op jit(solution)/shard_map/ppermute | solution.py:20
  57.1 8.0 %copy-start = (bf16[1280,384]{1,0:T(8,128)(2,1)S(1)}, bf16[1280,384]{1,0:T(8,128)(2,1)}, u32[]{:S(2)}) copy-start(bf16[1280,384]{1,0:T(8,128)(2,1)} %shard_map.82) | copy-start | bytes 2949124
  58.5 15.5 %collective-permute-start.8 = (bf16[4,1,160,384]{3,2,1,0:T(8,128)(2,1)S(1)}, bf16[4,1,160,384]{3,2,1,0:T(8,128)(2,1)S(1)}, u32[]{:S(2)}, u32[]{:S(2)}) collective-permute-start(bf16[4,1,160,384]{3,2,1,0:T(8,128)(2,1)S(1)} %get-tuple-element.6), channel_id=1, source_target_pairs={{0,1},{1,2},{2,3},{3,4},{4,5},{5,6},{6,7},{8,9},{9,10},{10,11},{11... | collective-permute-start | bytes 1474568 | tf_op jit(solution)/shard_map/ppermute | solution.py:20
  63.2 10.9 %collective-permute-start.9 = (bf16[4,1,160,384]{3,2,1,0:T(8,128)(2,1)S(1)}, bf16[4,1,160,384]{3,2,1,0:T(8,128)(2,1)S(1)}, u32[]{:S(2)}, u32[]{:S(2)}) collective-permute-start(bf16[4,1,160,384]{3,2,1,0:T(8,128)(2,1)S(1)} %get-tuple-element.5), channel_id=1, source_target_pairs={{1,0},{2,1},{3,2},{4,3},{5,4},{6,5},{7,6},{9,8},{10,9},{11,10},{12... | collective-permute-start | bytes 1474568 | tf_op jit(solution)/shard_map/ppermute | solution.py:20
  65.2 27.7 %collective-permute-start.10 = (bf16[2,2,160,384]{3,2,1,0:T(8,128)(2,1)S(1)}, bf16[2,2,160,384]{3,2,1,0:T(8,128)(2,1)S(1)}, u32[]{:S(2)}, u32[]{:S(2)}) collective-permute-start(bf16[2,2,160,384]{3,2,1,0:T(8,128)(2,1)S(1)} %bitcast.37), channel_id=1, source_target_pairs={{0,8},{8,16},{16,24},{24,32},{32,40},{40,48},{48,56},{56,64},{64,7... | collective-permute-start | bytes 1474568 | tf_op jit(solution)/shard_map/ppermute | solution.py:20
  67.2 25.7 %collective-permute-start.11 = (bf16[2,1,160,384]{3,2,1,0:T(8,128)(2,1)S(1)}, bf16[2,1,160,384]{3,2,1,0:T(8,128)(2,1)S(1)}, u32[]{:S(2)}, u32[]{:S(2)}) collective-permute-start(bf16[2,1,160,384]{3,2,1,0:T(8,128)(2,1)S(1)} %get-tuple-element.8), channel_id=1, source_target_pairs={{0,9},{1,10},{2,11},{3,12},{4,13},{5,14},{6,15},{8,17},{9,18},{10,... | collective-permute-start | bytes 737288 | tf_op jit(solution)/shard_map/ppermute | solution.py:31
  71.9 21.0 %collective-permute-start.12 = (bf16[2,1,160,384]{3,2,1,0:T(8,128)(2,1)S(1)}, bf16[2,1,160,384]{3,2,1,0:T(8,128)(2,1)S(1)}, u32[]{:S(2)}, u32[]{:S(2)}) collective-permute-start(bf16[2,1,160,384]{3,2,1,0:T(8,128)(2,1)S(1)} %get-tuple-element.7), channel_id=1, source_target_pairs={{1,8},{2,9},{3,10},{4,11},{5,12},{6,13},{7,14},{9,16},{10,17},{11,... | collective-permute-start | bytes 737288 | tf_op jit(solution)/shard_map/ppermute | solution.py:31
  74.0 0.8 copy-start.3
  74.1 0.9 copy-start.4
  92.8 0.7 copy-start.6
  92.9 0.8 copy-start.7
  93.6 0.8 copy-start.5

commit v8 on v5

--- a/solution.py
+++ b/solution.py
@@ -222,12 +222,7 @@
         slot_group_row.astype(jnp.bfloat16)[:, :, None], (1, slots_here, ID_LANES)
     )
     packed = jnp.concatenate([generator_latent_rows, ids], axis=-1)
-    parts_total = lax.axis_size("rows")
-    pieces = [packed]
-    for by in range(1, parts_total):
-        ring = [(i, (i + by) % parts_total) for i in range(parts_total)]
-        pieces.append(lax.ppermute(packed, "rows", ring))
-    gathered = jnp.concatenate(pieces, axis=1)[0]
+    gathered = lax.all_gather(packed, "rows", axis=1, tiled=True)[0]
     values = gathered[:, :packed_rows]
     slot_ids = gathered[:, packed_rows].astype(jnp.int32)
 

time: 107 us -> 107 us (level)
  blocking collectives: 0 us -> 12.2 us
  waiting for transfers between devices: 13.3 us -> 6.71 us
  starting transfers between devices: 25.5 us -> 19 us
    all_gather x0 -> x1, blocking collectives: none -> 12.2 us  [on_device(): gathered = lax.all_gather(packed, 'rows', axis=1, tiled=True)[0]]
    ppermute x7 -> x0, starting transfers between devices: 6.88 us -> none  [on_device(): pieces.append(lax.ppermute(packed, 'rows', ring))]
    ppermute x7 -> x0, waiting for transfers between devices: 3.23 us -> none  [on_device(): pieces.append(lax.ppermute(packed, 'rows', ring))]
    ppermute x4, waiting for transfers between devices: 4.53 us -> 1.48 us  [shifted(): return lax.ppermute(x, axis, pairs)]
    unnamed x42 -> x34, local copies, waits for them, and re-layouts: 4.14 us -> 4.09 us
  transfers between devices with their start and end apart: 13 -> 6, of which waited for: 5 -> 2; matrix products, arithmetic and copies ran while one was open for 3% -> 4% of each run, Pallas kernels for 12% -> 12%
where the time goes in v8:
time: 107 us
  Pallas kernels  44.7 us (42%)
  starting transfers between devices  19 us (18%)
  local copies, waits for them, and re-layouts  12.6 us (12%)
  blocking collectives  12.2 us (11%)
  waiting for transfers between devices  6.71 us (6%)
  matrix products  5.88 us (5%)
  other arithmetic  5.1 us (5%)
    pallas_call x3, Pallas kernels, conv_call(): pl.pallas_call(functools.partial(conv_kernel, layout=layout, mode=mode, p...  44.7 us
    all_gather x1, blocking collectives, on_device(): gathered = lax.all_gather(packed, 'rows', axis=1, tiled=True)[0]  12.2 us
    ppermute x4, starting transfers between devices, shifted(): return lax.ppermute(x, axis, pairs)  12.2 us
    ppermute x2, starting transfers between devices, diagonal(): return lax.ppermute(x, ('tm', 'rows'), pairs)  6.85 us
    dot_general x3, matrix products, local_conv(): jnp.dot(stacked, weight[tap_time].reshape(9 * channels, outputs), preferr...  5.65 us
    ppermute x2, waiting for transfers between devices, diagonal(): return lax.ppermute(x, ('tm', 'rows'), pairs)  5.23 us
    unnamed x34, local copies, waits for them, and re-layouts  4.09 us
    select_n x1, other arithmetic, on_device(): jnp.where(row_ok[None, :, None, None], first_act, jnp.zeros((), jnp.bfloa...  3.19 us
  transfers between devices with their start and end apart: 6, of which 2 were waited for; matrix products, arithmetic and copies ran while one was open for 4% of the time, Pallas kernels for 12%

profile of v8, /device:TPU:21, one launch (start us, length us, event | category | flops | bytes accessed | tf_op | source)
XLA Modules:
  0.0 106.8 jit_solution(8489016194241385448)
XLA Ops:
  0.1 0.1 add.82
  0.2 0.1 and.29
  0.3 0.7 convert_bitcast_fusion
  1.0 0.8 pad_maximum_fusion.1
  1.8 12.2 %all_gather.3 = bf16[1,64,2688]{2,1,0:T(8,128)(2,1)S(1)} all-gather(bf16[1,8,2688]{2,1,0:T(8,128)(2,1)S(1)} %pad_maximum_fusion.1), channel_id=1, replica_groups=mesh['tm'=16,'rows'=8] {'rows'}, dimensions={1}, use_global_device_ids=true | all-gather | bytes 387072 | tf_op jit(solution)/shard_map/all_gather | solution.py:225
  14.0 0.1 convert_reduce_fusion
  14.1 0.2 convolution_convert_fusion
  14.4 3.5 %collective-permute-start = (bf16[24,2560]{1,0:T(8,128)(2,1)S(1)}, bf16[24,2560]{1,0:T(8,128)(2,1)S(1)}, u32[]{:S(2)}, u32[]{:S(2)}) collective-permute-start(bf16[24,2560]{1,0:T(8,128)(2,1)S(1)} %convolution_convert_fusion), channel_id=1, source_target_pairs={{0,8},{8,16},{16,24},{24,32},{32,40},{40,48},{48,56},{56,64},{64,7... | collective-permute-start | bytes 368648 | tf_op jit(solution)/shard_map/ppermute | solution.py:20
  17.9 1.0 fusion.17
  19.0 0.7 pad_dynamic-slice_fusion
  20.0 0.6 reshape.102.keep_ref
  20.6 1.2 %reshape.98.refs_2_ = f32[1,384]{1,0:T(1,128)} reshape(f32[384]{0:T(512)} %param.14) | data formatting | bytes 3072 | tf_op jit(solution)/shard_map/reshape | solution.py:256
  21.8 1.5 %collective-permute-done = bf16[24,2560]{1,0:T(8,128)(2,1)S(1)} collective-permute-done((bf16[24,2560]{1,0:T(8,128)(2,1)S(1)}, bf16[24,2560]{1,0:T(8,128)(2,1)S(1)}, u32[]{:S(2)}, u32[]{:S(2)}) %collective-permute-start) | collective-permute-done | bytes 122912 | tf_op jit(solution)/shard_map/ppermute | solution.py:20
  23.3 1.6 %reshape.96 = bf16[8,6,160,16]{3,2,1,0:T(8,128)(2,1)S(1)} reshape(bf16[48,2560]{1,0:T(8,128)(2,1)S(1)} %pad_maximum_fusion) | data formatting | bytes 491520 | tf_op jit(solution)/shard_map/reshape | solution.py:237
  24.9 1.0 copy.20
  25.9 0.1 slice_dynamic-update-slice_fusion.14
  26.1 0.1 slice_dynamic-update-slice_fusion.13
  26.2 0.1 slice_dynamic-update-slice_fusion.12
  26.4 0.1 slice_dynamic-update-slice_fusion.11
  26.5 0.2 slice_dynamic-update-slice_fusion.10
  26.7 0.2 slice_dynamic-update-slice_fusion.9
  27.0 0.1 slice_dynamic-update-slice_fusion.24
  27.1 0.1 slice_dynamic-update-slice_fusion.23
  27.2 0.1 slice_dynamic-update-slice_fusion.22
  27.4 0.2 slice_dynamic-update-slice_fusion.21
  27.6 0.1 slice_dynamic-update-slice_fusion.18
  27.7 0.1 slice_dynamic-update-slice_fusion.17
  27.9 0.1 slice_dynamic-update-slice_fusion.16
  28.0 0.1 slice_dynamic-update-slice_fusion.15
  28.2 1.3 %fusion.19 = f32[6,4,160,384]{3,2,1,0:T(8,128)S(1)} fusion(bf16[6,4,160,144]{2,3,1,0:T(8,128)(2,1)S(1)} %slice_dynamic-update-slice_fusion.15, bf16[144,384,1,1]{1,0,3,2:T(8,128)(2,1)S(1)} %bitcast.43), kind=kOutput, calls=%fused_computation.66 | convolution fusion | flops 424673280 | bytes 7114752 | tf_op jit(solution)/shard_map/dot_general | solution.py:60
  29.4 1.3 %fusion.18 = f32[6,4,160,384]{3,2,1,0:T(8,128)S(1)} fusion(bf16[6,4,160,144]{2,3,1,0:T(8,128)(2,1)S(1)} %get-tuple-element.16, bf16[144,384,1,1]{1,0,3,2:T(8,128)(2,1)S(1)} %bitcast.42), kind=kOutput, calls=%fused_computation.65 | convolution fusion | flops 424673280 | bytes 7114752 | tf_op jit(solution)/shard_map/dot_general | solution.py:60
  30.7 3.1 %fusion = (f32[6,4,160]{2,1,0:T(4,128)S(1)}, bf16[6,4,160,384]{3,2,1,0:T(8,128)(2,1)S(1)}) fusion(bf16[6,4,160,144]{2,3,1,0:T(8,128)(2,1)S(1)} %get-tuple-element.9, bf16[144,384,1,1]{1,0,3,2:T(8,128)(2,1)S(1)} %bitcast.41, f32[6,4,160,384]{3,2,1,0:T(8,128)S(1)} %fusion.19, pred[6]{0:T(512)(128)(4,1)S(1)} %get-tuple-element.24, ...), kind=kOutput, calls=%fused_computation.2 | convolution fusion | flops 436465920 | bytes 15977484 | tf_op jit(solution)/shard_map/dot_general | solution.py:60
  33.9 3.2 %fusion.8.refs_0_ = bf16[6,4,160,384]{3,2,1,0:T(8,128)(2,1)} fusion(bf16[6,4,160,384]{3,2,1,0:T(8,128)(2,1)S(1)} %get-tuple-element.28.refs_4_.refs_7_, f32[384]{0:T(512)S(1)} %copy-done.2, f32[6,4,160]{2,1,0:T(4,128)S(1)} %add_rsqrt_fusion, pred[4]{0:T(512)(128)(4,1)S(1)} %compare_and_fusion.1), kind=kLoop, calls=%fused_computation.12 | loop fusion | flops 13271040 | bytes 5915140 | tf_op jit(solution)/shard_map/jit(_where)/select_n | solution.py:254
  37.1 19.3 %shard_map.82 = bf16[1280,384]{1,0:T(8,128)(2,1)} custom-call(s32[12]{0:T(128)} %reshape.102.keep_ref, bf16[6,4,160,384]{3,2,1,0:T(8,128)(2,1)} %fusion.8.refs_0_, bf16[10368,384]{1,0:T(8,128)(2,1)} %bitcast.44, f32[1,384]{1,0:T(1,128)} %reshape.98.refs_2_), custom_call_target="tpu_custom_call" | custom-call | flops 10192158720 | bytes 10911744 | tf_op jit(solution)/shard_map/pallas_call | solution.py:176
  56.4 1.4 %fusion.15 = (bf16[4,1,160,384]{3,2,1,0:T(8,128)(2,1)S(1)}, bf16[4,1,160,384]{3,2,1,0:T(8,128)(2,1)S(1)}) fusion(bf16[4,2,160,384]{3,2,1,0:T(8,128)(2,1)} %bitcast.34), kind=kLoop, calls=%fused_computation.62 | loop fusion | bytes 1966080 | tf_op jit(solution)/shard_map/slice | solution.py:269
  57.7 4.8 %collective-permute-start.1 = (bf16[4,1,160,384]{3,2,1,0:T(8,128)(2,1)S(1)}, bf16[4,1,160,384]{3,2,1,0:T(8,128)(2,1)S(1)}, u32[]{:S(2)}, u32[]{:S(2)}) collective-permute-start(bf16[4,1,160,384]{3,2,1,0:T(8,128)(2,1)S(1)} %get-tuple-element.6), channel_id=1, source_target_pairs={{0,1},{1,2},{2,3},{3,4},{4,5},{5,6},{6,7},{8,9},{9,10},{10,11},{11... | collective-permute-start | bytes 1474568 | tf_op jit(solution)/shard_map/ppermute | solution.py:20
  62.5 1.9 %collective-permute-start.2 = (bf16[4,1,160,384]{3,2,1,0:T(8,128)(2,1)S(1)}, bf16[4,1,160,384]{3,2,1,0:T(8,128)(2,1)S(1)}, u32[]{:S(2)}, u32[]{:S(2)}) collective-permute-start(bf16[4,1,160,384]{3,2,1,0:T(8,128)(2,1)S(1)} %get-tuple-element.5), channel_id=1, source_target_pairs={{1,0},{2,1},{3,2},{4,3},{5,4},{6,5},{7,6},{9,8},{10,9},{11,10},{12... | collective-permute-start | bytes 1474568 | tf_op jit(solution)/shard_map/ppermute | solution.py:20
  64.5 1.9 %collective-permute-start.3 = (bf16[2,2,160,384]{3,2,1,0:T(8,128)(2,1)S(1)}, bf16[2,2,160,384]{3,2,1,0:T(8,128)(2,1)S(1)}, u32[]{:S(2)}, u32[]{:S(2)}) collective-permute-start(bf16[2,2,160,384]{3,2,1,0:T(8,128)(2,1)S(1)} %bitcast.37), channel_id=1, source_target_pairs={{0,8},{8,16},{16,24},{24,32},{32,40},{40,48},{48,56},{56,64},{64,7... | collective-permute-start | bytes 1474568 | tf_op jit(solution)/shard_map/ppermute | solution.py:20
  66.5 4.7 %collective-permute-start.4 = (bf16[2,1,160,384]{3,2,1,0:T(8,128)(2,1)S(1)}, bf16[2,1,160,384]{3,2,1,0:T(8,128)(2,1)S(1)}, u32[]{:S(2)}, u32[]{:S(2)}) collective-permute-start(bf16[2,1,160,384]{3,2,1,0:T(8,128)(2,1)S(1)} %get-tuple-element.8), channel_id=1, source_target_pairs={{0,9},{1,10},{2,11},{3,12},{4,13},{5,14},{6,15},{8,17},{9,18},{10,... | collective-permute-start | bytes 737288 | tf_op jit(solution)/shard_map/ppermute | solution.py:31
  71.2 2.1 %collective-permute-start.5 = (bf16[2,1,160,384]{3,2,1,0:T(8,128)(2,1)S(1)}, bf16[2,1,160,384]{3,2,1,0:T(8,128)(2,1)S(1)}, u32[]{:S(2)}, u32[]{:S(2)}) collective-permute-start(bf16[2,1,160,384]{3,2,1,0:T(8,128)(2,1)S(1)} %get-tuple-element.7), channel_id=1, source_target_pairs={{1,8},{2,9},{3,10},{4,11},{5,12},{6,13},{7,14},{9,16},{10,17},{11,... | collective-permute-start | bytes 737288 | tf_op jit(solution)/shard_map/ppermute | solution.py:31
  73.4 0.8 copy-done.3
  74.2 0.2 copy-done.4
  74.4 12.5 %shard_map.83.refs_8_ = bf16[1280,384]{1,0:T(8,128)(2,1)} custom-call(s32[12]{0:T(128)} %reshape.102.keep_ref, bf16[4,2,160,384]{3,2,1,0:T(8,128)(2,1)} %bitcast.35, bf16[4,1,160,384]{3,2,1,0:T(8,128)(2,1)} %copy-done.3, bf16[4,1,160,384]{3,2,1,0:T(8,128)(2,1)} %copy-done.4, bf16[10368,384]{1,0:T(8,128)(2,1)} %bitcast.45, bf16[6,4,160,384]{3,2,1,0:T(8,128)(2,1)} %copy-done), custom_call_target="tpu_custom_call" | custom-call | flops 5096079360 | bytes 9437184 | tf_op jit(solution)/shard_map/pallas_call | solution.py:176
  86.9 5.2 %collective-permute-done.4.refs_4_ = bf16[2,1,160,384]{3,2,1,0:T(8,128)(2,1)S(1)} collective-permute-done((bf16[2,1,160,384]{3,2,1,0:T(8,128)(2,1)S(1)}, bf16[2,1,160,384]{3,2,1,0:T(8,128)(2,1)S(1)}, u32[]{:S(2)}, u32[]{:S(2)}) %collective-permute-start.4) | collective-permute-done | bytes 245792 | tf_op jit(solution)/shard_map/ppermute | solution.py:31
  92.2 0.7 copy-done.6
  92.8 0.1 copy-done.7
  92.9 0.8 copy-done.5
  93.7 12.8 %shard_map.84 = bf16[1280,384]{1,0:T(8,128)(2,1)} custom-call(s32[12]{0:T(128)} %reshape.102.keep_ref, bf16[4,2,160,384]{3,2,1,0:T(8,128)(2,1)} %bitcast.36, bf16[4,1,160,384]{3,2,1,0:T(8,128)(2,1)} %copy-done.3, bf16[4,1,160,384]{3,2,1,0:T(8,128)(2,1)} %copy-done.4, bf16[2,2,160,384]{3,2,1,0:T(8,128)(2,1)} %copy-done.5, ...), custom_call_target="tpu_custom_call", output_to_operand_aliasing={{}: (9, {})} | custom-call | flops 5096079360 | bytes 9437184 | tf_op jit(solution)/shard_map/pallas_call | solution.py:176
  (37 shorter events, 0.8 us)
Async XLA Ops:
  14.4 8.9 %collective-permute-start = (bf16[24,2560]{1,0:T(8,128)(2,1)S(1)}, bf16[24,2560]{1,0:T(8,128)(2,1)S(1)}, u32[]{:S(2)}, u32[]{:S(2)}) collective-permute-start(bf16[24,2560]{1,0:T(8,128)(2,1)S(1)} %convolution_convert_fusion), channel_id=1, source_target_pairs={{0,8},{8,16},{16,24},{24,32},{32,40},{40,48},{48,56},{56,64},{64,7... | collective-permute-start | bytes 368648 | tf_op jit(solution)/shard_map/ppermute | solution.py:20
  30.7 3.2 %copy-start.2 = (f32[384]{0:T(512)S(1)}, f32[384]{0:T(512)}, u32[]{:S(2)}) copy-start(f32[384]{0:T(512)} %param.12) | copy-start | bytes 4612
  33.8 3.2 %copy-start = (bf16[6,4,160,384]{3,2,1,0:T(8,128)(2,1)}, bf16[6,4,160,384]{3,2,1,0:T(8,128)(2,1)S(1)}, u32[]{:S(2)}) copy-start(bf16[6,4,160,384]{3,2,1,0:T(8,128)(2,1)S(1)} %get-tuple-element.28.refs_4_.refs_7_) | copy-start | bytes 8847364
  56.3 8.1 %copy-start.1 = (bf16[1280,384]{1,0:T(8,128)(2,1)S(1)}, bf16[1280,384]{1,0:T(8,128)(2,1)}, u32[]{:S(2)}) copy-start(bf16[1280,384]{1,0:T(8,128)(2,1)} %shard_map.82) | copy-start | bytes 2949124
  57.7 15.7 %collective-permute-start.1 = (bf16[4,1,160,384]{3,2,1,0:T(8,128)(2,1)S(1)}, bf16[4,1,160,384]{3,2,1,0:T(8,128)(2,1)S(1)}, u32[]{:S(2)}, u32[]{:S(2)}) collective-permute-start(bf16[4,1,160,384]{3,2,1,0:T(8,128)(2,1)S(1)} %get-tuple-element.6), channel_id=1, source_target_pairs={{0,1},{1,2},{2,3},{3,4},{4,5},{5,6},{6,7},{8,9},{9,10},{10,11},{11... | collective-permute-start | bytes 1474568 | tf_op jit(solution)/shard_map/ppermute | solution.py:20
  62.5 10.9 %collective-permute-start.2 = (bf16[4,1,160,384]{3,2,1,0:T(8,128)(2,1)S(1)}, bf16[4,1,160,384]{3,2,1,0:T(8,128)(2,1)S(1)}, u32[]{:S(2)}, u32[]{:S(2)}) collective-permute-start(bf16[4,1,160,384]{3,2,1,0:T(8,128)(2,1)S(1)} %get-tuple-element.5), channel_id=1, source_target_pairs={{1,0},{2,1},{3,2},{4,3},{5,4},{6,5},{7,6},{9,8},{10,9},{11,10},{12... | collective-permute-start | bytes 1474568 | tf_op jit(solution)/shard_map/ppermute | solution.py:20
  64.5 27.6 %collective-permute-start.3 = (bf16[2,2,160,384]{3,2,1,0:T(8,128)(2,1)S(1)}, bf16[2,2,160,384]{3,2,1,0:T(8,128)(2,1)S(1)}, u32[]{:S(2)}, u32[]{:S(2)}) collective-permute-start(bf16[2,2,160,384]{3,2,1,0:T(8,128)(2,1)S(1)} %bitcast.37), channel_id=1, source_target_pairs={{0,8},{8,16},{16,24},{24,32},{32,40},{40,48},{48,56},{56,64},{64,7... | collective-permute-start | bytes 1474568 | tf_op jit(solution)/shard_map/ppermute | solution.py:20
  66.5 25.6 %collective-permute-start.4 = (bf16[2,1,160,384]{3,2,1,0:T(8,128)(2,1)S(1)}, bf16[2,1,160,384]{3,2,1,0:T(8,128)(2,1)S(1)}, u32[]{:S(2)}, u32[]{:S(2)}) collective-permute-start(bf16[2,1,160,384]{3,2,1,0:T(8,128)(2,1)S(1)} %get-tuple-element.8), channel_id=1, source_target_pairs={{0,9},{1,10},{2,11},{3,12},{4,13},{5,14},{6,15},{8,17},{9,18},{10,... | collective-permute-start | bytes 737288 | tf_op jit(solution)/shard_map/ppermute | solution.py:31
  71.2 20.9 %collective-permute-start.5 = (bf16[2,1,160,384]{3,2,1,0:T(8,128)(2,1)S(1)}, bf16[2,1,160,384]{3,2,1,0:T(8,128)(2,1)S(1)}, u32[]{:S(2)}, u32[]{:S(2)}) collective-permute-start(bf16[2,1,160,384]{3,2,1,0:T(8,128)(2,1)S(1)} %get-tuple-element.7), channel_id=1, source_target_pairs={{1,8},{2,9},{3,10},{4,11},{5,12},{6,13},{7,14},{9,16},{10,17},{11,... | collective-permute-start | bytes 737288 | tf_op jit(solution)/shard_map/ppermute | solution.py:31
  73.4 0.8 copy-start.3
  73.4 0.9 copy-start.4
  92.1 0.7 copy-start.6
  92.1 0.8 copy-start.7
  92.9 0.8 copy-start.5

commit v9 on v5

--- a/solution.py
+++ b/solution.py
@@ -267,6 +267,7 @@
         keep_own,
         gain,
         "act",
+        per_step=frame_count,
     )
 
     last = second_act[frame_count - 2 :]

time: 107 us -> 107 us (level)
  no operation moved by 1% of the time
where the time goes in v9:
time: 107 us
  Pallas kernels  44.3 us (41%)
  starting transfers between devices  25.8 us (24%)
  waiting for transfers between devices  13 us (12%)
  local copies, waits for them, and re-layouts  12 us (11%)
  matrix products  5.89 us (6%)
  other arithmetic  5.05 us (5%)
    pallas_call x3, Pallas kernels, conv_call(): pl.pallas_call(functools.partial(conv_kernel, layout=layout, mode=mode, p...  44.3 us
    ppermute x4, starting transfers between devices, shifted(): return lax.ppermute(x, axis, pairs)  12 us
    ppermute x7, starting transfers between devices, on_device(): pieces.append(lax.ppermute(packed, 'rows', ring))  6.88 us
    ppermute x2, starting transfers between devices, diagonal(): return lax.ppermute(x, ('tm', 'rows'), pairs)  6.85 us
    dot_general x3, matrix products, local_conv(): jnp.dot(stacked, weight[tap_time].reshape(9 * channels, outputs), preferr...  5.65 us
    ppermute x2, waiting for transfers between devices, diagonal(): return lax.ppermute(x, ('tm', 'rows'), pairs)  5.27 us
    ppermute x4, waiting for transfers between devices, shifted(): return lax.ppermute(x, axis, pairs)  4.53 us
    unnamed x42, local copies, waits for them, and re-layouts  4.14 us
  transfers between devices with their start and end apart: 13, of which 5 were waited for; matrix products, arithmetic and copies ran while one was open for 3% of the time, Pallas kernels for 12%

profile of v9, /device:TPU:21, one launch (start us, length us, event | category | flops | bytes accessed | tf_op | source)
XLA Modules:
  0.0 106.6 jit_solution(1796055283132989356)
XLA Ops:
  0.0 0.7 convert_bitcast_fusion
  0.7 0.8 pad_maximum_fusion.1
  1.5 1.5 %collective-permute-start = (bf16[1,8,2688]{2,1,0:T(8,128)(2,1)S(1)}, bf16[1,8,2688]{2,1,0:T(8,128)(2,1)S(1)}, u32[]{:S(2)}, u32[]{:S(2)}) collective-permute-start(bf16[1,8,2688]{2,1,0:T(8,128)(2,1)S(1)} %get-tuple-element.23), channel_id=1, source_target_pairs={{0,1},{1,2},{2,3},{3,4},{4,5},{5,6},{6,7},{7,0},{8,9},{9,10},{10,1... | collective-permute-start | bytes 129032 | tf_op jit(solution)/shard_map/ppermute | solution.py:229
  3.0 0.2 collective-permute-start.1
  3.2 0.7 collective-permute-start.2
  3.9 2.5 %collective-permute-start.3 = (bf16[1,8,2688]{2,1,0:T(8,128)(2,1)S(1)}, bf16[1,8,2688]{2,1,0:T(8,128)(2,1)S(1)}, u32[]{:S(2)}, u32[]{:S(2)}) collective-permute-start(bf16[1,8,2688]{2,1,0:T(8,128)(2,1)S(1)} %get-tuple-element.23), channel_id=1, source_target_pairs={{0,4},{1,5},{2,6},{3,7},{4,0},{5,1},{6,2},{7,3},{8,12},{9,13},{10,... | collective-permute-start | bytes 129032 | tf_op jit(solution)/shard_map/ppermute | solution.py:229
  6.3 1.0 collective-permute-start.4
  7.4 1.0 fusion.17
  8.4 0.7 pad_dynamic-slice_fusion
  9.7 0.9 collective-permute-start.5
  10.5 0.2 collective-permute-start.6
  10.8 0.5 collective-permute-done.4
  11.3 1.7 %collective-permute-done.5 = bf16[1,8,2688]{2,1,0:T(8,128)(2,1)S(1)} collective-permute-done((bf16[1,8,2688]{2,1,0:T(8,128)(2,1)S(1)}, bf16[1,8,2688]{2,1,0:T(8,128)(2,1)S(1)}, u32[]{:S(2)}, u32[]{:S(2)}) %collective-permute-start.5) | collective-permute-done | bytes 43040 | tf_op jit(solution)/shard_map/ppermute | solution.py:229
  13.0 1.0 collective-permute-done.6
  14.1 0.2 convolution_convert_fusion
  14.4 3.5 %collective-permute-start.7 = (bf16[24,2560]{1,0:T(8,128)(2,1)S(1)}, bf16[24,2560]{1,0:T(8,128)(2,1)S(1)}, u32[]{:S(2)}, u32[]{:S(2)}) collective-permute-start(bf16[24,2560]{1,0:T(8,128)(2,1)S(1)} %convolution_convert_fusion), channel_id=1, source_target_pairs={{0,8},{8,16},{16,24},{24,32},{32,40},{40,48},{48,56},{56,64},{64,7... | collective-permute-start | bytes 368648 | tf_op jit(solution)/shard_map/ppermute | solution.py:20
  18.0 0.6 reshape.102.keep_ref
  18.6 0.6 reshape.98.refs_2_
  19.2 4.5 %collective-permute-done.7 = bf16[24,2560]{1,0:T(8,128)(2,1)S(1)} collective-permute-done((bf16[24,2560]{1,0:T(8,128)(2,1)S(1)}, bf16[24,2560]{1,0:T(8,128)(2,1)S(1)}, u32[]{:S(2)}, u32[]{:S(2)}) %collective-permute-start.7) | collective-permute-done | bytes 122912 | tf_op jit(solution)/shard_map/ppermute | solution.py:20
  23.7 1.6 %reshape.96 = bf16[8,6,160,16]{3,2,1,0:T(8,128)(2,1)S(1)} reshape(bf16[48,2560]{1,0:T(8,128)(2,1)S(1)} %pad_maximum_fusion) | data formatting | bytes 491520 | tf_op jit(solution)/shard_map/reshape | solution.py:242
  25.3 1.0 copy.20
  26.3 0.1 slice_dynamic-update-slice_fusion.14
  26.5 0.1 slice_dynamic-update-slice_fusion.13
  26.8 0.1 slice_dynamic-update-slice_fusion.11
  26.9 0.2 slice_dynamic-update-slice_fusion.10
  27.1 0.2 slice_dynamic-update-slice_fusion.9
  27.5 0.1 slice_dynamic-update-slice_fusion.23
  27.8 0.2 slice_dynamic-update-slice_fusion.21
  28.1 0.1 slice_dynamic-update-slice_fusion.17
  28.4 0.1 slice_dynamic-update-slice_fusion.15
  28.6 1.3 %fusion.19 = f32[6,4,160,384]{3,2,1,0:T(8,128)S(1)} fusion(bf16[6,4,160,144]{2,3,1,0:T(8,128)(2,1)S(1)} %slice_dynamic-update-slice_fusion.15, bf16[144,384,1,1]{1,0,3,2:T(8,128)(2,1)S(1)} %bitcast.41), kind=kOutput, calls=%fused_computation.74 | convolution fusion | flops 424673280 | bytes 7114752 | tf_op jit(solution)/shard_map/dot_general | solution.py:60
  29.8 1.3 %fusion.18 = f32[6,4,160,384]{3,2,1,0:T(8,128)S(1)} fusion(bf16[6,4,160,144]{2,3,1,0:T(8,128)(2,1)S(1)} %get-tuple-element.16, bf16[144,384,1,1]{1,0,3,2:T(8,128)(2,1)S(1)} %bitcast.40), kind=kOutput, calls=%fused_computation.73 | convolution fusion | flops 424673280 | bytes 7114752 | tf_op jit(solution)/shard_map/dot_general | solution.py:60
  31.1 3.1 %fusion = (f32[6,4,160]{2,1,0:T(4,128)S(1)}, bf16[6,4,160,384]{3,2,1,0:T(8,128)(2,1)S(1)}) fusion(bf16[6,4,160,144]{2,3,1,0:T(8,128)(2,1)S(1)} %get-tuple-element.9, bf16[144,384,1,1]{1,0,3,2:T(8,128)(2,1)S(1)} %bitcast.39, f32[6,4,160,384]{3,2,1,0:T(8,128)S(1)} %fusion.19, pred[6]{0:T(512)(128)(4,1)S(1)} %get-tuple-element.26, ...), kind=kOutput, calls=%fused_computation.2 | convolution fusion | flops 436465920 | bytes 15977484 | tf_op jit(solution)/shard_map/dot_general | solution.py:60
  34.3 3.1 %fusion.8.refs_0_ = bf16[6,4,160,384]{3,2,1,0:T(8,128)(2,1)} fusion(bf16[6,4,160,384]{3,2,1,0:T(8,128)(2,1)S(1)} %get-tuple-element.30.refs_4_.refs_7_, f32[384]{0:T(512)S(1)} %copy-done.2, f32[6,4,160]{2,1,0:T(4,128)S(1)} %add_rsqrt_fusion, pred[4]{0:T(512)(128)(4,1)S(1)} %compare_and_fusion.1), kind=kLoop, calls=%fused_computation.12 | loop fusion | flops 13271040 | bytes 5915140 | tf_op jit(solution)/shard_map/jit(_where)/select_n | solution.py:259
  37.4 18.9 %shard_map.82 = bf16[1280,384]{1,0:T(8,128)(2,1)} custom-call(s32[12]{0:T(128)} %reshape.102.keep_ref, bf16[6,4,160,384]{3,2,1,0:T(8,128)(2,1)} %fusion.8.refs_0_, bf16[10368,384]{1,0:T(8,128)(2,1)} %bitcast.44, f32[1,384]{1,0:T(1,128)} %reshape.98.refs_2_), custom_call_target="tpu_custom_call" | custom-call | flops 10192158720 | bytes 10911744 | tf_op jit(solution)/shard_map/pallas_call | solution.py:176
  56.3 1.4 %fusion.15 = (bf16[4,1,160,384]{3,2,1,0:T(8,128)(2,1)S(1)}, bf16[4,1,160,384]{3,2,1,0:T(8,128)(2,1)S(1)}) fusion(bf16[4,2,160,384]{3,2,1,0:T(8,128)(2,1)} %bitcast.34), kind=kLoop, calls=%fused_computation.70 | loop fusion | bytes 1966080 | tf_op jit(solution)/shard_map/slice | solution.py:275
  57.7 4.6 %collective-permute-start.8 = (bf16[4,1,160,384]{3,2,1,0:T(8,128)(2,1)S(1)}, bf16[4,1,160,384]{3,2,1,0:T(8,128)(2,1)S(1)}, u32[]{:S(2)}, u32[]{:S(2)}) collective-permute-start(bf16[4,1,160,384]{3,2,1,0:T(8,128)(2,1)S(1)} %get-tuple-element.6), channel_id=1, source_target_pairs={{0,1},{1,2},{2,3},{3,4},{4,5},{5,6},{6,7},{8,9},{9,10},{10,11},{11... | collective-permute-start | bytes 1474568 | tf_op jit(solution)/shard_map/ppermute | solution.py:20
  62.3 1.9 %collective-permute-start.9 = (bf16[4,1,160,384]{3,2,1,0:T(8,128)(2,1)S(1)}, bf16[4,1,160,384]{3,2,1,0:T(8,128)(2,1)S(1)}, u32[]{:S(2)}, u32[]{:S(2)}) collective-permute-start(bf16[4,1,160,384]{3,2,1,0:T(8,128)(2,1)S(1)} %get-tuple-element.5), channel_id=1, source_target_pairs={{1,0},{2,1},{3,2},{4,3},{5,4},{6,5},{7,6},{9,8},{10,9},{11,10},{12... | collective-permute-start | bytes 1474568 | tf_op jit(solution)/shard_map/ppermute | solution.py:20
  64.3 1.9 %collective-permute-start.10 = (bf16[2,2,160,384]{3,2,1,0:T(8,128)(2,1)S(1)}, bf16[2,2,160,384]{3,2,1,0:T(8,128)(2,1)S(1)}, u32[]{:S(2)}, u32[]{:S(2)}) collective-permute-start(bf16[2,2,160,384]{3,2,1,0:T(8,128)(2,1)S(1)} %bitcast.37), channel_id=1, source_target_pairs={{0,8},{8,16},{16,24},{24,32},{32,40},{40,48},{48,56},{56,64},{64,7... | collective-permute-start | bytes 1474568 | tf_op jit(solution)/shard_map/ppermute | solution.py:20
  66.3 4.7 %collective-permute-start.11 = (bf16[2,1,160,384]{3,2,1,0:T(8,128)(2,1)S(1)}, bf16[2,1,160,384]{3,2,1,0:T(8,128)(2,1)S(1)}, u32[]{:S(2)}, u32[]{:S(2)}) collective-permute-start(bf16[2,1,160,384]{3,2,1,0:T(8,128)(2,1)S(1)} %get-tuple-element.8), channel_id=1, source_target_pairs={{0,9},{1,10},{2,11},{3,12},{4,13},{5,14},{6,15},{8,17},{9,18},{10,... | collective-permute-start | bytes 737288 | tf_op jit(solution)/shard_map/ppermute | solution.py:31
  71.0 2.1 %collective-permute-start.12 = (bf16[2,1,160,384]{3,2,1,0:T(8,128)(2,1)S(1)}, bf16[2,1,160,384]{3,2,1,0:T(8,128)(2,1)S(1)}, u32[]{:S(2)}, u32[]{:S(2)}) collective-permute-start(bf16[2,1,160,384]{3,2,1,0:T(8,128)(2,1)S(1)} %get-tuple-element.7), channel_id=1, source_target_pairs={{1,8},{2,9},{3,10},{4,11},{5,12},{6,13},{7,14},{9,16},{10,17},{11,... | collective-permute-start | bytes 737288 | tf_op jit(solution)/shard_map/ppermute | solution.py:31
  73.2 0.8 copy-done.4
  74.0 0.2 copy-done.5
  74.2 12.5 %shard_map.83.refs_8_ = bf16[1280,384]{1,0:T(8,128)(2,1)} custom-call(s32[12]{0:T(128)} %reshape.102.keep_ref, bf16[4,2,160,384]{3,2,1,0:T(8,128)(2,1)} %bitcast.35, bf16[4,1,160,384]{3,2,1,0:T(8,128)(2,1)} %copy-done.4, bf16[4,1,160,384]{3,2,1,0:T(8,128)(2,1)} %copy-done.5, bf16[10368,384]{1,0:T(8,128)(2,1)} %bitcast.45, bf16[6,4,160,384]{3,2,1,0:T(8,128)(2,1)} %copy-done), custom_call_target="tpu_custom_call" | custom-call | flops 5096079360 | bytes 9437184 | tf_op jit(solution)/shard_map/pallas_call | solution.py:176
  86.7 5.3 %collective-permute-done.11.refs_4_ = bf16[2,1,160,384]{3,2,1,0:T(8,128)(2,1)S(1)} collective-permute-done((bf16[2,1,160,384]{3,2,1,0:T(8,128)(2,1)S(1)}, bf16[2,1,160,384]{3,2,1,0:T(8,128)(2,1)S(1)}, u32[]{:S(2)}, u32[]{:S(2)}) %collective-permute-start.11) | collective-permute-done | bytes 245792 | tf_op jit(solution)/shard_map/ppermute | solution.py:31
  92.0 0.7 copy-done.7
  92.8 0.8 copy-done.6
  93.6 12.8 %shard_map.84 = bf16[1280,384]{1,0:T(8,128)(2,1)} custom-call(s32[12]{0:T(128)} %reshape.102.keep_ref, bf16[4,2,160,384]{3,2,1,0:T(8,128)(2,1)} %bitcast.36, bf16[4,1,160,384]{3,2,1,0:T(8,128)(2,1)} %copy-done.4, bf16[4,1,160,384]{3,2,1,0:T(8,128)(2,1)} %copy-done.5, bf16[2,2,160,384]{3,2,1,0:T(8,128)(2,1)} %copy-done.6, ...), custom_call_target="tpu_custom_call", output_to_operand_aliasing={{}: (9, {})} | custom-call | flops 5096079360 | bytes 9437184 | tf_op jit(solution)/shard_map/pallas_call | solution.py:176
  (59 shorter events, 1.8 us)
Async XLA Ops:
  0.0 18.6 %copy-start.3 = (f32[384]{0:T(512)S(1)}, f32[384]{0:T(512)}, u32[]{:S(2)}) copy-start(f32[384]{0:T(512)} %param.14) | copy-start | bytes 4612
  1.5 8.1 %collective-permute-start = (bf16[1,8,2688]{2,1,0:T(8,128)(2,1)S(1)}, bf16[1,8,2688]{2,1,0:T(8,128)(2,1)S(1)}, u32[]{:S(2)}, u32[]{:S(2)}) collective-permute-start(bf16[1,8,2688]{2,1,0:T(8,128)(2,1)S(1)} %get-tuple-element.23), channel_id=1, source_target_pairs={{0,1},{1,2},{2,3},{3,4},{4,5},{5,6},{6,7},{7,0},{8,9},{9,10},{10,1... | collective-permute-start | bytes 129032 | tf_op jit(solution)/shard_map/ppermute | solution.py:229
  3.0 7.5 %collective-permute-start.1 = (bf16[1,8,2688]{2,1,0:T(8,128)(2,1)S(1)}, bf16[1,8,2688]{2,1,0:T(8,128)(2,1)S(1)}, u32[]{:S(2)}, u32[]{:S(2)}) collective-permute-start(bf16[1,8,2688]{2,1,0:T(8,128)(2,1)S(1)} %get-tuple-element.23), channel_id=1, source_target_pairs={{0,2},{1,3},{2,4},{3,5},{4,6},{5,7},{6,0},{7,1},{8,10},{9,11},{10,... | collective-permute-start | bytes 129032 | tf_op jit(solution)/shard_map/ppermute | solution.py:229
  3.2 7.5 %collective-permute-start.2 = (bf16[1,8,2688]{2,1,0:T(8,128)(2,1)S(1)}, bf16[1,8,2688]{2,1,0:T(8,128)(2,1)S(1)}, u32[]{:S(2)}, u32[]{:S(2)}) collective-permute-start(bf16[1,8,2688]{2,1,0:T(8,128)(2,1)S(1)} %get-tuple-element.23), channel_id=1, source_target_pairs={{0,3},{1,4},{2,5},{3,6},{4,7},{5,0},{6,1},{7,2},{8,11},{9,12},{10,... | collective-permute-start | bytes 129032 | tf_op jit(solution)/shard_map/ppermute | solution.py:229
  3.9 6.9 %collective-permute-start.3 = (bf16[1,8,2688]{2,1,0:T(8,128)(2,1)S(1)}, bf16[1,8,2688]{2,1,0:T(8,128)(2,1)S(1)}, u32[]{:S(2)}, u32[]{:S(2)}) collective-permute-start(bf16[1,8,2688]{2,1,0:T(8,128)(2,1)S(1)} %get-tuple-element.23), channel_id=1, source_target_pairs={{0,4},{1,5},{2,6},{3,7},{4,0},{5,1},{6,2},{7,3},{8,12},{9,13},{10,... | collective-permute-start | bytes 129032 | tf_op jit(solution)/shard_map/ppermute | solution.py:229
  6.3 5.0 %collective-permute-start.4 = (bf16[1,8,2688]{2,1,0:T(8,128)(2,1)S(1)}, bf16[1,8,2688]{2,1,0:T(8,128)(2,1)S(1)}, u32[]{:S(2)}, u32[]{:S(2)}) collective-permute-start(bf16[1,8,2688]{2,1,0:T(8,128)(2,1)S(1)} %get-tuple-element.23), channel_id=1, source_target_pairs={{0,5},{1,6},{2,7},{3,0},{4,1},{5,2},{6,3},{7,4},{8,13},{9,14},{10,... | collective-permute-start | bytes 129032 | tf_op jit(solution)/shard_map/ppermute | solution.py:229
  9.7 3.3 %collective-permute-start.5 = (bf16[1,8,2688]{2,1,0:T(8,128)(2,1)S(1)}, bf16[1,8,2688]{2,1,0:T(8,128)(2,1)S(1)}, u32[]{:S(2)}, u32[]{:S(2)}) collective-permute-start(bf16[1,8,2688]{2,1,0:T(8,128)(2,1)S(1)} %get-tuple-element.23), channel_id=1, source_target_pairs={{0,6},{1,7},{2,0},{3,1},{4,2},{5,3},{6,4},{7,5},{8,14},{9,15},{10,... | collective-permute-start | bytes 129032 | tf_op jit(solution)/shard_map/ppermute | solution.py:229
  10.5 3.5 %collective-permute-start.6 = (bf16[1,8,2688]{2,1,0:T(8,128)(2,1)S(1)}, bf16[1,8,2688]{2,1,0:T(8,128)(2,1)S(1)}, u32[]{:S(2)}, u32[]{:S(2)}) collective-permute-start(bf16[1,8,2688]{2,1,0:T(8,128)(2,1)S(1)} %get-tuple-element.23), channel_id=1, source_target_pairs={{0,7},{1,0},{2,1},{3,2},{4,3},{5,4},{6,5},{7,6},{8,15},{9,8},{10,9... | collective-permute-start | bytes 129032 | tf_op jit(solution)/shard_map/ppermute | solution.py:229
  14.4 9.3 %collective-permute-start.7 = (bf16[24,2560]{1,0:T(8,128)(2,1)S(1)}, bf16[24,2560]{1,0:T(8,128)(2,1)S(1)}, u32[]{:S(2)}, u32[]{:S(2)}) collective-permute-start(bf16[24,2560]{1,0:T(8,128)(2,1)S(1)} %convolution_convert_fusion), channel_id=1, source_target_pairs={{0,8},{8,16},{16,24},{24,32},{32,40},{40,48},{48,56},{56,64},{64,7... | collective-permute-start | bytes 368648 | tf_op jit(solution)/shard_map/ppermute | solution.py:20
  31.1 3.2 %copy-start.2 = (f32[384]{0:T(512)S(1)}, f32[384]{0:T(512)}, u32[]{:S(2)}) copy-start(f32[384]{0:T(512)} %param.12) | copy-start | bytes 4612
  34.2 3.2 %copy-start = (bf16[6,4,160,384]{3,2,1,0:T(8,128)(2,1)}, bf16[6,4,160,384]{3,2,1,0:T(8,128)(2,1)S(1)}, u32[]{:S(2)}) copy-start(bf16[6,4,160,384]{3,2,1,0:T(8,128)(2,1)S(1)} %get-tuple-element.30.refs_4_.refs_7_) | copy-start | bytes 8847364
  56.3 8.0 %copy-start.1 = (bf16[1280,384]{1,0:T(8,128)(2,1)S(1)}, bf16[1280,384]{1,0:T(8,128)(2,1)}, u32[]{:S(2)}) copy-start(bf16[1280,384]{1,0:T(8,128)(2,1)} %shard_map.82) | copy-start | bytes 2949124
  57.7 15.5 %collective-permute-start.8 = (bf16[4,1,160,384]{3,2,1,0:T(8,128)(2,1)S(1)}, bf16[4,1,160,384]{3,2,1,0:T(8,128)(2,1)S(1)}, u32[]{:S(2)}, u32[]{:S(2)}) collective-permute-start(bf16[4,1,160,384]{3,2,1,0:T(8,128)(2,1)S(1)} %get-tuple-element.6), channel_id=1, source_target_pairs={{0,1},{1,2},{2,3},{3,4},{4,5},{5,6},{6,7},{8,9},{9,10},{10,11},{11... | collective-permute-start | bytes 1474568 | tf_op jit(solution)/shard_map/ppermute | solution.py:20
  62.3 10.9 %collective-permute-start.9 = (bf16[4,1,160,384]{3,2,1,0:T(8,128)(2,1)S(1)}, bf16[4,1,160,384]{3,2,1,0:T(8,128)(2,1)S(1)}, u32[]{:S(2)}, u32[]{:S(2)}) collective-permute-start(bf16[4,1,160,384]{3,2,1,0:T(8,128)(2,1)S(1)} %get-tuple-element.5), channel_id=1, source_target_pairs={{1,0},{2,1},{3,2},{4,3},{5,4},{6,5},{7,6},{9,8},{10,9},{11,10},{12... | collective-permute-start | bytes 1474568 | tf_op jit(solution)/shard_map/ppermute | solution.py:20
  64.3 27.7 %collective-permute-start.10 = (bf16[2,2,160,384]{3,2,1,0:T(8,128)(2,1)S(1)}, bf16[2,2,160,384]{3,2,1,0:T(8,128)(2,1)S(1)}, u32[]{:S(2)}, u32[]{:S(2)}) collective-permute-start(bf16[2,2,160,384]{3,2,1,0:T(8,128)(2,1)S(1)} %bitcast.37), channel_id=1, source_target_pairs={{0,8},{8,16},{16,24},{24,32},{32,40},{40,48},{48,56},{56,64},{64,7... | collective-permute-start | bytes 1474568 | tf_op jit(solution)/shard_map/ppermute | solution.py:20
  66.3 25.7 %collective-permute-start.11 = (bf16[2,1,160,384]{3,2,1,0:T(8,128)(2,1)S(1)}, bf16[2,1,160,384]{3,2,1,0:T(8,128)(2,1)S(1)}, u32[]{:S(2)}, u32[]{:S(2)}) collective-permute-start(bf16[2,1,160,384]{3,2,1,0:T(8,128)(2,1)S(1)} %get-tuple-element.8), channel_id=1, source_target_pairs={{0,9},{1,10},{2,11},{3,12},{4,13},{5,14},{6,15},{8,17},{9,18},{10,... | collective-permute-start | bytes 737288 | tf_op jit(solution)/shard_map/ppermute | solution.py:31
  71.0 21.0 %collective-permute-start.12 = (bf16[2,1,160,384]{3,2,1,0:T(8,128)(2,1)S(1)}, bf16[2,1,160,384]{3,2,1,0:T(8,128)(2,1)S(1)}, u32[]{:S(2)}, u32[]{:S(2)}) collective-permute-start(bf16[2,1,160,384]{3,2,1,0:T(8,128)(2,1)S(1)} %get-tuple-element.7), channel_id=1, source_target_pairs={{1,8},{2,9},{3,10},{4,11},{5,12},{6,13},{7,14},{9,16},{10,17},{11,... | collective-permute-start | bytes 737288 | tf_op jit(solution)/shard_map/ppermute | solution.py:31
  73.2 0.8 copy-start.4
  73.2 1.0 copy-start.5
  92.0 0.7 copy-start.7
  92.0 0.8 copy-start.8
  92.8 0.8 copy-start.6

commit v10 on v9

--- a/solution.py
+++ b/solution.py
@@ -146,7 +146,7 @@
         scaled = values_f * inverse * side_ref[...]
         o_ref[...] = (scaled / (1.0 + jnp.exp(-scaled))).astype(o_ref.dtype)
     else:
-        residual = side_ref[pl.ds(2 + firsts[0] + step * per_step, per_step), 1 : 1 + height]
+        residual = side_ref[:, 1 : 1 + height]
         o_ref[...] = (residual.reshape(cells, outputs).astype(jnp.float32) + running).astype(
             o_ref.dtype
         )
@@ -167,6 +167,12 @@
     if firsts is None:
         firsts = tuple(range(0, frame_count, per_step))
     block_at = firsts[0] // per_step
+    if mode == "act":
+        side_spec = whole(side)
+    else:
+        side_spec = pl.BlockSpec(
+            (per_step,) + side.shape[1:], lambda step: (1 + block_at + step, 0, 0, 0)
+        )
     operands = [keep, *sources, weight_rows, side]
     extra_specs, aliases = [], {}
     if into is not None:
@@ -178,7 +184,7 @@
         out_shape=jax.ShapeDtypeStruct((cells, outputs), jnp.bfloat16),
         in_specs=[pl.BlockSpec(memory_space=pltpu.SMEM)]
         + [whole(x) for x in sources]
-        + [pl.BlockSpec(memory_space=pl.ANY), whole(side)]
+        + [pl.BlockSpec(memory_space=pl.ANY), side_spec]
         + extra_specs,
         out_specs=pl.BlockSpec((per_step * band, outputs), lambda step: (step + block_at, 0)),
         grid=(len(firsts),),

time: 107 us -> 106 us (level)
  Pallas kernels: 44.3 us -> 43 us
    pallas_call x3, Pallas kernels: 44.3 us -> 43 us  [conv_call(): pl.pallas_call(functools.partial(conv_kernel, layout=layout, mode=mode, p...]
  transfers between devices with their start and end apart: 13 -> 13, of which waited for: 5 -> 5; matrix products, arithmetic and copies ran while one was open for 3% -> 3% of each run, Pallas kernels for 12% -> 11%
where the time goes in v10:
time: 106 us
  Pallas kernels  43 us (41%)
  starting transfers between devices  25.8 us (24%)
  waiting for transfers between devices  13.7 us (13%)
  local copies, waits for them, and re-layouts  12 us (11%)
  matrix products  5.89 us (6%)
  other arithmetic  5.05 us (5%)
    pallas_call x3, Pallas kernels, conv_call(): pl.pallas_call(functools.partial(conv_kernel, layout=layout, mode=mode, p...  43 us
    ppermute x4, starting transfers between devices, shifted(): return lax.ppermute(x, axis, pairs)  12 us
    ppermute x7, starting transfers between devices, on_device(): pieces.append(lax.ppermute(packed, 'rows', ring))  6.88 us
    ppermute x2, starting transfers between devices, diagonal(): return lax.ppermute(x, ('tm', 'rows'), pairs)  6.85 us
    ppermute x2, waiting for transfers between devices, diagonal(): return lax.ppermute(x, ('tm', 'rows'), pairs)  5.92 us
    dot_general x3, matrix products, local_conv(): jnp.dot(stacked, weight[tap_time].reshape(9 * channels, outputs), preferr...  5.65 us
    ppermute x4, waiting for transfers between devices, shifted(): return lax.ppermute(x, axis, pairs)  4.53 us
    unnamed x42, local copies, waits for them, and re-layouts  4.14 us
  transfers between devices with their start and end apart: 13, of which 5 were waited for; matrix products, arithmetic and copies ran while one was open for 3% of the time, Pallas kernels for 11%

profile of v10, /device:TPU:21, one launch (start us, length us, event | category | flops | bytes accessed | tf_op | source)
XLA Modules:
  0.0 105.9 jit_solution(472636243416689114)
XLA Ops:
  0.0 0.7 convert_bitcast_fusion
  0.7 0.8 pad_maximum_fusion.1
  1.5 1.5 %collective-permute-start = (bf16[1,8,2688]{2,1,0:T(8,128)(2,1)S(1)}, bf16[1,8,2688]{2,1,0:T(8,128)(2,1)S(1)}, u32[]{:S(2)}, u32[]{:S(2)}) collective-permute-start(bf16[1,8,2688]{2,1,0:T(8,128)(2,1)S(1)} %get-tuple-element.23), channel_id=1, source_target_pairs={{0,1},{1,2},{2,3},{3,4},{4,5},{5,6},{6,7},{7,0},{8,9},{9,10},{10,1... | collective-permute-start | bytes 129032 | tf_op jit(solution)/shard_map/ppermute | solution.py:235
  3.0 0.2 collective-permute-start.1
  3.2 0.7 collective-permute-start.2
  3.9 2.5 %collective-permute-start.3 = (bf16[1,8,2688]{2,1,0:T(8,128)(2,1)S(1)}, bf16[1,8,2688]{2,1,0:T(8,128)(2,1)S(1)}, u32[]{:S(2)}, u32[]{:S(2)}) collective-permute-start(bf16[1,8,2688]{2,1,0:T(8,128)(2,1)S(1)} %get-tuple-element.23), channel_id=1, source_target_pairs={{0,4},{1,5},{2,6},{3,7},{4,0},{5,1},{6,2},{7,3},{8,12},{9,13},{10,... | collective-permute-start | bytes 129032 | tf_op jit(solution)/shard_map/ppermute | solution.py:235
  6.3 1.0 collective-permute-start.4
  7.4 1.0 fusion.17
  8.4 0.7 pad_dynamic-slice_fusion
  9.7 0.9 collective-permute-start.5
  10.5 0.2 collective-permute-start.6
  10.8 0.5 collective-permute-done.4
  11.3 1.7 %collective-permute-done.5 = bf16[1,8,2688]{2,1,0:T(8,128)(2,1)S(1)} collective-permute-done((bf16[1,8,2688]{2,1,0:T(8,128)(2,1)S(1)}, bf16[1,8,2688]{2,1,0:T(8,128)(2,1)S(1)}, u32[]{:S(2)}, u32[]{:S(2)}) %collective-permute-start.5) | collective-permute-done | bytes 43040 | tf_op jit(solution)/shard_map/ppermute | solution.py:235
  13.0 1.0 collective-permute-done.6
  14.1 0.2 convolution_convert_fusion
  14.4 3.5 %collective-permute-start.7 = (bf16[24,2560]{1,0:T(8,128)(2,1)S(1)}, bf16[24,2560]{1,0:T(8,128)(2,1)S(1)}, u32[]{:S(2)}, u32[]{:S(2)}) collective-permute-start(bf16[24,2560]{1,0:T(8,128)(2,1)S(1)} %convolution_convert_fusion), channel_id=1, source_target_pairs={{0,8},{8,16},{16,24},{24,32},{32,40},{40,48},{48,56},{56,64},{64,7... | collective-permute-start | bytes 368648 | tf_op jit(solution)/shard_map/ppermute | solution.py:20
  18.0 0.6 reshape.102.keep_ref
  18.6 0.6 reshape.98.refs_2_
  19.2 4.5 %collective-permute-done.7 = bf16[24,2560]{1,0:T(8,128)(2,1)S(1)} collective-permute-done((bf16[24,2560]{1,0:T(8,128)(2,1)S(1)}, bf16[24,2560]{1,0:T(8,128)(2,1)S(1)}, u32[]{:S(2)}, u32[]{:S(2)}) %collective-permute-start.7) | collective-permute-done | bytes 122912 | tf_op jit(solution)/shard_map/ppermute | solution.py:20
  23.7 1.6 %reshape.96 = bf16[8,6,160,16]{3,2,1,0:T(8,128)(2,1)S(1)} reshape(bf16[48,2560]{1,0:T(8,128)(2,1)S(1)} %pad_maximum_fusion) | data formatting | bytes 491520 | tf_op jit(solution)/shard_map/reshape | solution.py:248
  25.3 1.0 copy.20
  26.3 0.1 slice_dynamic-update-slice_fusion.14
  26.5 0.1 slice_dynamic-update-slice_fusion.13
  26.8 0.1 slice_dynamic-update-slice_fusion.11
  26.9 0.2 slice_dynamic-update-slice_fusion.10
  27.1 0.2 slice_dynamic-update-slice_fusion.9
  27.5 0.1 slice_dynamic-update-slice_fusion.23
  27.8 0.2 slice_dynamic-update-slice_fusion.21
  28.1 0.1 slice_dynamic-update-slice_fusion.17
  28.4 0.1 slice_dynamic-update-slice_fusion.15
  28.6 1.3 %fusion.19 = f32[6,4,160,384]{3,2,1,0:T(8,128)S(1)} fusion(bf16[6,4,160,144]{2,3,1,0:T(8,128)(2,1)S(1)} %slice_dynamic-update-slice_fusion.15, bf16[144,384,1,1]{1,0,3,2:T(8,128)(2,1)S(1)} %bitcast.41), kind=kOutput, calls=%fused_computation.74 | convolution fusion | flops 424673280 | bytes 7114752 | tf_op jit(solution)/shard_map/dot_general | solution.py:60
  29.8 1.3 %fusion.18 = f32[6,4,160,384]{3,2,1,0:T(8,128)S(1)} fusion(bf16[6,4,160,144]{2,3,1,0:T(8,128)(2,1)S(1)} %get-tuple-element.16, bf16[144,384,1,1]{1,0,3,2:T(8,128)(2,1)S(1)} %bitcast.40), kind=kOutput, calls=%fused_computation.73 | convolution fusion | flops 424673280 | bytes 7114752 | tf_op jit(solution)/shard_map/dot_general | solution.py:60
  31.1 3.1 %fusion = (f32[6,4,160]{2,1,0:T(4,128)S(1)}, bf16[6,4,160,384]{3,2,1,0:T(8,128)(2,1)S(1)}) fusion(bf16[6,4,160,144]{2,3,1,0:T(8,128)(2,1)S(1)} %get-tuple-element.9, bf16[144,384,1,1]{1,0,3,2:T(8,128)(2,1)S(1)} %bitcast.39, f32[6,4,160,384]{3,2,1,0:T(8,128)S(1)} %fusion.19, pred[6]{0:T(512)(128)(4,1)S(1)} %get-tuple-element.26, ...), kind=kOutput, calls=%fused_computation.2 | convolution fusion | flops 436465920 | bytes 15977484 | tf_op jit(solution)/shard_map/dot_general | solution.py:60
  34.3 3.1 %fusion.8.refs_0_ = bf16[6,4,160,384]{3,2,1,0:T(8,128)(2,1)} fusion(bf16[6,4,160,384]{3,2,1,0:T(8,128)(2,1)S(1)} %get-tuple-element.30.refs_4_.refs_7_, f32[384]{0:T(512)S(1)} %copy-done.2, f32[6,4,160]{2,1,0:T(4,128)S(1)} %add_rsqrt_fusion, pred[4]{0:T(512)(128)(4,1)S(1)} %compare_and_fusion.1), kind=kLoop, calls=%fused_computation.12 | loop fusion | flops 13271040 | bytes 5915140 | tf_op jit(solution)/shard_map/jit(_where)/select_n | solution.py:265
  37.4 18.9 %shard_map.82 = bf16[1280,384]{1,0:T(8,128)(2,1)} custom-call(s32[12]{0:T(128)} %reshape.102.keep_ref, bf16[6,4,160,384]{3,2,1,0:T(8,128)(2,1)} %fusion.8.refs_0_, bf16[10368,384]{1,0:T(8,128)(2,1)} %bitcast.44, f32[1,384]{1,0:T(1,128)} %reshape.98.refs_2_), custom_call_target="tpu_custom_call" | custom-call | flops 10192158720 | bytes 10911744 | tf_op jit(solution)/shard_map/pallas_call | solution.py:182
  56.3 1.4 %fusion.15 = (bf16[4,1,160,384]{3,2,1,0:T(8,128)(2,1)S(1)}, bf16[4,1,160,384]{3,2,1,0:T(8,128)(2,1)S(1)}) fusion(bf16[4,2,160,384]{3,2,1,0:T(8,128)(2,1)} %bitcast.34), kind=kLoop, calls=%fused_computation.70 | loop fusion | bytes 1966080 | tf_op jit(solution)/shard_map/slice | solution.py:281
  57.7 4.6 %collective-permute-start.8 = (bf16[4,1,160,384]{3,2,1,0:T(8,128)(2,1)S(1)}, bf16[4,1,160,384]{3,2,1,0:T(8,128)(2,1)S(1)}, u32[]{:S(2)}, u32[]{:S(2)}) collective-permute-start(bf16[4,1,160,384]{3,2,1,0:T(8,128)(2,1)S(1)} %get-tuple-element.6), channel_id=1, source_target_pairs={{0,1},{1,2},{2,3},{3,4},{4,5},{5,6},{6,7},{8,9},{9,10},{10,11},{11... | collective-permute-start | bytes 1474568 | tf_op jit(solution)/shard_map/ppermute | solution.py:20
  62.3 1.9 %collective-permute-start.9 = (bf16[4,1,160,384]{3,2,1,0:T(8,128)(2,1)S(1)}, bf16[4,1,160,384]{3,2,1,0:T(8,128)(2,1)S(1)}, u32[]{:S(2)}, u32[]{:S(2)}) collective-permute-start(bf16[4,1,160,384]{3,2,1,0:T(8,128)(2,1)S(1)} %get-tuple-element.5), channel_id=1, source_target_pairs={{1,0},{2,1},{3,2},{4,3},{5,4},{6,5},{7,6},{9,8},{10,9},{11,10},{12... | collective-permute-start | bytes 1474568 | tf_op jit(solution)/shard_map/ppermute | solution.py:20
  64.3 1.9 %collective-permute-start.10 = (bf16[2,2,160,384]{3,2,1,0:T(8,128)(2,1)S(1)}, bf16[2,2,160,384]{3,2,1,0:T(8,128)(2,1)S(1)}, u32[]{:S(2)}, u32[]{:S(2)}) collective-permute-start(bf16[2,2,160,384]{3,2,1,0:T(8,128)(2,1)S(1)} %bitcast.37), channel_id=1, source_target_pairs={{0,8},{8,16},{16,24},{24,32},{32,40},{40,48},{48,56},{56,64},{64,7... | collective-permute-start | bytes 1474568 | tf_op jit(solution)/shard_map/ppermute | solution.py:20
  66.3 4.7 %collective-permute-start.11 = (bf16[2,1,160,384]{3,2,1,0:T(8,128)(2,1)S(1)}, bf16[2,1,160,384]{3,2,1,0:T(8,128)(2,1)S(1)}, u32[]{:S(2)}, u32[]{:S(2)}) collective-permute-start(bf16[2,1,160,384]{3,2,1,0:T(8,128)(2,1)S(1)} %get-tuple-element.8), channel_id=1, source_target_pairs={{0,9},{1,10},{2,11},{3,12},{4,13},{5,14},{6,15},{8,17},{9,18},{10,... | collective-permute-start | bytes 737288 | tf_op jit(solution)/shard_map/ppermute | solution.py:31
  71.0 2.1 %collective-permute-start.12 = (bf16[2,1,160,384]{3,2,1,0:T(8,128)(2,1)S(1)}, bf16[2,1,160,384]{3,2,1,0:T(8,128)(2,1)S(1)}, u32[]{:S(2)}, u32[]{:S(2)}) collective-permute-start(bf16[2,1,160,384]{3,2,1,0:T(8,128)(2,1)S(1)} %get-tuple-element.7), channel_id=1, source_target_pairs={{1,8},{2,9},{3,10},{4,11},{5,12},{6,13},{7,14},{9,16},{10,17},{11,... | collective-permute-start | bytes 737288 | tf_op jit(solution)/shard_map/ppermute | solution.py:31
  73.2 0.8 copy-done.4
  74.0 0.2 copy-done.5
  74.2 11.9 %shard_map.83.refs_8_ = bf16[1280,384]{1,0:T(8,128)(2,1)} custom-call(s32[12]{0:T(128)} %reshape.102.keep_ref, bf16[4,2,160,384]{3,2,1,0:T(8,128)(2,1)} %bitcast.35, bf16[4,1,160,384]{3,2,1,0:T(8,128)(2,1)} %copy-done.4, bf16[4,1,160,384]{3,2,1,0:T(8,128)(2,1)} %copy-done.5, bf16[10368,384]{1,0:T(8,128)(2,1)} %bitcast.45, bf16[6,4,160,384]{3,2,1,0:T(8,128)(2,1)} %copy-done), custom_call_target="tpu_custom_call" | custom-call | flops 5096079360 | bytes 9437184 | tf_op jit(solution)/shard_map/pallas_call | solution.py:182
  86.1 5.9 %collective-permute-done.11.refs_4_ = bf16[2,1,160,384]{3,2,1,0:T(8,128)(2,1)S(1)} collective-permute-done((bf16[2,1,160,384]{3,2,1,0:T(8,128)(2,1)S(1)}, bf16[2,1,160,384]{3,2,1,0:T(8,128)(2,1)S(1)}, u32[]{:S(2)}, u32[]{:S(2)}) %collective-permute-start.11) | collective-permute-done | bytes 245792 | tf_op jit(solution)/shard_map/ppermute | solution.py:31
  92.0 0.7 copy-done.7
  92.8 0.8 copy-done.6
  93.6 12.2 %shard_map.84 = bf16[1280,384]{1,0:T(8,128)(2,1)} custom-call(s32[12]{0:T(128)} %reshape.102.keep_ref, bf16[4,2,160,384]{3,2,1,0:T(8,128)(2,1)} %bitcast.36, bf16[4,1,160,384]{3,2,1,0:T(8,128)(2,1)} %copy-done.4, bf16[4,1,160,384]{3,2,1,0:T(8,128)(2,1)} %copy-done.5, bf16[2,2,160,384]{3,2,1,0:T(8,128)(2,1)} %copy-done.6, ...), custom_call_target="tpu_custom_call", output_to_operand_aliasing={{}: (9, {})} | custom-call | flops 5096079360 | bytes 9437184 | tf_op jit(solution)/shard_map/pallas_call | solution.py:182
  (59 shorter events, 1.8 us)
Async XLA Ops:
  0.0 18.6 %copy-start.3 = (f32[384]{0:T(512)S(1)}, f32[384]{0:T(512)}, u32[]{:S(2)}) copy-start(f32[384]{0:T(512)} %param.14) | copy-start | bytes 4612
  1.5 8.1 %collective-permute-start = (bf16[1,8,2688]{2,1,0:T(8,128)(2,1)S(1)}, bf16[1,8,2688]{2,1,0:T(8,128)(2,1)S(1)}, u32[]{:S(2)}, u32[]{:S(2)}) collective-permute-start(bf16[1,8,2688]{2,1,0:T(8,128)(2,1)S(1)} %get-tuple-element.23), channel_id=1, source_target_pairs={{0,1},{1,2},{2,3},{3,4},{4,5},{5,6},{6,7},{7,0},{8,9},{9,10},{10,1... | collective-permute-start | bytes 129032 | tf_op jit(solution)/shard_map/ppermute | solution.py:235
  3.0 7.5 %collective-permute-start.1 = (bf16[1,8,2688]{2,1,0:T(8,128)(2,1)S(1)}, bf16[1,8,2688]{2,1,0:T(8,128)(2,1)S(1)}, u32[]{:S(2)}, u32[]{:S(2)}) collective-permute-start(bf16[1,8,2688]{2,1,0:T(8,128)(2,1)S(1)} %get-tuple-element.23), channel_id=1, source_target_pairs={{0,2},{1,3},{2,4},{3,5},{4,6},{5,7},{6,0},{7,1},{8,10},{9,11},{10,... | collective-permute-start | bytes 129032 | tf_op jit(solution)/shard_map/ppermute | solution.py:235
  3.2 7.5 %collective-permute-start.2 = (bf16[1,8,2688]{2,1,0:T(8,128)(2,1)S(1)}, bf16[1,8,2688]{2,1,0:T(8,128)(2,1)S(1)}, u32[]{:S(2)}, u32[]{:S(2)}) collective-permute-start(bf16[1,8,2688]{2,1,0:T(8,128)(2,1)S(1)} %get-tuple-element.23), channel_id=1, source_target_pairs={{0,3},{1,4},{2,5},{3,6},{4,7},{5,0},{6,1},{7,2},{8,11},{9,12},{10,... | collective-permute-start | bytes 129032 | tf_op jit(solution)/shard_map/ppermute | solution.py:235
  3.9 6.9 %collective-permute-start.3 = (bf16[1,8,2688]{2,1,0:T(8,128)(2,1)S(1)}, bf16[1,8,2688]{2,1,0:T(8,128)(2,1)S(1)}, u32[]{:S(2)}, u32[]{:S(2)}) collective-permute-start(bf16[1,8,2688]{2,1,0:T(8,128)(2,1)S(1)} %get-tuple-element.23), channel_id=1, source_target_pairs={{0,4},{1,5},{2,6},{3,7},{4,0},{5,1},{6,2},{7,3},{8,12},{9,13},{10,... | collective-permute-start | bytes 129032 | tf_op jit(solution)/shard_map/ppermute | solution.py:235
  6.3 5.0 %collective-permute-start.4 = (bf16[1,8,2688]{2,1,0:T(8,128)(2,1)S(1)}, bf16[1,8,2688]{2,1,0:T(8,128)(2,1)S(1)}, u32[]{:S(2)}, u32[]{:S(2)}) collective-permute-start(bf16[1,8,2688]{2,1,0:T(8,128)(2,1)S(1)} %get-tuple-element.23), channel_id=1, source_target_pairs={{0,5},{1,6},{2,7},{3,0},{4,1},{5,2},{6,3},{7,4},{8,13},{9,14},{10,... | collective-permute-start | bytes 129032 | tf_op jit(solution)/shard_map/ppermute | solution.py:235
  9.7 3.3 %collective-permute-start.5 = (bf16[1,8,2688]{2,1,0:T(8,128)(2,1)S(1)}, bf16[1,8,2688]{2,1,0:T(8,128)(2,1)S(1)}, u32[]{:S(2)}, u32[]{:S(2)}) collective-permute-start(bf16[1,8,2688]{2,1,0:T(8,128)(2,1)S(1)} %get-tuple-element.23), channel_id=1, source_target_pairs={{0,6},{1,7},{2,0},{3,1},{4,2},{5,3},{6,4},{7,5},{8,14},{9,15},{10,... | collective-permute-start | bytes 129032 | tf_op jit(solution)/shard_map/ppermute | solution.py:235
  10.5 3.5 %collective-permute-start.6 = (bf16[1,8,2688]{2,1,0:T(8,128)(2,1)S(1)}, bf16[1,8,2688]{2,1,0:T(8,128)(2,1)S(1)}, u32[]{:S(2)}, u32[]{:S(2)}) collective-permute-start(bf16[1,8,2688]{2,1,0:T(8,128)(2,1)S(1)} %get-tuple-element.23), channel_id=1, source_target_pairs={{0,7},{1,0},{2,1},{3,2},{4,3},{5,4},{6,5},{7,6},{8,15},{9,8},{10,9... | collective-permute-start | bytes 129032 | tf_op jit(solution)/shard_map/ppermute | solution.py:235
  14.4 9.3 %collective-permute-start.7 = (bf16[24,2560]{1,0:T(8,128)(2,1)S(1)}, bf16[24,2560]{1,0:T(8,128)(2,1)S(1)}, u32[]{:S(2)}, u32[]{:S(2)}) collective-permute-start(bf16[24,2560]{1,0:T(8,128)(2,1)S(1)} %convolution_convert_fusion), channel_id=1, source_target_pairs={{0,8},{8,16},{16,24},{24,32},{32,40},{40,48},{48,56},{56,64},{64,7... | collective-permute-start | bytes 368648 | tf_op jit(solution)/shard_map/ppermute | solution.py:20
  31.1 3.2 %copy-start.2 = (f32[384]{0:T(512)S(1)}, f32[384]{0:T(512)}, u32[]{:S(2)}) copy-start(f32[384]{0:T(512)} %param.12) | copy-start | bytes 4612
  34.2 3.2 %copy-start = (bf16[6,4,160,384]{3,2,1,0:T(8,128)(2,1)}, bf16[6,4,160,384]{3,2,1,0:T(8,128)(2,1)S(1)}, u32[]{:S(2)}) copy-start(bf16[6,4,160,384]{3,2,1,0:T(8,128)(2,1)S(1)} %get-tuple-element.30.refs_4_.refs_7_) | copy-start | bytes 8847364
  56.3 8.0 %copy-start.1 = (bf16[1280,384]{1,0:T(8,128)(2,1)S(1)}, bf16[1280,384]{1,0:T(8,128)(2,1)}, u32[]{:S(2)}) copy-start(bf16[1280,384]{1,0:T(8,128)(2,1)} %shard_map.82) | copy-start | bytes 2949124
  57.7 15.5 %collective-permute-start.8 = (bf16[4,1,160,384]{3,2,1,0:T(8,128)(2,1)S(1)}, bf16[4,1,160,384]{3,2,1,0:T(8,128)(2,1)S(1)}, u32[]{:S(2)}, u32[]{:S(2)}) collective-permute-start(bf16[4,1,160,384]{3,2,1,0:T(8,128)(2,1)S(1)} %get-tuple-element.6), channel_id=1, source_target_pairs={{0,1},{1,2},{2,3},{3,4},{4,5},{5,6},{6,7},{8,9},{9,10},{10,11},{11... | collective-permute-start | bytes 1474568 | tf_op jit(solution)/shard_map/ppermute | solution.py:20
  62.3 10.9 %collective-permute-start.9 = (bf16[4,1,160,384]{3,2,1,0:T(8,128)(2,1)S(1)}, bf16[4,1,160,384]{3,2,1,0:T(8,128)(2,1)S(1)}, u32[]{:S(2)}, u32[]{:S(2)}) collective-permute-start(bf16[4,1,160,384]{3,2,1,0:T(8,128)(2,1)S(1)} %get-tuple-element.5), channel_id=1, source_target_pairs={{1,0},{2,1},{3,2},{4,3},{5,4},{6,5},{7,6},{9,8},{10,9},{11,10},{12... | collective-permute-start | bytes 1474568 | tf_op jit(solution)/shard_map/ppermute | solution.py:20
  64.3 27.7 %collective-permute-start.10 = (bf16[2,2,160,384]{3,2,1,0:T(8,128)(2,1)S(1)}, bf16[2,2,160,384]{3,2,1,0:T(8,128)(2,1)S(1)}, u32[]{:S(2)}, u32[]{:S(2)}) collective-permute-start(bf16[2,2,160,384]{3,2,1,0:T(8,128)(2,1)S(1)} %bitcast.37), channel_id=1, source_target_pairs={{0,8},{8,16},{16,24},{24,32},{32,40},{40,48},{48,56},{56,64},{64,7... | collective-permute-start | bytes 1474568 | tf_op jit(solution)/shard_map/ppermute | solution.py:20
  66.3 25.7 %collective-permute-start.11 = (bf16[2,1,160,384]{3,2,1,0:T(8,128)(2,1)S(1)}, bf16[2,1,160,384]{3,2,1,0:T(8,128)(2,1)S(1)}, u32[]{:S(2)}, u32[]{:S(2)}) collective-permute-start(bf16[2,1,160,384]{3,2,1,0:T(8,128)(2,1)S(1)} %get-tuple-element.8), channel_id=1, source_target_pairs={{0,9},{1,10},{2,11},{3,12},{4,13},{5,14},{6,15},{8,17},{9,18},{10,... | collective-permute-start | bytes 737288 | tf_op jit(solution)/shard_map/ppermute | solution.py:31
  71.0 21.0 %collective-permute-start.12 = (bf16[2,1,160,384]{3,2,1,0:T(8,128)(2,1)S(1)}, bf16[2,1,160,384]{3,2,1,0:T(8,128)(2,1)S(1)}, u32[]{:S(2)}, u32[]{:S(2)}) collective-permute-start(bf16[2,1,160,384]{3,2,1,0:T(8,128)(2,1)S(1)} %get-tuple-element.7), channel_id=1, source_target_pairs={{1,8},{2,9},{3,10},{4,11},{5,12},{6,13},{7,14},{9,16},{10,17},{11,... | collective-permute-start | bytes 737288 | tf_op jit(solution)/shard_map/ppermute | solution.py:31
  73.2 0.8 copy-start.4
  73.2 1.0 copy-start.5
  92.0 0.7 copy-start.7
  92.0 0.8 copy-start.8
  92.8 0.8 copy-start.6

commit v11 on v10

--- a/solution.py
+++ b/solution.py
@@ -183,7 +183,10 @@
         functools.partial(conv_kernel, layout=layout, mode=mode, per_step=per_step, firsts=firsts),
         out_shape=jax.ShapeDtypeStruct((cells, outputs), jnp.bfloat16),
         in_specs=[pl.BlockSpec(memory_space=pltpu.SMEM)]
-        + [whole(x) for x in sources]
+        + [
+            pl.BlockSpec((hi - lo,) + x.shape[1:], lambda step: (0,) * x.ndim)
+            for x, (lo, hi, _, _) in zip(sources, layout.values())
+        ]
         + [pl.BlockSpec(memory_space=pl.ANY), side_spec]
         + extra_specs,
         out_specs=pl.BlockSpec((per_step * band, outputs), lambda step: (step + block_at, 0)),
@@ -296,8 +299,11 @@
         late_layout, late_sources, second_convolution_weight, keep_own, base_ext, "res",
         firsts=(frame_count - 2,),
     )
+    early_layout = dict(layout)
+    for name in ("own", "above", "below"):
+        early_layout[name] = (2, 4) + layout[name][2:]
     return conv_call(
-        layout,
+        early_layout,
         [second_act, from_above, from_below, prev_mid, prev_above, prev_below],
         second_convolution_weight,
         keep_own,

time: 106 us -> 106 us (level)
  no operation moved by 1% of the time
where the time goes in v11:
time: 106 us
  Pallas kernels  42.7 us (40%)
  starting transfers between devices  25.8 us (24%)
  waiting for transfers between devices  13.7 us (13%)
  local copies, waits for them, and re-layouts  12 us (11%)
  matrix products  5.89 us (6%)
  other arithmetic  5.05 us (5%)
    pallas_call x3, Pallas kernels, conv_call(): pl.pallas_call(functools.partial(conv_kernel, layout=layout, mode=mode, p...  42.7 us
    ppermute x4, starting transfers between devices, shifted(): return lax.ppermute(x, axis, pairs)  12 us
    ppermute x7, starting transfers between devices, on_device(): pieces.append(lax.ppermute(packed, 'rows', ring))  6.88 us
    ppermute x2, starting transfers between devices, diagonal(): return lax.ppermute(x, ('tm', 'rows'), pairs)  6.85 us
    ppermute x2, waiting for transfers between devices, diagonal(): return lax.ppermute(x, ('tm', 'rows'), pairs)  5.92 us
    dot_general x3, matrix products, local_conv(): jnp.dot(stacked, weight[tap_time].reshape(9 * channels, outputs), preferr...  5.65 us
    ppermute x4, waiting for transfers between devices, shifted(): return lax.ppermute(x, axis, pairs)  4.53 us
    unnamed x42, local copies, waits for them, and re-layouts  4.14 us
  transfers between devices with their start and end apart: 13, of which 5 were waited for; matrix products, arithmetic and copies ran while one was open for 3% of the time, Pallas kernels for 11%

profile of v11, /device:TPU:21, one launch (start us, length us, event | category | flops | bytes accessed | tf_op | source)
XLA Modules:
  0.0 105.7 jit_solution(10592315408496640215)
XLA Ops:
  0.0 0.7 convert_bitcast_fusion
  0.7 0.8 pad_maximum_fusion.1
  1.5 1.5 %collective-permute-start = (bf16[1,8,2688]{2,1,0:T(8,128)(2,1)S(1)}, bf16[1,8,2688]{2,1,0:T(8,128)(2,1)S(1)}, u32[]{:S(2)}, u32[]{:S(2)}) collective-permute-start(bf16[1,8,2688]{2,1,0:T(8,128)(2,1)S(1)} %get-tuple-element.23), channel_id=1, source_target_pairs={{0,1},{1,2},{2,3},{3,4},{4,5},{5,6},{6,7},{7,0},{8,9},{9,10},{10,1... | collective-permute-start | bytes 129032 | tf_op jit(solution)/shard_map/ppermute | solution.py:238
  3.0 0.2 collective-permute-start.1
  3.2 0.7 collective-permute-start.2
  3.9 2.5 %collective-permute-start.3 = (bf16[1,8,2688]{2,1,0:T(8,128)(2,1)S(1)}, bf16[1,8,2688]{2,1,0:T(8,128)(2,1)S(1)}, u32[]{:S(2)}, u32[]{:S(2)}) collective-permute-start(bf16[1,8,2688]{2,1,0:T(8,128)(2,1)S(1)} %get-tuple-element.23), channel_id=1, source_target_pairs={{0,4},{1,5},{2,6},{3,7},{4,0},{5,1},{6,2},{7,3},{8,12},{9,13},{10,... | collective-permute-start | bytes 129032 | tf_op jit(solution)/shard_map/ppermute | solution.py:238
  6.3 1.0 collective-permute-start.4
  7.4 1.0 fusion.17
  8.4 0.7 pad_dynamic-slice_fusion
  9.7 0.9 collective-permute-start.5
  10.5 0.2 collective-permute-start.6
  10.8 0.5 collective-permute-done.4
  11.3 1.7 %collective-permute-done.5 = bf16[1,8,2688]{2,1,0:T(8,128)(2,1)S(1)} collective-permute-done((bf16[1,8,2688]{2,1,0:T(8,128)(2,1)S(1)}, bf16[1,8,2688]{2,1,0:T(8,128)(2,1)S(1)}, u32[]{:S(2)}, u32[]{:S(2)}) %collective-permute-start.5) | collective-permute-done | bytes 43040 | tf_op jit(solution)/shard_map/ppermute | solution.py:238
  13.0 1.0 collective-permute-done.6
  14.1 0.2 convolution_convert_fusion
  14.4 3.5 %collective-permute-start.7 = (bf16[24,2560]{1,0:T(8,128)(2,1)S(1)}, bf16[24,2560]{1,0:T(8,128)(2,1)S(1)}, u32[]{:S(2)}, u32[]{:S(2)}) collective-permute-start(bf16[24,2560]{1,0:T(8,128)(2,1)S(1)} %convolution_convert_fusion), channel_id=1, source_target_pairs={{0,8},{8,16},{16,24},{24,32},{32,40},{40,48},{48,56},{56,64},{64,7... | collective-permute-start | bytes 368648 | tf_op jit(solution)/shard_map/ppermute | solution.py:20
  18.0 0.6 reshape.102.keep_ref
  18.6 0.6 reshape.98.refs_2_
  19.2 4.5 %collective-permute-done.7 = bf16[24,2560]{1,0:T(8,128)(2,1)S(1)} collective-permute-done((bf16[24,2560]{1,0:T(8,128)(2,1)S(1)}, bf16[24,2560]{1,0:T(8,128)(2,1)S(1)}, u32[]{:S(2)}, u32[]{:S(2)}) %collective-permute-start.7) | collective-permute-done | bytes 122912 | tf_op jit(solution)/shard_map/ppermute | solution.py:20
  23.7 1.6 %reshape.96 = bf16[8,6,160,16]{3,2,1,0:T(8,128)(2,1)S(1)} reshape(bf16[48,2560]{1,0:T(8,128)(2,1)S(1)} %pad_maximum_fusion) | data formatting | bytes 491520 | tf_op jit(solution)/shard_map/reshape | solution.py:251
  25.3 1.0 copy.20
  26.3 0.1 slice_dynamic-update-slice_fusion.14
  26.5 0.1 slice_dynamic-update-slice_fusion.13
  26.8 0.1 slice_dynamic-update-slice_fusion.11
  26.9 0.2 slice_dynamic-update-slice_fusion.10
  27.1 0.2 slice_dynamic-update-slice_fusion.9
  27.5 0.1 slice_dynamic-update-slice_fusion.23
  27.8 0.2 slice_dynamic-update-slice_fusion.21
  28.1 0.1 slice_dynamic-update-slice_fusion.17
  28.4 0.1 slice_dynamic-update-slice_fusion.15
  28.6 1.3 %fusion.19 = f32[6,4,160,384]{3,2,1,0:T(8,128)S(1)} fusion(bf16[6,4,160,144]{2,3,1,0:T(8,128)(2,1)S(1)} %slice_dynamic-update-slice_fusion.15, bf16[144,384,1,1]{1,0,3,2:T(8,128)(2,1)S(1)} %bitcast.41), kind=kOutput, calls=%fused_computation.74 | convolution fusion | flops 424673280 | bytes 7114752 | tf_op jit(solution)/shard_map/dot_general | solution.py:60
  29.8 1.3 %fusion.18 = f32[6,4,160,384]{3,2,1,0:T(8,128)S(1)} fusion(bf16[6,4,160,144]{2,3,1,0:T(8,128)(2,1)S(1)} %get-tuple-element.16, bf16[144,384,1,1]{1,0,3,2:T(8,128)(2,1)S(1)} %bitcast.40), kind=kOutput, calls=%fused_computation.73 | convolution fusion | flops 424673280 | bytes 7114752 | tf_op jit(solution)/shard_map/dot_general | solution.py:60
  31.1 3.1 %fusion = (f32[6,4,160]{2,1,0:T(4,128)S(1)}, bf16[6,4,160,384]{3,2,1,0:T(8,128)(2,1)S(1)}) fusion(bf16[6,4,160,144]{2,3,1,0:T(8,128)(2,1)S(1)} %get-tuple-element.9, bf16[144,384,1,1]{1,0,3,2:T(8,128)(2,1)S(1)} %bitcast.39, f32[6,4,160,384]{3,2,1,0:T(8,128)S(1)} %fusion.19, pred[6]{0:T(512)(128)(4,1)S(1)} %get-tuple-element.26, ...), kind=kOutput, calls=%fused_computation.2 | convolution fusion | flops 436465920 | bytes 15977484 | tf_op jit(solution)/shard_map/dot_general | solution.py:60
  34.3 3.1 %fusion.8.refs_0_ = bf16[6,4,160,384]{3,2,1,0:T(8,128)(2,1)} fusion(bf16[6,4,160,384]{3,2,1,0:T(8,128)(2,1)S(1)} %get-tuple-element.30.refs_4_.refs_7_, f32[384]{0:T(512)S(1)} %copy-done.2, f32[6,4,160]{2,1,0:T(4,128)S(1)} %add_rsqrt_fusion, pred[4]{0:T(512)(128)(4,1)S(1)} %compare_and_fusion.1), kind=kLoop, calls=%fused_computation.12 | loop fusion | flops 13271040 | bytes 5915140 | tf_op jit(solution)/shard_map/jit(_where)/select_n | solution.py:268
  37.4 18.9 %shard_map.82 = bf16[1280,384]{1,0:T(8,128)(2,1)} custom-call(s32[12]{0:T(128)} %reshape.102.keep_ref, bf16[6,4,160,384]{3,2,1,0:T(8,128)(2,1)} %fusion.8.refs_0_, bf16[10368,384]{1,0:T(8,128)(2,1)} %bitcast.44, f32[1,384]{1,0:T(1,128)} %reshape.98.refs_2_), custom_call_target="tpu_custom_call" | custom-call | flops 10192158720 | bytes 10911744 | tf_op jit(solution)/shard_map/pallas_call | solution.py:182
  56.3 1.4 %fusion.15 = (bf16[4,1,160,384]{3,2,1,0:T(8,128)(2,1)S(1)}, bf16[4,1,160,384]{3,2,1,0:T(8,128)(2,1)S(1)}) fusion(bf16[4,2,160,384]{3,2,1,0:T(8,128)(2,1)} %bitcast.34), kind=kLoop, calls=%fused_computation.70 | loop fusion | bytes 1966080 | tf_op jit(solution)/shard_map/slice | solution.py:284
  57.7 4.6 %collective-permute-start.8 = (bf16[4,1,160,384]{3,2,1,0:T(8,128)(2,1)S(1)}, bf16[4,1,160,384]{3,2,1,0:T(8,128)(2,1)S(1)}, u32[]{:S(2)}, u32[]{:S(2)}) collective-permute-start(bf16[4,1,160,384]{3,2,1,0:T(8,128)(2,1)S(1)} %get-tuple-element.6), channel_id=1, source_target_pairs={{0,1},{1,2},{2,3},{3,4},{4,5},{5,6},{6,7},{8,9},{9,10},{10,11},{11... | collective-permute-start | bytes 1474568 | tf_op jit(solution)/shard_map/ppermute | solution.py:20
  62.3 1.9 %collective-permute-start.9 = (bf16[4,1,160,384]{3,2,1,0:T(8,128)(2,1)S(1)}, bf16[4,1,160,384]{3,2,1,0:T(8,128)(2,1)S(1)}, u32[]{:S(2)}, u32[]{:S(2)}) collective-permute-start(bf16[4,1,160,384]{3,2,1,0:T(8,128)(2,1)S(1)} %get-tuple-element.5), channel_id=1, source_target_pairs={{1,0},{2,1},{3,2},{4,3},{5,4},{6,5},{7,6},{9,8},{10,9},{11,10},{12... | collective-permute-start | bytes 1474568 | tf_op jit(solution)/shard_map/ppermute | solution.py:20
  64.3 1.9 %collective-permute-start.10 = (bf16[2,2,160,384]{3,2,1,0:T(8,128)(2,1)S(1)}, bf16[2,2,160,384]{3,2,1,0:T(8,128)(2,1)S(1)}, u32[]{:S(2)}, u32[]{:S(2)}) collective-permute-start(bf16[2,2,160,384]{3,2,1,0:T(8,128)(2,1)S(1)} %bitcast.37), channel_id=1, source_target_pairs={{0,8},{8,16},{16,24},{24,32},{32,40},{40,48},{48,56},{56,64},{64,7... | collective-permute-start | bytes 1474568 | tf_op jit(solution)/shard_map/ppermute | solution.py:20
  66.3 4.7 %collective-permute-start.11 = (bf16[2,1,160,384]{3,2,1,0:T(8,128)(2,1)S(1)}, bf16[2,1,160,384]{3,2,1,0:T(8,128)(2,1)S(1)}, u32[]{:S(2)}, u32[]{:S(2)}) collective-permute-start(bf16[2,1,160,384]{3,2,1,0:T(8,128)(2,1)S(1)} %get-tuple-element.8), channel_id=1, source_target_pairs={{0,9},{1,10},{2,11},{3,12},{4,13},{5,14},{6,15},{8,17},{9,18},{10,... | collective-permute-start | bytes 737288 | tf_op jit(solution)/shard_map/ppermute | solution.py:31
  71.0 2.1 %collective-permute-start.12 = (bf16[2,1,160,384]{3,2,1,0:T(8,128)(2,1)S(1)}, bf16[2,1,160,384]{3,2,1,0:T(8,128)(2,1)S(1)}, u32[]{:S(2)}, u32[]{:S(2)}) collective-permute-start(bf16[2,1,160,384]{3,2,1,0:T(8,128)(2,1)S(1)} %get-tuple-element.7), channel_id=1, source_target_pairs={{1,8},{2,9},{3,10},{4,11},{5,12},{6,13},{7,14},{9,16},{10,17},{11,... | collective-permute-start | bytes 737288 | tf_op jit(solution)/shard_map/ppermute | solution.py:31
  73.2 0.8 copy-done.4
  74.0 0.2 copy-done.5
  74.2 11.9 %shard_map.83.refs_8_ = bf16[1280,384]{1,0:T(8,128)(2,1)} custom-call(s32[12]{0:T(128)} %reshape.102.keep_ref, bf16[4,2,160,384]{3,2,1,0:T(8,128)(2,1)} %bitcast.35, bf16[4,1,160,384]{3,2,1,0:T(8,128)(2,1)} %copy-done.4, bf16[4,1,160,384]{3,2,1,0:T(8,128)(2,1)} %copy-done.5, bf16[10368,384]{1,0:T(8,128)(2,1)} %bitcast.45, bf16[6,4,160,384]{3,2,1,0:T(8,128)(2,1)} %copy-done), custom_call_target="tpu_custom_call" | custom-call | flops 5096079360 | bytes 9437184 | tf_op jit(solution)/shard_map/pallas_call | solution.py:182
  86.1 5.9 %collective-permute-done.11.refs_4_ = bf16[2,1,160,384]{3,2,1,0:T(8,128)(2,1)S(1)} collective-permute-done((bf16[2,1,160,384]{3,2,1,0:T(8,128)(2,1)S(1)}, bf16[2,1,160,384]{3,2,1,0:T(8,128)(2,1)S(1)}, u32[]{:S(2)}, u32[]{:S(2)}) %collective-permute-start.11) | collective-permute-done | bytes 245792 | tf_op jit(solution)/shard_map/ppermute | solution.py:31
  92.0 0.7 copy-done.7
  92.8 0.8 copy-done.6
  93.6 12.0 %shard_map.84 = bf16[1280,384]{1,0:T(8,128)(2,1)} custom-call(s32[12]{0:T(128)} %reshape.102.keep_ref, bf16[4,2,160,384]{3,2,1,0:T(8,128)(2,1)} %bitcast.36, bf16[4,1,160,384]{3,2,1,0:T(8,128)(2,1)} %copy-done.4, bf16[4,1,160,384]{3,2,1,0:T(8,128)(2,1)} %copy-done.5, bf16[2,2,160,384]{3,2,1,0:T(8,128)(2,1)} %copy-done.6, ...), custom_call_target="tpu_custom_call", output_to_operand_aliasing={{}: (9, {})} | custom-call | flops 5096079360 | bytes 9437184 | tf_op jit(solution)/shard_map/pallas_call | solution.py:182
  (59 shorter events, 1.8 us)
Async XLA Ops:
  0.0 18.6 %copy-start.3 = (f32[384]{0:T(512)S(1)}, f32[384]{0:T(512)}, u32[]{:S(2)}) copy-start(f32[384]{0:T(512)} %param.14) | copy-start | bytes 4612
  1.5 8.1 %collective-permute-start = (bf16[1,8,2688]{2,1,0:T(8,128)(2,1)S(1)}, bf16[1,8,2688]{2,1,0:T(8,128)(2,1)S(1)}, u32[]{:S(2)}, u32[]{:S(2)}) collective-permute-start(bf16[1,8,2688]{2,1,0:T(8,128)(2,1)S(1)} %get-tuple-element.23), channel_id=1, source_target_pairs={{0,1},{1,2},{2,3},{3,4},{4,5},{5,6},{6,7},{7,0},{8,9},{9,10},{10,1... | collective-permute-start | bytes 129032 | tf_op jit(solution)/shard_map/ppermute | solution.py:238
  3.0 7.5 %collective-permute-start.1 = (bf16[1,8,2688]{2,1,0:T(8,128)(2,1)S(1)}, bf16[1,8,2688]{2,1,0:T(8,128)(2,1)S(1)}, u32[]{:S(2)}, u32[]{:S(2)}) collective-permute-start(bf16[1,8,2688]{2,1,0:T(8,128)(2,1)S(1)} %get-tuple-element.23), channel_id=1, source_target_pairs={{0,2},{1,3},{2,4},{3,5},{4,6},{5,7},{6,0},{7,1},{8,10},{9,11},{10,... | collective-permute-start | bytes 129032 | tf_op jit(solution)/shard_map/ppermute | solution.py:238
  3.2 7.5 %collective-permute-start.2 = (bf16[1,8,2688]{2,1,0:T(8,128)(2,1)S(1)}, bf16[1,8,2688]{2,1,0:T(8,128)(2,1)S(1)}, u32[]{:S(2)}, u32[]{:S(2)}) collective-permute-start(bf16[1,8,2688]{2,1,0:T(8,128)(2,1)S(1)} %get-tuple-element.23), channel_id=1, source_target_pairs={{0,3},{1,4},{2,5},{3,6},{4,7},{5,0},{6,1},{7,2},{8,11},{9,12},{10,... | collective-permute-start | bytes 129032 | tf_op jit(solution)/shard_map/ppermute | solution.py:238
  3.9 6.9 %collective-permute-start.3 = (bf16[1,8,2688]{2,1,0:T(8,128)(2,1)S(1)}, bf16[1,8,2688]{2,1,0:T(8,128)(2,1)S(1)}, u32[]{:S(2)}, u32[]{:S(2)}) collective-permute-start(bf16[1,8,2688]{2,1,0:T(8,128)(2,1)S(1)} %get-tuple-element.23), channel_id=1, source_target_pairs={{0,4},{1,5},{2,6},{3,7},{4,0},{5,1},{6,2},{7,3},{8,12},{9,13},{10,... | collective-permute-start | bytes 129032 | tf_op jit(solution)/shard_map/ppermute | solution.py:238
  6.3 5.0 %collective-permute-start.4 = (bf16[1,8,2688]{2,1,0:T(8,128)(2,1)S(1)}, bf16[1,8,2688]{2,1,0:T(8,128)(2,1)S(1)}, u32[]{:S(2)}, u32[]{:S(2)}) collective-permute-start(bf16[1,8,2688]{2,1,0:T(8,128)(2,1)S(1)} %get-tuple-element.23), channel_id=1, source_target_pairs={{0,5},{1,6},{2,7},{3,0},{4,1},{5,2},{6,3},{7,4},{8,13},{9,14},{10,... | collective-permute-start | bytes 129032 | tf_op jit(solution)/shard_map/ppermute | solution.py:238
  9.7 3.3 %collective-permute-start.5 = (bf16[1,8,2688]{2,1,0:T(8,128)(2,1)S(1)}, bf16[1,8,2688]{2,1,0:T(8,128)(2,1)S(1)}, u32[]{:S(2)}, u32[]{:S(2)}) collective-permute-start(bf16[1,8,2688]{2,1,0:T(8,128)(2,1)S(1)} %get-tuple-element.23), channel_id=1, source_target_pairs={{0,6},{1,7},{2,0},{3,1},{4,2},{5,3},{6,4},{7,5},{8,14},{9,15},{10,... | collective-permute-start | bytes 129032 | tf_op jit(solution)/shard_map/ppermute | solution.py:238
  10.5 3.5 %collective-permute-start.6 = (bf16[1,8,2688]{2,1,0:T(8,128)(2,1)S(1)}, bf16[1,8,2688]{2,1,0:T(8,128)(2,1)S(1)}, u32[]{:S(2)}, u32[]{:S(2)}) collective-permute-start(bf16[1,8,2688]{2,1,0:T(8,128)(2,1)S(1)} %get-tuple-element.23), channel_id=1, source_target_pairs={{0,7},{1,0},{2,1},{3,2},{4,3},{5,4},{6,5},{7,6},{8,15},{9,8},{10,9... | collective-permute-start | bytes 129032 | tf_op jit(solution)/shard_map/ppermute | solution.py:238
  14.4 9.3 %collective-permute-start.7 = (bf16[24,2560]{1,0:T(8,128)(2,1)S(1)}, bf16[24,2560]{1,0:T(8,128)(2,1)S(1)}, u32[]{:S(2)}, u32[]{:S(2)}) collective-permute-start(bf16[24,2560]{1,0:T(8,128)(2,1)S(1)} %convolution_convert_fusion), channel_id=1, source_target_pairs={{0,8},{8,16},{16,24},{24,32},{32,40},{40,48},{48,56},{56,64},{64,7... | collective-permute-start | bytes 368648 | tf_op jit(solution)/shard_map/ppermute | solution.py:20
  31.1 3.2 %copy-start.2 = (f32[384]{0:T(512)S(1)}, f32[384]{0:T(512)}, u32[]{:S(2)}) copy-start(f32[384]{0:T(512)} %param.12) | copy-start | bytes 4612
  34.2 3.2 %copy-start = (bf16[6,4,160,384]{3,2,1,0:T(8,128)(2,1)}, bf16[6,4,160,384]{3,2,1,0:T(8,128)(2,1)S(1)}, u32[]{:S(2)}) copy-start(bf16[6,4,160,384]{3,2,1,0:T(8,128)(2,1)S(1)} %get-tuple-element.30.refs_4_.refs_7_) | copy-start | bytes 8847364
  56.3 8.0 %copy-start.1 = (bf16[1280,384]{1,0:T(8,128)(2,1)S(1)}, bf16[1280,384]{1,0:T(8,128)(2,1)}, u32[]{:S(2)}) copy-start(bf16[1280,384]{1,0:T(8,128)(2,1)} %shard_map.82) | copy-start | bytes 2949124
  57.7 15.5 %collective-permute-start.8 = (bf16[4,1,160,384]{3,2,1,0:T(8,128)(2,1)S(1)}, bf16[4,1,160,384]{3,2,1,0:T(8,128)(2,1)S(1)}, u32[]{:S(2)}, u32[]{:S(2)}) collective-permute-start(bf16[4,1,160,384]{3,2,1,0:T(8,128)(2,1)S(1)} %get-tuple-element.6), channel_id=1, source_target_pairs={{0,1},{1,2},{2,3},{3,4},{4,5},{5,6},{6,7},{8,9},{9,10},{10,11},{11... | collective-permute-start | bytes 1474568 | tf_op jit(solution)/shard_map/ppermute | solution.py:20
  62.3 10.9 %collective-permute-start.9 = (bf16[4,1,160,384]{3,2,1,0:T(8,128)(2,1)S(1)}, bf16[4,1,160,384]{3,2,1,0:T(8,128)(2,1)S(1)}, u32[]{:S(2)}, u32[]{:S(2)}) collective-permute-start(bf16[4,1,160,384]{3,2,1,0:T(8,128)(2,1)S(1)} %get-tuple-element.5), channel_id=1, source_target_pairs={{1,0},{2,1},{3,2},{4,3},{5,4},{6,5},{7,6},{9,8},{10,9},{11,10},{12... | collective-permute-start | bytes 1474568 | tf_op jit(solution)/shard_map/ppermute | solution.py:20
  64.3 27.7 %collective-permute-start.10 = (bf16[2,2,160,384]{3,2,1,0:T(8,128)(2,1)S(1)}, bf16[2,2,160,384]{3,2,1,0:T(8,128)(2,1)S(1)}, u32[]{:S(2)}, u32[]{:S(2)}) collective-permute-start(bf16[2,2,160,384]{3,2,1,0:T(8,128)(2,1)S(1)} %bitcast.37), channel_id=1, source_target_pairs={{0,8},{8,16},{16,24},{24,32},{32,40},{40,48},{48,56},{56,64},{64,7... | collective-permute-start | bytes 1474568 | tf_op jit(solution)/shard_map/ppermute | solution.py:20
  66.3 25.7 %collective-permute-start.11 = (bf16[2,1,160,384]{3,2,1,0:T(8,128)(2,1)S(1)}, bf16[2,1,160,384]{3,2,1,0:T(8,128)(2,1)S(1)}, u32[]{:S(2)}, u32[]{:S(2)}) collective-permute-start(bf16[2,1,160,384]{3,2,1,0:T(8,128)(2,1)S(1)} %get-tuple-element.8), channel_id=1, source_target_pairs={{0,9},{1,10},{2,11},{3,12},{4,13},{5,14},{6,15},{8,17},{9,18},{10,... | collective-permute-start | bytes 737288 | tf_op jit(solution)/shard_map/ppermute | solution.py:31
  71.0 21.0 %collective-permute-start.12 = (bf16[2,1,160,384]{3,2,1,0:T(8,128)(2,1)S(1)}, bf16[2,1,160,384]{3,2,1,0:T(8,128)(2,1)S(1)}, u32[]{:S(2)}, u32[]{:S(2)}) collective-permute-start(bf16[2,1,160,384]{3,2,1,0:T(8,128)(2,1)S(1)} %get-tuple-element.7), channel_id=1, source_target_pairs={{1,8},{2,9},{3,10},{4,11},{5,12},{6,13},{7,14},{9,16},{10,17},{11,... | collective-permute-start | bytes 737288 | tf_op jit(solution)/shard_map/ppermute | solution.py:31
  73.2 0.8 copy-start.4
  73.2 1.0 copy-start.5
  92.0 0.7 copy-start.7
  92.0 0.8 copy-start.8
  92.8 0.8 copy-start.6

commit v12 on v10

--- a/solution.py
+++ b/solution.py
@@ -280,8 +280,8 @@
     from_above = shifted(second_act[:, rows_here - 1 :], "rows", 1)
     from_below = shifted(second_act[:, :1], "rows", -1)
     prev_mid = shifted(last, "tm", 1)
-    prev_above = diagonal(last[:, rows_here - 1 :], 1, 1)
-    prev_below = diagonal(last[:, :1], 1, -1)
+    prev_above = shifted(from_above[frame_count - 2 :], "tm", 1)
+    prev_below = shifted(from_below[frame_count - 2 :], "tm", 1)
     layout = {
         "own": (2, 2 + frame_count, 1, 1 + rows_here),
         "above": (2, 2 + frame_count, 0, 1),

time: 106 us -> 106 us (level)
  waiting for transfers between devices: 13.7 us -> 17.3 us
  starting transfers between devices: 25.8 us -> 23 us
  local copies, waits for them, and re-layouts: 12 us -> 10.3 us
    ppermute x4 -> x6, waiting for transfers between devices: 4.53 us -> 14.1 us  [shifted(): return lax.ppermute(x, axis, pairs)]
    ppermute x2 -> x0, starting transfers between devices: 6.85 us -> none  [diagonal(): return lax.ppermute(x, ('tm', 'rows'), pairs)]
    ppermute x2 -> x0, waiting for transfers between devices: 5.92 us -> none  [diagonal(): return lax.ppermute(x, ('tm', 'rows'), pairs)]
    ppermute x4 -> x6, starting transfers between devices: 12 us -> 16.1 us  [shifted(): return lax.ppermute(x, axis, pairs)]
    unnamed x42, local copies, waits for them, and re-layouts: 4.14 us -> 2.34 us
  transfers between devices with their start and end apart: 13 -> 13, of which waited for: 5 -> 7; matrix products, arithmetic and copies ran while one was open for 3% -> 4% of each run, Pallas kernels for 11% -> 11%
where the time goes in v12:
time: 106 us; the launch traced here: 105 us
  Pallas kernels  43 us (41%)
  starting transfers between devices  23 us (22%)
  waiting for transfers between devices  17.3 us (16%)
  local copies, waits for them, and re-layouts  10.3 us (10%)
  matrix products  5.89 us (6%)
  other arithmetic  5.07 us (5%)
    pallas_call x3, Pallas kernels, conv_call(): pl.pallas_call(functools.partial(conv_kernel, layout=layout, mode=mode, p...  43 us
    ppermute x6, starting transfers between devices, shifted(): return lax.ppermute(x, axis, pairs)  16.1 us
    ppermute x6, waiting for transfers between devices, shifted(): return lax.ppermute(x, axis, pairs)  14.1 us
    ppermute x7, starting transfers between devices, on_device(): pieces.append(lax.ppermute(packed, 'rows', ring))  6.88 us
    dot_general x3, matrix products, local_conv(): jnp.dot(stacked, weight[tap_time].reshape(9 * channels, outputs), preferr...  5.65 us
    ppermute x7, waiting for transfers between devices, on_device(): pieces.append(lax.ppermute(packed, 'rows', ring))  3.23 us
    select_n x1, other arithmetic, on_device(): jnp.where(row_ok[None, :, None, None], first_act, jnp.zeros((), jnp.bfloa...  3.15 us
    reshape x2, local copies, waits for them, and re-layouts, on_device(): jnp.concatenate([prev_window, own_window], axis=0)  2.59 us
  transfers between devices with their start and end apart: 13, of which 7 were waited for; matrix products, arithmetic and copies ran while one was open for 4% of the time, Pallas kernels for 11%

profile of v12, /device:TPU:21, one launch (start us, length us, event | category | flops | bytes accessed | tf_op | source)
XLA Modules:
  0.0 105.1 jit_solution(3426937707237409342)
XLA Ops:
  0.0 0.7 convert_bitcast_fusion
  0.7 0.8 pad_maximum_fusion.1
  1.5 1.5 %collective-permute-start = (bf16[1,8,2688]{2,1,0:T(8,128)(2,1)S(1)}, bf16[1,8,2688]{2,1,0:T(8,128)(2,1)S(1)}, u32[]{:S(2)}, u32[]{:S(2)}) collective-permute-start(bf16[1,8,2688]{2,1,0:T(8,128)(2,1)S(1)} %get-tuple-element.21), channel_id=1, source_target_pairs={{0,1},{1,2},{2,3},{3,4},{4,5},{5,6},{6,7},{7,0},{8,9},{9,10},{10,1... | collective-permute-start | bytes 129032 | tf_op jit(solution)/shard_map/ppermute | solution.py:235
  3.0 0.2 collective-permute-start.1
  3.2 0.7 collective-permute-start.2
  3.9 2.5 %collective-permute-start.3 = (bf16[1,8,2688]{2,1,0:T(8,128)(2,1)S(1)}, bf16[1,8,2688]{2,1,0:T(8,128)(2,1)S(1)}, u32[]{:S(2)}, u32[]{:S(2)}) collective-permute-start(bf16[1,8,2688]{2,1,0:T(8,128)(2,1)S(1)} %get-tuple-element.21), channel_id=1, source_target_pairs={{0,4},{1,5},{2,6},{3,7},{4,0},{5,1},{6,2},{7,3},{8,12},{9,13},{10,... | collective-permute-start | bytes 129032 | tf_op jit(solution)/shard_map/ppermute | solution.py:235
  6.3 1.0 collective-permute-start.4
  7.4 1.0 fusion.16
  8.4 0.7 pad_dynamic-slice_fusion
  9.7 0.9 collective-permute-start.5
  10.5 0.2 collective-permute-start.6
  10.8 0.5 collective-permute-done.4
  11.3 1.7 %collective-permute-done.5 = bf16[1,8,2688]{2,1,0:T(8,128)(2,1)S(1)} collective-permute-done((bf16[1,8,2688]{2,1,0:T(8,128)(2,1)S(1)}, bf16[1,8,2688]{2,1,0:T(8,128)(2,1)S(1)}, u32[]{:S(2)}, u32[]{:S(2)}) %collective-permute-start.5) | collective-permute-done | bytes 43040 | tf_op jit(solution)/shard_map/ppermute | solution.py:235
  13.0 1.0 collective-permute-done.6
  14.1 0.2 convolution_convert_fusion
  14.4 3.5 %collective-permute-start.7 = (bf16[24,2560]{1,0:T(8,128)(2,1)S(1)}, bf16[24,2560]{1,0:T(8,128)(2,1)S(1)}, u32[]{:S(2)}, u32[]{:S(2)}) collective-permute-start(bf16[24,2560]{1,0:T(8,128)(2,1)S(1)} %convolution_convert_fusion), channel_id=1, source_target_pairs={{0,8},{8,16},{16,24},{24,32},{32,40},{40,48},{48,56},{56,64},{64,7... | collective-permute-start | bytes 368648 | tf_op jit(solution)/shard_map/ppermute | solution.py:20
  18.0 0.7 reshape.102.keep_ref
  18.7 0.6 reshape.98.refs_2_
  19.3 4.5 %collective-permute-done.7 = bf16[24,2560]{1,0:T(8,128)(2,1)S(1)} collective-permute-done((bf16[24,2560]{1,0:T(8,128)(2,1)S(1)}, bf16[24,2560]{1,0:T(8,128)(2,1)S(1)}, u32[]{:S(2)}, u32[]{:S(2)}) %collective-permute-start.7) | collective-permute-done | bytes 122912 | tf_op jit(solution)/shard_map/ppermute | solution.py:20
  23.7 1.6 %reshape.96 = bf16[8,6,160,16]{3,2,1,0:T(8,128)(2,1)S(1)} reshape(bf16[48,2560]{1,0:T(8,128)(2,1)S(1)} %pad_maximum_fusion) | data formatting | bytes 491520 | tf_op jit(solution)/shard_map/reshape | solution.py:248
  25.3 1.0 copy.20
  26.3 0.1 slice_dynamic-update-slice_fusion.14
  26.5 0.1 slice_dynamic-update-slice_fusion.13
  26.6 0.1 slice_dynamic-update-slice_fusion.12
  26.8 0.1 slice_dynamic-update-slice_fusion.11
  26.9 0.2 slice_dynamic-update-slice_fusion.10
  27.1 0.2 slice_dynamic-update-slice_fusion.9
  27.5 0.1 slice_dynamic-update-slice_fusion.23
  27.8 0.2 slice_dynamic-update-slice_fusion.21
  28.1 0.1 slice_dynamic-update-slice_fusion.17
  28.4 0.1 slice_dynamic-update-slice_fusion.15
  28.6 1.3 %fusion.18 = f32[6,4,160,384]{3,2,1,0:T(8,128)S(1)} fusion(bf16[6,4,160,144]{2,3,1,0:T(8,128)(2,1)S(1)} %slice_dynamic-update-slice_fusion.15, bf16[144,384,1,1]{1,0,3,2:T(8,128)(2,1)S(1)} %bitcast.40), kind=kOutput, calls=%fused_computation.73 | convolution fusion | flops 424673280 | bytes 7114752 | tf_op jit(solution)/shard_map/dot_general | solution.py:60
  29.8 1.3 %fusion.17 = f32[6,4,160,384]{3,2,1,0:T(8,128)S(1)} fusion(bf16[6,4,160,144]{2,3,1,0:T(8,128)(2,1)S(1)} %get-tuple-element.14, bf16[144,384,1,1]{1,0,3,2:T(8,128)(2,1)S(1)} %bitcast.39), kind=kOutput, calls=%fused_computation.72 | convolution fusion | flops 424673280 | bytes 7114752 | tf_op jit(solution)/shard_map/dot_general | solution.py:60
  31.1 3.1 %fusion = (f32[6,4,160]{2,1,0:T(4,128)S(1)}, bf16[6,4,160,384]{3,2,1,0:T(8,128)(2,1)S(1)}) fusion(bf16[6,4,160,144]{2,3,1,0:T(8,128)(2,1)S(1)} %get-tuple-element.7, bf16[144,384,1,1]{1,0,3,2:T(8,128)(2,1)S(1)} %bitcast.38, f32[6,4,160,384]{3,2,1,0:T(8,128)S(1)} %fusion.18, pred[6]{0:T(512)(128)(4,1)S(1)} %get-tuple-element.24, ...), kind=kOutput, calls=%fused_computation.2 | convolution fusion | flops 436465920 | bytes 15977484 | tf_op jit(solution)/shard_map/dot_general | solution.py:60
  34.3 3.2 %fusion.8.refs_0_ = bf16[6,4,160,384]{3,2,1,0:T(8,128)(2,1)} fusion(bf16[6,4,160,384]{3,2,1,0:T(8,128)(2,1)S(1)} %get-tuple-element.28.refs_4_.refs_7_, f32[384]{0:T(512)S(1)} %copy-done.4, f32[6,4,160]{2,1,0:T(4,128)S(1)} %add_rsqrt_fusion, pred[4]{0:T(512)(128)(4,1)S(1)} %compare_and_fusion.1), kind=kLoop, calls=%fused_computation.12 | loop fusion | flops 13271040 | bytes 5915140 | tf_op jit(solution)/shard_map/jit(_where)/select_n | solution.py:265
  37.4 18.9 %shard_map.82 = bf16[1280,384]{1,0:T(8,128)(2,1)} custom-call(s32[12]{0:T(128)} %reshape.102.keep_ref, bf16[6,4,160,384]{3,2,1,0:T(8,128)(2,1)} %fusion.8.refs_0_, bf16[10368,384]{1,0:T(8,128)(2,1)} %bitcast.43, f32[1,384]{1,0:T(1,128)} %reshape.98.refs_2_), custom_call_target="tpu_custom_call" | custom-call | flops 10192158720 | bytes 10911744 | tf_op jit(solution)/shard_map/pallas_call | solution.py:182
  56.3 1.4 %fusion.15 = (bf16[4,1,160,384]{3,2,1,0:T(8,128)(2,1)S(1)}, bf16[4,1,160,384]{3,2,1,0:T(8,128)(2,1)S(1)}) fusion(bf16[4,2,160,384]{3,2,1,0:T(8,128)(2,1)} %bitcast.34), kind=kLoop, calls=%fused_computation.70 | loop fusion | bytes 1966080 | tf_op jit(solution)/shard_map/slice | solution.py:281
  57.7 4.6 %collective-permute-start.8 = (bf16[4,1,160,384]{3,2,1,0:T(8,128)(2,1)S(1)}, bf16[4,1,160,384]{3,2,1,0:T(8,128)(2,1)S(1)}, u32[]{:S(2)}, u32[]{:S(2)}) collective-permute-start(bf16[4,1,160,384]{3,2,1,0:T(8,128)(2,1)S(1)} %get-tuple-element.6), channel_id=1, source_target_pairs={{0,1},{1,2},{2,3},{3,4},{4,5},{5,6},{6,7},{8,9},{9,10},{10,11},{11... | collective-permute-start | bytes 1474568 | tf_op jit(solution)/shard_map/ppermute | solution.py:20
  62.3 1.9 %collective-permute-start.9 = (bf16[4,1,160,384]{3,2,1,0:T(8,128)(2,1)S(1)}, bf16[4,1,160,384]{3,2,1,0:T(8,128)(2,1)S(1)}, u32[]{:S(2)}, u32[]{:S(2)}) collective-permute-start(bf16[4,1,160,384]{3,2,1,0:T(8,128)(2,1)S(1)} %get-tuple-element.5), channel_id=1, source_target_pairs={{1,0},{2,1},{3,2},{4,3},{5,4},{6,5},{7,6},{9,8},{10,9},{11,10},{12... | collective-permute-start | bytes 1474568 | tf_op jit(solution)/shard_map/ppermute | solution.py:20
  64.3 1.9 %collective-permute-start.10 = (bf16[2,2,160,384]{3,2,1,0:T(8,128)(2,1)S(1)}, bf16[2,2,160,384]{3,2,1,0:T(8,128)(2,1)S(1)}, u32[]{:S(2)}, u32[]{:S(2)}) collective-permute-start(bf16[2,2,160,384]{3,2,1,0:T(8,128)(2,1)S(1)} %bitcast.37), channel_id=1, source_target_pairs={{0,8},{8,16},{16,24},{24,32},{32,40},{40,48},{48,56},{56,64},{64,7... | collective-permute-start | bytes 1474568 | tf_op jit(solution)/shard_map/ppermute | solution.py:20
  66.3 1.8 %collective-permute-done.8.refs_1_ = bf16[4,1,160,384]{3,2,1,0:T(8,128)(2,1)S(1)} collective-permute-done((bf16[4,1,160,384]{3,2,1,0:T(8,128)(2,1)S(1)}, bf16[4,1,160,384]{3,2,1,0:T(8,128)(2,1)S(1)}, u32[]{:S(2)}, u32[]{:S(2)}) %collective-permute-start.8) | collective-permute-done | bytes 491552 | tf_op jit(solution)/shard_map/ppermute | solution.py:20
  68.1 1.9 %collective-permute-start.11 = (bf16[2,1,160,384]{3,2,1,0:T(8,128)(2,1)S(1)}, bf16[2,1,160,384]{3,2,1,0:T(8,128)(2,1)S(1)}, u32[]{:S(2)}, u32[]{:S(2)}) collective-permute-start(bf16[2,1,160,384]{3,2,1,0:T(8,128)(2,1)S(1)} %slice.201), channel_id=1, source_target_pairs={{0,8},{8,16},{16,24},{24,32},{32,40},{40,48},{48,56},{56,64},{64,7... | collective-permute-start | bytes 737288 | tf_op jit(solution)/shard_map/ppermute | solution.py:20
  70.0 2.7 %collective-permute-done.9.refs_2_ = bf16[4,1,160,384]{3,2,1,0:T(8,128)(2,1)S(1)} collective-permute-done((bf16[4,1,160,384]{3,2,1,0:T(8,128)(2,1)S(1)}, bf16[4,1,160,384]{3,2,1,0:T(8,128)(2,1)S(1)}, u32[]{:S(2)}, u32[]{:S(2)}) %collective-permute-start.9) | collective-permute-done | bytes 491552 | tf_op jit(solution)/shard_map/ppermute | solution.py:20
  72.8 2.1 %collective-permute-start.12 = (bf16[2,1,160,384]{3,2,1,0:T(8,128)(2,1)S(1)}, bf16[2,1,160,384]{3,2,1,0:T(8,128)(2,1)S(1)}, u32[]{:S(2)}, u32[]{:S(2)}) collective-permute-start(bf16[2,1,160,384]{3,2,1,0:T(8,128)(2,1)S(1)} %slice.202), channel_id=1, source_target_pairs={{0,8},{8,16},{16,24},{24,32},{32,40},{40,48},{48,56},{56,64},{64,7... | collective-permute-start | bytes 737288 | tf_op jit(solution)/shard_map/ppermute | solution.py:20
  75.0 11.9 %shard_map.83.refs_8_ = bf16[1280,384]{1,0:T(8,128)(2,1)} custom-call(s32[12]{0:T(128)} %reshape.102.keep_ref, bf16[4,2,160,384]{3,2,1,0:T(8,128)(2,1)} %bitcast.35, bf16[4,1,160,384]{3,2,1,0:T(8,128)(2,1)} %copy-done.2, bf16[4,1,160,384]{3,2,1,0:T(8,128)(2,1)} %copy-done.3, bf16[10368,384]{1,0:T(8,128)(2,1)} %bitcast.44, bf16[6,4,160,384]{3,2,1,0:T(8,128)(2,1)} %copy-done), custom_call_target="tpu_custom_call" | custom-call | flops 5096079360 | bytes 9437184 | tf_op jit(solution)/shard_map/pallas_call | solution.py:182
  86.9 5.1 %collective-permute-done.12.refs_5_ = bf16[2,1,160,384]{3,2,1,0:T(8,128)(2,1)S(1)} collective-permute-done((bf16[2,1,160,384]{3,2,1,0:T(8,128)(2,1)S(1)}, bf16[2,1,160,384]{3,2,1,0:T(8,128)(2,1)S(1)}, u32[]{:S(2)}, u32[]{:S(2)}) %collective-permute-start.12) | collective-permute-done | bytes 245792 | tf_op jit(solution)/shard_map/ppermute | solution.py:20
  92.0 0.7 copy-done.8
  92.7 12.2 %shard_map.84 = bf16[1280,384]{1,0:T(8,128)(2,1)} custom-call(s32[12]{0:T(128)} %reshape.102.keep_ref, bf16[4,2,160,384]{3,2,1,0:T(8,128)(2,1)} %bitcast.36, bf16[4,1,160,384]{3,2,1,0:T(8,128)(2,1)} %copy-done.2, bf16[4,1,160,384]{3,2,1,0:T(8,128)(2,1)} %copy-done.3, bf16[2,2,160,384]{3,2,1,0:T(8,128)(2,1)} %copy-done.6, ...), custom_call_target="tpu_custom_call", output_to_operand_aliasing={{}: (9, {})} | custom-call | flops 5096079360 | bytes 9437184 | tf_op jit(solution)/shard_map/pallas_call | solution.py:182
  (60 shorter events, 1.6 us)
Async XLA Ops:
  0.0 18.7 %copy-start.5 = (f32[384]{0:T(512)S(1)}, f32[384]{0:T(512)}, u32[]{:S(2)}) copy-start(f32[384]{0:T(512)} %param.14) | copy-start | bytes 4612
  1.5 8.1 %collective-permute-start = (bf16[1,8,2688]{2,1,0:T(8,128)(2,1)S(1)}, bf16[1,8,2688]{2,1,0:T(8,128)(2,1)S(1)}, u32[]{:S(2)}, u32[]{:S(2)}) collective-permute-start(bf16[1,8,2688]{2,1,0:T(8,128)(2,1)S(1)} %get-tuple-element.21), channel_id=1, source_target_pairs={{0,1},{1,2},{2,3},{3,4},{4,5},{5,6},{6,7},{7,0},{8,9},{9,10},{10,1... | collective-permute-start | bytes 129032 | tf_op jit(solution)/shard_map/ppermute | solution.py:235
  3.0 7.5 %collective-permute-start.1 = (bf16[1,8,2688]{2,1,0:T(8,128)(2,1)S(1)}, bf16[1,8,2688]{2,1,0:T(8,128)(2,1)S(1)}, u32[]{:S(2)}, u32[]{:S(2)}) collective-permute-start(bf16[1,8,2688]{2,1,0:T(8,128)(2,1)S(1)} %get-tuple-element.21), channel_id=1, source_target_pairs={{0,2},{1,3},{2,4},{3,5},{4,6},{5,7},{6,0},{7,1},{8,10},{9,11},{10,... | collective-permute-start | bytes 129032 | tf_op jit(solution)/shard_map/ppermute | solution.py:235
  3.2 7.5 %collective-permute-start.2 = (bf16[1,8,2688]{2,1,0:T(8,128)(2,1)S(1)}, bf16[1,8,2688]{2,1,0:T(8,128)(2,1)S(1)}, u32[]{:S(2)}, u32[]{:S(2)}) collective-permute-start(bf16[1,8,2688]{2,1,0:T(8,128)(2,1)S(1)} %get-tuple-element.21), channel_id=1, source_target_pairs={{0,3},{1,4},{2,5},{3,6},{4,7},{5,0},{6,1},{7,2},{8,11},{9,12},{10,... | collective-permute-start | bytes 129032 | tf_op jit(solution)/shard_map/ppermute | solution.py:235
  3.9 6.9 %collective-permute-start.3 = (bf16[1,8,2688]{2,1,0:T(8,128)(2,1)S(1)}, bf16[1,8,2688]{2,1,0:T(8,128)(2,1)S(1)}, u32[]{:S(2)}, u32[]{:S(2)}) collective-permute-start(bf16[1,8,2688]{2,1,0:T(8,128)(2,1)S(1)} %get-tuple-element.21), channel_id=1, source_target_pairs={{0,4},{1,5},{2,6},{3,7},{4,0},{5,1},{6,2},{7,3},{8,12},{9,13},{10,... | collective-permute-start | bytes 129032 | tf_op jit(solution)/shard_map/ppermute | solution.py:235
  6.3 5.0 %collective-permute-start.4 = (bf16[1,8,2688]{2,1,0:T(8,128)(2,1)S(1)}, bf16[1,8,2688]{2,1,0:T(8,128)(2,1)S(1)}, u32[]{:S(2)}, u32[]{:S(2)}) collective-permute-start(bf16[1,8,2688]{2,1,0:T(8,128)(2,1)S(1)} %get-tuple-element.21), channel_id=1, source_target_pairs={{0,5},{1,6},{2,7},{3,0},{4,1},{5,2},{6,3},{7,4},{8,13},{9,14},{10,... | collective-permute-start | bytes 129032 | tf_op jit(solution)/shard_map/ppermute | solution.py:235
  9.7 3.3 %collective-permute-start.5 = (bf16[1,8,2688]{2,1,0:T(8,128)(2,1)S(1)}, bf16[1,8,2688]{2,1,0:T(8,128)(2,1)S(1)}, u32[]{:S(2)}, u32[]{:S(2)}) collective-permute-start(bf16[1,8,2688]{2,1,0:T(8,128)(2,1)S(1)} %get-tuple-element.21), channel_id=1, source_target_pairs={{0,6},{1,7},{2,0},{3,1},{4,2},{5,3},{6,4},{7,5},{8,14},{9,15},{10,... | collective-permute-start | bytes 129032 | tf_op jit(solution)/shard_map/ppermute | solution.py:235
  10.5 3.5 %collective-permute-start.6 = (bf16[1,8,2688]{2,1,0:T(8,128)(2,1)S(1)}, bf16[1,8,2688]{2,1,0:T(8,128)(2,1)S(1)}, u32[]{:S(2)}, u32[]{:S(2)}) collective-permute-start(bf16[1,8,2688]{2,1,0:T(8,128)(2,1)S(1)} %get-tuple-element.21), channel_id=1, source_target_pairs={{0,7},{1,0},{2,1},{3,2},{4,3},{5,4},{6,5},{7,6},{8,15},{9,8},{10,9... | collective-permute-start | bytes 129032 | tf_op jit(solution)/shard_map/ppermute | solution.py:235
  14.4 9.3 %collective-permute-start.7 = (bf16[24,2560]{1,0:T(8,128)(2,1)S(1)}, bf16[24,2560]{1,0:T(8,128)(2,1)S(1)}, u32[]{:S(2)}, u32[]{:S(2)}) collective-permute-start(bf16[24,2560]{1,0:T(8,128)(2,1)S(1)} %convolution_convert_fusion), channel_id=1, source_target_pairs={{0,8},{8,16},{16,24},{24,32},{32,40},{40,48},{48,56},{56,64},{64,7... | collective-permute-start | bytes 368648 | tf_op jit(solution)/shard_map/ppermute | solution.py:20
  31.1 3.2 %copy-start.4 = (f32[384]{0:T(512)S(1)}, f32[384]{0:T(512)}, u32[]{:S(2)}) copy-start(f32[384]{0:T(512)} %param.12) | copy-start | bytes 4612
  34.2 3.2 %copy-start = (bf16[6,4,160,384]{3,2,1,0:T(8,128)(2,1)}, bf16[6,4,160,384]{3,2,1,0:T(8,128)(2,1)S(1)}, u32[]{:S(2)}) copy-start(bf16[6,4,160,384]{3,2,1,0:T(8,128)(2,1)S(1)} %get-tuple-element.28.refs_4_.refs_7_) | copy-start | bytes 8847364
  56.3 8.0 %copy-start.1 = (bf16[1280,384]{1,0:T(8,128)(2,1)S(1)}, bf16[1280,384]{1,0:T(8,128)(2,1)}, u32[]{:S(2)}) copy-start(bf16[1280,384]{1,0:T(8,128)(2,1)} %shard_map.82) | copy-start | bytes 2949124
  57.7 10.4 %collective-permute-start.8 = (bf16[4,1,160,384]{3,2,1,0:T(8,128)(2,1)S(1)}, bf16[4,1,160,384]{3,2,1,0:T(8,128)(2,1)S(1)}, u32[]{:S(2)}, u32[]{:S(2)}) collective-permute-start(bf16[4,1,160,384]{3,2,1,0:T(8,128)(2,1)S(1)} %get-tuple-element.6), channel_id=1, source_target_pairs={{0,1},{1,2},{2,3},{3,4},{4,5},{5,6},{6,7},{8,9},{9,10},{10,11},{11... | collective-permute-start | bytes 1474568 | tf_op jit(solution)/shard_map/ppermute | solution.py:20
  62.3 10.4 %collective-permute-start.9 = (bf16[4,1,160,384]{3,2,1,0:T(8,128)(2,1)S(1)}, bf16[4,1,160,384]{3,2,1,0:T(8,128)(2,1)S(1)}, u32[]{:S(2)}, u32[]{:S(2)}) collective-permute-start(bf16[4,1,160,384]{3,2,1,0:T(8,128)(2,1)S(1)} %get-tuple-element.5), channel_id=1, source_target_pairs={{1,0},{2,1},{3,2},{4,3},{5,4},{6,5},{7,6},{9,8},{10,9},{11,10},{12... | collective-permute-start | bytes 1474568 | tf_op jit(solution)/shard_map/ppermute | solution.py:20
  64.3 22.6 %collective-permute-start.10 = (bf16[2,2,160,384]{3,2,1,0:T(8,128)(2,1)S(1)}, bf16[2,2,160,384]{3,2,1,0:T(8,128)(2,1)S(1)}, u32[]{:S(2)}, u32[]{:S(2)}) collective-permute-start(bf16[2,2,160,384]{3,2,1,0:T(8,128)(2,1)S(1)} %bitcast.37), channel_id=1, source_target_pairs={{0,8},{8,16},{16,24},{24,32},{32,40},{40,48},{48,56},{56,64},{64,7... | collective-permute-start | bytes 1474568 | tf_op jit(solution)/shard_map/ppermute | solution.py:20
  68.1 6.9 %copy-start.2 = (bf16[4,1,160,384]{3,2,1,0:T(8,128)(2,1)}, bf16[4,1,160,384]{3,2,1,0:T(8,128)(2,1)S(1)}, u32[]{:S(2)}) copy-start(bf16[4,1,160,384]{3,2,1,0:T(8,128)(2,1)S(1)} %collective-permute-done.8.refs_1_) | copy-start | bytes 1474564
  68.1 18.8 %collective-permute-start.11 = (bf16[2,1,160,384]{3,2,1,0:T(8,128)(2,1)S(1)}, bf16[2,1,160,384]{3,2,1,0:T(8,128)(2,1)S(1)}, u32[]{:S(2)}, u32[]{:S(2)}) collective-permute-start(bf16[2,1,160,384]{3,2,1,0:T(8,128)(2,1)S(1)} %slice.201), channel_id=1, source_target_pairs={{0,8},{8,16},{16,24},{24,32},{32,40},{40,48},{48,56},{56,64},{64,7... | collective-permute-start | bytes 737288 | tf_op jit(solution)/shard_map/ppermute | solution.py:20
  72.8 2.2 %copy-start.3 = (bf16[4,1,160,384]{3,2,1,0:T(8,128)(2,1)}, bf16[4,1,160,384]{3,2,1,0:T(8,128)(2,1)S(1)}, u32[]{:S(2)}) copy-start(bf16[4,1,160,384]{3,2,1,0:T(8,128)(2,1)S(1)} %collective-permute-done.9.refs_2_) | copy-start | bytes 1474564
  72.8 19.2 %collective-permute-start.12 = (bf16[2,1,160,384]{3,2,1,0:T(8,128)(2,1)S(1)}, bf16[2,1,160,384]{3,2,1,0:T(8,128)(2,1)S(1)}, u32[]{:S(2)}, u32[]{:S(2)}) collective-permute-start(bf16[2,1,160,384]{3,2,1,0:T(8,128)(2,1)S(1)} %slice.202), channel_id=1, source_target_pairs={{0,8},{8,16},{16,24},{24,32},{32,40},{40,48},{48,56},{56,64},{64,7... | collective-permute-start | bytes 737288 | tf_op jit(solution)/shard_map/ppermute | solution.py:20
  86.9 5.1 %copy-start.6 = (bf16[2,2,160,384]{3,2,1,0:T(8,128)(2,1)}, bf16[2,2,160,384]{3,2,1,0:T(8,128)(2,1)S(1)}, u32[]{:S(2)}) copy-start(bf16[2,2,160,384]{3,2,1,0:T(8,128)(2,1)S(1)} %collective-permute-done.10.refs_3_) | copy-start | bytes 1474564
  86.9 5.1 %copy-start.7 = (bf16[2,1,160,384]{3,2,1,0:T(8,128)(2,1)}, bf16[2,1,160,384]{3,2,1,0:T(8,128)(2,1)S(1)}, u32[]{:S(2)}) copy-start(bf16[2,1,160,384]{3,2,1,0:T(8,128)(2,1)S(1)} %collective-permute-done.11.refs_4_) | copy-start | bytes 737284
  92.0 0.7 copy-start.8

commit v13 on v12

--- a/solution.py
+++ b/solution.py
@@ -279,9 +279,13 @@
     last = second_act[frame_count - 2 :]
     from_above = shifted(second_act[:, rows_here - 1 :], "rows", 1)
     from_below = shifted(second_act[:, :1], "rows", -1)
-    prev_mid = shifted(last, "tm", 1)
-    prev_above = shifted(from_above[frame_count - 2 :], "tm", 1)
-    prev_below = shifted(from_below[frame_count - 2 :], "tm", 1)
+    last_ext = jnp.concatenate(
+        [from_above[frame_count - 2 :], last, from_below[frame_count - 2 :]], axis=1
+    )
+    prev_ext = shifted(last_ext, "tm", 1)
+    prev_above = prev_ext[:, :1]
+    prev_mid = prev_ext[:, 1 : 1 + rows_here]
+    prev_below = prev_ext[:, 1 + rows_here :]
     layout = {
         "own": (2, 2 + frame_count, 1, 1 + rows_here),
         "above": (2, 2 + frame_count, 0, 1),

time: 106 us -> 114 us (1.075)
  waiting for transfers between devices: 17.3 us -> 27.3 us
  starting transfers between devices: 23 us -> 19.1 us
    ppermute x6 -> x4, waiting for transfers between devices: 14.1 us -> 24 us  [shifted(): return lax.ppermute(x, axis, pairs)]
    ppermute x6 -> x4, starting transfers between devices: 16.1 us -> 12.3 us  [shifted(): return lax.ppermute(x, axis, pairs)]
    slice x2 -> x4, local copies, waits for them, and re-layouts: 0.05 us -> 1.75 us  [the longest x1 0.86 us: on_device(): prev_below = prev_ext[:, 1 + rows_here:]]
    unnamed x42 -> x36, local copies, waits for them, and re-layouts: 2.34 us -> 1.64 us
  transfers between devices with their start and end apart: 13 -> 11, of which waited for: 7 -> 7; matrix products, arithmetic and copies ran while one was open for 4% -> 3% of each run, Pallas kernels for 11% -> 11%
where the time goes in v13:
time: 114 us; the launch traced here: 112 us
  Pallas kernels  43 us (38%)
  waiting for transfers between devices  27.3 us (24%)
  starting transfers between devices  19.1 us (17%)
  local copies, waits for them, and re-layouts  11.3 us (10%)
  matrix products  5.89 us (5%)
  other arithmetic  5.25 us (5%)
    pallas_call x3, Pallas kernels, conv_call(): pl.pallas_call(functools.partial(conv_kernel, layout=layout, mode=mode, p...  43 us
    ppermute x4, waiting for transfers between devices, shifted(): return lax.ppermute(x, axis, pairs)  24 us
    ppermute x4, starting transfers between devices, shifted(): return lax.ppermute(x, axis, pairs)  12.3 us
    ppermute x7, starting transfers between devices, on_device(): pieces.append(lax.ppermute(packed, 'rows', ring))  6.88 us
    dot_general x3, matrix products, local_conv(): jnp.dot(stacked, weight[tap_time].reshape(9 * channels, outputs), preferr...  5.65 us
    ppermute x7, waiting for transfers between devices, on_device(): pieces.append(lax.ppermute(packed, 'rows', ring))  3.23 us
    select_n x1, other arithmetic, on_device(): jnp.where(row_ok[None, :, None, None], first_act, jnp.zeros((), jnp.bfloa...  3.19 us
    reshape x2, local copies, waits for them, and re-layouts, on_device(): jnp.concatenate([prev_window, own_window], axis=0)  2.59 us
  transfers between devices with their start and end apart: 11, of which 7 were waited for; matrix products, arithmetic and copies ran while one was open for 3% of the time, Pallas kernels for 11%

profile of v13, /device:TPU:21, one launch (start us, length us, event | category | flops | bytes accessed | tf_op | source)
XLA Modules:
  0.0 112.3 jit_solution(16293627395289708023)
XLA Ops:
  0.0 0.7 convert_bitcast_fusion
  0.7 0.8 pad_maximum_fusion.2
  1.5 1.5 %collective-permute-start = (bf16[1,8,2688]{2,1,0:T(8,128)(2,1)S(1)}, bf16[1,8,2688]{2,1,0:T(8,128)(2,1)S(1)}, u32[]{:S(2)}, u32[]{:S(2)}) collective-permute-start(bf16[1,8,2688]{2,1,0:T(8,128)(2,1)S(1)} %get-tuple-element.23), channel_id=1, source_target_pairs={{0,1},{1,2},{2,3},{3,4},{4,5},{5,6},{6,7},{7,0},{8,9},{9,10},{10,1... | collective-permute-start | bytes 129032 | tf_op jit(solution)/shard_map/ppermute | solution.py:235
  3.0 0.2 collective-permute-start.1
  3.2 0.7 collective-permute-start.2
  3.9 2.5 %collective-permute-start.3 = (bf16[1,8,2688]{2,1,0:T(8,128)(2,1)S(1)}, bf16[1,8,2688]{2,1,0:T(8,128)(2,1)S(1)}, u32[]{:S(2)}, u32[]{:S(2)}) collective-permute-start(bf16[1,8,2688]{2,1,0:T(8,128)(2,1)S(1)} %get-tuple-element.23), channel_id=1, source_target_pairs={{0,4},{1,5},{2,6},{3,7},{4,0},{5,1},{6,2},{7,3},{8,12},{9,13},{10,... | collective-permute-start | bytes 129032 | tf_op jit(solution)/shard_map/ppermute | solution.py:235
  6.3 1.0 collective-permute-start.4
  7.4 1.0 fusion.17
  8.4 0.7 pad_dynamic-slice_fusion
  9.7 0.9 collective-permute-start.5
  10.5 0.2 collective-permute-start.6
  10.8 0.5 collective-permute-done.4
  11.3 1.7 %collective-permute-done.5 = bf16[1,8,2688]{2,1,0:T(8,128)(2,1)S(1)} collective-permute-done((bf16[1,8,2688]{2,1,0:T(8,128)(2,1)S(1)}, bf16[1,8,2688]{2,1,0:T(8,128)(2,1)S(1)}, u32[]{:S(2)}, u32[]{:S(2)}) %collective-permute-start.5) | collective-permute-done | bytes 43040 | tf_op jit(solution)/shard_map/ppermute | solution.py:235
  13.0 1.0 collective-permute-done.6
  14.1 0.2 convolution_convert_fusion
  14.4 3.5 %collective-permute-start.7 = (bf16[24,2560]{1,0:T(8,128)(2,1)S(1)}, bf16[24,2560]{1,0:T(8,128)(2,1)S(1)}, u32[]{:S(2)}, u32[]{:S(2)}) collective-permute-start(bf16[24,2560]{1,0:T(8,128)(2,1)S(1)} %convolution_convert_fusion), channel_id=1, source_target_pairs={{0,8},{8,16},{16,24},{24,32},{32,40},{40,48},{48,56},{56,64},{64,7... | collective-permute-start | bytes 368648 | tf_op jit(solution)/shard_map/ppermute | solution.py:20
  18.0 0.7 reshape.102.keep_ref
  18.7 0.6 reshape.98.refs_2_
  19.2 4.5 %collective-permute-done.7 = bf16[24,2560]{1,0:T(8,128)(2,1)S(1)} collective-permute-done((bf16[24,2560]{1,0:T(8,128)(2,1)S(1)}, bf16[24,2560]{1,0:T(8,128)(2,1)S(1)}, u32[]{:S(2)}, u32[]{:S(2)}) %collective-permute-start.7) | collective-permute-done | bytes 122912 | tf_op jit(solution)/shard_map/ppermute | solution.py:20
  23.7 1.6 %reshape.96 = bf16[8,6,160,16]{3,2,1,0:T(8,128)(2,1)S(1)} reshape(bf16[48,2560]{1,0:T(8,128)(2,1)S(1)} %pad_maximum_fusion.1) | data formatting | bytes 491520 | tf_op jit(solution)/shard_map/reshape | solution.py:248
  25.3 1.0 copy.20
  26.3 0.1 slice_dynamic-update-slice_fusion.14
  26.5 0.1 slice_dynamic-update-slice_fusion.13
  26.8 0.1 slice_dynamic-update-slice_fusion.11
  26.9 0.2 slice_dynamic-update-slice_fusion.10
  27.1 0.2 slice_dynamic-update-slice_fusion.9
  27.4 0.1 slice_dynamic-update-slice_fusion.24
  27.5 0.1 slice_dynamic-update-slice_fusion.23
  27.8 0.2 slice_dynamic-update-slice_fusion.21
  28.1 0.1 slice_dynamic-update-slice_fusion.17
  28.4 0.1 slice_dynamic-update-slice_fusion.15
  28.6 1.3 %fusion.19 = f32[6,4,160,384]{3,2,1,0:T(8,128)S(1)} fusion(bf16[6,4,160,144]{2,3,1,0:T(8,128)(2,1)S(1)} %slice_dynamic-update-slice_fusion.15, bf16[144,384,1,1]{1,0,3,2:T(8,128)(2,1)S(1)} %bitcast.40), kind=kOutput, calls=%fused_computation.75 | convolution fusion | flops 424673280 | bytes 7114752 | tf_op jit(solution)/shard_map/dot_general | solution.py:60
  29.8 1.3 %fusion.18 = f32[6,4,160,384]{3,2,1,0:T(8,128)S(1)} fusion(bf16[6,4,160,144]{2,3,1,0:T(8,128)(2,1)S(1)} %get-tuple-element.16, bf16[144,384,1,1]{1,0,3,2:T(8,128)(2,1)S(1)} %bitcast.39), kind=kOutput, calls=%fused_computation.74 | convolution fusion | flops 424673280 | bytes 7114752 | tf_op jit(solution)/shard_map/dot_general | solution.py:60
  31.1 3.1 %fusion = (f32[6,4,160]{2,1,0:T(4,128)S(1)}, bf16[6,4,160,384]{3,2,1,0:T(8,128)(2,1)S(1)}) fusion(bf16[6,4,160,144]{2,3,1,0:T(8,128)(2,1)S(1)} %get-tuple-element.9, bf16[144,384,1,1]{1,0,3,2:T(8,128)(2,1)S(1)} %bitcast.38, f32[6,4,160,384]{3,2,1,0:T(8,128)S(1)} %fusion.19, pred[6]{0:T(512)(128)(4,1)S(1)} %get-tuple-element.26, ...), kind=kOutput, calls=%fused_computation.2 | convolution fusion | flops 436465920 | bytes 15977484 | tf_op jit(solution)/shard_map/dot_general | solution.py:60
  34.3 3.2 %fusion.8.refs_0_ = bf16[6,4,160,384]{3,2,1,0:T(8,128)(2,1)} fusion(bf16[6,4,160,384]{3,2,1,0:T(8,128)(2,1)S(1)} %get-tuple-element.30.refs_4_.refs_7_, f32[384]{0:T(512)S(1)} %copy-done.4, f32[6,4,160]{2,1,0:T(4,128)S(1)} %add_rsqrt_fusion, pred[4]{0:T(512)(128)(4,1)S(1)} %compare_and_fusion.1), kind=kLoop, calls=%fused_computation.12 | loop fusion | flops 13271040 | bytes 5915140 | tf_op jit(solution)/shard_map/jit(_where)/select_n | solution.py:265
  37.5 18.9 %shard_map.82 = bf16[1280,384]{1,0:T(8,128)(2,1)} custom-call(s32[12]{0:T(128)} %reshape.102.keep_ref, bf16[6,4,160,384]{3,2,1,0:T(8,128)(2,1)} %fusion.8.refs_0_, bf16[10368,384]{1,0:T(8,128)(2,1)} %bitcast.43, f32[1,384]{1,0:T(1,128)} %reshape.98.refs_2_), custom_call_target="tpu_custom_call" | custom-call | flops 10192158720 | bytes 10911744 | tf_op jit(solution)/shard_map/pallas_call | solution.py:182
  56.3 1.4 %fusion.16 = (bf16[4,1,160,384]{3,2,1,0:T(8,128)(2,1)S(1)}, bf16[4,1,160,384]{3,2,1,0:T(8,128)(2,1)S(1)}) fusion(bf16[4,2,160,384]{3,2,1,0:T(8,128)(2,1)} %bitcast.34), kind=kLoop, calls=%fused_computation.72 | loop fusion | bytes 1966080 | tf_op jit(solution)/shard_map/slice | solution.py:281
  57.7 4.6 %collective-permute-start.8 = (bf16[4,1,160,384]{3,2,1,0:T(8,128)(2,1)S(1)}, bf16[4,1,160,384]{3,2,1,0:T(8,128)(2,1)S(1)}, u32[]{:S(2)}, u32[]{:S(2)}) collective-permute-start(bf16[4,1,160,384]{3,2,1,0:T(8,128)(2,1)S(1)} %get-tuple-element.8), channel_id=1, source_target_pairs={{0,1},{1,2},{2,3},{3,4},{4,5},{5,6},{6,7},{8,9},{9,10},{10,11},{11... | collective-permute-start | bytes 1474568 | tf_op jit(solution)/shard_map/ppermute | solution.py:20
  62.4 1.9 %collective-permute-start.9 = (bf16[4,1,160,384]{3,2,1,0:T(8,128)(2,1)S(1)}, bf16[4,1,160,384]{3,2,1,0:T(8,128)(2,1)S(1)}, u32[]{:S(2)}, u32[]{:S(2)}) collective-permute-start(bf16[4,1,160,384]{3,2,1,0:T(8,128)(2,1)S(1)} %get-tuple-element.7), channel_id=1, source_target_pairs={{1,0},{2,1},{3,2},{4,3},{5,4},{6,5},{7,6},{9,8},{10,9},{11,10},{12... | collective-permute-start | bytes 1474568 | tf_op jit(solution)/shard_map/ppermute | solution.py:20
  64.4 3.8 %collective-permute-done.8.refs_1_ = bf16[4,1,160,384]{3,2,1,0:T(8,128)(2,1)S(1)} collective-permute-done((bf16[4,1,160,384]{3,2,1,0:T(8,128)(2,1)S(1)}, bf16[4,1,160,384]{3,2,1,0:T(8,128)(2,1)S(1)}, u32[]{:S(2)}, u32[]{:S(2)}) %collective-permute-start.8) | collective-permute-done | bytes 491552 | tf_op jit(solution)/shard_map/ppermute | solution.py:20
  68.1 4.4 %collective-permute-done.9.refs_2_ = bf16[4,1,160,384]{3,2,1,0:T(8,128)(2,1)S(1)} collective-permute-done((bf16[4,1,160,384]{3,2,1,0:T(8,128)(2,1)S(1)}, bf16[4,1,160,384]{3,2,1,0:T(8,128)(2,1)S(1)}, u32[]{:S(2)}, u32[]{:S(2)}) %collective-permute-start.9) | collective-permute-done | bytes 491552 | tf_op jit(solution)/shard_map/ppermute | solution.py:20
  72.5 0.1 pad_maximum_fusion
  72.7 2.1 %collective-permute-start.10 = (bf16[2,4,160,384]{3,2,1,0:T(8,128)(2,1)S(1)}, bf16[2,4,160,384]{3,2,1,0:T(8,128)(2,1)S(1)}, u32[]{:S(2)}, u32[]{:S(2)}) collective-permute-start(bf16[2,4,160,384]{3,2,1,0:T(8,128)(2,1)S(1)} %pad_maximum_fusion), channel_id=1, source_target_pairs={{0,8},{8,16},{16,24},{24,32},{32,40},{40,48},{48,56},{56,64},{64,7... | collective-permute-start | bytes 2949128 | tf_op jit(solution)/shard_map/ppermute | solution.py:20
  74.9 11.9 %shard_map.83.refs_8_ = bf16[1280,384]{1,0:T(8,128)(2,1)} custom-call(s32[12]{0:T(128)} %reshape.102.keep_ref, bf16[4,2,160,384]{3,2,1,0:T(8,128)(2,1)} %bitcast.35, bf16[4,1,160,384]{3,2,1,0:T(8,128)(2,1)} %copy-done.2, bf16[4,1,160,384]{3,2,1,0:T(8,128)(2,1)} %copy-done.3, bf16[10368,384]{1,0:T(8,128)(2,1)} %bitcast.44, bf16[6,4,160,384]{3,2,1,0:T(8,128)(2,1)} %copy-done), custom_call_target="tpu_custom_call" | custom-call | flops 5096079360 | bytes 9437184 | tf_op jit(solution)/shard_map/pallas_call | solution.py:182
  86.8 11.5 %collective-permute-done.10 = bf16[2,4,160,384]{3,2,1,0:T(8,128)(2,1)S(1)} collective-permute-done((bf16[2,4,160,384]{3,2,1,0:T(8,128)(2,1)S(1)}, bf16[2,4,160,384]{3,2,1,0:T(8,128)(2,1)S(1)}, u32[]{:S(2)}, u32[]{:S(2)}) %collective-permute-start.10) | collective-permute-done | bytes 983072 | tf_op jit(solution)/shard_map/ppermute | solution.py:20
  98.2 0.9 fusion.15
  99.1 0.8 slice.215.refs_3_
  99.9 12.2 %shard_map.84 = bf16[1280,384]{1,0:T(8,128)(2,1)} custom-call(s32[12]{0:T(128)} %reshape.102.keep_ref, bf16[4,2,160,384]{3,2,1,0:T(8,128)(2,1)} %bitcast.36, bf16[4,1,160,384]{3,2,1,0:T(8,128)(2,1)} %copy-done.2, bf16[4,1,160,384]{3,2,1,0:T(8,128)(2,1)} %copy-done.3, bf16[2,2,160,384]{3,2,1,0:T(8,128)(2,1)} %slice.215.refs_3_, ...), custom_call_target="tpu_custom_call", output_to_operand_aliasing={{}: (9, {})} | custom-call | flops 5096079360 | bytes 9437184 | tf_op jit(solution)/shard_map/pallas_call | solution.py:182
  (53 shorter events, 1.6 us)
Async XLA Ops:
  0.0 18.7 %copy-start.5 = (f32[384]{0:T(512)S(1)}, f32[384]{0:T(512)}, u32[]{:S(2)}) copy-start(f32[384]{0:T(512)} %param.14) | copy-start | bytes 4612
  1.5 8.1 %collective-permute-start = (bf16[1,8,2688]{2,1,0:T(8,128)(2,1)S(1)}, bf16[1,8,2688]{2,1,0:T(8,128)(2,1)S(1)}, u32[]{:S(2)}, u32[]{:S(2)}) collective-permute-start(bf16[1,8,2688]{2,1,0:T(8,128)(2,1)S(1)} %get-tuple-element.23), channel_id=1, source_target_pairs={{0,1},{1,2},{2,3},{3,4},{4,5},{5,6},{6,7},{7,0},{8,9},{9,10},{10,1... | collective-permute-start | bytes 129032 | tf_op jit(solution)/shard_map/ppermute | solution.py:235
  3.0 7.5 %collective-permute-start.1 = (bf16[1,8,2688]{2,1,0:T(8,128)(2,1)S(1)}, bf16[1,8,2688]{2,1,0:T(8,128)(2,1)S(1)}, u32[]{:S(2)}, u32[]{:S(2)}) collective-permute-start(bf16[1,8,2688]{2,1,0:T(8,128)(2,1)S(1)} %get-tuple-element.23), channel_id=1, source_target_pairs={{0,2},{1,3},{2,4},{3,5},{4,6},{5,7},{6,0},{7,1},{8,10},{9,11},{10,... | collective-permute-start | bytes 129032 | tf_op jit(solution)/shard_map/ppermute | solution.py:235
  3.2 7.5 %collective-permute-start.2 = (bf16[1,8,2688]{2,1,0:T(8,128)(2,1)S(1)}, bf16[1,8,2688]{2,1,0:T(8,128)(2,1)S(1)}, u32[]{:S(2)}, u32[]{:S(2)}) collective-permute-start(bf16[1,8,2688]{2,1,0:T(8,128)(2,1)S(1)} %get-tuple-element.23), channel_id=1, source_target_pairs={{0,3},{1,4},{2,5},{3,6},{4,7},{5,0},{6,1},{7,2},{8,11},{9,12},{10,... | collective-permute-start | bytes 129032 | tf_op jit(solution)/shard_map/ppermute | solution.py:235
  3.9 6.9 %collective-permute-start.3 = (bf16[1,8,2688]{2,1,0:T(8,128)(2,1)S(1)}, bf16[1,8,2688]{2,1,0:T(8,128)(2,1)S(1)}, u32[]{:S(2)}, u32[]{:S(2)}) collective-permute-start(bf16[1,8,2688]{2,1,0:T(8,128)(2,1)S(1)} %get-tuple-element.23), channel_id=1, source_target_pairs={{0,4},{1,5},{2,6},{3,7},{4,0},{5,1},{6,2},{7,3},{8,12},{9,13},{10,... | collective-permute-start | bytes 129032 | tf_op jit(solution)/shard_map/ppermute | solution.py:235
  6.3 5.0 %collective-permute-start.4 = (bf16[1,8,2688]{2,1,0:T(8,128)(2,1)S(1)}, bf16[1,8,2688]{2,1,0:T(8,128)(2,1)S(1)}, u32[]{:S(2)}, u32[]{:S(2)}) collective-permute-start(bf16[1,8,2688]{2,1,0:T(8,128)(2,1)S(1)} %get-tuple-element.23), channel_id=1, source_target_pairs={{0,5},{1,6},{2,7},{3,0},{4,1},{5,2},{6,3},{7,4},{8,13},{9,14},{10,... | collective-permute-start | bytes 129032 | tf_op jit(solution)/shard_map/ppermute | solution.py:235
  9.7 3.3 %collective-permute-start.5 = (bf16[1,8,2688]{2,1,0:T(8,128)(2,1)S(1)}, bf16[1,8,2688]{2,1,0:T(8,128)(2,1)S(1)}, u32[]{:S(2)}, u32[]{:S(2)}) collective-permute-start(bf16[1,8,2688]{2,1,0:T(8,128)(2,1)S(1)} %get-tuple-element.23), channel_id=1, source_target_pairs={{0,6},{1,7},{2,0},{3,1},{4,2},{5,3},{6,4},{7,5},{8,14},{9,15},{10,... | collective-permute-start | bytes 129032 | tf_op jit(solution)/shard_map/ppermute | solution.py:235
  10.5 3.5 %collective-permute-start.6 = (bf16[1,8,2688]{2,1,0:T(8,128)(2,1)S(1)}, bf16[1,8,2688]{2,1,0:T(8,128)(2,1)S(1)}, u32[]{:S(2)}, u32[]{:S(2)}) collective-permute-start(bf16[1,8,2688]{2,1,0:T(8,128)(2,1)S(1)} %get-tuple-element.23), channel_id=1, source_target_pairs={{0,7},{1,0},{2,1},{3,2},{4,3},{5,4},{6,5},{7,6},{8,15},{9,8},{10,9... | collective-permute-start | bytes 129032 | tf_op jit(solution)/shard_map/ppermute | solution.py:235
  14.4 9.3 %collective-permute-start.7 = (bf16[24,2560]{1,0:T(8,128)(2,1)S(1)}, bf16[24,2560]{1,0:T(8,128)(2,1)S(1)}, u32[]{:S(2)}, u32[]{:S(2)}) collective-permute-start(bf16[24,2560]{1,0:T(8,128)(2,1)S(1)} %convolution_convert_fusion), channel_id=1, source_target_pairs={{0,8},{8,16},{16,24},{24,32},{32,40},{40,48},{48,56},{56,64},{64,7... | collective-permute-start | bytes 368648 | tf_op jit(solution)/shard_map/ppermute | solution.py:20
  31.1 3.2 %copy-start.4 = (f32[384]{0:T(512)S(1)}, f32[384]{0:T(512)}, u32[]{:S(2)}) copy-start(f32[384]{0:T(512)} %param.12) | copy-start | bytes 4612
  34.2 3.2 %copy-start = (bf16[6,4,160,384]{3,2,1,0:T(8,128)(2,1)}, bf16[6,4,160,384]{3,2,1,0:T(8,128)(2,1)S(1)}, u32[]{:S(2)}) copy-start(bf16[6,4,160,384]{3,2,1,0:T(8,128)(2,1)S(1)} %get-tuple-element.30.refs_4_.refs_7_) | copy-start | bytes 8847364
  56.3 8.0 %copy-start.1 = (bf16[1280,384]{1,0:T(8,128)(2,1)S(1)}, bf16[1280,384]{1,0:T(8,128)(2,1)}, u32[]{:S(2)}) copy-start(bf16[1280,384]{1,0:T(8,128)(2,1)} %shard_map.82) | copy-start | bytes 2949124
  57.7 10.4 %collective-permute-start.8 = (bf16[4,1,160,384]{3,2,1,0:T(8,128)(2,1)S(1)}, bf16[4,1,160,384]{3,2,1,0:T(8,128)(2,1)S(1)}, u32[]{:S(2)}, u32[]{:S(2)}) collective-permute-start(bf16[4,1,160,384]{3,2,1,0:T(8,128)(2,1)S(1)} %get-tuple-element.8), channel_id=1, source_target_pairs={{0,1},{1,2},{2,3},{3,4},{4,5},{5,6},{6,7},{8,9},{9,10},{10,11},{11... | collective-permute-start | bytes 1474568 | tf_op jit(solution)/shard_map/ppermute | solution.py:20
  62.4 10.1 %collective-permute-start.9 = (bf16[4,1,160,384]{3,2,1,0:T(8,128)(2,1)S(1)}, bf16[4,1,160,384]{3,2,1,0:T(8,128)(2,1)S(1)}, u32[]{:S(2)}, u32[]{:S(2)}) collective-permute-start(bf16[4,1,160,384]{3,2,1,0:T(8,128)(2,1)S(1)} %get-tuple-element.7), channel_id=1, source_target_pairs={{1,0},{2,1},{3,2},{4,3},{5,4},{6,5},{7,6},{9,8},{10,9},{11,10},{12... | collective-permute-start | bytes 1474568 | tf_op jit(solution)/shard_map/ppermute | solution.py:20
  68.1 6.7 %copy-start.2 = (bf16[4,1,160,384]{3,2,1,0:T(8,128)(2,1)}, bf16[4,1,160,384]{3,2,1,0:T(8,128)(2,1)S(1)}, u32[]{:S(2)}) copy-start(bf16[4,1,160,384]{3,2,1,0:T(8,128)(2,1)S(1)} %collective-permute-done.8.refs_1_) | copy-start | bytes 1474564
  72.5 2.3 %copy-start.3 = (bf16[4,1,160,384]{3,2,1,0:T(8,128)(2,1)}, bf16[4,1,160,384]{3,2,1,0:T(8,128)(2,1)S(1)}, u32[]{:S(2)}) copy-start(bf16[4,1,160,384]{3,2,1,0:T(8,128)(2,1)S(1)} %collective-permute-done.9.refs_2_) | copy-start | bytes 1474564
  72.7 25.5 %collective-permute-start.10 = (bf16[2,4,160,384]{3,2,1,0:T(8,128)(2,1)S(1)}, bf16[2,4,160,384]{3,2,1,0:T(8,128)(2,1)S(1)}, u32[]{:S(2)}, u32[]{:S(2)}) collective-permute-start(bf16[2,4,160,384]{3,2,1,0:T(8,128)(2,1)S(1)} %pad_maximum_fusion), channel_id=1, source_target_pairs={{0,8},{8,16},{16,24},{24,32},{32,40},{40,48},{48,56},{56,64},{64,7... | collective-permute-start | bytes 2949128 | tf_op jit(solution)/shard_map/ppermute | solution.py:20

commit v14 on v12

--- a/solution.py
+++ b/solution.py
@@ -120,9 +120,13 @@
                         j = k * 3 + a
                         for i in range(height):
                             piece = row_of(f + k, a + i)
+                            if k == 2:
+                                kept_piece = piece
+                            else:
+                                kept_piece = jnp.where(kept, piece, jnp.zeros_like(piece))
                             col_ref[
                                 pl.ds(fl * band + i * columns, columns), pl.ds(j * channels, channels)
-                            ] = jnp.where(kept, piece, jnp.zeros_like(piece))
+                            ] = kept_piece
 
     position = lax.broadcasted_iota(jnp.int32, (cells, outputs), 0) % columns
 

time: 106 us -> 106 us (level)
  no operation moved by 1% of the time
where the time goes in v14:
time: 106 us; the launch traced here: 105 us
  Pallas kernels  43 us (41%)
  starting transfers between devices  23 us (22%)
  waiting for transfers between devices  17.3 us (16%)
  local copies, waits for them, and re-layouts  10.3 us (10%)
  matrix products  5.89 us (6%)
  other arithmetic  5.07 us (5%)
    pallas_call x3, Pallas kernels, conv_call(): pl.pallas_call(functools.partial(conv_kernel, layout=layout, mode=mode, p...  43 us
    ppermute x6, starting transfers between devices, shifted(): return lax.ppermute(x, axis, pairs)  16.1 us
    ppermute x6, waiting for transfers between devices, shifted(): return lax.ppermute(x, axis, pairs)  14.1 us
    ppermute x7, starting transfers between devices, on_device(): pieces.append(lax.ppermute(packed, 'rows', ring))  6.88 us
    dot_general x3, matrix products, local_conv(): jnp.dot(stacked, weight[tap_time].reshape(9 * channels, outputs), preferr...  5.65 us
    ppermute x7, waiting for transfers between devices, on_device(): pieces.append(lax.ppermute(packed, 'rows', ring))  3.23 us
    select_n x1, other arithmetic, on_device(): jnp.where(row_ok[None, :, None, None], first_act, jnp.zeros((), jnp.bfloa...  3.15 us
    reshape x2, local copies, waits for them, and re-layouts, on_device(): jnp.concatenate([prev_window, own_window], axis=0)  2.59 us
  transfers between devices with their start and end apart: 13, of which 7 were waited for; matrix products, arithmetic and copies ran while one was open for 4% of the time, Pallas kernels for 11%

profile of v14, /device:TPU:21, one launch (start us, length us, event | category | flops | bytes accessed | tf_op | source)
XLA Modules:
  0.0 105.1 jit_solution(17659176951451237487)
XLA Ops:
  0.0 0.7 convert_bitcast_fusion
  0.7 0.8 pad_maximum_fusion.1
  1.5 1.5 %collective-permute-start = (bf16[1,8,2688]{2,1,0:T(8,128)(2,1)S(1)}, bf16[1,8,2688]{2,1,0:T(8,128)(2,1)S(1)}, u32[]{:S(2)}, u32[]{:S(2)}) collective-permute-start(bf16[1,8,2688]{2,1,0:T(8,128)(2,1)S(1)} %get-tuple-element.21), channel_id=1, source_target_pairs={{0,1},{1,2},{2,3},{3,4},{4,5},{5,6},{6,7},{7,0},{8,9},{9,10},{10,1... | collective-permute-start | bytes 129032 | tf_op jit(solution)/shard_map/ppermute | solution.py:239
  3.0 0.2 collective-permute-start.1
  3.2 0.7 collective-permute-start.2
  3.9 2.5 %collective-permute-start.3 = (bf16[1,8,2688]{2,1,0:T(8,128)(2,1)S(1)}, bf16[1,8,2688]{2,1,0:T(8,128)(2,1)S(1)}, u32[]{:S(2)}, u32[]{:S(2)}) collective-permute-start(bf16[1,8,2688]{2,1,0:T(8,128)(2,1)S(1)} %get-tuple-element.21), channel_id=1, source_target_pairs={{0,4},{1,5},{2,6},{3,7},{4,0},{5,1},{6,2},{7,3},{8,12},{9,13},{10,... | collective-permute-start | bytes 129032 | tf_op jit(solution)/shard_map/ppermute | solution.py:239
  6.3 1.0 collective-permute-start.4
  7.4 1.0 fusion.16
  8.4 0.7 pad_dynamic-slice_fusion
  9.7 0.9 collective-permute-start.5
  10.5 0.2 collective-permute-start.6
  10.8 0.5 collective-permute-done.4
  11.3 1.7 %collective-permute-done.5 = bf16[1,8,2688]{2,1,0:T(8,128)(2,1)S(1)} collective-permute-done((bf16[1,8,2688]{2,1,0:T(8,128)(2,1)S(1)}, bf16[1,8,2688]{2,1,0:T(8,128)(2,1)S(1)}, u32[]{:S(2)}, u32[]{:S(2)}) %collective-permute-start.5) | collective-permute-done | bytes 43040 | tf_op jit(solution)/shard_map/ppermute | solution.py:239
  13.0 1.0 collective-permute-done.6
  14.1 0.2 convolution_convert_fusion
  14.4 3.5 %collective-permute-start.7 = (bf16[24,2560]{1,0:T(8,128)(2,1)S(1)}, bf16[24,2560]{1,0:T(8,128)(2,1)S(1)}, u32[]{:S(2)}, u32[]{:S(2)}) collective-permute-start(bf16[24,2560]{1,0:T(8,128)(2,1)S(1)} %convolution_convert_fusion), channel_id=1, source_target_pairs={{0,8},{8,16},{16,24},{24,32},{32,40},{40,48},{48,56},{56,64},{64,7... | collective-permute-start | bytes 368648 | tf_op jit(solution)/shard_map/ppermute | solution.py:20
  18.0 0.7 reshape.102.keep_ref
  18.7 0.6 reshape.98.refs_2_
  19.3 4.5 %collective-permute-done.7 = bf16[24,2560]{1,0:T(8,128)(2,1)S(1)} collective-permute-done((bf16[24,2560]{1,0:T(8,128)(2,1)S(1)}, bf16[24,2560]{1,0:T(8,128)(2,1)S(1)}, u32[]{:S(2)}, u32[]{:S(2)}) %collective-permute-start.7) | collective-permute-done | bytes 122912 | tf_op jit(solution)/shard_map/ppermute | solution.py:20
  23.7 1.6 %reshape.96 = bf16[8,6,160,16]{3,2,1,0:T(8,128)(2,1)S(1)} reshape(bf16[48,2560]{1,0:T(8,128)(2,1)S(1)} %pad_maximum_fusion) | data formatting | bytes 491520 | tf_op jit(solution)/shard_map/reshape | solution.py:252
  25.3 1.0 copy.20
  26.3 0.1 slice_dynamic-update-slice_fusion.14
  26.5 0.1 slice_dynamic-update-slice_fusion.13
  26.6 0.1 slice_dynamic-update-slice_fusion.12
  26.8 0.1 slice_dynamic-update-slice_fusion.11
  26.9 0.2 slice_dynamic-update-slice_fusion.10
  27.1 0.2 slice_dynamic-update-slice_fusion.9
  27.5 0.1 slice_dynamic-update-slice_fusion.23
  27.8 0.2 slice_dynamic-update-slice_fusion.21
  28.1 0.1 slice_dynamic-update-slice_fusion.17
  28.4 0.1 slice_dynamic-update-slice_fusion.15
  28.6 1.3 %fusion.18 = f32[6,4,160,384]{3,2,1,0:T(8,128)S(1)} fusion(bf16[6,4,160,144]{2,3,1,0:T(8,128)(2,1)S(1)} %slice_dynamic-update-slice_fusion.15, bf16[144,384,1,1]{1,0,3,2:T(8,128)(2,1)S(1)} %bitcast.40), kind=kOutput, calls=%fused_computation.73 | convolution fusion | flops 424673280 | bytes 7114752 | tf_op jit(solution)/shard_map/dot_general | solution.py:60
  29.8 1.3 %fusion.17 = f32[6,4,160,384]{3,2,1,0:T(8,128)S(1)} fusion(bf16[6,4,160,144]{2,3,1,0:T(8,128)(2,1)S(1)} %get-tuple-element.14, bf16[144,384,1,1]{1,0,3,2:T(8,128)(2,1)S(1)} %bitcast.39), kind=kOutput, calls=%fused_computation.72 | convolution fusion | flops 424673280 | bytes 7114752 | tf_op jit(solution)/shard_map/dot_general | solution.py:60
  31.1 3.1 %fusion = (f32[6,4,160]{2,1,0:T(4,128)S(1)}, bf16[6,4,160,384]{3,2,1,0:T(8,128)(2,1)S(1)}) fusion(bf16[6,4,160,144]{2,3,1,0:T(8,128)(2,1)S(1)} %get-tuple-element.7, bf16[144,384,1,1]{1,0,3,2:T(8,128)(2,1)S(1)} %bitcast.38, f32[6,4,160,384]{3,2,1,0:T(8,128)S(1)} %fusion.18, pred[6]{0:T(512)(128)(4,1)S(1)} %get-tuple-element.24, ...), kind=kOutput, calls=%fused_computation.2 | convolution fusion | flops 436465920 | bytes 15977484 | tf_op jit(solution)/shard_map/dot_general | solution.py:60
  34.3 3.2 %fusion.8.refs_0_ = bf16[6,4,160,384]{3,2,1,0:T(8,128)(2,1)} fusion(bf16[6,4,160,384]{3,2,1,0:T(8,128)(2,1)S(1)} %get-tuple-element.28.refs_4_.refs_7_, f32[384]{0:T(512)S(1)} %copy-done.4, f32[6,4,160]{2,1,0:T(4,128)S(1)} %add_rsqrt_fusion, pred[4]{0:T(512)(128)(4,1)S(1)} %compare_and_fusion.1), kind=kLoop, calls=%fused_computation.12 | loop fusion | flops 13271040 | bytes 5915140 | tf_op jit(solution)/shard_map/jit(_where)/select_n | solution.py:269
  37.4 18.9 %shard_map.82 = bf16[1280,384]{1,0:T(8,128)(2,1)} custom-call(s32[12]{0:T(128)} %reshape.102.keep_ref, bf16[6,4,160,384]{3,2,1,0:T(8,128)(2,1)} %fusion.8.refs_0_, bf16[10368,384]{1,0:T(8,128)(2,1)} %bitcast.43, f32[1,384]{1,0:T(1,128)} %reshape.98.refs_2_), custom_call_target="tpu_custom_call" | custom-call | flops 10192158720 | bytes 10911744 | tf_op jit(solution)/shard_map/pallas_call | solution.py:186
  56.3 1.4 %fusion.15 = (bf16[4,1,160,384]{3,2,1,0:T(8,128)(2,1)S(1)}, bf16[4,1,160,384]{3,2,1,0:T(8,128)(2,1)S(1)}) fusion(bf16[4,2,160,384]{3,2,1,0:T(8,128)(2,1)} %bitcast.34), kind=kLoop, calls=%fused_computation.70 | loop fusion | bytes 1966080 | tf_op jit(solution)/shard_map/slice | solution.py:285
  57.7 4.6 %collective-permute-start.8 = (bf16[4,1,160,384]{3,2,1,0:T(8,128)(2,1)S(1)}, bf16[4,1,160,384]{3,2,1,0:T(8,128)(2,1)S(1)}, u32[]{:S(2)}, u32[]{:S(2)}) collective-permute-start(bf16[4,1,160,384]{3,2,1,0:T(8,128)(2,1)S(1)} %get-tuple-element.6), channel_id=1, source_target_pairs={{0,1},{1,2},{2,3},{3,4},{4,5},{5,6},{6,7},{8,9},{9,10},{10,11},{11... | collective-permute-start | bytes 1474568 | tf_op jit(solution)/shard_map/ppermute | solution.py:20
  62.3 1.9 %collective-permute-start.9 = (bf16[4,1,160,384]{3,2,1,0:T(8,128)(2,1)S(1)}, bf16[4,1,160,384]{3,2,1,0:T(8,128)(2,1)S(1)}, u32[]{:S(2)}, u32[]{:S(2)}) collective-permute-start(bf16[4,1,160,384]{3,2,1,0:T(8,128)(2,1)S(1)} %get-tuple-element.5), channel_id=1, source_target_pairs={{1,0},{2,1},{3,2},{4,3},{5,4},{6,5},{7,6},{9,8},{10,9},{11,10},{12... | collective-permute-start | bytes 1474568 | tf_op jit(solution)/shard_map/ppermute | solution.py:20
  64.3 1.9 %collective-permute-start.10 = (bf16[2,2,160,384]{3,2,1,0:T(8,128)(2,1)S(1)}, bf16[2,2,160,384]{3,2,1,0:T(8,128)(2,1)S(1)}, u32[]{:S(2)}, u32[]{:S(2)}) collective-permute-start(bf16[2,2,160,384]{3,2,1,0:T(8,128)(2,1)S(1)} %bitcast.37), channel_id=1, source_target_pairs={{0,8},{8,16},{16,24},{24,32},{32,40},{40,48},{48,56},{56,64},{64,7... | collective-permute-start | bytes 1474568 | tf_op jit(solution)/shard_map/ppermute | solution.py:20
  66.3 1.8 %collective-permute-done.8.refs_1_ = bf16[4,1,160,384]{3,2,1,0:T(8,128)(2,1)S(1)} collective-permute-done((bf16[4,1,160,384]{3,2,1,0:T(8,128)(2,1)S(1)}, bf16[4,1,160,384]{3,2,1,0:T(8,128)(2,1)S(1)}, u32[]{:S(2)}, u32[]{:S(2)}) %collective-permute-start.8) | collective-permute-done | bytes 491552 | tf_op jit(solution)/shard_map/ppermute | solution.py:20
  68.1 1.9 %collective-permute-start.11 = (bf16[2,1,160,384]{3,2,1,0:T(8,128)(2,1)S(1)}, bf16[2,1,160,384]{3,2,1,0:T(8,128)(2,1)S(1)}, u32[]{:S(2)}, u32[]{:S(2)}) collective-permute-start(bf16[2,1,160,384]{3,2,1,0:T(8,128)(2,1)S(1)} %slice.201), channel_id=1, source_target_pairs={{0,8},{8,16},{16,24},{24,32},{32,40},{40,48},{48,56},{56,64},{64,7... | collective-permute-start | bytes 737288 | tf_op jit(solution)/shard_map/ppermute | solution.py:20
  70.0 2.7 %collective-permute-done.9.refs_2_ = bf16[4,1,160,384]{3,2,1,0:T(8,128)(2,1)S(1)} collective-permute-done((bf16[4,1,160,384]{3,2,1,0:T(8,128)(2,1)S(1)}, bf16[4,1,160,384]{3,2,1,0:T(8,128)(2,1)S(1)}, u32[]{:S(2)}, u32[]{:S(2)}) %collective-permute-start.9) | collective-permute-done | bytes 491552 | tf_op jit(solution)/shard_map/ppermute | solution.py:20
  72.8 2.1 %collective-permute-start.12 = (bf16[2,1,160,384]{3,2,1,0:T(8,128)(2,1)S(1)}, bf16[2,1,160,384]{3,2,1,0:T(8,128)(2,1)S(1)}, u32[]{:S(2)}, u32[]{:S(2)}) collective-permute-start(bf16[2,1,160,384]{3,2,1,0:T(8,128)(2,1)S(1)} %slice.202), channel_id=1, source_target_pairs={{0,8},{8,16},{16,24},{24,32},{32,40},{40,48},{48,56},{56,64},{64,7... | collective-permute-start | bytes 737288 | tf_op jit(solution)/shard_map/ppermute | solution.py:20
  75.0 11.9 %shard_map.83.refs_8_ = bf16[1280,384]{1,0:T(8,128)(2,1)} custom-call(s32[12]{0:T(128)} %reshape.102.keep_ref, bf16[4,2,160,384]{3,2,1,0:T(8,128)(2,1)} %bitcast.35, bf16[4,1,160,384]{3,2,1,0:T(8,128)(2,1)} %copy-done.2, bf16[4,1,160,384]{3,2,1,0:T(8,128)(2,1)} %copy-done.3, bf16[10368,384]{1,0:T(8,128)(2,1)} %bitcast.44, bf16[6,4,160,384]{3,2,1,0:T(8,128)(2,1)} %copy-done), custom_call_target="tpu_custom_call" | custom-call | flops 5096079360 | bytes 9437184 | tf_op jit(solution)/shard_map/pallas_call | solution.py:186
  86.9 5.1 %collective-permute-done.12.refs_5_ = bf16[2,1,160,384]{3,2,1,0:T(8,128)(2,1)S(1)} collective-permute-done((bf16[2,1,160,384]{3,2,1,0:T(8,128)(2,1)S(1)}, bf16[2,1,160,384]{3,2,1,0:T(8,128)(2,1)S(1)}, u32[]{:S(2)}, u32[]{:S(2)}) %collective-permute-start.12) | collective-permute-done | bytes 245792 | tf_op jit(solution)/shard_map/ppermute | solution.py:20
  92.0 0.7 copy-done.8
  92.7 12.2 %shard_map.84 = bf16[1280,384]{1,0:T(8,128)(2,1)} custom-call(s32[12]{0:T(128)} %reshape.102.keep_ref, bf16[4,2,160,384]{3,2,1,0:T(8,128)(2,1)} %bitcast.36, bf16[4,1,160,384]{3,2,1,0:T(8,128)(2,1)} %copy-done.2, bf16[4,1,160,384]{3,2,1,0:T(8,128)(2,1)} %copy-done.3, bf16[2,2,160,384]{3,2,1,0:T(8,128)(2,1)} %copy-done.6, ...), custom_call_target="tpu_custom_call", output_to_operand_aliasing={{}: (9, {})} | custom-call | flops 5096079360 | bytes 9437184 | tf_op jit(solution)/shard_map/pallas_call | solution.py:186
  (60 shorter events, 1.6 us)
Async XLA Ops:
  0.0 18.7 %copy-start.5 = (f32[384]{0:T(512)S(1)}, f32[384]{0:T(512)}, u32[]{:S(2)}) copy-start(f32[384]{0:T(512)} %param.14) | copy-start | bytes 4612
  1.5 8.1 %collective-permute-start = (bf16[1,8,2688]{2,1,0:T(8,128)(2,1)S(1)}, bf16[1,8,2688]{2,1,0:T(8,128)(2,1)S(1)}, u32[]{:S(2)}, u32[]{:S(2)}) collective-permute-start(bf16[1,8,2688]{2,1,0:T(8,128)(2,1)S(1)} %get-tuple-element.21), channel_id=1, source_target_pairs={{0,1},{1,2},{2,3},{3,4},{4,5},{5,6},{6,7},{7,0},{8,9},{9,10},{10,1... | collective-permute-start | bytes 129032 | tf_op jit(solution)/shard_map/ppermute | solution.py:239
  3.0 7.5 %collective-permute-start.1 = (bf16[1,8,2688]{2,1,0:T(8,128)(2,1)S(1)}, bf16[1,8,2688]{2,1,0:T(8,128)(2,1)S(1)}, u32[]{:S(2)}, u32[]{:S(2)}) collective-permute-start(bf16[1,8,2688]{2,1,0:T(8,128)(2,1)S(1)} %get-tuple-element.21), channel_id=1, source_target_pairs={{0,2},{1,3},{2,4},{3,5},{4,6},{5,7},{6,0},{7,1},{8,10},{9,11},{10,... | collective-permute-start | bytes 129032 | tf_op jit(solution)/shard_map/ppermute | solution.py:239
  3.2 7.5 %collective-permute-start.2 = (bf16[1,8,2688]{2,1,0:T(8,128)(2,1)S(1)}, bf16[1,8,2688]{2,1,0:T(8,128)(2,1)S(1)}, u32[]{:S(2)}, u32[]{:S(2)}) collective-permute-start(bf16[1,8,2688]{2,1,0:T(8,128)(2,1)S(1)} %get-tuple-element.21), channel_id=1, source_target_pairs={{0,3},{1,4},{2,5},{3,6},{4,7},{5,0},{6,1},{7,2},{8,11},{9,12},{10,... | collective-permute-start | bytes 129032 | tf_op jit(solution)/shard_map/ppermute | solution.py:239
  3.9 6.9 %collective-permute-start.3 = (bf16[1,8,2688]{2,1,0:T(8,128)(2,1)S(1)}, bf16[1,8,2688]{2,1,0:T(8,128)(2,1)S(1)}, u32[]{:S(2)}, u32[]{:S(2)}) collective-permute-start(bf16[1,8,2688]{2,1,0:T(8,128)(2,1)S(1)} %get-tuple-element.21), channel_id=1, source_target_pairs={{0,4},{1,5},{2,6},{3,7},{4,0},{5,1},{6,2},{7,3},{8,12},{9,13},{10,... | collective-permute-start | bytes 129032 | tf_op jit(solution)/shard_map/ppermute | solution.py:239
  6.3 5.0 %collective-permute-start.4 = (bf16[1,8,2688]{2,1,0:T(8,128)(2,1)S(1)}, bf16[1,8,2688]{2,1,0:T(8,128)(2,1)S(1)}, u32[]{:S(2)}, u32[]{:S(2)}) collective-permute-start(bf16[1,8,2688]{2,1,0:T(8,128)(2,1)S(1)} %get-tuple-element.21), channel_id=1, source_target_pairs={{0,5},{1,6},{2,7},{3,0},{4,1},{5,2},{6,3},{7,4},{8,13},{9,14},{10,... | collective-permute-start | bytes 129032 | tf_op jit(solution)/shard_map/ppermute | solution.py:239
  9.7 3.3 %collective-permute-start.5 = (bf16[1,8,2688]{2,1,0:T(8,128)(2,1)S(1)}, bf16[1,8,2688]{2,1,0:T(8,128)(2,1)S(1)}, u32[]{:S(2)}, u32[]{:S(2)}) collective-permute-start(bf16[1,8,2688]{2,1,0:T(8,128)(2,1)S(1)} %get-tuple-element.21), channel_id=1, source_target_pairs={{0,6},{1,7},{2,0},{3,1},{4,2},{5,3},{6,4},{7,5},{8,14},{9,15},{10,... | collective-permute-start | bytes 129032 | tf_op jit(solution)/shard_map/ppermute | solution.py:239
  10.5 3.5 %collective-permute-start.6 = (bf16[1,8,2688]{2,1,0:T(8,128)(2,1)S(1)}, bf16[1,8,2688]{2,1,0:T(8,128)(2,1)S(1)}, u32[]{:S(2)}, u32[]{:S(2)}) collective-permute-start(bf16[1,8,2688]{2,1,0:T(8,128)(2,1)S(1)} %get-tuple-element.21), channel_id=1, source_target_pairs={{0,7},{1,0},{2,1},{3,2},{4,3},{5,4},{6,5},{7,6},{8,15},{9,8},{10,9... | collective-permute-start | bytes 129032 | tf_op jit(solution)/shard_map/ppermute | solution.py:239
  14.4 9.3 %collective-permute-start.7 = (bf16[24,2560]{1,0:T(8,128)(2,1)S(1)}, bf16[24,2560]{1,0:T(8,128)(2,1)S(1)}, u32[]{:S(2)}, u32[]{:S(2)}) collective-permute-start(bf16[24,2560]{1,0:T(8,128)(2,1)S(1)} %convolution_convert_fusion), channel_id=1, source_target_pairs={{0,8},{8,16},{16,24},{24,32},{32,40},{40,48},{48,56},{56,64},{64,7... | collective-permute-start | bytes 368648 | tf_op jit(solution)/shard_map/ppermute | solution.py:20
  31.1 3.2 %copy-start.4 = (f32[384]{0:T(512)S(1)}, f32[384]{0:T(512)}, u32[]{:S(2)}) copy-start(f32[384]{0:T(512)} %param.12) | copy-start | bytes 4612
  34.2 3.2 %copy-start = (bf16[6,4,160,384]{3,2,1,0:T(8,128)(2,1)}, bf16[6,4,160,384]{3,2,1,0:T(8,128)(2,1)S(1)}, u32[]{:S(2)}) copy-start(bf16[6,4,160,384]{3,2,1,0:T(8,128)(2,1)S(1)} %get-tuple-element.28.refs_4_.refs_7_) | copy-start | bytes 8847364
  56.3 8.0 %copy-start.1 = (bf16[1280,384]{1,0:T(8,128)(2,1)S(1)}, bf16[1280,384]{1,0:T(8,128)(2,1)}, u32[]{:S(2)}) copy-start(bf16[1280,384]{1,0:T(8,128)(2,1)} %shard_map.82) | copy-start | bytes 2949124
  57.7 10.4 %collective-permute-start.8 = (bf16[4,1,160,384]{3,2,1,0:T(8,128)(2,1)S(1)}, bf16[4,1,160,384]{3,2,1,0:T(8,128)(2,1)S(1)}, u32[]{:S(2)}, u32[]{:S(2)}) collective-permute-start(bf16[4,1,160,384]{3,2,1,0:T(8,128)(2,1)S(1)} %get-tuple-element.6), channel_id=1, source_target_pairs={{0,1},{1,2},{2,3},{3,4},{4,5},{5,6},{6,7},{8,9},{9,10},{10,11},{11... | collective-permute-start | bytes 1474568 | tf_op jit(solution)/shard_map/ppermute | solution.py:20
  62.3 10.4 %collective-permute-start.9 = (bf16[4,1,160,384]{3,2,1,0:T(8,128)(2,1)S(1)}, bf16[4,1,160,384]{3,2,1,0:T(8,128)(2,1)S(1)}, u32[]{:S(2)}, u32[]{:S(2)}) collective-permute-start(bf16[4,1,160,384]{3,2,1,0:T(8,128)(2,1)S(1)} %get-tuple-element.5), channel_id=1, source_target_pairs={{1,0},{2,1},{3,2},{4,3},{5,4},{6,5},{7,6},{9,8},{10,9},{11,10},{12... | collective-permute-start | bytes 1474568 | tf_op jit(solution)/shard_map/ppermute | solution.py:20
  64.3 22.6 %collective-permute-start.10 = (bf16[2,2,160,384]{3,2,1,0:T(8,128)(2,1)S(1)}, bf16[2,2,160,384]{3,2,1,0:T(8,128)(2,1)S(1)}, u32[]{:S(2)}, u32[]{:S(2)}) collective-permute-start(bf16[2,2,160,384]{3,2,1,0:T(8,128)(2,1)S(1)} %bitcast.37), channel_id=1, source_target_pairs={{0,8},{8,16},{16,24},{24,32},{32,40},{40,48},{48,56},{56,64},{64,7... | collective-permute-start | bytes 1474568 | tf_op jit(solution)/shard_map/ppermute | solution.py:20
  68.1 6.9 %copy-start.2 = (bf16[4,1,160,384]{3,2,1,0:T(8,128)(2,1)}, bf16[4,1,160,384]{3,2,1,0:T(8,128)(2,1)S(1)}, u32[]{:S(2)}) copy-start(bf16[4,1,160,384]{3,2,1,0:T(8,128)(2,1)S(1)} %collective-permute-done.8.refs_1_) | copy-start | bytes 1474564
  68.1 18.8 %collective-permute-start.11 = (bf16[2,1,160,384]{3,2,1,0:T(8,128)(2,1)S(1)}, bf16[2,1,160,384]{3,2,1,0:T(8,128)(2,1)S(1)}, u32[]{:S(2)}, u32[]{:S(2)}) collective-permute-start(bf16[2,1,160,384]{3,2,1,0:T(8,128)(2,1)S(1)} %slice.201), channel_id=1, source_target_pairs={{0,8},{8,16},{16,24},{24,32},{32,40},{40,48},{48,56},{56,64},{64,7... | collective-permute-start | bytes 737288 | tf_op jit(solution)/shard_map/ppermute | solution.py:20
  72.8 2.2 %copy-start.3 = (bf16[4,1,160,384]{3,2,1,0:T(8,128)(2,1)}, bf16[4,1,160,384]{3,2,1,0:T(8,128)(2,1)S(1)}, u32[]{:S(2)}) copy-start(bf16[4,1,160,384]{3,2,1,0:T(8,128)(2,1)S(1)} %collective-permute-done.9.refs_2_) | copy-start | bytes 1474564
  72.8 19.2 %collective-permute-start.12 = (bf16[2,1,160,384]{3,2,1,0:T(8,128)(2,1)S(1)}, bf16[2,1,160,384]{3,2,1,0:T(8,128)(2,1)S(1)}, u32[]{:S(2)}, u32[]{:S(2)}) collective-permute-start(bf16[2,1,160,384]{3,2,1,0:T(8,128)(2,1)S(1)} %slice.202), channel_id=1, source_target_pairs={{0,8},{8,16},{16,24},{24,32},{32,40},{40,48},{48,56},{56,64},{64,7... | collective-permute-start | bytes 737288 | tf_op jit(solution)/shard_map/ppermute | solution.py:20
  86.9 5.1 %copy-start.6 = (bf16[2,2,160,384]{3,2,1,0:T(8,128)(2,1)}, bf16[2,2,160,384]{3,2,1,0:T(8,128)(2,1)S(1)}, u32[]{:S(2)}) copy-start(bf16[2,2,160,384]{3,2,1,0:T(8,128)(2,1)S(1)} %collective-permute-done.10.refs_3_) | copy-start | bytes 1474564
  86.9 5.1 %copy-start.7 = (bf16[2,1,160,384]{3,2,1,0:T(8,128)(2,1)}, bf16[2,1,160,384]{3,2,1,0:T(8,128)(2,1)S(1)}, u32[]{:S(2)}) copy-start(bf16[2,1,160,384]{3,2,1,0:T(8,128)(2,1)S(1)} %collective-permute-done.11.refs_4_) | copy-start | bytes 737284
  92.0 0.7 copy-start.8
